TPU v7x, 32 devices: a whole 2x2x4 slice. The times are simulated.
32 devices in a mesh: groups: 2 (over y), dom: 4 (over z), section: 4 (over x, core).
Axes of the slice: x: 2, y: 2, z: 4, core: 2. Of those that a mesh axis runs over, the one named last changes fastest.
Arguments:
- node_input: bfloat16 [4, 1024, 512], P('groups', 'dom'), parts along dimension 0, may hold values from -6 to 6
- cotangent: bfloat16 [4, 1024, 512], P('groups', 'dom'), parts along dimension 0, may hold values from -6 to 6
- w_one: bfloat16 [4, 1024, 512], P('section'), may hold values from -0.1875 to 0.1875
- w_two: bfloat16 [4, 512, 512], P('section'), may hold values from -0.25 to 0.25
- gain: float32 [4, 512], P('section'), may hold values from 0.1 to 1.9
- tile_weights: bfloat16 [40, 128, 128], P('dom'), may hold values from -0.25 to 0.25
- tile_rows: int32 [40], P('dom'), may hold values from 0 to 1, as said below
- tile_cols: int32 [40], P('dom'), may hold values from 0 to 3, as said below
- tile_count: int32 [4], P('dom'), may hold values from 4 to 10, as said below
- halo_from_left: int32 [4, 1], replicated, may hold values from 0 to 7, as said below
- halo_from_right: int32 [4, 1], replicated, may hold values from 0 to 7, as said below
Outputs:
- layer_out: bfloat16 [4, 4, 1024, 512], P('section', 'groups', 'dom'), parts along dimension 1
- input_grad: bfloat16 [4, 4, 1024, 512], P('section', 'groups', 'dom'), parts along dimension 1
- grad_w_one: float32 [4, 1024, 1024], P('section', 'dom', 'groups'), parts along dimension 2
- grad_w_two: float32 [4, 512, 1024], P('section', 'dom', 'groups'), parts along dimension 2
- grad_gain: float32 [4, 1024], P('section', ('groups', 'dom')), parts along dimension 1
There are 2 independent parts, one for each index of `groups`. A program takes and returns all parts, laid end to end along the dimension named above; an argument that names none is the same for every part. Nothing has to cross between parts.
Inputs may be any that keep to these rules, and one draw needn't show every extreme that they name: Each partition's own blocks are tile_rows values; slots at or beyond tile_count hold valid but unused entries. `tile_cols`: index into the extended list of a partition: its 1 block from halo_from_left, its own 2 blocks, its 1 block from halo_from_right. `tile_count`: the live slots of a partition come first; some partition uses all 10 slots. `halo_from_left`: row d lists 1 distinct blocks owned by partition (d - 1) mod 4. `halo_from_right`: row d lists 1 distinct blocks owned by partition (d + 1) mod 4.
All inputs are finite; a program needn't handle non-finite values.
Results may differ from a plain program's by a relative error of at most 0.02.
Values may be sent and summed in bfloat16 or wider, within the bound.
No kernel may reach another device: no remote copies, remote signals or barrier semaphores. Data moves between devices by JAX's collectives and lax.ppermute only.
A program may use at most 128 MiB of HBM per device.

v0:
```python
import math

import jax
import jax.numpy as jnp
from jax import lax
from jax.sharding import PartitionSpec as P

EPSILON = 1e-05
HIGHEST_PRECISION = lax.Precision.HIGHEST
F32 = jnp.float32
BF16 = jnp.bfloat16


def pick_blocks(blocks, index, count):
    parts = [lax.dynamic_index_in_dim(blocks, index[i], axis=1, keepdims=False) for i in range(count)]
    return jnp.concatenate(parts, axis=1)


def add_blocks(blocks, index, count, values):
    samples, nb, blk, width = blocks.shape
    values = values.reshape(samples, count, blk, width).astype(F32)
    for i in range(count):
        hit = (jnp.arange(nb) == index[i])[None, :, None, None]
        blocks = blocks + jnp.where(hit, values[:, i][:, None], 0.0)
    return blocks


def shards(
    node_input,
    cotangent,
    w_one,
    w_two,
    gain,
    tile_weights,
    tile_rows,
    tile_cols,
    tile_count,
    halo_from_left,
    halo_from_right,
):
    sections = lax.axis_size("section")
    section_index = lax.axis_index("section")
    domains = lax.axis_size("dom")
    domain_index = lax.axis_index("dom")
    samples, node_rows, width = node_input.shape
    slot_count, blk, _ = tile_weights.shape
    nb = node_rows // blk
    hs = halo_from_left.shape[1]
    ext = nb + 2 * hs
    margin = hs * blk
    offset = domain_index * nb
    send_right = jnp.take(halo_from_left, (domain_index + 1) % domains, axis=0) - offset
    send_left = jnp.take(halo_from_right, (domain_index + domains - 1) % domains, axis=0) - offset

    live = (jnp.arange(slot_count) < tile_count[0]).astype(F32)
    row_oh = (tile_rows[:, None] == jnp.arange(nb)[None, :]).astype(F32) * live[:, None]
    col_oh = (tile_cols[:, None] == jnp.arange(ext)[None, :]).astype(F32)
    pair = (row_oh[:, :, None] * col_oh[:, None, :]).reshape(slot_count, nb * ext)
    adj = jnp.einsum("tp,tij->pij", pair, tile_weights.astype(F32), precision=HIGHEST_PRECISION)
    adj = adj.reshape(nb, ext, blk, blk).transpose(0, 2, 1, 3).reshape(nb * blk, ext * blk)
    adj_hi = adj.astype(BF16)
    adj_lo = (adj - adj_hi.astype(F32)).astype(BF16)
    adj2 = jnp.concatenate([adj_hi, adj_lo], axis=0)

    w_a = w_one[0, :width]
    w_b = w_one[0, width:]
    w_2 = w_two[0]
    gain_row = gain[0]

    dom_up = [(i, (i + 1) % domains) for i in range(domains)]
    dom_down = [((i + 1) % domains, i) for i in range(domains)]
    sec_up = [(i, i + 1) for i in range(sections - 1)]
    sec_down = [(i + 1, i) for i in range(sections - 1)]

    def linear(d, s):
        return d * sections + s

    diag_right = [
        (linear(d, s), linear((d + 1) % domains, s + 1))
        for d in range(domains)
        for s in range(sections - 1)
    ]
    diag_left = [
        (linear(d, s), linear((d + domains - 1) % domains, s + 1))
        for d in range(domains)
        for s in range(sections - 1)
    ]
    diag_down_left = [
        (linear(d, s + 1), linear((d + domains - 1) % domains, s))
        for d in range(domains)
        for s in range(sections - 1)
    ]
    diag_down_right = [
        (linear(d, s + 1), linear((d + 1) % domains, s))
        for d in range(domains)
        for s in range(sections - 1)
    ]
    both = ("dom", "section")

    def forward_layer(h, left, right):
        h_ext = jnp.concatenate([left, h, right], axis=1)
        agg2 = jnp.einsum("ij,sjd->sid", adj2, h_ext, preferred_element_type=F32)
        agg = (agg2[:, : nb * blk] + agg2[:, nb * blk :]).astype(BF16)
        pre = jnp.einsum("sic,ct->sit", h, w_a, preferred_element_type=F32)
        pre = pre + jnp.einsum("sic,ct->sit", agg, w_b, preferred_element_type=F32)
        act = jax.nn.silu(pre).astype(BF16)
        mixed = jnp.einsum("sic,ct->sit", act, w_2, preferred_element_type=F32)
        center = mixed - jnp.mean(mixed, axis=-1, keepdims=True)
        rstd = lax.rsqrt(jnp.mean(center * center, axis=-1, keepdims=True) + EPSILON)
        normed = center * rstd
        out = (h.astype(F32) + normed * gain_row).astype(BF16)
        return out, (h, agg, pre, act, normed, rstd)

    in_blocks = node_input.reshape(samples, nb, blk, width)
    left = lax.ppermute(pick_blocks(in_blocks, send_right, hs), "dom", dom_up)
    right = lax.ppermute(pick_blocks(in_blocks, send_left, hs), "dom", dom_down)
    h = node_input
    saved = None
    saved_out = None
    for tick in range(sections):
        out, res = forward_layer(h, left, right)
        if saved is None:
            saved = res
            saved_out = out
        else:
            mine = section_index == tick
            saved = tuple(jnp.where(mine, a, b) for a, b in zip(res, saved))
            saved_out = jnp.where(mine, out, saved_out)
        if tick + 1 < sections:
            out_blocks = out.reshape(samples, nb, blk, width)
            h = lax.ppermute(out, "section", sec_up)
            left = lax.ppermute(pick_blocks(out_blocks, send_right, hs), both, diag_right)
            right = lax.ppermute(pick_blocks(out_blocks, send_left, hs), both, diag_left)

    h_in, agg, pre, act, normed, rstd = saved

    g = cotangent
    grad_in = None
    dpre_keep = None
    dout_keep = None
    gain_keep = None
    for tick in range(sections):
        gf = g.astype(F32)
        gain_term = jnp.sum(gf * normed, axis=(0, 1))
        dn = gf * gain_row
        dout = (
            rstd
            * (
                dn
                - jnp.mean(dn, axis=-1, keepdims=True)
                - normed * jnp.mean(dn * normed, axis=-1, keepdims=True)
            )
        ).astype(BF16)
        dact = jnp.einsum("sip,vp->siv", dout, w_2, preferred_element_type=F32)
        sig = jax.nn.sigmoid(pre)
        dpre = (dact * sig * (1.0 + pre * (1.0 - sig))).astype(BF16)
        gnode = gf + jnp.einsum("sip,vp->siv", dpre, w_a, preferred_element_type=F32)
        dagg = jnp.einsum("sip,vp->siv", dpre, w_b, preferred_element_type=F32).astype(BF16)
        spread = jnp.einsum(
            "ij,sid->sjd", adj2, jnp.concatenate([dagg, dagg], axis=1), preferred_element_type=F32
        )
        left_grad = spread[:, :margin].astype(BF16)
        right_grad = spread[:, margin + nb * blk :].astype(BF16)
        own = gnode + spread[:, margin : margin + nb * blk]

        def finish(partial, from_right, from_left):
            blocks = partial.reshape(samples, nb, blk, width)
            blocks = add_blocks(blocks, send_right, hs, from_right)
            blocks = add_blocks(blocks, send_left, hs, from_left)
            return blocks.reshape(samples, node_rows, width).astype(BF16)

        g_new = finish(
            own,
            lax.ppermute(left_grad, "dom", dom_down),
            lax.ppermute(right_grad, "dom", dom_up),
        )
        if grad_in is None:
            grad_in, dpre_keep, dout_keep = g_new, dpre, dout
            gain_keep = gain_term
        else:
            mine = section_index == sections - 1 - tick
            grad_in = jnp.where(mine, g_new, grad_in)
            dpre_keep = jnp.where(mine, dpre, dpre_keep)
            dout_keep = jnp.where(mine, dout, dout_keep)
            gain_keep = jnp.where(mine, gain_term, gain_keep)
        if tick + 1 < sections:
            g = finish(
                lax.ppermute(own, "section", sec_down),
                lax.ppermute(left_grad, both, diag_down_left),
                lax.ppermute(right_grad, both, diag_down_right),
            )

    norm_factor = 1.0 / math.sqrt(samples * node_rows * domains)
    stacked = jnp.concatenate([h_in, agg], axis=2)
    gw1 = jnp.einsum("via,vid->ad", stacked, dpre_keep, preferred_element_type=F32)
    gw2 = jnp.einsum("via,vid->ad", act, dout_keep, preferred_element_type=F32)
    r1 = gw1.shape[0] // domains
    r2 = gw2.shape[0] // domains
    r3 = gain_keep.shape[0] // domains
    pad_rows = 16
    gain_rows = jnp.pad(gain_keep.reshape(domains, 1, r3), ((0, 0), (0, pad_rows - 1), (0, width - r3)))
    packed = jnp.concatenate(
        [
            gw1.reshape(domains, r1, width),
            gw2.reshape(domains, r2, width),
            gain_rows,
        ],
        axis=1,
    ).astype(BF16)
    packed = packed.reshape(domains * (r1 + r2 + pad_rows), width)
    reduced = lax.psum_scatter(packed, "dom", scatter_dimension=0, tiled=True)
    reduced = reduced.astype(F32) * norm_factor
    g1 = reduced[:r1]
    g2 = reduced[r1 : r1 + r2]
    g3 = reduced[r1 + r2, :r3]
    return (
        saved_out[None],
        grad_in[None],
        g1[None],
        g2[None],
        g3[None],
    )


def solution(mesh):
    return jax.shard_map(
        shards,
        mesh=mesh,
        in_specs=(
            P("groups", "dom", None),
            P("groups", "dom", None),
            P("section", None, None),
            P("section", None, None),
            P("section", None),
            P("dom", None, None),
            P("dom"),
            P("dom"),
            P("dom"),
            P(),
            P(),
        ),
        out_specs=(
            P("section", "groups", "dom", None),
            P("section", "groups", "dom", None),
            P("section", "dom", "groups"),
            P("section", "dom", "groups"),
            P("section", ("groups", "dom")),
        ),
        check_vma=False,
    )
```

profile of v0, /device:TPU:0, one launch (start us, length us, event | category | flops | bytes accessed | tf_op | source)
XLA Modules:
  0.0 279.9 jit_solution(10211641217494192747)
XLA Ops:
  13.1 5.1 %collective-permute-start.1 = (bf16[2,128,512]{1,2,0:T(8,128)(2,1)}, bf16[2,128,512]{1,2,0:T(8,128)(2,1)}, u32[]{:S(2)}, u32[]{:S(2)}) collective-permute-start(bf16[2,128,512]{1,2,0:T(8,128)(2,1)} %bitcast.11), channel_id=1, source_target_pairs={{4,0},{8,4},{12,8},{0,12},{5,1},{9,5},{13,9},{1,13},{6,2},{10,6},{... | collective-permute-start | bytes 786440 | tf_op jit(solution)/shard_map/ppermute | solution.py:116
  21.1 4.1 %collective-permute-done.1 = bf16[2,128,512]{1,2,0:T(8,128)(2,1)} collective-permute-done((bf16[2,128,512]{1,2,0:T(8,128)(2,1)}, bf16[2,128,512]{1,2,0:T(8,128)(2,1)}, u32[]{:S(2)}, u32[]{:S(2)}) %collective-permute-start.1) | collective-permute-done | bytes 262176 | tf_op jit(solution)/shard_map/ppermute | solution.py:116
  25.2 5.3 %collective-permute-done = bf16[2,128,512]{1,2,0:T(8,128)(2,1)S(1)} collective-permute-done((bf16[2,128,512]{1,2,0:T(8,128)(2,1)}, bf16[2,128,512]{1,2,0:T(8,128)(2,1)S(1)}, u32[]{:S(2)}, u32[]{:S(2)}) %collective-permute-start) | collective-permute-done | bytes 262176 | tf_op jit(solution)/shard_map/ppermute | solution.py:115
  36.9 6.3 %collective-permute-start.4 = (bf16[2,128,512]{2,1,0:T(8,128)(2,1)S(1)}, bf16[2,128,512]{2,1,0:T(8,128)(2,1)S(1)}, u32[]{:S(2)}, u32[]{:S(2)}) collective-permute-start(bf16[2,128,512]{2,1,0:T(8,128)(2,1)S(1)} %get-tuple-element.60), channel_id=1, source_target_pairs={{0,13},{1,14},{2,15},{4,1},{5,2},{6,3},{8,5},{9,6},{10,7},{12,9},{... | collective-permute-start | bytes 786440 | tf_op jit(solution)/shard_map/ppermute | solution.py:133
  44.6 5.4 %collective-permute-done.4 = bf16[2,128,512]{2,1,0:T(8,128)(2,1)S(1)} collective-permute-done((bf16[2,128,512]{2,1,0:T(8,128)(2,1)S(1)}, bf16[2,128,512]{2,1,0:T(8,128)(2,1)S(1)}, u32[]{:S(2)}, u32[]{:S(2)}) %collective-permute-start.4) | collective-permute-done | bytes 262176 | tf_op jit(solution)/shard_map/ppermute | solution.py:133
  49.9 4.8 %collective-permute-done.3 = bf16[2,128,512]{2,1,0:T(8,128)(2,1)S(1)} collective-permute-done((bf16[2,128,512]{2,1,0:T(8,128)(2,1)S(1)}, bf16[2,128,512]{2,1,0:T(8,128)(2,1)S(1)}, u32[]{:S(2)}, u32[]{:S(2)}) %collective-permute-start.3) | collective-permute-done | bytes 262176 | tf_op jit(solution)/shard_map/ppermute | solution.py:132
  61.2 6.4 %collective-permute-start.7 = (bf16[2,128,512]{2,1,0:T(8,128)(2,1)S(1)}, bf16[2,128,512]{2,1,0:T(8,128)(2,1)S(1)}, u32[]{:S(2)}, u32[]{:S(2)}) collective-permute-start(bf16[2,128,512]{2,1,0:T(8,128)(2,1)S(1)} %get-tuple-element.58), channel_id=1, source_target_pairs={{0,13},{1,14},{2,15},{4,1},{5,2},{6,3},{8,5},{9,6},{10,7},{12,9},{... | collective-permute-start | bytes 786440 | tf_op jit(solution)/shard_map/ppermute | solution.py:133
  69.0 5.4 %collective-permute-done.7 = bf16[2,128,512]{2,1,0:T(8,128)(2,1)S(1)} collective-permute-done((bf16[2,128,512]{2,1,0:T(8,128)(2,1)S(1)}, bf16[2,128,512]{2,1,0:T(8,128)(2,1)S(1)}, u32[]{:S(2)}, u32[]{:S(2)}) %collective-permute-start.7) | collective-permute-done | bytes 262176 | tf_op jit(solution)/shard_map/ppermute | solution.py:133
  74.4 4.8 %collective-permute-done.6 = bf16[2,128,512]{2,1,0:T(8,128)(2,1)S(1)} collective-permute-done((bf16[2,128,512]{2,1,0:T(8,128)(2,1)S(1)}, bf16[2,128,512]{2,1,0:T(8,128)(2,1)S(1)}, u32[]{:S(2)}, u32[]{:S(2)}) %collective-permute-start.6) | collective-permute-done | bytes 262176 | tf_op jit(solution)/shard_map/ppermute | solution.py:132
  86.3 7.1 %collective-permute-start.10 = (bf16[2,128,512]{2,1,0:T(8,128)(2,1)}, bf16[2,128,512]{2,1,0:T(8,128)(2,1)}, u32[]{:S(2)}, u32[]{:S(2)}) collective-permute-start(bf16[2,128,512]{2,1,0:T(8,128)(2,1)} %get-tuple-element.56), channel_id=1, source_target_pairs={{0,13},{1,14},{2,15},{4,1},{5,2},{6,3},{8,5},{9,6},{10,7},{12,9},{... | collective-permute-start | bytes 786440 | tf_op jit(solution)/shard_map/ppermute | solution.py:133
  95.4 4.4 %collective-permute-done.10 = bf16[2,128,512]{2,1,0:T(8,128)(2,1)} collective-permute-done((bf16[2,128,512]{2,1,0:T(8,128)(2,1)}, bf16[2,128,512]{2,1,0:T(8,128)(2,1)}, u32[]{:S(2)}, u32[]{:S(2)}) %collective-permute-start.10) | collective-permute-done | bytes 262176 | tf_op jit(solution)/shard_map/ppermute | solution.py:133
  99.8 4.8 %collective-permute-done.9 = bf16[2,128,512]{2,1,0:T(8,128)(2,1)} collective-permute-done((bf16[2,128,512]{2,1,0:T(8,128)(2,1)}, bf16[2,128,512]{2,1,0:T(8,128)(2,1)}, u32[]{:S(2)}, u32[]{:S(2)}) %collective-permute-start.9) | collective-permute-done | bytes 262176 | tf_op jit(solution)/shard_map/ppermute | solution.py:132
  106.6 3.4 %select_select_fusion.2 = (bf16[2,256,512]{2,1,0:T(8,128)(2,1)}, bf16[2,256,512]{2,1,0:T(8,128)(2,1)S(1)}) fusion(pred[]{:T(512)S(6)} %eq.103, pred[]{:T(512)S(6)} %eq.102, pred[]{:T(512)S(6)} %eq.47, f32[2,512,512]{2,1,0:T(8,128)S(1)} %convolution_bitcast_fusion, f32[2,512,512]{2,1,0:T(8,128)} %copy-done.14, f32[2,512,512]{2,1,0:T(8,128)S(1)} %copy-done.13, ...), kind=kLoop, calls=%fused_computation.232 | loop fusion | flops 2883584 | bytes 9437187 | tf_op jit(solution)/shard_map/jit(_where)/select_n | solution.py:127
  123.2 7.7 %collective-permute-done.13 = bf16[2,128,512]{2,1,0:T(8,128)(2,1)S(1)} collective-permute-done((bf16[2,128,512]{2,1,0:T(8,128)(2,1)S(1)}, bf16[2,128,512]{2,1,0:T(8,128)(2,1)S(1)}, u32[]{:S(2)}, u32[]{:S(2)}) %collective-permute-start.13) | collective-permute-done | bytes 262176 | tf_op jit(solution)/shard_map/ppermute | solution.py:190
  141.7 3.3 %collective-permute-start.26 = (bf16[2,128,512]{2,1,0:T(8,128)(2,1)S(1)}, bf16[2,128,512]{2,1,0:T(8,128)(2,1)S(1)}, u32[]{:S(2)}, u32[]{:S(2)}) collective-permute-start(bf16[2,128,512]{2,1,0:T(8,128)(2,1)S(1)} %get-tuple-element.51), channel_id=1, source_target_pairs={{4,0},{8,4},{12,8},{0,12},{5,1},{9,5},{13,9},{1,13},{6,2},{10,6},{... | collective-permute-start | bytes 786440 | tf_op jit(solution)/shard_map/ppermute | solution.py:174
  145.0 11.1 %collective-permute-done.16 = bf16[2,128,512]{2,1,0:T(8,128)(2,1)S(1)} collective-permute-done((bf16[2,128,512]{2,1,0:T(8,128)(2,1)S(1)}, bf16[2,128,512]{2,1,0:T(8,128)(2,1)S(1)}, u32[]{:S(2)}, u32[]{:S(2)}) %collective-permute-start.16) | collective-permute-done | bytes 262176 | tf_op jit(solution)/shard_map/ppermute | solution.py:190
  164.1 3.3 %collective-permute-start.22 = (bf16[2,128,512]{2,1,0:T(8,128)(2,1)S(1)}, bf16[2,128,512]{2,1,0:T(8,128)(2,1)S(1)}, u32[]{:S(2)}, u32[]{:S(2)}) collective-permute-start(bf16[2,128,512]{2,1,0:T(8,128)(2,1)S(1)} %get-tuple-element.47), channel_id=1, source_target_pairs={{4,0},{8,4},{12,8},{0,12},{5,1},{9,5},{13,9},{1,13},{6,2},{10,6},{... | collective-permute-start | bytes 786440 | tf_op jit(solution)/shard_map/ppermute | solution.py:174
  167.5 6.1 %collective-permute-done.24 = bf16[2,128,512]{2,1,0:T(8,128)(2,1)S(1)} collective-permute-done((bf16[2,128,512]{2,1,0:T(8,128)(2,1)S(1)}, bf16[2,128,512]{2,1,0:T(8,128)(2,1)S(1)}, u32[]{:S(2)}, u32[]{:S(2)}) %collective-permute-start.24) | collective-permute-done | bytes 262176 | tf_op jit(solution)/shard_map/ppermute | solution.py:174
  173.7 4.7 %collective-permute-done.23 = bf16[2,128,512]{2,1,0:T(8,128)(2,1)S(1)} collective-permute-done((bf16[2,128,512]{2,1,0:T(8,128)(2,1)S(1)}, bf16[2,128,512]{2,1,0:T(8,128)(2,1)S(1)}, u32[]{:S(2)}, u32[]{:S(2)}) %collective-permute-start.23) | collective-permute-done | bytes 262176 | tf_op jit(solution)/shard_map/ppermute | solution.py:175
  178.4 6.0 %collective-permute-done.22 = bf16[2,128,512]{2,1,0:T(8,128)(2,1)S(1)} collective-permute-done((bf16[2,128,512]{2,1,0:T(8,128)(2,1)S(1)}, bf16[2,128,512]{2,1,0:T(8,128)(2,1)S(1)}, u32[]{:S(2)}, u32[]{:S(2)}) %collective-permute-start.22) | collective-permute-done | bytes 262176 | tf_op jit(solution)/shard_map/ppermute | solution.py:174
  193.3 4.4 %collective-permute-done.19 = bf16[2,128,512]{2,1,0:T(8,128)(2,1)S(1)} collective-permute-done((bf16[2,128,512]{2,1,0:T(8,128)(2,1)}, bf16[2,128,512]{2,1,0:T(8,128)(2,1)S(1)}, u32[]{:S(2)}, u32[]{:S(2)}) %collective-permute-start.19) | collective-permute-done | bytes 262176 | tf_op jit(solution)/shard_map/ppermute | solution.py:190
  211.4 3.3 %collective-permute-start.20 = (bf16[2,128,512]{2,1,0:T(8,128)(2,1)S(1)}, bf16[2,128,512]{2,1,0:T(8,128)(2,1)S(1)}, u32[]{:S(2)}, u32[]{:S(2)}) collective-permute-start(bf16[2,128,512]{2,1,0:T(8,128)(2,1)S(1)} %get-tuple-element.45), channel_id=1, source_target_pairs={{4,0},{8,4},{12,8},{0,12},{5,1},{9,5},{13,9},{1,13},{6,2},{10,6},{... | collective-permute-start | bytes 786440 | tf_op jit(solution)/shard_map/ppermute | solution.py:174
  214.7 4.5 %collective-permute-done.21 = bf16[2,128,512]{2,1,0:T(8,128)(2,1)S(1)} collective-permute-done((bf16[2,128,512]{2,1,0:T(8,128)(2,1)S(1)}, bf16[2,128,512]{2,1,0:T(8,128)(2,1)S(1)}, u32[]{:S(2)}, u32[]{:S(2)}) %collective-permute-start.21) | collective-permute-done | bytes 262176 | tf_op jit(solution)/shard_map/ppermute | solution.py:175
  222.3 47.6 %reduce-scatter.2.cloned.1.call-done = bf16[400,512]{1,0:T(8,128)(2,1)} async-done(((bf16[1600,512]{1,0:T(8,128)(2,1)}), bf16[400,512]{1,0:T(8,128)(2,1)}) %reduce-scatter.2.cloned.1.call-update) | async-done | bytes 409616 | tf_op jit(solution)/shard_map/reduce_scatter | solution.py:211
  (262 shorter events, 93.6 us)
Async XLA Ops:
  7.2 262.6 %reduce-scatter.2.cloned.1.call-start = ((), (), s32[]{:S(2)}) async-start(), calls=%async_computation.1 | async-start | bytes 2048000 | tf_op jit(solution)/shard_map/reduce_scatter | solution.py:211
  13.1 12.1 %collective-permute-start.1 = (bf16[2,128,512]{1,2,0:T(8,128)(2,1)}, bf16[2,128,512]{1,2,0:T(8,128)(2,1)}, u32[]{:S(2)}, u32[]{:S(2)}) collective-permute-start(bf16[2,128,512]{1,2,0:T(8,128)(2,1)} %bitcast.11), channel_id=1, source_target_pairs={{4,0},{8,4},{12,8},{0,12},{5,1},{9,5},{13,9},{1,13},{6,2},{10,6},{... | collective-permute-start | bytes 786440 | tf_op jit(solution)/shard_map/ppermute | solution.py:116
  19.0 11.5 %collective-permute-start = (bf16[2,128,512]{1,2,0:T(8,128)(2,1)}, bf16[2,128,512]{1,2,0:T(8,128)(2,1)S(1)}, u32[]{:S(2)}, u32[]{:S(2)}) collective-permute-start(bf16[2,128,512]{1,2,0:T(8,128)(2,1)} %bitcast.7), channel_id=1, source_target_pairs={{0,4},{4,8},{8,12},{12,0},{1,5},{5,9},{9,13},{13,1},{2,6},{6,10},{... | collective-permute-start | bytes 786440 | tf_op jit(solution)/shard_map/ppermute | solution.py:115
  35.5 19.2 %collective-permute-start.2 = (bf16[2,256,512]{2,1,0:T(8,128)(2,1)S(1)}, bf16[2,256,512]{2,1,0:T(8,128)(2,1)S(1)}, u32[]{:S(2)}, u32[]{:S(2)}) collective-permute-start(bf16[2,256,512]{2,1,0:T(8,128)(2,1)S(1)} %add_convert_fusion.3), channel_id=1, source_target_pairs={{0,1},{1,2},{2,3},{4,5},{5,6},{6,7},{8,9},{9,10},{10,11},{12,13},{... | collective-permute-start | bytes 1572872 | tf_op jit(solution)/shard_map/ppermute | solution.py:131
  36.9 13.0 %collective-permute-start.4 = (bf16[2,128,512]{2,1,0:T(8,128)(2,1)S(1)}, bf16[2,128,512]{2,1,0:T(8,128)(2,1)S(1)}, u32[]{:S(2)}, u32[]{:S(2)}) collective-permute-start(bf16[2,128,512]{2,1,0:T(8,128)(2,1)S(1)} %get-tuple-element.60), channel_id=1, source_target_pairs={{0,13},{1,14},{2,15},{4,1},{5,2},{6,3},{8,5},{9,6},{10,7},{12,9},{... | collective-permute-start | bytes 786440 | tf_op jit(solution)/shard_map/ppermute | solution.py:133
  43.2 11.5 %collective-permute-start.3 = (bf16[2,128,512]{2,1,0:T(8,128)(2,1)S(1)}, bf16[2,128,512]{2,1,0:T(8,128)(2,1)S(1)}, u32[]{:S(2)}, u32[]{:S(2)}) collective-permute-start(bf16[2,128,512]{2,1,0:T(8,128)(2,1)S(1)} %get-tuple-element.59), channel_id=1, source_target_pairs={{0,5},{1,6},{2,7},{4,9},{5,10},{6,11},{8,13},{9,14},{10,15},{12,1}... | collective-permute-start | bytes 786440 | tf_op jit(solution)/shard_map/ppermute | solution.py:132
  58.4 20.7 %collective-permute-start.5 = (bf16[2,256,512]{2,1,0:T(8,128)(2,1)S(1)}, bf16[2,256,512]{2,1,0:T(8,128)(2,1)S(1)}, u32[]{:S(2)}, u32[]{:S(2)}) collective-permute-start(bf16[2,256,512]{2,1,0:T(8,128)(2,1)S(1)} %add_convert_fusion.2), channel_id=1, source_target_pairs={{0,1},{1,2},{2,3},{4,5},{5,6},{6,7},{8,9},{9,10},{10,11},{12,13},{... | collective-permute-start | bytes 1572872 | tf_op jit(solution)/shard_map/ppermute | solution.py:131
  61.2 13.2 %collective-permute-start.7 = (bf16[2,128,512]{2,1,0:T(8,128)(2,1)S(1)}, bf16[2,128,512]{2,1,0:T(8,128)(2,1)S(1)}, u32[]{:S(2)}, u32[]{:S(2)}) collective-permute-start(bf16[2,128,512]{2,1,0:T(8,128)(2,1)S(1)} %get-tuple-element.58), channel_id=1, source_target_pairs={{0,13},{1,14},{2,15},{4,1},{5,2},{6,3},{8,5},{9,6},{10,7},{12,9},{... | collective-permute-start | bytes 786440 | tf_op jit(solution)/shard_map/ppermute | solution.py:133
  67.6 11.5 %collective-permute-start.6 = (bf16[2,128,512]{2,1,0:T(8,128)(2,1)S(1)}, bf16[2,128,512]{2,1,0:T(8,128)(2,1)S(1)}, u32[]{:S(2)}, u32[]{:S(2)}) collective-permute-start(bf16[2,128,512]{2,1,0:T(8,128)(2,1)S(1)} %get-tuple-element.57), channel_id=1, source_target_pairs={{0,5},{1,6},{2,7},{4,9},{5,10},{6,11},{8,13},{9,14},{10,15},{12,1}... | collective-permute-start | bytes 786440 | tf_op jit(solution)/shard_map/ppermute | solution.py:132
  82.8 21.8 %collective-permute-start.8 = (bf16[2,256,512]{2,1,0:T(8,128)(2,1)S(1)}, bf16[2,256,512]{2,1,0:T(8,128)(2,1)S(1)}, u32[]{:S(2)}, u32[]{:S(2)}) collective-permute-start(bf16[2,256,512]{2,1,0:T(8,128)(2,1)S(1)} %add_convert_fusion.1), channel_id=1, source_target_pairs={{0,1},{1,2},{2,3},{4,5},{5,6},{6,7},{8,9},{9,10},{10,11},{12,13},{... | collective-permute-start | bytes 1572872 | tf_op jit(solution)/shard_map/ppermute | solution.py:131
  86.3 13.5 %collective-permute-start.10 = (bf16[2,128,512]{2,1,0:T(8,128)(2,1)}, bf16[2,128,512]{2,1,0:T(8,128)(2,1)}, u32[]{:S(2)}, u32[]{:S(2)}) collective-permute-start(bf16[2,128,512]{2,1,0:T(8,128)(2,1)} %get-tuple-element.56), channel_id=1, source_target_pairs={{0,13},{1,14},{2,15},{4,1},{5,2},{6,3},{8,5},{9,6},{10,7},{12,9},{... | collective-permute-start | bytes 786440 | tf_op jit(solution)/shard_map/ppermute | solution.py:133
  119.2 14.5 %collective-permute-start.11 = (f32[2,256,512]{2,1,0:T(8,128)S(1)}, f32[2,256,512]{2,1,0:T(8,128)S(1)}, u32[]{:S(2)}, u32[]{:S(2)}) collective-permute-start(f32[2,256,512]{2,1,0:T(8,128)S(1)} %fusion.22), channel_id=1, source_target_pairs={{1,0},{2,1},{3,2},{5,4},{6,5},{7,6},{9,8},{10,9},{11,10},{13,12},{... | collective-permute-start | bytes 3145736 | tf_op jit(solution)/shard_map/ppermute | solution.py:188
  121.8 11.8 %collective-permute-start.12 = (bf16[2,128,512]{2,1,0:T(8,128)(2,1)S(1)}, bf16[2,128,512]{2,1,0:T(8,128)(2,1)S(1)}, u32[]{:S(2)}, u32[]{:S(2)}) collective-permute-start(bf16[2,128,512]{2,1,0:T(8,128)(2,1)S(1)} %get-tuple-element.51), channel_id=1, source_target_pairs={{1,12},{2,13},{3,14},{5,0},{6,1},{7,2},{9,4},{10,5},{11,6},{13,8},... | collective-permute-start | bytes 786440 | tf_op jit(solution)/shard_map/ppermute | solution.py:189
  137.1 23.2 %collective-permute-start.14 = (f32[2,256,512]{2,1,0:T(8,128)S(1)}, f32[2,256,512]{2,1,0:T(8,128)S(1)}, u32[]{:S(2)}, u32[]{:S(2)}) collective-permute-start(f32[2,256,512]{2,1,0:T(8,128)S(1)} %fusion.20), channel_id=1, source_target_pairs={{1,0},{2,1},{3,2},{5,4},{6,5},{7,6},{9,8},{10,9},{11,10},{13,12},{... | collective-permute-start | bytes 3145736 | tf_op jit(solution)/shard_map/ppermute | solution.py:188
  138.5 17.6 %collective-permute-start.16 = (bf16[2,128,512]{2,1,0:T(8,128)(2,1)S(1)}, bf16[2,128,512]{2,1,0:T(8,128)(2,1)S(1)}, u32[]{:S(2)}, u32[]{:S(2)}) collective-permute-start(bf16[2,128,512]{2,1,0:T(8,128)(2,1)S(1)} %get-tuple-element.50), channel_id=1, source_target_pairs={{1,4},{2,5},{3,6},{5,8},{6,9},{7,10},{9,12},{10,13},{11,14},{13,0}... | collective-permute-start | bytes 786440 | tf_op jit(solution)/shard_map/ppermute | solution.py:190
  139.8 19.0 %collective-permute-start.15 = (bf16[2,128,512]{2,1,0:T(8,128)(2,1)S(1)}, bf16[2,128,512]{2,1,0:T(8,128)(2,1)S(1)}, u32[]{:S(2)}, u32[]{:S(2)}) collective-permute-start(bf16[2,128,512]{2,1,0:T(8,128)(2,1)S(1)} %get-tuple-element.49), channel_id=1, source_target_pairs={{1,12},{2,13},{3,14},{5,0},{6,1},{7,2},{9,4},{10,5},{11,6},{13,8},... | collective-permute-start | bytes 786440 | tf_op jit(solution)/shard_map/ppermute | solution.py:189
  141.1 23.0 %collective-permute-start.27 = (bf16[2,128,512]{2,1,0:T(8,128)(2,1)S(1)}, bf16[2,128,512]{2,1,0:T(8,128)(2,1)S(1)}, u32[]{:S(2)}, u32[]{:S(2)}) collective-permute-start(bf16[2,128,512]{2,1,0:T(8,128)(2,1)S(1)} %get-tuple-element.52), channel_id=1, source_target_pairs={{0,4},{4,8},{8,12},{12,0},{1,5},{5,9},{9,13},{13,1},{2,6},{6,10},{... | collective-permute-start | bytes 786440 | tf_op jit(solution)/shard_map/ppermute | solution.py:175
  141.7 25.7 %collective-permute-start.26 = (bf16[2,128,512]{2,1,0:T(8,128)(2,1)S(1)}, bf16[2,128,512]{2,1,0:T(8,128)(2,1)S(1)}, u32[]{:S(2)}, u32[]{:S(2)}) collective-permute-start(bf16[2,128,512]{2,1,0:T(8,128)(2,1)S(1)} %get-tuple-element.51), channel_id=1, source_target_pairs={{4,0},{8,4},{12,8},{0,12},{5,1},{9,5},{13,9},{1,13},{6,2},{10,6},{... | collective-permute-start | bytes 786440 | tf_op jit(solution)/shard_map/ppermute | solution.py:174
  156.1 11.4 %collective-permute-start.25 = (bf16[2,128,512]{2,1,0:T(8,128)(2,1)S(1)}, bf16[2,128,512]{2,1,0:T(8,128)(2,1)S(1)}, u32[]{:S(2)}, u32[]{:S(2)}) collective-permute-start(bf16[2,128,512]{2,1,0:T(8,128)(2,1)S(1)} %get-tuple-element.50), channel_id=1, source_target_pairs={{0,4},{4,8},{8,12},{12,0},{1,5},{5,9},{9,13},{13,1},{2,6},{6,10},{... | collective-permute-start | bytes 786440 | tf_op jit(solution)/shard_map/ppermute | solution.py:175
  158.8 14.8 %collective-permute-start.24 = (bf16[2,128,512]{2,1,0:T(8,128)(2,1)S(1)}, bf16[2,128,512]{2,1,0:T(8,128)(2,1)S(1)}, u32[]{:S(2)}, u32[]{:S(2)}) collective-permute-start(bf16[2,128,512]{2,1,0:T(8,128)(2,1)S(1)} %get-tuple-element.49), channel_id=1, source_target_pairs={{4,0},{8,4},{12,8},{0,12},{5,1},{9,5},{13,9},{1,13},{6,2},{10,6},{... | collective-permute-start | bytes 786440 | tf_op jit(solution)/shard_map/ppermute | solution.py:174
  163.5 14.9 %collective-permute-start.23 = (bf16[2,128,512]{2,1,0:T(8,128)(2,1)S(1)}, bf16[2,128,512]{2,1,0:T(8,128)(2,1)S(1)}, u32[]{:S(2)}, u32[]{:S(2)}) collective-permute-start(bf16[2,128,512]{2,1,0:T(8,128)(2,1)S(1)} %get-tuple-element.48), channel_id=1, source_target_pairs={{0,4},{4,8},{8,12},{12,0},{1,5},{5,9},{9,13},{13,1},{2,6},{6,10},{... | collective-permute-start | bytes 786440 | tf_op jit(solution)/shard_map/ppermute | solution.py:175
  164.1 20.3 %collective-permute-start.22 = (bf16[2,128,512]{2,1,0:T(8,128)(2,1)S(1)}, bf16[2,128,512]{2,1,0:T(8,128)(2,1)S(1)}, u32[]{:S(2)}, u32[]{:S(2)}) collective-permute-start(bf16[2,128,512]{2,1,0:T(8,128)(2,1)S(1)} %get-tuple-element.47), channel_id=1, source_target_pairs={{4,0},{8,4},{12,8},{0,12},{5,1},{9,5},{13,9},{1,13},{6,2},{10,6},{... | collective-permute-start | bytes 786440 | tf_op jit(solution)/shard_map/ppermute | solution.py:174
  186.6 13.9 %collective-permute-start.17 = (f32[2,256,512]{2,1,0:T(8,128)}, f32[2,256,512]{2,1,0:T(8,128)}, u32[]{:S(2)}, u32[]{:S(2)}) collective-permute-start(f32[2,256,512]{2,1,0:T(8,128)} %get-tuple-element.82), channel_id=1, source_target_pairs={{1,0},{2,1},{3,2},{5,4},{6,5},{7,6},{9,8},{10,9},{11,10},{13,12},{... | collective-permute-start | bytes 3145736 | tf_op jit(solution)/shard_map/ppermute | solution.py:188
  189.2 11.2 %collective-permute-start.18 = (bf16[2,128,512]{2,1,0:T(8,128)(2,1)}, bf16[2,128,512]{2,1,0:T(8,128)(2,1)S(1)}, u32[]{:S(2)}, u32[]{:S(2)}) collective-permute-start(bf16[2,128,512]{2,1,0:T(8,128)(2,1)} %copy-done.54), channel_id=1, source_target_pairs={{1,12},{2,13},{3,14},{5,0},{6,1},{7,2},{9,4},{10,5},{11,6},{13,8},... | collective-permute-start | bytes 786440 | tf_op jit(solution)/shard_map/ppermute | solution.py:189
  (63 other events, 468.6 us)
Sparse Core Ops, SparseCore 0:
  209.2 60.6 reduce-scatter.1
where the time goes:
time: 281 us; the launch traced here: 280 us
  waiting for transfers between devices  140 us (50%)
  starting transfers between devices  61.1 us (22%)
  matrix products  25.6 us (9%)
  local copies, waits for them, and re-layouts  18.6 us (7%)
  other arithmetic  17.3 us (6%)
  between operations  17.3 us (6%)
    reduce_scatter x1, waiting for transfers between devices, shards(): reduced = lax.psum_scatter(packed, 'dom', scatter_dimension=0, tiled=True)  47.6 us
    ppermute x3, waiting for transfers between devices, shards(): lax.ppermute(right_grad, both, diag_down_right)  23.2 us
    ppermute x3, starting transfers between devices, shards(): lax.ppermute(pick_blocks(out_blocks, send_left, hs), both, diag_left)  19.9 us
    ppermute x3, waiting for transfers between devices, shards(): lax.ppermute(pick_blocks(out_blocks, send_left, hs), both, diag_left)  15.2 us
    ppermute x3, waiting for transfers between devices, shards(): lax.ppermute(pick_blocks(out_blocks, send_right, hs), both, diag_right)  14.3 us
    ppermute x4, waiting for transfers between devices, shards(): lax.ppermute(left_grad, 'dom', dom_down)  13.3 us
    unnamed x121, local copies, waits for them, and re-layouts  11.7 us
    ppermute x4, starting transfers between devices, shards(): lax.ppermute(left_grad, 'dom', dom_down)  11.2 us
  transfers between devices with their start and end apart: 29, of which 20 were waited for; matrix products, arithmetic and copies ran while one was open for 4% of the time, Pallas kernels for 0%

commit v1 on v0

--- a/solution.py
+++ b/solution.py
@@ -23,6 +23,25 @@
         hit = (jnp.arange(nb) == index[i])[None, :, None, None]
         blocks = blocks + jnp.where(hit, values[:, i][:, None], 0.0)
     return blocks
+
+
+def halving_reduce_scatter(x, axis, devices, index):
+    if devices & (devices - 1):
+        return lax.psum_scatter(x, axis, scatter_dimension=0, tiled=True)
+    rows = x.shape[0] // devices
+    cur = x.reshape(devices, rows, x.shape[1]).astype(F32)
+    dist = 1
+    while dist < devices:
+        cur = cur.reshape(cur.shape[0] // 2, 2, rows, x.shape[1])
+        bit = (index // dist) % 2
+        low, high = cur[:, 0], cur[:, 1]
+        keep = jnp.where(bit == 0, low, high)
+        send = jnp.where(bit == 0, high, low).astype(x.dtype)
+        pairs = [(i, i ^ dist) for i in range(devices)]
+        recv = lax.ppermute(send, axis, pairs)
+        cur = keep + recv.astype(F32)
+        dist *= 2
+    return cur[0]
 
 
 def shards(
@@ -208,7 +227,7 @@
         axis=1,
     ).astype(BF16)
     packed = packed.reshape(domains * (r1 + r2 + pad_rows), width)
-    reduced = lax.psum_scatter(packed, "dom", scatter_dimension=0, tiled=True)
+    reduced = halving_reduce_scatter(packed, "dom", domains, domain_index)
     reduced = reduced.astype(F32) * norm_factor
     g1 = reduced[:r1]
     g2 = reduced[r1 : r1 + r2]

time: 281 us -> 270 us (0.961)
  the two profiles are of different devices: /device:TPU:0 before, /device:TPU:2 now
where the time goes in v1:
time: 270 us; the launch traced here: 269 us
  waiting for transfers between devices  140 us (52%)
  starting transfers between devices  61.3 us (23%)
  matrix products  27.8 us (10%)
  local copies, waits for them, and re-layouts  19.3 us (7%)
  other arithmetic  17.3 us (6%)
  between operations  4.08 us (2%)
    ppermute x2, waiting for transfers between devices, halving_reduce_scatter(): recv = lax.ppermute(send, axis, pairs)  31.4 us
    ppermute x3, waiting for transfers between devices, shards(): lax.ppermute(pick_blocks(out_blocks, send_right, hs), both, diag_right)  23 us
    ppermute x3, waiting for transfers between devices, shards(): lax.ppermute(pick_blocks(out_blocks, send_left, hs), both, diag_left)  19.4 us
    ppermute x3, waiting for transfers between devices, shards(): lax.ppermute(left_grad, both, diag_down_left)  14.9 us
    ppermute x4, waiting for transfers between devices, shards(): lax.ppermute(left_grad, 'dom', dom_down)  14.9 us
    ppermute x3, waiting for transfers between devices, shards(): lax.ppermute(right_grad, both, diag_down_right)  13.3 us
    unnamed x131, local copies, waits for them, and re-layouts  12.5 us
    ppermute x4, waiting for transfers between devices, shards(): lax.ppermute(right_grad, 'dom', dom_up)  11.8 us
  transfers between devices with their start and end apart: 30, of which 24 were waited for; matrix products, arithmetic and copies ran while one was open for 5% of the time, Pallas kernels for 0%

profile of v1, /device:TPU:2, one launch (start us, length us, event | category | flops | bytes accessed | tf_op | source)
XLA Modules:
  0.0 269.3 jit_solution(1278301580375179224)
XLA Ops:
  5.9 3.7 %collective-permute-start.1 = (bf16[2,128,512]{1,2,0:T(8,128)(2,1)S(1)}, bf16[2,128,512]{1,2,0:T(8,128)(2,1)}, u32[]{:S(2)}, u32[]{:S(2)}) collective-permute-start(bf16[2,128,512]{1,2,0:T(8,128)(2,1)S(1)} %bitcast.347), channel_id=1, source_target_pairs={{4,0},{8,4},{12,8},{0,12},{5,1},{9,5},{13,9},{1,13},{6,2},{10,6},{... | collective-permute-start | bytes 786440 | tf_op jit(solution)/shard_map/ppermute | solution.py:135
  12.4 3.8 %collective-permute-done.1 = bf16[2,128,512]{1,2,0:T(8,128)(2,1)} collective-permute-done((bf16[2,128,512]{1,2,0:T(8,128)(2,1)S(1)}, bf16[2,128,512]{1,2,0:T(8,128)(2,1)}, u32[]{:S(2)}, u32[]{:S(2)}) %collective-permute-start.1) | collective-permute-done | bytes 262176 | tf_op jit(solution)/shard_map/ppermute | solution.py:135
  16.2 5.5 %collective-permute-done = bf16[2,128,512]{1,2,0:T(8,128)(2,1)} collective-permute-done((bf16[2,128,512]{1,2,0:T(8,128)(2,1)}, bf16[2,128,512]{1,2,0:T(8,128)(2,1)}, u32[]{:S(2)}, u32[]{:S(2)}) %collective-permute-start) | collective-permute-done | bytes 262176 | tf_op jit(solution)/shard_map/ppermute | solution.py:134
  33.9 5.8 %collective-permute-done.4 = bf16[2,128,512]{2,1,0:T(8,128)(2,1)S(1)} collective-permute-done((bf16[2,128,512]{2,1,0:T(8,128)(2,1)S(1)}, bf16[2,128,512]{2,1,0:T(8,128)(2,1)S(1)}, u32[]{:S(2)}, u32[]{:S(2)}) %collective-permute-start.4) | collective-permute-done | bytes 262176 | tf_op jit(solution)/shard_map/ppermute | solution.py:152
  39.7 6.7 %collective-permute-done.3 = bf16[2,128,512]{2,1,0:T(8,128)(2,1)S(1)} collective-permute-done((bf16[2,128,512]{2,1,0:T(8,128)(2,1)S(1)}, bf16[2,128,512]{2,1,0:T(8,128)(2,1)S(1)}, u32[]{:S(2)}, u32[]{:S(2)}) %collective-permute-start.3) | collective-permute-done | bytes 262176 | tf_op jit(solution)/shard_map/ppermute | solution.py:151
  56.0 6.7 %collective-permute-done.7 = bf16[2,128,512]{2,1,0:T(8,128)(2,1)S(1)} collective-permute-done((bf16[2,128,512]{2,1,0:T(8,128)(2,1)S(1)}, bf16[2,128,512]{2,1,0:T(8,128)(2,1)S(1)}, u32[]{:S(2)}, u32[]{:S(2)}) %collective-permute-start.7) | collective-permute-done | bytes 262176 | tf_op jit(solution)/shard_map/ppermute | solution.py:152
  62.7 8.1 %collective-permute-done.6 = bf16[2,128,512]{2,1,0:T(8,128)(2,1)S(1)} collective-permute-done((bf16[2,128,512]{2,1,0:T(8,128)(2,1)S(1)}, bf16[2,128,512]{2,1,0:T(8,128)(2,1)S(1)}, u32[]{:S(2)}, u32[]{:S(2)}) %collective-permute-start.6) | collective-permute-done | bytes 262176 | tf_op jit(solution)/shard_map/ppermute | solution.py:151
  81.2 6.8 %collective-permute-done.10 = bf16[2,128,512]{2,1,0:T(8,128)(2,1)} collective-permute-done((bf16[2,128,512]{2,1,0:T(8,128)(2,1)}, bf16[2,128,512]{2,1,0:T(8,128)(2,1)}, u32[]{:S(2)}, u32[]{:S(2)}) %collective-permute-start.10) | collective-permute-done | bytes 262176 | tf_op jit(solution)/shard_map/ppermute | solution.py:152
  88.1 8.1 %collective-permute-done.9 = bf16[2,128,512]{2,1,0:T(8,128)(2,1)} collective-permute-done((bf16[2,128,512]{2,1,0:T(8,128)(2,1)S(1)}, bf16[2,128,512]{2,1,0:T(8,128)(2,1)}, u32[]{:S(2)}, u32[]{:S(2)}) %collective-permute-start.9) | collective-permute-done | bytes 262176 | tf_op jit(solution)/shard_map/ppermute | solution.py:151
  117.4 3.6 %collective-permute-start.12 = (bf16[2,128,512]{2,1,0:T(8,128)(2,1)S(1)}, bf16[2,128,512]{2,1,0:T(8,128)(2,1)S(1)}, u32[]{:S(2)}, u32[]{:S(2)}) collective-permute-start(bf16[2,128,512]{2,1,0:T(8,128)(2,1)S(1)} %get-tuple-element.51), channel_id=1, source_target_pairs={{1,12},{2,13},{3,14},{5,0},{6,1},{7,2},{9,4},{10,5},{11,6},{13,8},... | collective-permute-start | bytes 786440 | tf_op jit(solution)/shard_map/ppermute | solution.py:208
  121.2 5.8 %collective-permute-done.13 = bf16[2,128,512]{2,1,0:T(8,128)(2,1)S(1)} collective-permute-done((bf16[2,128,512]{2,1,0:T(8,128)(2,1)S(1)}, bf16[2,128,512]{2,1,0:T(8,128)(2,1)S(1)}, u32[]{:S(2)}, u32[]{:S(2)}) %collective-permute-start.13) | collective-permute-done | bytes 262176 | tf_op jit(solution)/shard_map/ppermute | solution.py:209
  127.0 5.5 %collective-permute-done.12 = bf16[2,128,512]{2,1,0:T(8,128)(2,1)S(1)} collective-permute-done((bf16[2,128,512]{2,1,0:T(8,128)(2,1)S(1)}, bf16[2,128,512]{2,1,0:T(8,128)(2,1)S(1)}, u32[]{:S(2)}, u32[]{:S(2)}) %collective-permute-start.12) | collective-permute-done | bytes 262176 | tf_op jit(solution)/shard_map/ppermute | solution.py:208
  136.1 3.7 %collective-permute-start.14 = (f32[2,256,512]{2,1,0:T(8,128)S(1)}, f32[2,256,512]{2,1,0:T(8,128)S(1)}, u32[]{:S(2)}, u32[]{:S(2)}) collective-permute-start(f32[2,256,512]{2,1,0:T(8,128)S(1)} %fusion.19), channel_id=1, source_target_pairs={{1,0},{2,1},{3,2},{5,4},{6,5},{7,6},{9,8},{10,9},{11,10},{13,12},{... | collective-permute-start | bytes 3145736 | tf_op jit(solution)/shard_map/ppermute | solution.py:207
  142.7 3.6 %collective-permute-start.15 = (bf16[2,128,512]{2,1,0:T(8,128)(2,1)S(1)}, bf16[2,128,512]{2,1,0:T(8,128)(2,1)S(1)}, u32[]{:S(2)}, u32[]{:S(2)}) collective-permute-start(bf16[2,128,512]{2,1,0:T(8,128)(2,1)S(1)} %get-tuple-element.49), channel_id=1, source_target_pairs={{1,12},{2,13},{3,14},{5,0},{6,1},{7,2},{9,4},{10,5},{11,6},{13,8},... | collective-permute-start | bytes 786440 | tf_op jit(solution)/shard_map/ppermute | solution.py:208
  146.4 3.8 %collective-permute-start.26 = (bf16[2,128,512]{2,1,0:T(8,128)(2,1)S(1)}, bf16[2,128,512]{2,1,0:T(8,128)(2,1)S(1)}, u32[]{:S(2)}, u32[]{:S(2)}) collective-permute-start(bf16[2,128,512]{2,1,0:T(8,128)(2,1)S(1)} %get-tuple-element.51), channel_id=1, source_target_pairs={{4,0},{8,4},{12,8},{0,12},{5,1},{9,5},{13,9},{1,13},{6,2},{10,6},{... | collective-permute-start | bytes 786440 | tf_op jit(solution)/shard_map/ppermute | solution.py:193
  152.2 5.5 %collective-permute-done.15 = bf16[2,128,512]{2,1,0:T(8,128)(2,1)S(1)} collective-permute-done((bf16[2,128,512]{2,1,0:T(8,128)(2,1)S(1)}, bf16[2,128,512]{2,1,0:T(8,128)(2,1)S(1)}, u32[]{:S(2)}, u32[]{:S(2)}) %collective-permute-start.15) | collective-permute-done | bytes 262176 | tf_op jit(solution)/shard_map/ppermute | solution.py:208
  169.0 5.8 %collective-permute-done.25 = bf16[2,128,512]{2,1,0:T(8,128)(2,1)S(1)} collective-permute-done((bf16[2,128,512]{2,1,0:T(8,128)(2,1)S(1)}, bf16[2,128,512]{2,1,0:T(8,128)(2,1)S(1)}, u32[]{:S(2)}, u32[]{:S(2)}) %collective-permute-start.25) | collective-permute-done | bytes 262176 | tf_op jit(solution)/shard_map/ppermute | solution.py:194
  174.8 5.4 %collective-permute-done.24 = bf16[2,128,512]{2,1,0:T(8,128)(2,1)S(1)} collective-permute-done((bf16[2,128,512]{2,1,0:T(8,128)(2,1)S(1)}, bf16[2,128,512]{2,1,0:T(8,128)(2,1)S(1)}, u32[]{:S(2)}, u32[]{:S(2)}) %collective-permute-start.24) | collective-permute-done | bytes 262176 | tf_op jit(solution)/shard_map/ppermute | solution.py:193
  180.3 5.8 %collective-permute-done.23 = bf16[2,128,512]{2,1,0:T(8,128)(2,1)S(1)} collective-permute-done((bf16[2,128,512]{2,1,0:T(8,128)(2,1)S(1)}, bf16[2,128,512]{2,1,0:T(8,128)(2,1)S(1)}, u32[]{:S(2)}, u32[]{:S(2)}) %collective-permute-start.23) | collective-permute-done | bytes 262176 | tf_op jit(solution)/shard_map/ppermute | solution.py:194
  186.1 5.3 %collective-permute-done.22 = bf16[2,128,512]{2,1,0:T(8,128)(2,1)S(1)} collective-permute-done((bf16[2,128,512]{2,1,0:T(8,128)(2,1)S(1)}, bf16[2,128,512]{2,1,0:T(8,128)(2,1)S(1)}, u32[]{:S(2)}, u32[]{:S(2)}) %collective-permute-start.22) | collective-permute-done | bytes 262176 | tf_op jit(solution)/shard_map/ppermute | solution.py:193
  202.6 5.6 %collective-permute-done.19 = bf16[2,128,512]{2,1,0:T(8,128)(2,1)S(1)} collective-permute-done((bf16[2,128,512]{2,1,0:T(8,128)(2,1)}, bf16[2,128,512]{2,1,0:T(8,128)(2,1)S(1)}, u32[]{:S(2)}, u32[]{:S(2)}) %collective-permute-start.19) | collective-permute-done | bytes 262176 | tf_op jit(solution)/shard_map/ppermute | solution.py:209
  208.2 4.0 %collective-permute-done.18 = bf16[2,128,512]{2,1,0:T(8,128)(2,1)S(1)} collective-permute-done((bf16[2,128,512]{2,1,0:T(8,128)(2,1)}, bf16[2,128,512]{2,1,0:T(8,128)(2,1)S(1)}, u32[]{:S(2)}, u32[]{:S(2)}) %collective-permute-start.18) | collective-permute-done | bytes 262176 | tf_op jit(solution)/shard_map/ppermute | solution.py:208
  231.1 23.0 %collective-permute-done.28 = bf16[2,400,512]{2,1,0:T(8,128)(2,1)S(1)} collective-permute-done((bf16[2,400,512]{2,1,0:T(8,128)(2,1)}, bf16[2,400,512]{2,1,0:T(8,128)(2,1)S(1)}, u32[]{:S(2)}, u32[]{:S(2)}) %collective-permute-start.28) | collective-permute-done | bytes 819232 | tf_op jit(solution)/shard_map/ppermute | solution.py:41
  258.6 8.4 %collective-permute-done.29 = bf16[1,400,512]{2,1,0:T(8,128)(2,1)S(1)} collective-permute-done((bf16[1,400,512]{2,1,0:T(8,128)(2,1)S(1)}, bf16[1,400,512]{2,1,0:T(8,128)(2,1)S(1)}, u32[]{:S(2)}, u32[]{:S(2)}) %collective-permute-start.29) | collective-permute-done | bytes 409632 | tf_op jit(solution)/shard_map/ppermute | solution.py:41
  (277 shorter events, 115.3 us)
Async XLA Ops:
  26.9 19.6 %collective-permute-start.2 = (bf16[2,256,512]{2,1,0:T(8,128)(2,1)S(1)}, bf16[2,256,512]{2,1,0:T(8,128)(2,1)S(1)}, u32[]{:S(2)}, u32[]{:S(2)}) collective-permute-start(bf16[2,256,512]{2,1,0:T(8,128)(2,1)S(1)} %add_convert_fusion.3), channel_id=1, source_target_pairs={{0,1},{1,2},{2,3},{4,5},{5,6},{6,7},{8,9},{9,10},{10,11},{12,13},{... | collective-permute-start | bytes 1572872 | tf_op jit(solution)/shard_map/ppermute | solution.py:150
  32.0 14.5 %collective-permute-start.3 = (bf16[2,128,512]{2,1,0:T(8,128)(2,1)S(1)}, bf16[2,128,512]{2,1,0:T(8,128)(2,1)S(1)}, u32[]{:S(2)}, u32[]{:S(2)}) collective-permute-start(bf16[2,128,512]{2,1,0:T(8,128)(2,1)S(1)} %get-tuple-element.59), channel_id=1, source_target_pairs={{0,5},{1,6},{2,7},{4,9},{5,10},{6,11},{8,13},{9,14},{10,15},{12,1}... | collective-permute-start | bytes 786440 | tf_op jit(solution)/shard_map/ppermute | solution.py:151
  50.2 20.6 %collective-permute-start.5 = (bf16[2,256,512]{2,1,0:T(8,128)(2,1)S(1)}, bf16[2,256,512]{2,1,0:T(8,128)(2,1)S(1)}, u32[]{:S(2)}, u32[]{:S(2)}) collective-permute-start(bf16[2,256,512]{2,1,0:T(8,128)(2,1)S(1)} %add_convert_fusion.2), channel_id=1, source_target_pairs={{0,1},{1,2},{2,3},{4,5},{5,6},{6,7},{8,9},{9,10},{10,11},{12,13},{... | collective-permute-start | bytes 1572872 | tf_op jit(solution)/shard_map/ppermute | solution.py:150
  54.1 16.7 %collective-permute-start.6 = (bf16[2,128,512]{2,1,0:T(8,128)(2,1)S(1)}, bf16[2,128,512]{2,1,0:T(8,128)(2,1)S(1)}, u32[]{:S(2)}, u32[]{:S(2)}) collective-permute-start(bf16[2,128,512]{2,1,0:T(8,128)(2,1)S(1)} %get-tuple-element.57), channel_id=1, source_target_pairs={{0,5},{1,6},{2,7},{4,9},{5,10},{6,11},{8,13},{9,14},{10,15},{12,1}... | collective-permute-start | bytes 786440 | tf_op jit(solution)/shard_map/ppermute | solution.py:151
  74.5 21.7 %collective-permute-start.8 = (bf16[2,256,512]{2,1,0:T(8,128)(2,1)S(1)}, bf16[2,256,512]{2,1,0:T(8,128)(2,1)}, u32[]{:S(2)}, u32[]{:S(2)}) collective-permute-start(bf16[2,256,512]{2,1,0:T(8,128)(2,1)S(1)} %add_convert_fusion.1), channel_id=1, source_target_pairs={{0,1},{1,2},{2,3},{4,5},{5,6},{6,7},{8,9},{9,10},{10,11},{12,13},{... | collective-permute-start | bytes 1572872 | tf_op jit(solution)/shard_map/ppermute | solution.py:150
  79.1 17.1 %collective-permute-start.9 = (bf16[2,128,512]{2,1,0:T(8,128)(2,1)S(1)}, bf16[2,128,512]{2,1,0:T(8,128)(2,1)}, u32[]{:S(2)}, u32[]{:S(2)}) collective-permute-start(bf16[2,128,512]{2,1,0:T(8,128)(2,1)S(1)} %get-tuple-element.55), channel_id=1, source_target_pairs={{0,5},{1,6},{2,7},{4,9},{5,10},{6,11},{8,13},{9,14},{10,15},{12,1}... | collective-permute-start | bytes 786440 | tf_op jit(solution)/shard_map/ppermute | solution.py:151
  111.8 20.8 %collective-permute-start.11 = (f32[2,256,512]{2,1,0:T(8,128)S(1)}, f32[2,256,512]{2,1,0:T(8,128)S(1)}, u32[]{:S(2)}, u32[]{:S(2)}) collective-permute-start(f32[2,256,512]{2,1,0:T(8,128)S(1)} %fusion.21), channel_id=1, source_target_pairs={{1,0},{2,1},{3,2},{5,4},{6,5},{7,6},{9,8},{10,9},{11,10},{13,12},{... | collective-permute-start | bytes 3145736 | tf_op jit(solution)/shard_map/ppermute | solution.py:207
  114.6 12.4 %collective-permute-start.13 = (bf16[2,128,512]{2,1,0:T(8,128)(2,1)S(1)}, bf16[2,128,512]{2,1,0:T(8,128)(2,1)S(1)}, u32[]{:S(2)}, u32[]{:S(2)}) collective-permute-start(bf16[2,128,512]{2,1,0:T(8,128)(2,1)S(1)} %get-tuple-element.52), channel_id=1, source_target_pairs={{1,4},{2,5},{3,6},{5,8},{6,9},{7,10},{9,12},{10,13},{11,14},{13,0}... | collective-permute-start | bytes 786440 | tf_op jit(solution)/shard_map/ppermute | solution.py:209
  117.4 15.0 %collective-permute-start.12 = (bf16[2,128,512]{2,1,0:T(8,128)(2,1)S(1)}, bf16[2,128,512]{2,1,0:T(8,128)(2,1)S(1)}, u32[]{:S(2)}, u32[]{:S(2)}) collective-permute-start(bf16[2,128,512]{2,1,0:T(8,128)(2,1)S(1)} %get-tuple-element.51), channel_id=1, source_target_pairs={{1,12},{2,13},{3,14},{5,0},{6,1},{7,2},{9,4},{10,5},{11,6},{13,8},... | collective-permute-start | bytes 786440 | tf_op jit(solution)/shard_map/ppermute | solution.py:208
  136.1 23.3 %collective-permute-start.14 = (f32[2,256,512]{2,1,0:T(8,128)S(1)}, f32[2,256,512]{2,1,0:T(8,128)S(1)}, u32[]{:S(2)}, u32[]{:S(2)}) collective-permute-start(f32[2,256,512]{2,1,0:T(8,128)S(1)} %fusion.19), channel_id=1, source_target_pairs={{1,0},{2,1},{3,2},{5,4},{6,5},{7,6},{9,8},{10,9},{11,10},{13,12},{... | collective-permute-start | bytes 3145736 | tf_op jit(solution)/shard_map/ppermute | solution.py:207
  142.7 15.0 %collective-permute-start.15 = (bf16[2,128,512]{2,1,0:T(8,128)(2,1)S(1)}, bf16[2,128,512]{2,1,0:T(8,128)(2,1)S(1)}, u32[]{:S(2)}, u32[]{:S(2)}) collective-permute-start(bf16[2,128,512]{2,1,0:T(8,128)(2,1)S(1)} %get-tuple-element.49), channel_id=1, source_target_pairs={{1,12},{2,13},{3,14},{5,0},{6,1},{7,2},{9,4},{10,5},{11,6},{13,8},... | collective-permute-start | bytes 786440 | tf_op jit(solution)/shard_map/ppermute | solution.py:208
  146.3 17.2 %collective-permute-start.27 = (bf16[2,128,512]{2,1,0:T(8,128)(2,1)S(1)}, bf16[2,128,512]{2,1,0:T(8,128)(2,1)S(1)}, u32[]{:S(2)}, u32[]{:S(2)}) collective-permute-start(bf16[2,128,512]{2,1,0:T(8,128)(2,1)S(1)} %get-tuple-element.52), channel_id=1, source_target_pairs={{0,4},{4,8},{8,12},{12,0},{1,5},{5,9},{9,13},{13,1},{2,6},{6,10},{... | collective-permute-start | bytes 786440 | tf_op jit(solution)/shard_map/ppermute | solution.py:194
  146.4 22.6 %collective-permute-start.26 = (bf16[2,128,512]{2,1,0:T(8,128)(2,1)S(1)}, bf16[2,128,512]{2,1,0:T(8,128)(2,1)S(1)}, u32[]{:S(2)}, u32[]{:S(2)}) collective-permute-start(bf16[2,128,512]{2,1,0:T(8,128)(2,1)S(1)} %get-tuple-element.51), channel_id=1, source_target_pairs={{4,0},{8,4},{12,8},{0,12},{5,1},{9,5},{13,9},{1,13},{6,2},{10,6},{... | collective-permute-start | bytes 786440 | tf_op jit(solution)/shard_map/ppermute | solution.py:193
  152.2 22.6 %collective-permute-start.25 = (bf16[2,128,512]{2,1,0:T(8,128)(2,1)S(1)}, bf16[2,128,512]{2,1,0:T(8,128)(2,1)S(1)}, u32[]{:S(2)}, u32[]{:S(2)}) collective-permute-start(bf16[2,128,512]{2,1,0:T(8,128)(2,1)S(1)} %get-tuple-element.50), channel_id=1, source_target_pairs={{0,4},{4,8},{8,12},{12,0},{1,5},{5,9},{9,13},{13,1},{2,6},{6,10},{... | collective-permute-start | bytes 786440 | tf_op jit(solution)/shard_map/ppermute | solution.py:194
  157.7 22.5 %collective-permute-start.24 = (bf16[2,128,512]{2,1,0:T(8,128)(2,1)S(1)}, bf16[2,128,512]{2,1,0:T(8,128)(2,1)S(1)}, u32[]{:S(2)}, u32[]{:S(2)}) collective-permute-start(bf16[2,128,512]{2,1,0:T(8,128)(2,1)S(1)} %get-tuple-element.49), channel_id=1, source_target_pairs={{4,0},{8,4},{12,8},{0,12},{5,1},{9,5},{13,9},{1,13},{6,2},{10,6},{... | collective-permute-start | bytes 786440 | tf_op jit(solution)/shard_map/ppermute | solution.py:193
  162.5 23.5 %collective-permute-start.23 = (bf16[2,128,512]{2,1,0:T(8,128)(2,1)S(1)}, bf16[2,128,512]{2,1,0:T(8,128)(2,1)S(1)}, u32[]{:S(2)}, u32[]{:S(2)}) collective-permute-start(bf16[2,128,512]{2,1,0:T(8,128)(2,1)S(1)} %get-tuple-element.48), channel_id=1, source_target_pairs={{0,4},{4,8},{8,12},{12,0},{1,5},{5,9},{9,13},{13,1},{2,6},{6,10},{... | collective-permute-start | bytes 786440 | tf_op jit(solution)/shard_map/ppermute | solution.py:194
  163.5 27.9 %collective-permute-start.22 = (bf16[2,128,512]{2,1,0:T(8,128)(2,1)S(1)}, bf16[2,128,512]{2,1,0:T(8,128)(2,1)S(1)}, u32[]{:S(2)}, u32[]{:S(2)}) collective-permute-start(bf16[2,128,512]{2,1,0:T(8,128)(2,1)S(1)} %get-tuple-element.47), channel_id=1, source_target_pairs={{4,0},{8,4},{12,8},{0,12},{5,1},{9,5},{13,9},{1,13},{6,2},{10,6},{... | collective-permute-start | bytes 786440 | tf_op jit(solution)/shard_map/ppermute | solution.py:193
  193.7 20.1 %collective-permute-start.17 = (f32[2,256,512]{2,1,0:T(8,128)}, f32[2,256,512]{2,1,0:T(8,128)}, u32[]{:S(2)}, u32[]{:S(2)}) collective-permute-start(f32[2,256,512]{2,1,0:T(8,128)} %get-tuple-element.82), channel_id=1, source_target_pairs={{1,0},{2,1},{3,2},{5,4},{6,5},{7,6},{9,8},{10,9},{11,10},{13,12},{... | collective-permute-start | bytes 3145736 | tf_op jit(solution)/shard_map/ppermute | solution.py:207
  195.6 12.6 %collective-permute-start.19 = (bf16[2,128,512]{2,1,0:T(8,128)(2,1)}, bf16[2,128,512]{2,1,0:T(8,128)(2,1)S(1)}, u32[]{:S(2)}, u32[]{:S(2)}) collective-permute-start(bf16[2,128,512]{2,1,0:T(8,128)(2,1)} %copy-done.60), channel_id=1, source_target_pairs={{1,4},{2,5},{3,6},{5,8},{6,9},{7,10},{9,12},{10,13},{11,14},{13,0}... | collective-permute-start | bytes 786440 | tf_op jit(solution)/shard_map/ppermute | solution.py:209
  197.5 14.7 %collective-permute-start.18 = (bf16[2,128,512]{2,1,0:T(8,128)(2,1)}, bf16[2,128,512]{2,1,0:T(8,128)(2,1)S(1)}, u32[]{:S(2)}, u32[]{:S(2)}) collective-permute-start(bf16[2,128,512]{2,1,0:T(8,128)(2,1)} %copy-done.59), channel_id=1, source_target_pairs={{1,12},{2,13},{3,14},{5,0},{6,1},{7,2},{9,4},{10,5},{11,6},{13,8},... | collective-permute-start | bytes 786440 | tf_op jit(solution)/shard_map/ppermute | solution.py:208
  224.3 29.8 %collective-permute-start.28 = (bf16[2,400,512]{2,1,0:T(8,128)(2,1)}, bf16[2,400,512]{2,1,0:T(8,128)(2,1)S(1)}, u32[]{:S(2)}, u32[]{:S(2)}) collective-permute-start(bf16[2,400,512]{2,1,0:T(8,128)(2,1)} %fusion.108), channel_id=1, source_target_pairs={{0,4},{4,0},{8,12},{12,8},{1,5},{5,1},{9,13},{13,9},{2,6},{6,2},{1... | collective-permute-start | bytes 2457608 | tf_op jit(solution)/shard_map/ppermute | solution.py:41
  227.2 27.5 %collective-permute-start.21 = (bf16[2,128,512]{2,1,0:T(8,128)(2,1)S(1)}, bf16[2,128,512]{2,1,0:T(8,128)(2,1)S(1)}, u32[]{:S(2)}, u32[]{:S(2)}) collective-permute-start(bf16[2,128,512]{2,1,0:T(8,128)(2,1)S(1)} %get-tuple-element.46), channel_id=1, source_target_pairs={{0,4},{4,8},{8,12},{12,0},{1,5},{5,9},{9,13},{13,1},{2,6},{6,10},{... | collective-permute-start | bytes 786440 | tf_op jit(solution)/shard_map/ppermute | solution.py:194
  228.7 28.2 %collective-permute-start.20 = (bf16[2,128,512]{2,1,0:T(8,128)(2,1)S(1)}, bf16[2,128,512]{2,1,0:T(8,128)(2,1)S(1)}, u32[]{:S(2)}, u32[]{:S(2)}) collective-permute-start(bf16[2,128,512]{2,1,0:T(8,128)(2,1)S(1)} %get-tuple-element.45), channel_id=1, source_target_pairs={{4,0},{8,4},{12,8},{0,12},{5,1},{9,5},{13,9},{1,13},{6,2},{10,6},{... | collective-permute-start | bytes 786440 | tf_op jit(solution)/shard_map/ppermute | solution.py:193
  254.6 12.4 %collective-permute-start.29 = (bf16[1,400,512]{2,1,0:T(8,128)(2,1)S(1)}, bf16[1,400,512]{2,1,0:T(8,128)(2,1)S(1)}, u32[]{:S(2)}, u32[]{:S(2)}) collective-permute-start(bf16[1,400,512]{2,1,0:T(8,128)(2,1)S(1)} %fusion.166), channel_id=1, source_target_pairs={{0,8},{4,12},{8,0},{12,4},{1,9},{5,13},{9,1},{13,5},{2,10},{6,14},... | collective-permute-start | bytes 1228808 | tf_op jit(solution)/shard_map/ppermute | solution.py:41
  (69 other events, 577.7 us)

commit v2 on v1

--- a/solution.py
+++ b/solution.py
@@ -86,35 +86,16 @@
     w_2 = w_two[0]
     gain_row = gain[0]
 
-    dom_up = [(i, (i + 1) % domains) for i in range(domains)]
-    dom_down = [((i + 1) % domains, i) for i in range(domains)]
-    sec_up = [(i, i + 1) for i in range(sections - 1)]
-    sec_down = [(i + 1, i) for i in range(sections - 1)]
+    both = ("dom", "section")
 
     def linear(d, s):
         return d * sections + s
 
-    diag_right = [
-        (linear(d, s), linear((d + 1) % domains, s + 1))
-        for d in range(domains)
-        for s in range(sections - 1)
-    ]
-    diag_left = [
-        (linear(d, s), linear((d + domains - 1) % domains, s + 1))
-        for d in range(domains)
-        for s in range(sections - 1)
-    ]
-    diag_down_left = [
-        (linear(d, s + 1), linear((d + domains - 1) % domains, s))
-        for d in range(domains)
-        for s in range(sections - 1)
-    ]
-    diag_down_right = [
-        (linear(d, s + 1), linear((d + 1) % domains, s))
-        for d in range(domains)
-        for s in range(sections - 1)
-    ]
-    both = ("dom", "section")
+    def route(src_section, dst_section, shift):
+        return [
+            (linear(d, src_section), linear((d + shift) % domains, dst_section))
+            for d in range(domains)
+        ]
 
     def forward_layer(h, left, right):
         h_ext = jnp.concatenate([left, h, right], axis=1)
@@ -131,8 +112,8 @@
         return out, (h, agg, pre, act, normed, rstd)
 
     in_blocks = node_input.reshape(samples, nb, blk, width)
-    left = lax.ppermute(pick_blocks(in_blocks, send_right, hs), "dom", dom_up)
-    right = lax.ppermute(pick_blocks(in_blocks, send_left, hs), "dom", dom_down)
+    left = lax.ppermute(pick_blocks(in_blocks, send_right, hs), both, route(0, 0, 1))
+    right = lax.ppermute(pick_blocks(in_blocks, send_left, hs), both, route(0, 0, -1))
     h = node_input
     saved = None
     saved_out = None
@@ -147,9 +128,9 @@
             saved_out = jnp.where(mine, out, saved_out)
         if tick + 1 < sections:
             out_blocks = out.reshape(samples, nb, blk, width)
-            h = lax.ppermute(out, "section", sec_up)
-            left = lax.ppermute(pick_blocks(out_blocks, send_right, hs), both, diag_right)
-            right = lax.ppermute(pick_blocks(out_blocks, send_left, hs), both, diag_left)
+            h = lax.ppermute(out, both, route(tick, tick + 1, 0))
+            left = lax.ppermute(pick_blocks(out_blocks, send_right, hs), both, route(tick, tick + 1, 1))
+            right = lax.ppermute(pick_blocks(out_blocks, send_left, hs), both, route(tick, tick + 1, -1))
 
     h_in, agg, pre, act, normed, rstd = saved
 
@@ -188,25 +169,26 @@
             blocks = add_blocks(blocks, send_left, hs, from_left)
             return blocks.reshape(samples, node_rows, width).astype(BF16)
 
+        active = sections - 1 - tick
         g_new = finish(
             own,
-            lax.ppermute(left_grad, "dom", dom_down),
-            lax.ppermute(right_grad, "dom", dom_up),
+            lax.ppermute(left_grad, both, route(active, active, -1)),
+            lax.ppermute(right_grad, both, route(active, active, 1)),
         )
         if grad_in is None:
             grad_in, dpre_keep, dout_keep = g_new, dpre, dout
             gain_keep = gain_term
         else:
-            mine = section_index == sections - 1 - tick
+            mine = section_index == active
             grad_in = jnp.where(mine, g_new, grad_in)
             dpre_keep = jnp.where(mine, dpre, dpre_keep)
             dout_keep = jnp.where(mine, dout, dout_keep)
             gain_keep = jnp.where(mine, gain_term, gain_keep)
         if tick + 1 < sections:
             g = finish(
-                lax.ppermute(own, "section", sec_down),
-                lax.ppermute(left_grad, both, diag_down_left),
-                lax.ppermute(right_grad, both, diag_down_right),
+                lax.ppermute(own, both, route(active, active - 1, 0)),
+                lax.ppermute(left_grad, both, route(active, active - 1, -1)),
+                lax.ppermute(right_grad, both, route(active, active - 1, 1)),
             )
 
     norm_factor = 1.0 / math.sqrt(samples * node_rows * domains)

time: 270 us -> 208 us (0.77)
  the two profiles are of different devices: /device:TPU:2 before, /device:TPU:0 now
where the time goes in v2:
time: 208 us; the launch traced here: 207 us
  waiting for transfers between devices  96.4 us (46%)
  starting transfers between devices  41.6 us (20%)
  matrix products  27.9 us (13%)
  local copies, waits for them, and re-layouts  19.8 us (10%)
  other arithmetic  17 us (8%)
  between operations  4.21 us (2%)
    ppermute x3, waiting for transfers between devices, shards(): lax.ppermute(right_grad, both, route(active, active - 1, 1))  58 us
    ppermute x2, waiting for transfers between devices, halving_reduce_scatter(): recv = lax.ppermute(send, axis, pairs)  18.2 us
    unnamed x131, local copies, waits for them, and re-layouts  13 us
    ppermute x1, starting transfers between devices, shards(): lax.ppermute(pick_blocks(in_blocks, send_left, hs), both, route(0, 0, -1))  6.99 us
    ppermute x1, waiting for transfers between devices, shards(): lax.ppermute(pick_blocks(in_blocks, send_right, hs), both, route(0, 0, 1))  6.41 us
    ppermute x4, starting transfers between devices, shards(): lax.ppermute(left_grad, both, route(active, active, -1))  6.31 us
    select_n x3, other arithmetic, shards(): saved = tuple((jnp.where(mine, a, b) for a, b in zip(res, saved)))  6.26 us
    ppermute x4, starting transfers between devices, shards(): lax.ppermute(right_grad, both, route(active, active, 1))  5.74 us
  transfers between devices with their start and end apart: 30, of which 9 were waited for; matrix products, arithmetic and copies ran while one was open for 7% of the time, Pallas kernels for 0%

profile of v2, /device:TPU:0, one launch (start us, length us, event | category | flops | bytes accessed | tf_op | source)
XLA Modules:
  0.0 206.9 jit_solution(8756738874947698832)
XLA Ops:
  5.9 7.0 %collective-permute-start.1 = (bf16[2,128,512]{1,2,0:T(8,128)(2,1)S(1)}, bf16[2,128,512]{1,2,0:T(8,128)(2,1)}, u32[]{:S(2)}, u32[]{:S(2)}) collective-permute-start(bf16[2,128,512]{1,2,0:T(8,128)(2,1)S(1)} %bitcast.347), channel_id=1, source_target_pairs={{0,12},{4,0},{8,4},{12,8},{16,28},{20,16},{24,20},{28,24}} | collective-permute-start | bytes 786440 | tf_op jit(solution)/shard_map/ppermute | solution.py:116
  13.7 1.9 collective-permute-start
  17.7 6.4 %collective-permute-done = bf16[2,128,512]{1,2,0:T(8,128)(2,1)} collective-permute-done((bf16[2,128,512]{1,2,0:T(8,128)(2,1)}, bf16[2,128,512]{1,2,0:T(8,128)(2,1)}, u32[]{:S(2)}, u32[]{:S(2)}) %collective-permute-start) | collective-permute-done | bytes 262176 | tf_op jit(solution)/shard_map/ppermute | solution.py:115
  24.1 1.8 convolution_bitcast_fusion.7
  33.3 2.6 %collective-permute-done.4 = bf16[2,128,512]{2,1,0:T(8,128)(2,1)S(1)} collective-permute-done((bf16[2,128,512]{2,1,0:T(8,128)(2,1)S(1)}, bf16[2,128,512]{2,1,0:T(8,128)(2,1)S(1)}, u32[]{:S(2)}, u32[]{:S(2)}) %collective-permute-start.4) | collective-permute-done | bytes 262176 | tf_op jit(solution)/shard_map/ppermute | solution.py:133
  35.8 2.8 %collective-permute-done.3 = bf16[2,128,512]{2,1,0:T(8,128)(2,1)S(1)} collective-permute-done((bf16[2,128,512]{2,1,0:T(8,128)(2,1)S(1)}, bf16[2,128,512]{2,1,0:T(8,128)(2,1)S(1)}, u32[]{:S(2)}, u32[]{:S(2)}) %collective-permute-start.3) | collective-permute-done | bytes 262176 | tf_op jit(solution)/shard_map/ppermute | solution.py:132
  48.2 1.5 collective-permute-start.8
  53.2 2.0 convolution_bitcast_fusion
  55.7 3.4 %select_select_fusion.2 = (bf16[2,256,512]{2,1,0:T(8,128)(2,1)}, bf16[2,256,512]{2,1,0:T(8,128)(2,1)S(1)}) fusion(pred[]{:T(512)S(6)} %eq.113, pred[]{:T(512)S(6)} %eq.112, pred[]{:T(512)S(6)} %eq.53, f32[2,512,512]{2,1,0:T(8,128)S(1)} %convolution_bitcast_fusion, f32[2,512,512]{2,1,0:T(8,128)} %copy-done.19, f32[2,512,512]{2,1,0:T(8,128)S(1)} %copy-done.18, ...), kind=kLoop, calls=%fused_computation.236 | loop fusion | flops 2883584 | bytes 9437187 | tf_op jit(solution)/shard_map/jit(_where)/select_n | solution.py:127
  60.6 1.5 select_select_fusion
  85.4 2.2 %fusion.112 = (bf16[2,256,512]{2,1,0:T(8,128)(2,1)}, f32[2,256,512]{2,1,0:T(8,128)}) fusion(f32[2,256,512]{2,1,0:T(8,128)S(1)} %fusion.19, f32[2,256,512]{2,1,0:T(8,128)S(1)} %fusion.21, f32[2,128,512]{2,1,0:T(8,128)S(1)} %convert_element_type.296, f32[2,128,512]{2,1,0:T(8,128)S(1)} %convert_element_type.295, ...), kind=kOutput, calls=%fused_computation.186 | convolution fusion | flops 273678336 | bytes 9438210 | tf_op jit(solution)/shard_map/sip,vp->siv/dot_general | solution.py:157
  91.5 2.8 %select_select_fusion.3 = (bf16[2,256,512]{2,1,0:T(8,128)(2,1)S(1)}, bf16[1,2,256,512]{3,2,1,0:T(8,128)(2,1)}) fusion(bf16[2,256,512]{2,1,0:T(8,128)(2,1)} %collective-permute-done.8, bf16[2,256,512]{2,1,0:T(8,128)(2,1)} %copy-done.27, bf16[2,256,512]{2,1,0:T(8,128)(2,1)} %copy-done.26, bf16[2,256,512]{2,1,0:T(8,128)(2,1)S(1)} %copy-done.4, pred[]{:T(512)S(6)} %eq.113, ...), kind=kLoop, calls=%fused_computation.237 | loop fusion | flops 3145728 | bytes 5773315 | tf_op jit(solution)/shard_map/jit(_where)/select_n | solution.py:127
  94.3 58.0 %collective-permute-done.19 = bf16[2,128,512]{2,1,0:T(8,128)(2,1)S(1)} collective-permute-done((bf16[2,128,512]{2,1,0:T(8,128)(2,1)}, bf16[2,128,512]{2,1,0:T(8,128)(2,1)S(1)}, u32[]{:S(2)}, u32[]{:S(2)}) %collective-permute-start.19) | collective-permute-done | bytes 262176 | tf_op jit(solution)/shard_map/ppermute | solution.py:191
  152.4 1.6 collective-permute-done.18
  154.1 2.0 fusion.50
  162.0 1.7 copy-done.2
  165.3 1.5 convolution_convert_fusion
  167.6 3.5 %collective-permute-start.21 = (bf16[2,128,512]{2,1,0:T(8,128)(2,1)S(1)}, bf16[2,128,512]{2,1,0:T(8,128)(2,1)S(1)}, u32[]{:S(2)}, u32[]{:S(2)}) collective-permute-start(bf16[2,128,512]{2,1,0:T(8,128)(2,1)S(1)} %get-tuple-element.46), channel_id=1, source_target_pairs={{0,4},{4,8},{8,12},{12,0},{16,20},{20,24},{24,28},{28,16}} | collective-permute-start | bytes 786440 | tf_op jit(solution)/shard_map/ppermute | solution.py:176
  171.1 4.3 %collective-permute-start.20 = (bf16[2,128,512]{2,1,0:T(8,128)(2,1)S(1)}, bf16[2,128,512]{2,1,0:T(8,128)(2,1)S(1)}, u32[]{:S(2)}, u32[]{:S(2)}) collective-permute-start(bf16[2,128,512]{2,1,0:T(8,128)(2,1)S(1)} %get-tuple-element.45), channel_id=1, source_target_pairs={{0,12},{4,0},{8,4},{12,8},{16,28},{20,16},{24,20},{28,24}} | collective-permute-start | bytes 786440 | tf_op jit(solution)/shard_map/ppermute | solution.py:175
  175.4 7.7 %collective-permute-done.28 = bf16[2,400,512]{2,1,0:T(8,128)(2,1)S(1)} collective-permute-done((bf16[2,400,512]{2,1,0:T(8,128)(2,1)}, bf16[2,400,512]{2,1,0:T(8,128)(2,1)S(1)}, u32[]{:S(2)}, u32[]{:S(2)}) %collective-permute-start.28) | collective-permute-done | bytes 819232 | tf_op jit(solution)/shard_map/ppermute | solution.py:41
  183.6 1.8 collective-permute-start.29
  185.4 2.3 %collective-permute-done.21 = bf16[2,128,512]{2,1,0:T(8,128)(2,1)S(1)} collective-permute-done((bf16[2,128,512]{2,1,0:T(8,128)(2,1)S(1)}, bf16[2,128,512]{2,1,0:T(8,128)(2,1)S(1)}, u32[]{:S(2)}, u32[]{:S(2)}) %collective-permute-start.21) | collective-permute-done | bytes 262176 | tf_op jit(solution)/shard_map/ppermute | solution.py:176
  187.9 4.4 %collective-permute-done.20 = bf16[2,128,512]{2,1,0:T(8,128)(2,1)S(1)} collective-permute-done((bf16[2,128,512]{2,1,0:T(8,128)(2,1)S(1)}, bf16[2,128,512]{2,1,0:T(8,128)(2,1)S(1)}, u32[]{:S(2)}, u32[]{:S(2)}) %collective-permute-start.20) | collective-permute-done | bytes 262176 | tf_op jit(solution)/shard_map/ppermute | solution.py:175
  194.1 10.6 %collective-permute-done.29 = bf16[1,400,512]{2,1,0:T(8,128)(2,1)S(1)} collective-permute-done((bf16[1,400,512]{2,1,0:T(8,128)(2,1)S(1)}, bf16[1,400,512]{2,1,0:T(8,128)(2,1)S(1)}, u32[]{:S(2)}, u32[]{:S(2)}) %collective-permute-start.29) | collective-permute-done | bytes 409632 | tf_op jit(solution)/shard_map/ppermute | solution.py:41
  (277 shorter events, 67.5 us)
Async XLA Ops:
  5.9 11.8 %collective-permute-start.1 = (bf16[2,128,512]{1,2,0:T(8,128)(2,1)S(1)}, bf16[2,128,512]{1,2,0:T(8,128)(2,1)}, u32[]{:S(2)}, u32[]{:S(2)}) collective-permute-start(bf16[2,128,512]{1,2,0:T(8,128)(2,1)S(1)} %bitcast.347), channel_id=1, source_target_pairs={{0,12},{4,0},{8,4},{12,8},{16,28},{20,16},{24,20},{28,24}} | collective-permute-start | bytes 786440 | tf_op jit(solution)/shard_map/ppermute | solution.py:116
  13.7 10.4 %collective-permute-start = (bf16[2,128,512]{1,2,0:T(8,128)(2,1)}, bf16[2,128,512]{1,2,0:T(8,128)(2,1)}, u32[]{:S(2)}, u32[]{:S(2)}) collective-permute-start(bf16[2,128,512]{1,2,0:T(8,128)(2,1)} %bitcast.7), channel_id=1, source_target_pairs={{0,4},{4,8},{8,12},{12,0},{16,20},{20,24},{24,28},{28,16}} | collective-permute-start | bytes 786440 | tf_op jit(solution)/shard_map/ppermute | solution.py:115
  29.2 9.4 %collective-permute-start.2 = (bf16[2,256,512]{2,1,0:T(8,128)(2,1)S(1)}, bf16[2,256,512]{2,1,0:T(8,128)(2,1)S(1)}, u32[]{:S(2)}, u32[]{:S(2)}) collective-permute-start(bf16[2,256,512]{2,1,0:T(8,128)(2,1)S(1)} %add_convert_fusion.3), channel_id=1, source_target_pairs={{0,1},{4,5},{8,9},{12,13},{16,17},{20,21},{24,25},{28,29}} | collective-permute-start | bytes 1572872 | tf_op jit(solution)/shard_map/ppermute | solution.py:131
  30.6 5.2 %collective-permute-start.4 = (bf16[2,128,512]{2,1,0:T(8,128)(2,1)S(1)}, bf16[2,128,512]{2,1,0:T(8,128)(2,1)S(1)}, u32[]{:S(2)}, u32[]{:S(2)}) collective-permute-start(bf16[2,128,512]{2,1,0:T(8,128)(2,1)S(1)} %get-tuple-element.60), channel_id=1, source_target_pairs={{0,13},{4,1},{8,5},{12,9},{16,29},{20,17},{24,21},{28,25}} | collective-permute-start | bytes 786440 | tf_op jit(solution)/shard_map/ppermute | solution.py:133
  31.9 6.7 %collective-permute-start.3 = (bf16[2,128,512]{2,1,0:T(8,128)(2,1)S(1)}, bf16[2,128,512]{2,1,0:T(8,128)(2,1)S(1)}, u32[]{:S(2)}, u32[]{:S(2)}) collective-permute-start(bf16[2,128,512]{2,1,0:T(8,128)(2,1)S(1)} %get-tuple-element.59), channel_id=1, source_target_pairs={{0,5},{4,9},{8,13},{12,1},{16,21},{20,25},{24,29},{28,17}} | collective-permute-start | bytes 786440 | tf_op jit(solution)/shard_map/ppermute | solution.py:132
  42.4 2.2 %collective-permute-start.5 = (bf16[2,256,512]{2,1,0:T(8,128)(2,1)S(1)}, bf16[2,256,512]{2,1,0:T(8,128)(2,1)S(1)}, u32[]{:S(2)}, u32[]{:S(2)}) collective-permute-start(bf16[2,256,512]{2,1,0:T(8,128)(2,1)S(1)} %add_convert_fusion.2), channel_id=1, source_target_pairs={{1,2},{5,6},{9,10},{13,14},{17,18},{21,22},{25,26},{29,30}} | collective-permute-start | bytes 1572872 | tf_op jit(solution)/shard_map/ppermute | solution.py:131
  48.2 5.0 %collective-permute-start.8 = (bf16[2,256,512]{2,1,0:T(8,128)(2,1)S(1)}, bf16[2,256,512]{2,1,0:T(8,128)(2,1)}, u32[]{:S(2)}, u32[]{:S(2)}) collective-permute-start(bf16[2,256,512]{2,1,0:T(8,128)(2,1)S(1)} %add_convert_fusion.1), channel_id=1, source_target_pairs={{2,3},{6,7},{10,11},{14,15},{18,19},{22,23},{26,27},{30,31}} | collective-permute-start | bytes 1572872 | tf_op jit(solution)/shard_map/ppermute | solution.py:131
  50.4 2.7 %collective-permute-start.10 = (bf16[2,128,512]{2,1,0:T(8,128)(2,1)}, bf16[2,128,512]{2,1,0:T(8,128)(2,1)}, u32[]{:S(2)}, u32[]{:S(2)}) collective-permute-start(bf16[2,128,512]{2,1,0:T(8,128)(2,1)} %get-tuple-element.56), channel_id=1, source_target_pairs={{2,15},{6,3},{10,7},{14,11},{18,31},{22,19},{26,23},{30,27}} | collective-permute-start | bytes 786440 | tf_op jit(solution)/shard_map/ppermute | solution.py:133
  69.3 2.4 %collective-permute-start.11 = (f32[2,256,512]{2,1,0:T(8,128)S(1)}, f32[2,256,512]{2,1,0:T(8,128)S(1)}, u32[]{:S(2)}, u32[]{:S(2)}) collective-permute-start(f32[2,256,512]{2,1,0:T(8,128)S(1)} %fusion.21), channel_id=1, source_target_pairs={{3,2},{7,6},{11,10},{15,14},{19,18},{23,22},{27,26},{31,30}} | collective-permute-start | bytes 3145736 | tf_op jit(solution)/shard_map/ppermute | solution.py:189
  75.2 5.0 %collective-permute-start.14 = (f32[2,256,512]{2,1,0:T(8,128)S(1)}, f32[2,256,512]{2,1,0:T(8,128)S(1)}, u32[]{:S(2)}, u32[]{:S(2)}) collective-permute-start(f32[2,256,512]{2,1,0:T(8,128)S(1)} %fusion.19), channel_id=1, source_target_pairs={{2,1},{6,5},{10,9},{14,13},{18,17},{22,21},{26,25},{30,29}} | collective-permute-start | bytes 3145736 | tf_op jit(solution)/shard_map/ppermute | solution.py:189
  76.0 2.7 %collective-permute-start.16 = (bf16[2,128,512]{2,1,0:T(8,128)(2,1)S(1)}, bf16[2,128,512]{2,1,0:T(8,128)(2,1)S(1)}, u32[]{:S(2)}, u32[]{:S(2)}) collective-permute-start(bf16[2,128,512]{2,1,0:T(8,128)(2,1)S(1)} %get-tuple-element.50), channel_id=1, source_target_pairs={{2,5},{6,9},{10,13},{14,1},{18,21},{22,25},{26,29},{30,17}} | collective-permute-start | bytes 786440 | tf_op jit(solution)/shard_map/ppermute | solution.py:191
  76.7 2.8 %collective-permute-start.15 = (bf16[2,128,512]{2,1,0:T(8,128)(2,1)S(1)}, bf16[2,128,512]{2,1,0:T(8,128)(2,1)S(1)}, u32[]{:S(2)}, u32[]{:S(2)}) collective-permute-start(bf16[2,128,512]{2,1,0:T(8,128)(2,1)S(1)} %get-tuple-element.49), channel_id=1, source_target_pairs={{2,13},{6,1},{10,5},{14,9},{18,29},{22,17},{26,21},{30,25}} | collective-permute-start | bytes 786440 | tf_op jit(solution)/shard_map/ppermute | solution.py:190
  77.4 6.9 %collective-permute-start.27 = (bf16[2,128,512]{2,1,0:T(8,128)(2,1)S(1)}, bf16[2,128,512]{2,1,0:T(8,128)(2,1)S(1)}, u32[]{:S(2)}, u32[]{:S(2)}) collective-permute-start(bf16[2,128,512]{2,1,0:T(8,128)(2,1)S(1)} %get-tuple-element.52), channel_id=1, source_target_pairs={{3,7},{7,11},{11,15},{15,3},{19,23},{23,27},{27,31},{31,19}} | collective-permute-start | bytes 786440 | tf_op jit(solution)/shard_map/ppermute | solution.py:176
  78.1 7.0 %collective-permute-start.26 = (bf16[2,128,512]{2,1,0:T(8,128)(2,1)S(1)}, bf16[2,128,512]{2,1,0:T(8,128)(2,1)S(1)}, u32[]{:S(2)}, u32[]{:S(2)}) collective-permute-start(bf16[2,128,512]{2,1,0:T(8,128)(2,1)S(1)} %get-tuple-element.51), channel_id=1, source_target_pairs={{3,15},{7,3},{11,7},{15,11},{19,31},{23,19},{27,23},{31,27}} | collective-permute-start | bytes 786440 | tf_op jit(solution)/shard_map/ppermute | solution.py:175
  78.8 6.4 %collective-permute-start.25 = (bf16[2,128,512]{2,1,0:T(8,128)(2,1)S(1)}, bf16[2,128,512]{2,1,0:T(8,128)(2,1)S(1)}, u32[]{:S(2)}, u32[]{:S(2)}) collective-permute-start(bf16[2,128,512]{2,1,0:T(8,128)(2,1)S(1)} %get-tuple-element.50), channel_id=1, source_target_pairs={{2,6},{6,10},{10,14},{14,2},{18,22},{22,26},{26,30},{30,18}} | collective-permute-start | bytes 786440 | tf_op jit(solution)/shard_map/ppermute | solution.py:176
  79.5 5.7 %collective-permute-start.24 = (bf16[2,128,512]{2,1,0:T(8,128)(2,1)S(1)}, bf16[2,128,512]{2,1,0:T(8,128)(2,1)S(1)}, u32[]{:S(2)}, u32[]{:S(2)}) collective-permute-start(bf16[2,128,512]{2,1,0:T(8,128)(2,1)S(1)} %get-tuple-element.49), channel_id=1, source_target_pairs={{2,14},{6,2},{10,6},{14,10},{18,30},{22,18},{26,22},{30,26}} | collective-permute-start | bytes 786440 | tf_op jit(solution)/shard_map/ppermute | solution.py:175
  83.4 1.9 collective-permute-start.23
  87.6 66.5 %collective-permute-start.17 = (f32[2,256,512]{2,1,0:T(8,128)}, f32[2,256,512]{2,1,0:T(8,128)}, u32[]{:S(2)}, u32[]{:S(2)}) collective-permute-start(f32[2,256,512]{2,1,0:T(8,128)} %get-tuple-element.82), channel_id=1, source_target_pairs={{1,0},{5,4},{9,8},{13,12},{17,16},{21,20},{25,24},{29,28}} | collective-permute-start | bytes 3145736 | tf_op jit(solution)/shard_map/ppermute | solution.py:189
  88.9 63.4 %collective-permute-start.19 = (bf16[2,128,512]{2,1,0:T(8,128)(2,1)}, bf16[2,128,512]{2,1,0:T(8,128)(2,1)S(1)}, u32[]{:S(2)}, u32[]{:S(2)}) collective-permute-start(bf16[2,128,512]{2,1,0:T(8,128)(2,1)} %copy-done.60), channel_id=1, source_target_pairs={{1,4},{5,8},{9,12},{13,0},{17,20},{21,24},{25,28},{29,16}} | collective-permute-start | bytes 786440 | tf_op jit(solution)/shard_map/ppermute | solution.py:191
  90.2 63.8 %collective-permute-start.18 = (bf16[2,128,512]{2,1,0:T(8,128)(2,1)}, bf16[2,128,512]{2,1,0:T(8,128)(2,1)S(1)}, u32[]{:S(2)}, u32[]{:S(2)}) collective-permute-start(bf16[2,128,512]{2,1,0:T(8,128)(2,1)} %copy-done.59), channel_id=1, source_target_pairs={{1,12},{5,0},{9,4},{13,8},{17,28},{21,16},{25,20},{29,24}} | collective-permute-start | bytes 786440 | tf_op jit(solution)/shard_map/ppermute | solution.py:190
  164.7 18.4 %collective-permute-start.28 = (bf16[2,400,512]{2,1,0:T(8,128)(2,1)}, bf16[2,400,512]{2,1,0:T(8,128)(2,1)S(1)}, u32[]{:S(2)}, u32[]{:S(2)}) collective-permute-start(bf16[2,400,512]{2,1,0:T(8,128)(2,1)} %fusion.108), channel_id=1, source_target_pairs={{0,4},{4,0},{8,12},{12,8},{1,5},{5,1},{9,13},{13,9},{2,6},{6,2},{1... | collective-permute-start | bytes 2457608 | tf_op jit(solution)/shard_map/ppermute | solution.py:41
  167.6 20.1 %collective-permute-start.21 = (bf16[2,128,512]{2,1,0:T(8,128)(2,1)S(1)}, bf16[2,128,512]{2,1,0:T(8,128)(2,1)S(1)}, u32[]{:S(2)}, u32[]{:S(2)}) collective-permute-start(bf16[2,128,512]{2,1,0:T(8,128)(2,1)S(1)} %get-tuple-element.46), channel_id=1, source_target_pairs={{0,4},{4,8},{8,12},{12,0},{16,20},{20,24},{24,28},{28,16}} | collective-permute-start | bytes 786440 | tf_op jit(solution)/shard_map/ppermute | solution.py:176
  171.1 21.3 %collective-permute-start.20 = (bf16[2,128,512]{2,1,0:T(8,128)(2,1)S(1)}, bf16[2,128,512]{2,1,0:T(8,128)(2,1)S(1)}, u32[]{:S(2)}, u32[]{:S(2)}) collective-permute-start(bf16[2,128,512]{2,1,0:T(8,128)(2,1)S(1)} %get-tuple-element.45), channel_id=1, source_target_pairs={{0,12},{4,0},{8,4},{12,8},{16,28},{20,16},{24,20},{28,24}} | collective-permute-start | bytes 786440 | tf_op jit(solution)/shard_map/ppermute | solution.py:175
  183.6 21.1 %collective-permute-start.29 = (bf16[1,400,512]{2,1,0:T(8,128)(2,1)S(1)}, bf16[1,400,512]{2,1,0:T(8,128)(2,1)S(1)}, u32[]{:S(2)}, u32[]{:S(2)}) collective-permute-start(bf16[1,400,512]{2,1,0:T(8,128)(2,1)S(1)} %fusion.166), channel_id=1, source_target_pairs={{0,8},{4,12},{8,0},{12,4},{1,9},{5,13},{9,1},{13,5},{2,10},{6,14},... | collective-permute-start | bytes 1228808 | tf_op jit(solution)/shard_map/ppermute | solution.py:41
  (69 other events, 295.6 us)

commit v3 on v2

--- a/solution.py
+++ b/solution.py
@@ -170,26 +170,28 @@
             return blocks.reshape(samples, node_rows, width).astype(BF16)
 
         active = sections - 1 - tick
-        g_new = finish(
-            own,
-            lax.ppermute(left_grad, both, route(active, active, -1)),
-            lax.ppermute(right_grad, both, route(active, active, 1)),
-        )
-        if grad_in is None:
-            grad_in, dpre_keep, dout_keep = g_new, dpre, dout
-            gain_keep = gain_term
-        else:
-            mine = section_index == active
-            grad_in = jnp.where(mine, g_new, grad_in)
-            dpre_keep = jnp.where(mine, dpre, dpre_keep)
-            dout_keep = jnp.where(mine, dout, dout_keep)
-            gain_keep = jnp.where(mine, gain_term, gain_keep)
+        mine = section_index == active
         if tick + 1 < sections:
             g = finish(
                 lax.ppermute(own, both, route(active, active - 1, 0)),
                 lax.ppermute(left_grad, both, route(active, active - 1, -1)),
                 lax.ppermute(right_grad, both, route(active, active - 1, 1)),
             )
+            g_new = lax.ppermute(g, both, route(active - 1, active, 0))
+        else:
+            g_new = finish(
+                own,
+                lax.ppermute(left_grad, both, route(active, active, -1)),
+                lax.ppermute(right_grad, both, route(active, active, 1)),
+            )
+        if grad_in is None:
+            grad_in, dpre_keep, dout_keep = g_new, dpre, dout
+            gain_keep = gain_term
+        else:
+            grad_in = jnp.where(mine, g_new, grad_in)
+            dpre_keep = jnp.where(mine, dpre, dpre_keep)
+            dout_keep = jnp.where(mine, dout, dout_keep)
+            gain_keep = jnp.where(mine, gain_term, gain_keep)
 
     norm_factor = 1.0 / math.sqrt(samples * node_rows * domains)
     stacked = jnp.concatenate([h_in, agg], axis=2)

time: 208 us -> 200 us (0.962)
  waiting for transfers between devices: 96.4 us -> 88.6 us
  starting transfers between devices: 41.6 us -> 39.2 us
    ppermute x3, waiting for transfers between devices: 58 us -> 50.1 us  [shards(): lax.ppermute(right_grad, both, route(active, active - 1, 1))]
    ppermute x2, waiting for transfers between devices: 18.2 us -> 22.4 us  [halving_reduce_scatter(): recv = lax.ppermute(send, axis, pairs)]
    ppermute x0 -> x3, starting transfers between devices: none -> 2.76 us  [shards(): g_new = lax.ppermute(g, both, route(active - 1, active, 0))]
    ppermute x4 -> x1, waiting for transfers between devices: 4.45 us -> 2.1 us  [shards(): lax.ppermute(left_grad, both, route(active, active, -1))]
    ppermute x4 -> x1, starting transfers between devices: 5.74 us -> 3.45 us  [shards(): lax.ppermute(right_grad, both, route(active, active, 1))]
    ppermute x4 -> x1, waiting for transfers between devices: 2.27 us -> 0.01 us  [shards(): lax.ppermute(right_grad, both, route(active, active, 1))]
    ppermute x4 -> x1, starting transfers between devices: 6.31 us -> 4.19 us  [shards(): lax.ppermute(left_grad, both, route(active, active, -1))]
    unnamed x131 -> x133, local copies, waits for them, and re-layouts: 13 us -> 12.9 us
  transfers between devices with their start and end apart: 30 -> 27, of which waited for: 9 -> 8; matrix products, arithmetic and copies ran while one was open for 7% -> 7% of each run, Pallas kernels for 0% -> 0%
where the time goes in v3:
time: 200 us; the launch traced here: 199 us
  waiting for transfers between devices  88.6 us (44%)
  starting transfers between devices  39.2 us (20%)
  matrix products  28.3 us (14%)
  local copies, waits for them, and re-layouts  20.8 us (10%)
  other arithmetic  17.9 us (9%)
  between operations  4.1 us (2%)
    ppermute x3, waiting for transfers between devices, shards(): lax.ppermute(right_grad, both, route(active, active - 1, 1))  50.1 us
    ppermute x2, waiting for transfers between devices, halving_reduce_scatter(): recv = lax.ppermute(send, axis, pairs)  22.4 us
    unnamed x133, local copies, waits for them, and re-layouts  12.9 us
    ppermute x1, starting transfers between devices, shards(): lax.ppermute(pick_blocks(in_blocks, send_left, hs), both, route(0, 0, -1))  6.99 us
    ppermute x1, waiting for transfers between devices, shards(): lax.ppermute(pick_blocks(in_blocks, send_right, hs), both, route(0, 0, 1))  6.41 us
    select_n x3, other arithmetic, shards(): saved = tuple((jnp.where(mine, a, b) for a, b in zip(res, saved)))  6.25 us
    dot_general x4, matrix products, forward_layer(): agg2 = jnp.einsum('ij,sjd->sid', adj2, h_ext, preferred_element_type=F32)  5.24 us
    reduce_sum x4, other arithmetic, shards(): gain_term = jnp.sum(gf * normed, axis=(0, 1))  4.43 us
  transfers between devices with their start and end apart: 27, of which 8 were waited for; matrix products, arithmetic and copies ran while one was open for 7% of the time, Pallas kernels for 0%

profile of v3, /device:TPU:0, one launch (start us, length us, event | category | flops | bytes accessed | tf_op | source)
XLA Modules:
  0.0 198.8 jit_solution(15451487092449922970)
XLA Ops:
  5.9 7.0 %collective-permute-start.1 = (bf16[2,128,512]{1,2,0:T(8,128)(2,1)S(1)}, bf16[2,128,512]{1,2,0:T(8,128)(2,1)}, u32[]{:S(2)}, u32[]{:S(2)}) collective-permute-start(bf16[2,128,512]{1,2,0:T(8,128)(2,1)S(1)} %bitcast.293), channel_id=1, source_target_pairs={{0,12},{4,0},{8,4},{12,8},{16,28},{20,16},{24,20},{28,24}} | collective-permute-start | bytes 786440 | tf_op jit(solution)/shard_map/ppermute | solution.py:116
  13.7 1.9 collective-permute-start
  17.7 6.4 %collective-permute-done = bf16[2,128,512]{1,2,0:T(8,128)(2,1)} collective-permute-done((bf16[2,128,512]{1,2,0:T(8,128)(2,1)}, bf16[2,128,512]{1,2,0:T(8,128)(2,1)}, u32[]{:S(2)}, u32[]{:S(2)}) %collective-permute-start) | collective-permute-done | bytes 262176 | tf_op jit(solution)/shard_map/ppermute | solution.py:115
  24.1 1.8 convolution_bitcast_fusion.7
  33.2 2.6 %collective-permute-done.4 = bf16[2,128,512]{2,1,0:T(8,128)(2,1)S(1)} collective-permute-done((bf16[2,128,512]{2,1,0:T(8,128)(2,1)S(1)}, bf16[2,128,512]{2,1,0:T(8,128)(2,1)S(1)}, u32[]{:S(2)}, u32[]{:S(2)}) %collective-permute-start.4) | collective-permute-done | bytes 262176 | tf_op jit(solution)/shard_map/ppermute | solution.py:133
  35.8 2.8 %collective-permute-done.3 = bf16[2,128,512]{2,1,0:T(8,128)(2,1)S(1)} collective-permute-done((bf16[2,128,512]{2,1,0:T(8,128)(2,1)S(1)}, bf16[2,128,512]{2,1,0:T(8,128)(2,1)S(1)}, u32[]{:S(2)}, u32[]{:S(2)}) %collective-permute-start.3) | collective-permute-done | bytes 262176 | tf_op jit(solution)/shard_map/ppermute | solution.py:132
  53.1 2.0 %convolution_bitcast_fusion = f32[2,512,512]{2,1,0:T(8,128)S(1)} fusion(bf16[2,128,512]{2,1,0:T(8,128)(2,1)} %collective-permute-done.10, bf16[2,256,512]{2,1,0:T(8,128)(2,1)} %collective-permute-done.8, bf16[2,128,512]{2,1,0:T(8,128)(2,1)} %collective-permute-done.9, bf16[256,512]{1,0:T(8,128)(2,1)S(1)} %fusion.103, bf16[256,512]{1,0:T(8,128)(2,1)S(1)} %bitcast.267), kind=kOutput, calls=%fused_computation.6 | convolution fusion | flops 541065216 | bytes 3670016 | tf_op jit(solution)/shard_map/ij,sjd->sid/dot_general | solution.py:102
  55.6 3.4 %select_select_fusion.2 = (bf16[2,256,512]{2,1,0:T(8,128)(2,1)}, bf16[2,256,512]{2,1,0:T(8,128)(2,1)S(1)}) fusion(pred[]{:T(512)S(6)} %eq.101, pred[]{:T(512)S(6)} %eq.100, pred[]{:T(512)S(6)} %eq.93, f32[2,512,512]{2,1,0:T(8,128)S(1)} %convolution_bitcast_fusion, f32[2,512,512]{2,1,0:T(8,128)} %copy-done.19, f32[2,512,512]{2,1,0:T(8,128)S(1)} %copy-done.18, ...), kind=kLoop, calls=%fused_computation.219 | loop fusion | flops 2883584 | bytes 9437187 | tf_op jit(solution)/shard_map/jit(_where)/select_n | solution.py:127
  60.6 1.5 select_select_fusion
  79.8 1.8 fusion.201
  83.0 1.5 collective-permute-start.17
  88.2 2.8 %select_select_fusion.3 = (bf16[2,256,512]{2,1,0:T(8,128)(2,1)S(1)}, bf16[1,2,256,512]{3,2,1,0:T(8,128)(2,1)}) fusion(bf16[2,256,512]{2,1,0:T(8,128)(2,1)} %collective-permute-done.8, bf16[2,256,512]{2,1,0:T(8,128)(2,1)} %copy-done.31, bf16[2,256,512]{2,1,0:T(8,128)(2,1)} %copy-done.30, bf16[2,256,512]{2,1,0:T(8,128)(2,1)S(1)} %copy-done.4, pred[]{:T(512)S(6)} %eq.101, ...), kind=kLoop, calls=%fused_computation.220 | loop fusion | flops 3145728 | bytes 5773315 | tf_op jit(solution)/shard_map/jit(_where)/select_n | solution.py:127
  91.0 50.0 %collective-permute-done.19 = bf16[2,128,512]{2,1,0:T(8,128)(2,1)S(1)} collective-permute-done((bf16[2,128,512]{2,1,0:T(8,128)(2,1)S(1)}, bf16[2,128,512]{2,1,0:T(8,128)(2,1)S(1)}, u32[]{:S(2)}, u32[]{:S(2)}) %collective-permute-start.19) | collective-permute-done | bytes 262176 | tf_op jit(solution)/shard_map/ppermute | solution.py:178
  141.1 2.1 %collective-permute-done.18 = bf16[2,128,512]{2,1,0:T(8,128)(2,1)S(1)} collective-permute-done((bf16[2,128,512]{2,1,0:T(8,128)(2,1)S(1)}, bf16[2,128,512]{2,1,0:T(8,128)(2,1)S(1)}, u32[]{:S(2)}, u32[]{:S(2)}) %collective-permute-start.18) | collective-permute-done | bytes 262176 | tf_op jit(solution)/shard_map/ppermute | solution.py:177
  143.4 2.0 %fusion.50 = (bf16[512]{0:T(512)(128)(2,1)S(1)}, f32[2,256]{1,0:T(2,128)S(1)}, f32[2,256]{1,0:T(2,128)S(1)}, bf16[2,256,512]{2,1,0:T(8,128)(2,1)S(1)}) fusion(f32[2,256,512]{2,1,0:T(8,128)S(1)} %get-tuple-element.44, f32[512]{0:T(512)S(1)} %bitcast.290, f32[2,128,512]{2,1,0:T(8,128)S(1)} %convert_element_type.247, pred[256]{0:T(512)(128)(4,1)S(1)} %get-tuple-element.85, ...), kind=kLoop, calls=%fused_computation.88 | loop fusion | flops 3144192 | bytes 3677696 | tf_op jit(solution)/shard_map/reduce_sum | solution.py:144
  151.2 1.7 copy-done.2
  157.3 1.5 convolution_convert_fusion
  159.6 3.4 %collective-permute-start.21 = (bf16[2,128,512]{2,1,0:T(8,128)(2,1)S(1)}, bf16[2,128,512]{2,1,0:T(8,128)(2,1)S(1)}, u32[]{:S(2)}, u32[]{:S(2)}) collective-permute-start(bf16[2,128,512]{2,1,0:T(8,128)(2,1)S(1)} %get-tuple-element.46), channel_id=1, source_target_pairs={{0,4},{4,8},{8,12},{12,0},{16,20},{20,24},{24,28},{28,16}} | collective-permute-start | bytes 786440 | tf_op jit(solution)/shard_map/ppermute | solution.py:185
  163.1 9.2 %collective-permute-done.25 = bf16[2,400,512]{2,1,0:T(8,128)(2,1)} collective-permute-done((bf16[2,400,512]{2,1,0:T(8,128)(2,1)}, bf16[2,400,512]{2,1,0:T(8,128)(2,1)}, u32[]{:S(2)}, u32[]{:S(2)}) %collective-permute-start.25) | collective-permute-done | bytes 819232 | tf_op jit(solution)/shard_map/ppermute | solution.py:41
  172.3 4.2 %collective-permute-start.20 = (bf16[2,128,512]{2,1,0:T(8,128)(2,1)S(1)}, bf16[2,128,512]{2,1,0:T(8,128)(2,1)S(1)}, u32[]{:S(2)}, u32[]{:S(2)}) collective-permute-start(bf16[2,128,512]{2,1,0:T(8,128)(2,1)S(1)} %get-tuple-element.45), channel_id=1, source_target_pairs={{0,12},{4,0},{8,4},{12,8},{16,28},{20,16},{24,20},{28,24}} | collective-permute-start | bytes 786440 | tf_op jit(solution)/shard_map/ppermute | solution.py:184
  176.5 1.6 fusion
  179.4 2.1 %collective-permute-done.20 = bf16[2,128,512]{2,1,0:T(8,128)(2,1)S(1)} collective-permute-done((bf16[2,128,512]{2,1,0:T(8,128)(2,1)S(1)}, bf16[2,128,512]{2,1,0:T(8,128)(2,1)S(1)}, u32[]{:S(2)}, u32[]{:S(2)}) %collective-permute-start.20) | collective-permute-done | bytes 262176 | tf_op jit(solution)/shard_map/ppermute | solution.py:184
  181.8 1.6 fusion.30
  183.4 13.2 %collective-permute-done.26 = bf16[1,400,512]{2,1,0:T(8,128)(2,1)S(1)} collective-permute-done((bf16[1,400,512]{2,1,0:T(8,128)(2,1)S(1)}, bf16[1,400,512]{2,1,0:T(8,128)(2,1)S(1)}, u32[]{:S(2)}, u32[]{:S(2)}) %collective-permute-start.26) | collective-permute-done | bytes 409632 | tf_op jit(solution)/shard_map/ppermute | solution.py:41
  (267 shorter events, 66.5 us)
Async XLA Ops:
  5.9 11.8 %collective-permute-start.1 = (bf16[2,128,512]{1,2,0:T(8,128)(2,1)S(1)}, bf16[2,128,512]{1,2,0:T(8,128)(2,1)}, u32[]{:S(2)}, u32[]{:S(2)}) collective-permute-start(bf16[2,128,512]{1,2,0:T(8,128)(2,1)S(1)} %bitcast.293), channel_id=1, source_target_pairs={{0,12},{4,0},{8,4},{12,8},{16,28},{20,16},{24,20},{28,24}} | collective-permute-start | bytes 786440 | tf_op jit(solution)/shard_map/ppermute | solution.py:116
  13.7 10.4 %collective-permute-start = (bf16[2,128,512]{1,2,0:T(8,128)(2,1)}, bf16[2,128,512]{1,2,0:T(8,128)(2,1)}, u32[]{:S(2)}, u32[]{:S(2)}) collective-permute-start(bf16[2,128,512]{1,2,0:T(8,128)(2,1)} %bitcast.7), channel_id=1, source_target_pairs={{0,4},{4,8},{8,12},{12,0},{16,20},{20,24},{24,28},{28,16}} | collective-permute-start | bytes 786440 | tf_op jit(solution)/shard_map/ppermute | solution.py:115
  29.2 9.4 %collective-permute-start.2 = (bf16[2,256,512]{2,1,0:T(8,128)(2,1)S(1)}, bf16[2,256,512]{2,1,0:T(8,128)(2,1)S(1)}, u32[]{:S(2)}, u32[]{:S(2)}) collective-permute-start(bf16[2,256,512]{2,1,0:T(8,128)(2,1)S(1)} %add_convert_fusion.3), channel_id=1, source_target_pairs={{0,1},{4,5},{8,9},{12,13},{16,17},{20,21},{24,25},{28,29}} | collective-permute-start | bytes 1572872 | tf_op jit(solution)/shard_map/ppermute | solution.py:131
  30.6 5.2 %collective-permute-start.4 = (bf16[2,128,512]{2,1,0:T(8,128)(2,1)S(1)}, bf16[2,128,512]{2,1,0:T(8,128)(2,1)S(1)}, u32[]{:S(2)}, u32[]{:S(2)}) collective-permute-start(bf16[2,128,512]{2,1,0:T(8,128)(2,1)S(1)} %get-tuple-element.60), channel_id=1, source_target_pairs={{0,13},{4,1},{8,5},{12,9},{16,29},{20,17},{24,21},{28,25}} | collective-permute-start | bytes 786440 | tf_op jit(solution)/shard_map/ppermute | solution.py:133
  31.9 6.7 %collective-permute-start.3 = (bf16[2,128,512]{2,1,0:T(8,128)(2,1)S(1)}, bf16[2,128,512]{2,1,0:T(8,128)(2,1)S(1)}, u32[]{:S(2)}, u32[]{:S(2)}) collective-permute-start(bf16[2,128,512]{2,1,0:T(8,128)(2,1)S(1)} %get-tuple-element.59), channel_id=1, source_target_pairs={{0,5},{4,9},{8,13},{12,1},{16,21},{20,25},{24,29},{28,17}} | collective-permute-start | bytes 786440 | tf_op jit(solution)/shard_map/ppermute | solution.py:132
  42.4 2.2 %collective-permute-start.5 = (bf16[2,256,512]{2,1,0:T(8,128)(2,1)S(1)}, bf16[2,256,512]{2,1,0:T(8,128)(2,1)S(1)}, u32[]{:S(2)}, u32[]{:S(2)}) collective-permute-start(bf16[2,256,512]{2,1,0:T(8,128)(2,1)S(1)} %add_convert_fusion.2), channel_id=1, source_target_pairs={{1,2},{5,6},{9,10},{13,14},{17,18},{21,22},{25,26},{29,30}} | collective-permute-start | bytes 1572872 | tf_op jit(solution)/shard_map/ppermute | solution.py:131
  43.1 1.4 collective-permute-start.7
  48.2 4.9 %collective-permute-start.8 = (bf16[2,256,512]{2,1,0:T(8,128)(2,1)S(1)}, bf16[2,256,512]{2,1,0:T(8,128)(2,1)}, u32[]{:S(2)}, u32[]{:S(2)}) collective-permute-start(bf16[2,256,512]{2,1,0:T(8,128)(2,1)S(1)} %add_convert_fusion.1), channel_id=1, source_target_pairs={{2,3},{6,7},{10,11},{14,15},{18,19},{22,23},{26,27},{30,31}} | collective-permute-start | bytes 1572872 | tf_op jit(solution)/shard_map/ppermute | solution.py:131
  50.4 2.7 %collective-permute-start.10 = (bf16[2,128,512]{2,1,0:T(8,128)(2,1)}, bf16[2,128,512]{2,1,0:T(8,128)(2,1)}, u32[]{:S(2)}, u32[]{:S(2)}) collective-permute-start(bf16[2,128,512]{2,1,0:T(8,128)(2,1)} %get-tuple-element.56), channel_id=1, source_target_pairs={{2,15},{6,3},{10,7},{14,11},{18,31},{22,19},{26,23},{30,27}} | collective-permute-start | bytes 786440 | tf_op jit(solution)/shard_map/ppermute | solution.py:133
  51.7 1.4 collective-permute-start.9
  69.2 2.4 %collective-permute-start.11 = (f32[2,256,512]{2,1,0:T(8,128)S(1)}, f32[2,256,512]{2,1,0:T(8,128)S(1)}, u32[]{:S(2)}, u32[]{:S(2)}) collective-permute-start(f32[2,256,512]{2,1,0:T(8,128)S(1)} %fusion.21), channel_id=1, source_target_pairs={{3,2},{7,6},{11,10},{15,14},{19,18},{23,22},{27,26},{31,30}} | collective-permute-start | bytes 3145736 | tf_op jit(solution)/shard_map/ppermute | solution.py:176
  70.0 1.5 collective-permute-start.13
  75.2 2.3 %collective-permute-start.14 = (f32[2,256,512]{2,1,0:T(8,128)S(1)}, f32[2,256,512]{2,1,0:T(8,128)S(1)}, u32[]{:S(2)}, u32[]{:S(2)}) collective-permute-start(f32[2,256,512]{2,1,0:T(8,128)S(1)} %fusion.19), channel_id=1, source_target_pairs={{2,1},{6,5},{10,9},{14,13},{18,17},{22,21},{26,25},{30,29}} | collective-permute-start | bytes 3145736 | tf_op jit(solution)/shard_map/ppermute | solution.py:176
  76.0 1.4 collective-permute-start.16
  83.0 60.3 %collective-permute-start.17 = (f32[2,256,512]{2,1,0:T(8,128)}, f32[2,256,512]{2,1,0:T(8,128)}, u32[]{:S(2)}, u32[]{:S(2)}) collective-permute-start(f32[2,256,512]{2,1,0:T(8,128)} %fusion.17), channel_id=1, source_target_pairs={{1,0},{5,4},{9,8},{13,12},{17,16},{21,20},{25,24},{29,28}} | collective-permute-start | bytes 3145736 | tf_op jit(solution)/shard_map/ppermute | solution.py:176
  85.6 55.5 %collective-permute-start.19 = (bf16[2,128,512]{2,1,0:T(8,128)(2,1)S(1)}, bf16[2,128,512]{2,1,0:T(8,128)(2,1)S(1)}, u32[]{:S(2)}, u32[]{:S(2)}) collective-permute-start(bf16[2,128,512]{2,1,0:T(8,128)(2,1)S(1)} %get-tuple-element.48), channel_id=1, source_target_pairs={{1,4},{5,8},{9,12},{13,0},{17,20},{21,24},{25,28},{29,16}} | collective-permute-start | bytes 786440 | tf_op jit(solution)/shard_map/ppermute | solution.py:178
  86.9 56.4 %collective-permute-start.18 = (bf16[2,128,512]{2,1,0:T(8,128)(2,1)S(1)}, bf16[2,128,512]{2,1,0:T(8,128)(2,1)S(1)}, u32[]{:S(2)}, u32[]{:S(2)}) collective-permute-start(bf16[2,128,512]{2,1,0:T(8,128)(2,1)S(1)} %get-tuple-element.47), channel_id=1, source_target_pairs={{1,12},{5,0},{9,4},{13,8},{17,28},{21,16},{25,20},{29,24}} | collective-permute-start | bytes 786440 | tf_op jit(solution)/shard_map/ppermute | solution.py:177
  153.9 18.4 %collective-permute-start.25 = (bf16[2,400,512]{2,1,0:T(8,128)(2,1)}, bf16[2,400,512]{2,1,0:T(8,128)(2,1)}, u32[]{:S(2)}, u32[]{:S(2)}) collective-permute-start(bf16[2,400,512]{2,1,0:T(8,128)(2,1)} %fusion.99), channel_id=1, source_target_pairs={{0,4},{4,0},{8,12},{12,8},{1,5},{5,1},{9,13},{13,9},{2,6},{6,2},{1... | collective-permute-start | bytes 2457608 | tf_op jit(solution)/shard_map/ppermute | solution.py:41
  154.5 27.3 %collective-permute-start.24 = (bf16[2,256,512]{2,1,0:T(8,128)(2,1)S(1)}, bf16[2,256,512]{2,1,0:T(8,128)(2,1)S(1)}, u32[]{:S(2)}, u32[]{:S(2)}) collective-permute-start(bf16[2,256,512]{2,1,0:T(8,128)(2,1)S(1)} %copy-done.22), channel_id=1, source_target_pairs={{2,3},{6,7},{10,11},{14,15},{18,19},{22,23},{26,27},{30,31}} | collective-permute-start | bytes 1572872 | tf_op jit(solution)/shard_map/ppermute | solution.py:180
  155.2 26.6 %collective-permute-start.23 = (bf16[2,256,512]{2,1,0:T(8,128)(2,1)S(1)}, bf16[2,256,512]{2,1,0:T(8,128)(2,1)S(1)}, u32[]{:S(2)}, u32[]{:S(2)}) collective-permute-start(bf16[2,256,512]{2,1,0:T(8,128)(2,1)S(1)} %copy-done.24), channel_id=1, source_target_pairs={{1,2},{5,6},{9,10},{13,14},{17,18},{21,22},{25,26},{29,30}} | collective-permute-start | bytes 1572872 | tf_op jit(solution)/shard_map/ppermute | solution.py:180
  155.9 25.9 %collective-permute-start.22 = (bf16[2,256,512]{2,1,0:T(8,128)(2,1)}, bf16[2,256,512]{2,1,0:T(8,128)(2,1)S(1)}, u32[]{:S(2)}, u32[]{:S(2)}) collective-permute-start(bf16[2,256,512]{2,1,0:T(8,128)(2,1)} %copy-done.25), channel_id=1, source_target_pairs={{0,1},{4,5},{8,9},{12,13},{16,17},{20,21},{24,25},{28,29}} | collective-permute-start | bytes 1572872 | tf_op jit(solution)/shard_map/ppermute | solution.py:180
  159.6 18.6 %collective-permute-start.21 = (bf16[2,128,512]{2,1,0:T(8,128)(2,1)S(1)}, bf16[2,128,512]{2,1,0:T(8,128)(2,1)S(1)}, u32[]{:S(2)}, u32[]{:S(2)}) collective-permute-start(bf16[2,128,512]{2,1,0:T(8,128)(2,1)S(1)} %get-tuple-element.46), channel_id=1, source_target_pairs={{0,4},{4,8},{8,12},{12,0},{16,20},{20,24},{24,28},{28,16}} | collective-permute-start | bytes 786440 | tf_op jit(solution)/shard_map/ppermute | solution.py:185
  172.3 9.2 %collective-permute-start.20 = (bf16[2,128,512]{2,1,0:T(8,128)(2,1)S(1)}, bf16[2,128,512]{2,1,0:T(8,128)(2,1)S(1)}, u32[]{:S(2)}, u32[]{:S(2)}) collective-permute-start(bf16[2,128,512]{2,1,0:T(8,128)(2,1)S(1)} %get-tuple-element.45), channel_id=1, source_target_pairs={{0,12},{4,0},{8,4},{12,8},{16,28},{20,16},{24,20},{28,24}} | collective-permute-start | bytes 786440 | tf_op jit(solution)/shard_map/ppermute | solution.py:184
  178.2 18.3 %collective-permute-start.26 = (bf16[1,400,512]{2,1,0:T(8,128)(2,1)S(1)}, bf16[1,400,512]{2,1,0:T(8,128)(2,1)S(1)}, u32[]{:S(2)}, u32[]{:S(2)}) collective-permute-start(bf16[1,400,512]{2,1,0:T(8,128)(2,1)S(1)} %fusion.155), channel_id=1, source_target_pairs={{0,8},{4,12},{8,0},{12,4},{1,9},{5,13},{9,1},{13,5},{2,10},{6,14},... | collective-permute-start | bytes 1228808 | tf_op jit(solution)/shard_map/ppermute | solution.py:41
  (67 other events, 287.4 us)

commit v4 on v3

--- a/solution.py
+++ b/solution.py
@@ -25,9 +25,7 @@
     return blocks
 
 
-def halving_reduce_scatter(x, axis, devices, index):
-    if devices & (devices - 1):
-        return lax.psum_scatter(x, axis, scatter_dimension=0, tiled=True)
+def halving_reduce_scatter(x, axis, devices, index, pairs_of):
     rows = x.shape[0] // devices
     cur = x.reshape(devices, rows, x.shape[1]).astype(F32)
     dist = 1
@@ -37,8 +35,7 @@
         low, high = cur[:, 0], cur[:, 1]
         keep = jnp.where(bit == 0, low, high)
         send = jnp.where(bit == 0, high, low).astype(x.dtype)
-        pairs = [(i, i ^ dist) for i in range(devices)]
-        recv = lax.ppermute(send, axis, pairs)
+        recv = lax.ppermute(send, axis, pairs_of(dist))
         cur = keep + recv.astype(F32)
         dist *= 2
     return cur[0]
@@ -134,11 +131,35 @@
 
     h_in, agg, pre, act, normed, rstd = saved
 
+    norm_factor = 1.0 / math.sqrt(samples * node_rows * domains)
+    stacked = jnp.concatenate([h_in, agg], axis=2)
+    r1 = 2 * width // domains
+    r2 = width // domains
+    r3 = width // domains
+    pad_rows = 16
+    power_of_two = (domains & (domains - 1)) == 0
+
+    def reduce_grads(dpre, dout, gain_term, active):
+        gw1 = jnp.einsum("via,vid->ad", stacked, dpre, preferred_element_type=F32)
+        gw2 = jnp.einsum("via,vid->ad", act, dout, preferred_element_type=F32)
+        gain_rows = jnp.pad(
+            gain_term.reshape(domains, 1, r3), ((0, 0), (0, pad_rows - 1), (0, width - r3))
+        )
+        packed = jnp.concatenate(
+            [gw1.reshape(domains, r1, width), gw2.reshape(domains, r2, width), gain_rows], axis=1
+        ).astype(BF16)
+        packed = packed.reshape(domains * (r1 + r2 + pad_rows), width)
+        if not power_of_two:
+            return lax.psum_scatter(packed, "dom", scatter_dimension=0, tiled=True).astype(F32)
+
+        def pairs_of(dist):
+            return [(linear(d, active), linear(d ^ dist, active)) for d in range(domains)]
+
+        return halving_reduce_scatter(packed, both, domains, domain_index, pairs_of)
+
     g = cotangent
     grad_in = None
-    dpre_keep = None
-    dout_keep = None
-    gain_keep = None
+    reduced = None
     for tick in range(sections):
         gf = g.astype(F32)
         gain_term = jnp.sum(gf * normed, axis=(0, 1))
@@ -184,35 +205,15 @@
                 lax.ppermute(left_grad, both, route(active, active, -1)),
                 lax.ppermute(right_grad, both, route(active, active, 1)),
             )
+        reduced_now = reduce_grads(dpre, dout, gain_term, active)
         if grad_in is None:
-            grad_in, dpre_keep, dout_keep = g_new, dpre, dout
-            gain_keep = gain_term
+            grad_in = g_new
+            reduced = reduced_now
         else:
             grad_in = jnp.where(mine, g_new, grad_in)
-            dpre_keep = jnp.where(mine, dpre, dpre_keep)
-            dout_keep = jnp.where(mine, dout, dout_keep)
-            gain_keep = jnp.where(mine, gain_term, gain_keep)
-
-    norm_factor = 1.0 / math.sqrt(samples * node_rows * domains)
-    stacked = jnp.concatenate([h_in, agg], axis=2)
-    gw1 = jnp.einsum("via,vid->ad", stacked, dpre_keep, preferred_element_type=F32)
-    gw2 = jnp.einsum("via,vid->ad", act, dout_keep, preferred_element_type=F32)
-    r1 = gw1.shape[0] // domains
-    r2 = gw2.shape[0] // domains
-    r3 = gain_keep.shape[0] // domains
-    pad_rows = 16
-    gain_rows = jnp.pad(gain_keep.reshape(domains, 1, r3), ((0, 0), (0, pad_rows - 1), (0, width - r3)))
-    packed = jnp.concatenate(
-        [
-            gw1.reshape(domains, r1, width),
-            gw2.reshape(domains, r2, width),
-            gain_rows,
-        ],
-        axis=1,
-    ).astype(BF16)
-    packed = packed.reshape(domains * (r1 + r2 + pad_rows), width)
-    reduced = halving_reduce_scatter(packed, "dom", domains, domain_index)
-    reduced = reduced.astype(F32) * norm_factor
+            reduced = jnp.where(mine, reduced_now, reduced)
+
+    reduced = reduced * norm_factor
     g1 = reduced[:r1]
     g2 = reduced[r1 : r1 + r2]
     g3 = reduced[r1 + r2, :r3]

time: 200 us -> 223 us (1.11)
  starting transfers between devices: 39.2 us -> 57.7 us
  other arithmetic: 17.9 us -> 33.3 us
  waiting for transfers between devices: 88.6 us -> 80.1 us
  local copies, waits for them, and re-layouts: 20.8 us -> 15.1 us
  matrix products: 28.3 us -> 31.6 us
    ppermute x2 -> x8, starting transfers between devices: 1.54 us -> 16.3 us  [halving_reduce_scatter(): recv = lax.ppermute(send, axis, pairs_of(dist))]
    ppermute x2 -> x8, waiting for transfers between devices: 22.4 us -> 8.52 us  [halving_reduce_scatter(): recv = lax.ppermute(send, axis, pairs_of(dist))]
    ppermute x3, waiting for transfers between devices: 50.1 us -> 58.4 us  [shards(): lax.ppermute(right_grad, both, route(active, active - 1, 1))]
    unnamed x133 -> x120, local copies, waits for them, and re-layouts: 12.9 us -> 6.52 us
    convert_element_type x2 -> x8, other arithmetic: 1.12 us -> 5.22 us  [halving_reduce_scatter(): send = jnp.where(bit == 0, high, low).astype(x.dtype)]
    convert_element_type x8, other arithmetic: 0.4 us -> 3.4 us  [add_blocks(): values = values.reshape(samples, count, blk, width).astype(F32)]
    dot_general x2 -> x8, matrix products: 2.15 us -> 4.79 us  [the longest x4 2.94 us: reduce_grads(): gw1 = jnp.einsum('via,vid->ad', stacked, dpre, preferred_element_type=F32)]
    reshape x1 -> x4, other arithmetic: 1.59 us -> 3.98 us  [halving_reduce_scatter(): cur = cur.reshape(cur.shape[0] // 2, 2, rows, x.shape[1])]
  transfers between devices with their start and end apart: 27 -> 33, of which waited for: 8 -> 7; matrix products, arithmetic and copies ran while one was open for 7% -> 17% of each run, Pallas kernels for 0% -> 0%
where the time goes in v4:
time: 223 us; the launch traced here: 222 us
  waiting for transfers between devices  80.1 us (36%)
  starting transfers between devices  57.7 us (26%)
  other arithmetic  33.3 us (15%)
  matrix products  31.6 us (14%)
  local copies, waits for them, and re-layouts  15.1 us (7%)
  between operations  4.17 us (2%)
    ppermute x3, waiting for transfers between devices, shards(): lax.ppermute(right_grad, both, route(active, active - 1, 1))  58.4 us
    ppermute x8, starting transfers between devices, halving_reduce_scatter(): recv = lax.ppermute(send, axis, pairs_of(dist))  16.3 us
    ppermute x8, waiting for transfers between devices, halving_reduce_scatter(): recv = lax.ppermute(send, axis, pairs_of(dist))  8.52 us
    ppermute x1, starting transfers between devices, shards(): lax.ppermute(pick_blocks(in_blocks, send_left, hs), both, route(0, 0, -1))  6.99 us
    unnamed x120, local copies, waits for them, and re-layouts  6.52 us
    ppermute x1, waiting for transfers between devices, shards(): lax.ppermute(pick_blocks(in_blocks, send_right, hs), both, route(0, 0, 1))  6.41 us
    select_n x4, other arithmetic, shards(): saved = tuple((jnp.where(mine, a, b) for a, b in zip(res, saved)))  6.14 us
    dot_general x4, matrix products, forward_layer(): agg2 = jnp.einsum('ij,sjd->sid', adj2, h_ext, preferred_element_type=F32)  5.3 us
  transfers between devices with their start and end apart: 33, of which 7 were waited for; matrix products, arithmetic and copies ran while one was open for 17% of the time, Pallas kernels for 0%

profile of v4, /device:TPU:0, one launch (start us, length us, event | category | flops | bytes accessed | tf_op | source)
XLA Modules:
  0.0 221.9 jit_solution(1785283124783182080)
XLA Ops:
  5.9 7.0 %collective-permute-start.1 = (bf16[2,128,512]{1,2,0:T(8,128)(2,1)S(1)}, bf16[2,128,512]{1,2,0:T(8,128)(2,1)}, u32[]{:S(2)}, u32[]{:S(2)}) collective-permute-start(bf16[2,128,512]{1,2,0:T(8,128)(2,1)S(1)} %bitcast.394), channel_id=1, source_target_pairs={{0,12},{4,0},{8,4},{12,8},{16,28},{20,16},{24,20},{28,24}} | collective-permute-start | bytes 786440 | tf_op jit(solution)/shard_map/ppermute | solution.py:113
  13.7 1.9 collective-permute-start
  17.7 6.4 %collective-permute-done = bf16[2,128,512]{1,2,0:T(8,128)(2,1)} collective-permute-done((bf16[2,128,512]{1,2,0:T(8,128)(2,1)}, bf16[2,128,512]{1,2,0:T(8,128)(2,1)}, u32[]{:S(2)}, u32[]{:S(2)}) %collective-permute-start) | collective-permute-done | bytes 262176 | tf_op jit(solution)/shard_map/ppermute | solution.py:112
  24.1 1.8 convolution_bitcast_fusion.7
  31.8 2.6 %collective-permute-done.4 = bf16[2,128,512]{2,1,0:T(8,128)(2,1)S(1)} collective-permute-done((bf16[2,128,512]{2,1,0:T(8,128)(2,1)S(1)}, bf16[2,128,512]{2,1,0:T(8,128)(2,1)S(1)}, u32[]{:S(2)}, u32[]{:S(2)}) %collective-permute-start.4) | collective-permute-done | bytes 262176 | tf_op jit(solution)/shard_map/ppermute | solution.py:130
  34.4 2.8 %collective-permute-done.3 = bf16[2,128,512]{2,1,0:T(8,128)(2,1)S(1)} collective-permute-done((bf16[2,128,512]{2,1,0:T(8,128)(2,1)S(1)}, bf16[2,128,512]{2,1,0:T(8,128)(2,1)S(1)}, u32[]{:S(2)}, u32[]{:S(2)}) %collective-permute-start.3) | collective-permute-done | bytes 262176 | tf_op jit(solution)/shard_map/ppermute | solution.py:129
  48.9 1.9 dynamic-slice_bitcast_fusion.1
  53.5 2.1 convolution_bitcast_fusion
  56.1 2.5 %select_select_fusion.3 = (bf16[2,256,512]{2,1,0:T(8,128)(2,1)S(1)}, bf16[2,256,512]{2,1,0:T(8,128)(2,1)S(1)}) fusion(pred[]{:T(512)S(6)} %eq.119, pred[]{:T(512)S(6)} %eq.118, pred[]{:T(512)S(6)} %eq.111, f32[2,512,512]{2,1,0:T(8,128)S(1)} %convolution_bitcast_fusion, f32[2,512,512]{2,1,0:T(8,128)} %copy-done.27, f32[2,512,512]{2,1,0:T(8,128)S(1)} %copy-done.26, ...), kind=kLoop, calls=%fused_computation.245 | loop fusion | flops 2883584 | bytes 9437187 | tf_op jit(solution)/shard_map/jit(_where)/select_n | solution.py:124
  60.4 1.6 select_select_fusion
  68.7 2.5 %select_select_fusion.4 = (bf16[2,256,512]{2,1,0:T(8,128)(2,1)S(1)}, bf16[1,2,256,512]{3,2,1,0:T(8,128)(2,1)}) fusion(bf16[2,256,512]{2,1,0:T(8,128)(2,1)} %collective-permute-done.8, bf16[2,256,512]{2,1,0:T(8,128)(2,1)S(1)} %copy-done.37, bf16[2,256,512]{2,1,0:T(8,128)(2,1)S(1)} %copy-done.35, bf16[2,256,512]{2,1,0:T(8,128)(2,1)S(1)} %copy-done.3, ...), kind=kLoop, calls=%fused_computation.246 | loop fusion | flops 3145728 | bytes 5773315 | tf_op jit(solution)/shard_map/jit(_where)/select_n | solution.py:124
  83.9 2.6 %fusion = f32[1,2,400,512]{3,2,1,0:T(8,128)S(1)} fusion(bf16[2,400,512]{2,1,0:T(8,128)(2,1)} %collective-permute-done.31, f32[2,2,400,512]{3,2,0,1:T(8,128)} %copy-done.2, pred[]{:T(512)S(6)} %eq.126), kind=kLoop, calls=%fused_computation.9 | loop fusion | flops 1228800 | bytes 5734401 | tf_op jit(solution)/shard_map/reshape | solution.py:33
  87.5 2.0 fusion.54
  109.5 58.3 %collective-permute-done.19 = bf16[2,128,512]{2,1,0:T(8,128)(2,1)S(1)} collective-permute-done((bf16[2,128,512]{2,1,0:T(8,128)(2,1)S(1)}, bf16[2,128,512]{2,1,0:T(8,128)(2,1)S(1)}, u32[]{:S(2)}, u32[]{:S(2)}) %collective-permute-start.19) | collective-permute-done | bytes 262176 | tf_op jit(solution)/shard_map/ppermute | solution.py:199
  176.0 1.9 collective-permute-start.25
  178.8 2.1 collective-permute-start.22
  181.4 2.1 fusion.196
  183.5 3.9 %collective-permute-start.21 = (bf16[2,128,512]{2,1,0:T(8,128)(2,1)S(1)}, bf16[2,128,512]{2,1,0:T(8,128)(2,1)S(1)}, u32[]{:S(2)}, u32[]{:S(2)}) collective-permute-start(bf16[2,128,512]{2,1,0:T(8,128)(2,1)S(1)} %get-tuple-element.46), channel_id=1, source_target_pairs={{0,4},{4,8},{8,12},{12,0},{16,20},{20,24},{24,28},{28,16}} | collective-permute-start | bytes 786440 | tf_op jit(solution)/shard_map/ppermute | solution.py:206
  187.4 2.8 %collective-permute-done.25 = bf16[2,400,512]{2,1,0:T(8,128)(2,1)S(1)} collective-permute-done((bf16[2,400,512]{2,1,0:T(8,128)(2,1)S(1)}, bf16[2,400,512]{2,1,0:T(8,128)(2,1)S(1)}, u32[]{:S(2)}, u32[]{:S(2)}) %collective-permute-start.25) | collective-permute-done | bytes 819232 | tf_op jit(solution)/shard_map/ppermute | solution.py:38
  190.2 4.0 %collective-permute-start.20 = (bf16[2,128,512]{2,1,0:T(8,128)(2,1)S(1)}, bf16[2,128,512]{2,1,0:T(8,128)(2,1)}, u32[]{:S(2)}, u32[]{:S(2)}) collective-permute-start(bf16[2,128,512]{2,1,0:T(8,128)(2,1)S(1)} %get-tuple-element.45), channel_id=1, source_target_pairs={{0,12},{4,0},{8,4},{12,8},{16,28},{20,16},{24,20},{28,24}} | collective-permute-start | bytes 786440 | tf_op jit(solution)/shard_map/ppermute | solution.py:205
  199.8 7.1 %collective-permute-start.26 = (bf16[1,400,512]{2,1,0:T(8,128)(2,1)}, bf16[1,400,512]{2,1,0:T(8,128)(2,1)}, u32[]{:S(2)}, u32[]{:S(2)}) collective-permute-start(bf16[1,400,512]{2,1,0:T(8,128)(2,1)} %fusion.148), channel_id=1, source_target_pairs={{0,8},{4,12},{8,0},{12,4},{16,24},{20,28},{24,16},{28,20}} | collective-permute-start | bytes 1228808 | tf_op jit(solution)/shard_map/ppermute | solution.py:38
  209.0 2.7 %fusion.36 = bf16[1,2,256,512]{3,2,1,0:T(8,128)(2,1)} fusion(f32[2,256,512]{2,1,0:T(8,128)S(1)} %bitcast_select_fusion, f32[2,256,512]{2,1,0:T(8,128)S(1)} %bitcast_select_fusion.1, bf16[2,256,512]{2,1,0:T(8,128)(2,1)S(1)} %copy-done.48, bf16[2,256,512]{2,1,0:T(8,128)(2,1)} %get-tuple-element.41, f32[2,512,512]{2,1,0:T(8,128)S(1)} %copy-done.29, ...), kind=kOutput, calls=%fused_computation.92 | convolution fusion | flops 270794752 | bytes 6815747 | tf_op jit(solution)/shard_map/sip,vp->siv/dot_general | solution.py:178
  211.8 5.7 %collective-permute-done.26 = bf16[1,400,512]{2,1,0:T(8,128)(2,1)} collective-permute-done((bf16[1,400,512]{2,1,0:T(8,128)(2,1)}, bf16[1,400,512]{2,1,0:T(8,128)(2,1)}, u32[]{:S(2)}, u32[]{:S(2)}) %collective-permute-start.26) | collective-permute-done | bytes 409632 | tf_op jit(solution)/shard_map/ppermute | solution.py:38
  217.5 2.3 %fusion.109 = f32[1,400,512]{2,1,0:T(8,128)S(1)} fusion(bf16[1,400,512]{2,1,0:T(8,128)(2,1)} %collective-permute-done.32, bf16[1,400,512]{2,1,0:T(8,128)(2,1)} %collective-permute-done.30, bf16[1,400,512]{2,1,0:T(8,128)(2,1)} %collective-permute-done.28, bf16[1,400,512]{2,1,0:T(8,128)(2,1)} %collective-permute-done.26, f32[1,2,400,512]{3,2,1,0:T(8,128)S(1)} %copy-done.5, ...), kind=kLoop, calls=%fused_computation.195 | loop fusion | flops 3276800 | bytes 9011204 | tf_op jit(solution)/shard_map/mul | solution.py:216
  (287 shorter events, 87.0 us)
Async XLA Ops:
  5.9 11.8 %collective-permute-start.1 = (bf16[2,128,512]{1,2,0:T(8,128)(2,1)S(1)}, bf16[2,128,512]{1,2,0:T(8,128)(2,1)}, u32[]{:S(2)}, u32[]{:S(2)}) collective-permute-start(bf16[2,128,512]{1,2,0:T(8,128)(2,1)S(1)} %bitcast.394), channel_id=1, source_target_pairs={{0,12},{4,0},{8,4},{12,8},{16,28},{20,16},{24,20},{28,24}} | collective-permute-start | bytes 786440 | tf_op jit(solution)/shard_map/ppermute | solution.py:113
  13.7 10.4 %collective-permute-start = (bf16[2,128,512]{1,2,0:T(8,128)(2,1)}, bf16[2,128,512]{1,2,0:T(8,128)(2,1)}, u32[]{:S(2)}, u32[]{:S(2)}) collective-permute-start(bf16[2,128,512]{1,2,0:T(8,128)(2,1)} %bitcast.7), channel_id=1, source_target_pairs={{0,4},{4,8},{8,12},{12,0},{16,20},{20,24},{24,28},{28,16}} | collective-permute-start | bytes 786440 | tf_op jit(solution)/shard_map/ppermute | solution.py:112
  27.8 9.4 %collective-permute-start.2 = (bf16[2,256,512]{2,1,0:T(8,128)(2,1)S(1)}, bf16[2,256,512]{2,1,0:T(8,128)(2,1)S(1)}, u32[]{:S(2)}, u32[]{:S(2)}) collective-permute-start(bf16[2,256,512]{2,1,0:T(8,128)(2,1)S(1)} %add_convert_fusion.3), channel_id=1, source_target_pairs={{0,1},{4,5},{8,9},{12,13},{16,17},{20,21},{24,25},{28,29}} | collective-permute-start | bytes 1572872 | tf_op jit(solution)/shard_map/ppermute | solution.py:128
  29.2 5.2 %collective-permute-start.4 = (bf16[2,128,512]{2,1,0:T(8,128)(2,1)S(1)}, bf16[2,128,512]{2,1,0:T(8,128)(2,1)S(1)}, u32[]{:S(2)}, u32[]{:S(2)}) collective-permute-start(bf16[2,128,512]{2,1,0:T(8,128)(2,1)S(1)} %get-tuple-element.60), channel_id=1, source_target_pairs={{0,13},{4,1},{8,5},{12,9},{16,29},{20,17},{24,21},{28,25}} | collective-permute-start | bytes 786440 | tf_op jit(solution)/shard_map/ppermute | solution.py:130
  30.5 6.7 %collective-permute-start.3 = (bf16[2,128,512]{2,1,0:T(8,128)(2,1)S(1)}, bf16[2,128,512]{2,1,0:T(8,128)(2,1)S(1)}, u32[]{:S(2)}, u32[]{:S(2)}) collective-permute-start(bf16[2,128,512]{2,1,0:T(8,128)(2,1)S(1)} %get-tuple-element.59), channel_id=1, source_target_pairs={{0,5},{4,9},{8,13},{12,1},{16,21},{20,25},{24,29},{28,17}} | collective-permute-start | bytes 786440 | tf_op jit(solution)/shard_map/ppermute | solution.py:129
  47.4 6.1 %collective-permute-start.8 = (bf16[2,256,512]{2,1,0:T(8,128)(2,1)}, bf16[2,256,512]{2,1,0:T(8,128)(2,1)}, u32[]{:S(2)}, u32[]{:S(2)}) collective-permute-start(bf16[2,256,512]{2,1,0:T(8,128)(2,1)} %add_convert_fusion.1), channel_id=1, source_target_pairs={{2,3},{6,7},{10,11},{14,15},{18,19},{22,23},{26,27},{30,31}} | collective-permute-start | bytes 1572872 | tf_op jit(solution)/shard_map/ppermute | solution.py:128
  73.7 10.2 %collective-permute-start.31 = (bf16[2,400,512]{2,1,0:T(8,128)(2,1)}, bf16[2,400,512]{2,1,0:T(8,128)(2,1)}, u32[]{:S(2)}, u32[]{:S(2)}) collective-permute-start(bf16[2,400,512]{2,1,0:T(8,128)(2,1)} %fusion.105), channel_id=1, source_target_pairs={{3,7},{7,3},{11,15},{15,11},{19,23},{23,19},{27,31},{31,27}} | collective-permute-start | bytes 2457608 | tf_op jit(solution)/shard_map/ppermute | solution.py:38
  76.7 10.8 %collective-permute-start.11 = (f32[2,256,512]{2,1,0:T(8,128)}, f32[2,256,512]{2,1,0:T(8,128)}, u32[]{:S(2)}, u32[]{:S(2)}) collective-permute-start(f32[2,256,512]{2,1,0:T(8,128)} %fusion.24), channel_id=1, source_target_pairs={{3,2},{7,6},{11,10},{15,14},{19,18},{23,22},{27,26},{31,30}} | collective-permute-start | bytes 3145736 | tf_op jit(solution)/shard_map/ppermute | solution.py:197
  89.5 106.1 %collective-permute-start.24 = (bf16[2,256,512]{2,1,0:T(8,128)(2,1)S(1)}, bf16[2,256,512]{2,1,0:T(8,128)(2,1)S(1)}, u32[]{:S(2)}, u32[]{:S(2)}) collective-permute-start(bf16[2,256,512]{2,1,0:T(8,128)(2,1)S(1)} %get-tuple-element.43), channel_id=1, source_target_pairs={{2,3},{6,7},{10,11},{14,15},{18,19},{22,23},{26,27},{30,31}} | collective-permute-start | bytes 1572872 | tf_op jit(solution)/shard_map/ppermute | solution.py:201
  93.2 5.0 %collective-permute-start.14 = (f32[2,256,512]{2,1,0:T(8,128)S(1)}, f32[2,256,512]{2,1,0:T(8,128)S(1)}, u32[]{:S(2)}, u32[]{:S(2)}) collective-permute-start(f32[2,256,512]{2,1,0:T(8,128)S(1)} %fusion.22), channel_id=1, source_target_pairs={{2,1},{6,5},{10,9},{14,13},{18,17},{22,21},{26,25},{30,29}} | collective-permute-start | bytes 3145736 | tf_op jit(solution)/shard_map/ppermute | solution.py:197
  97.3 9.5 %collective-permute-start.29 = (bf16[2,400,512]{2,1,0:T(8,128)(2,1)S(1)}, bf16[2,400,512]{2,1,0:T(8,128)(2,1)S(1)}, u32[]{:S(2)}, u32[]{:S(2)}) collective-permute-start(bf16[2,400,512]{2,1,0:T(8,128)(2,1)S(1)} %fusion.104), channel_id=1, source_target_pairs={{2,6},{6,2},{10,14},{14,10},{18,22},{22,18},{26,30},{30,26}} | collective-permute-start | bytes 2457608 | tf_op jit(solution)/shard_map/ppermute | solution.py:38
  102.8 67.9 %collective-permute-start.17 = (f32[2,256,512]{2,1,0:T(8,128)S(1)}, f32[2,256,512]{2,1,0:T(8,128)S(1)}, u32[]{:S(2)}, u32[]{:S(2)}) collective-permute-start(f32[2,256,512]{2,1,0:T(8,128)S(1)} %fusion.20), channel_id=1, source_target_pairs={{1,0},{5,4},{9,8},{13,12},{17,16},{21,20},{25,24},{29,28}} | collective-permute-start | bytes 3145736 | tf_op jit(solution)/shard_map/ppermute | solution.py:197
  104.7 65.5 %collective-permute-start.27 = (bf16[2,400,512]{2,1,0:T(8,128)(2,1)S(1)}, bf16[2,400,512]{2,1,0:T(8,128)(2,1)S(1)}, u32[]{:S(2)}, u32[]{:S(2)}) collective-permute-start(bf16[2,400,512]{2,1,0:T(8,128)(2,1)S(1)} %fusion.103), channel_id=1, source_target_pairs={{1,5},{5,1},{9,13},{13,9},{17,21},{21,17},{25,29},{29,25}} | collective-permute-start | bytes 2457608 | tf_op jit(solution)/shard_map/ppermute | solution.py:38
  105.5 62.3 %collective-permute-start.19 = (bf16[2,128,512]{2,1,0:T(8,128)(2,1)S(1)}, bf16[2,128,512]{2,1,0:T(8,128)(2,1)S(1)}, u32[]{:S(2)}, u32[]{:S(2)}) collective-permute-start(bf16[2,128,512]{2,1,0:T(8,128)(2,1)S(1)} %get-tuple-element.48), channel_id=1, source_target_pairs={{1,4},{5,8},{9,12},{13,0},{17,20},{21,24},{25,28},{29,16}} | collective-permute-start | bytes 786440 | tf_op jit(solution)/shard_map/ppermute | solution.py:199
  106.8 63.4 %collective-permute-start.18 = (bf16[2,128,512]{2,1,0:T(8,128)(2,1)S(1)}, bf16[2,128,512]{2,1,0:T(8,128)(2,1)S(1)}, u32[]{:S(2)}, u32[]{:S(2)}) collective-permute-start(bf16[2,128,512]{2,1,0:T(8,128)(2,1)S(1)} %get-tuple-element.47), channel_id=1, source_target_pairs={{1,12},{5,0},{9,4},{13,8},{17,28},{21,16},{25,20},{29,24}} | collective-permute-start | bytes 786440 | tf_op jit(solution)/shard_map/ppermute | solution.py:198
  167.8 29.2 %collective-permute-start.23 = (bf16[2,256,512]{2,1,0:T(8,128)(2,1)S(1)}, bf16[2,256,512]{2,1,0:T(8,128)(2,1)S(1)}, u32[]{:S(2)}, u32[]{:S(2)}) collective-permute-start(bf16[2,256,512]{2,1,0:T(8,128)(2,1)S(1)} %get-tuple-element.42), channel_id=1, source_target_pairs={{1,2},{5,6},{9,10},{13,14},{17,18},{21,22},{25,26},{29,30}} | collective-permute-start | bytes 1572872 | tf_op jit(solution)/shard_map/ppermute | solution.py:201
  176.0 14.2 %collective-permute-start.25 = (bf16[2,400,512]{2,1,0:T(8,128)(2,1)S(1)}, bf16[2,400,512]{2,1,0:T(8,128)(2,1)S(1)}, u32[]{:S(2)}, u32[]{:S(2)}) collective-permute-start(bf16[2,400,512]{2,1,0:T(8,128)(2,1)S(1)} %fusion.102), channel_id=1, source_target_pairs={{0,4},{4,0},{8,12},{12,8},{16,20},{20,16},{24,28},{28,24}} | collective-permute-start | bytes 2457608 | tf_op jit(solution)/shard_map/ppermute | solution.py:38
  178.8 29.7 %collective-permute-start.22 = (bf16[2,256,512]{2,1,0:T(8,128)(2,1)}, bf16[2,256,512]{2,1,0:T(8,128)(2,1)}, u32[]{:S(2)}, u32[]{:S(2)}) collective-permute-start(bf16[2,256,512]{2,1,0:T(8,128)(2,1)} %get-tuple-element.41), channel_id=1, source_target_pairs={{0,1},{4,5},{8,9},{12,13},{16,17},{20,21},{24,25},{28,29}} | collective-permute-start | bytes 1572872 | tf_op jit(solution)/shard_map/ppermute | solution.py:201
  183.5 14.9 %collective-permute-start.21 = (bf16[2,128,512]{2,1,0:T(8,128)(2,1)S(1)}, bf16[2,128,512]{2,1,0:T(8,128)(2,1)S(1)}, u32[]{:S(2)}, u32[]{:S(2)}) collective-permute-start(bf16[2,128,512]{2,1,0:T(8,128)(2,1)S(1)} %get-tuple-element.46), channel_id=1, source_target_pairs={{0,4},{4,8},{8,12},{12,0},{16,20},{20,24},{24,28},{28,16}} | collective-permute-start | bytes 786440 | tf_op jit(solution)/shard_map/ppermute | solution.py:206
  190.2 9.6 %collective-permute-start.20 = (bf16[2,128,512]{2,1,0:T(8,128)(2,1)S(1)}, bf16[2,128,512]{2,1,0:T(8,128)(2,1)}, u32[]{:S(2)}, u32[]{:S(2)}) collective-permute-start(bf16[2,128,512]{2,1,0:T(8,128)(2,1)S(1)} %get-tuple-element.45), channel_id=1, source_target_pairs={{0,12},{4,0},{8,4},{12,8},{16,28},{20,16},{24,20},{28,24}} | collective-permute-start | bytes 786440 | tf_op jit(solution)/shard_map/ppermute | solution.py:205
  195.6 16.2 %collective-permute-start.32 = (bf16[1,400,512]{2,1,0:T(8,128)(2,1)}, bf16[1,400,512]{2,1,0:T(8,128)(2,1)}, u32[]{:S(2)}, u32[]{:S(2)}) collective-permute-start(bf16[1,400,512]{2,1,0:T(8,128)(2,1)} %fusion.151), channel_id=1, source_target_pairs={{3,11},{7,15},{11,3},{15,7},{19,27},{23,31},{27,19},{31,23}} | collective-permute-start | bytes 1228808 | tf_op jit(solution)/shard_map/ppermute | solution.py:38
  197.0 14.8 %collective-permute-start.30 = (bf16[1,400,512]{2,1,0:T(8,128)(2,1)}, bf16[1,400,512]{2,1,0:T(8,128)(2,1)}, u32[]{:S(2)}, u32[]{:S(2)}) collective-permute-start(bf16[1,400,512]{2,1,0:T(8,128)(2,1)} %fusion.150), channel_id=1, source_target_pairs={{2,10},{6,14},{10,2},{14,6},{18,26},{22,30},{26,18},{30,22}} | collective-permute-start | bytes 1228808 | tf_op jit(solution)/shard_map/ppermute | solution.py:38
  198.4 13.4 %collective-permute-start.28 = (bf16[1,400,512]{2,1,0:T(8,128)(2,1)}, bf16[1,400,512]{2,1,0:T(8,128)(2,1)}, u32[]{:S(2)}, u32[]{:S(2)}) collective-permute-start(bf16[1,400,512]{2,1,0:T(8,128)(2,1)} %fusion.149), channel_id=1, source_target_pairs={{1,9},{5,13},{9,1},{13,5},{17,25},{21,29},{25,17},{29,21}} | collective-permute-start | bytes 1228808 | tf_op jit(solution)/shard_map/ppermute | solution.py:38
  199.8 17.7 %collective-permute-start.26 = (bf16[1,400,512]{2,1,0:T(8,128)(2,1)}, bf16[1,400,512]{2,1,0:T(8,128)(2,1)}, u32[]{:S(2)}, u32[]{:S(2)}) collective-permute-start(bf16[1,400,512]{2,1,0:T(8,128)(2,1)} %fusion.148), channel_id=1, source_target_pairs={{0,8},{4,12},{8,0},{12,4},{16,24},{20,28},{24,16},{28,20}} | collective-permute-start | bytes 1228808 | tf_op jit(solution)/shard_map/ppermute | solution.py:38
  (65 other events, 347.0 us)

commit v5 on v3

--- a/solution.py
+++ b/solution.py
@@ -68,8 +68,12 @@
     ext = nb + 2 * hs
     margin = hs * blk
     offset = domain_index * nb
-    send_right = jnp.take(halo_from_left, (domain_index + 1) % domains, axis=0) - offset
-    send_left = jnp.take(halo_from_right, (domain_index + domains - 1) % domains, axis=0) - offset
+    dom_ids = jnp.arange(domains)[:, None]
+    send_right = jnp.sum(jnp.where(dom_ids == (domain_index + 1) % domains, halo_from_left, 0), axis=0) - offset
+    send_left = (
+        jnp.sum(jnp.where(dom_ids == (domain_index + domains - 1) % domains, halo_from_right, 0), axis=0)
+        - offset
+    )
 
     live = (jnp.arange(slot_count) < tile_count[0]).astype(F32)
     row_oh = (tile_rows[:, None] == jnp.arange(nb)[None, :]).astype(F32) * live[:, None]
@@ -117,8 +121,10 @@
     h = node_input
     saved = None
     saved_out = None
+    last_res = None
     for tick in range(sections):
         out, res = forward_layer(h, left, right)
+        last_res = res
         if saved is None:
             saved = res
             saved_out = out
@@ -133,6 +139,7 @@
             right = lax.ppermute(pick_blocks(out_blocks, send_left, hs), both, route(tick, tick + 1, -1))
 
     h_in, agg, pre, act, normed, rstd = saved
+    _, _, pre_last, _, normed_last, rstd_last = last_res
 
     g = cotangent
     grad_in = None
@@ -140,20 +147,24 @@
     dout_keep = None
     gain_keep = None
     for tick in range(sections):
+        if tick == 0:
+            pre_t, normed_t, rstd_t = pre_last, normed_last, rstd_last
+        else:
+            pre_t, normed_t, rstd_t = pre, normed, rstd
         gf = g.astype(F32)
-        gain_term = jnp.sum(gf * normed, axis=(0, 1))
+        gain_term = jnp.sum(gf * normed_t, axis=(0, 1))
         dn = gf * gain_row
         dout = (
-            rstd
+            rstd_t
             * (
                 dn
                 - jnp.mean(dn, axis=-1, keepdims=True)
-                - normed * jnp.mean(dn * normed, axis=-1, keepdims=True)
+                - normed_t * jnp.mean(dn * normed_t, axis=-1, keepdims=True)
             )
         ).astype(BF16)
         dact = jnp.einsum("sip,vp->siv", dout, w_2, preferred_element_type=F32)
-        sig = jax.nn.sigmoid(pre)
-        dpre = (dact * sig * (1.0 + pre * (1.0 - sig))).astype(BF16)
+        sig = jax.nn.sigmoid(pre_t)
+        dpre = (dact * sig * (1.0 + pre_t * (1.0 - sig))).astype(BF16)
         gnode = gf + jnp.einsum("sip,vp->siv", dpre, w_a, preferred_element_type=F32)
         dagg = jnp.einsum("sip,vp->siv", dpre, w_b, preferred_element_type=F32).astype(BF16)
         spread = jnp.einsum(

time: 200 us -> 197 us (0.985)
  local copies, waits for them, and re-layouts: 20.8 us -> 16.7 us
    another operation x2 -> x0, local copies, waits for them, and re-layouts: 2.57 us -> none  [the longest x1 1.33 us: shards(): jnp.take(halo_from_left, (domain_index + 1) % domains, axis=0) - offset]
    reduce_sum x4 -> x5, other arithmetic: 4.43 us -> 5.85 us  [the longest x4 4.44 us: shards(): gain_term = jnp.sum(gf * normed_t, axis=(0, 1))]
where the time goes in v5:
time: 197 us; the launch traced here: 196 us
  waiting for transfers between devices  88.6 us (45%)
  starting transfers between devices  39.4 us (20%)
  matrix products  28.3 us (14%)
  other arithmetic  19.4 us (10%)
  local copies, waits for them, and re-layouts  16.7 us (8%)
  between operations  4.1 us (2%)
    ppermute x3, waiting for transfers between devices, shards(): lax.ppermute(right_grad, both, route(active, active - 1, 1))  50.1 us
    ppermute x2, waiting for transfers between devices, halving_reduce_scatter(): recv = lax.ppermute(send, axis, pairs)  22.4 us
    unnamed x133, local copies, waits for them, and re-layouts  11.4 us
    ppermute x1, starting transfers between devices, shards(): lax.ppermute(pick_blocks(in_blocks, send_left, hs), both, route(0, 0, -1))  6.99 us
    ppermute x1, waiting for transfers between devices, shards(): lax.ppermute(pick_blocks(in_blocks, send_right, hs), both, route(0, 0, 1))  6.41 us
    select_n x3, other arithmetic, shards(): saved = tuple((jnp.where(mine, a, b) for a, b in zip(res, saved)))  6.27 us
    dot_general x4, matrix products, forward_layer(): agg2 = jnp.einsum('ij,sjd->sid', adj2, h_ext, preferred_element_type=F32)  5.24 us
    reduce_sum x4, other arithmetic, shards(): gain_term = jnp.sum(gf * normed_t, axis=(0, 1))  4.44 us
  transfers between devices with their start and end apart: 27, of which 8 were waited for; matrix products, arithmetic and copies ran while one was open for 7% of the time, Pallas kernels for 0%

profile of v5, /device:TPU:0, one launch (start us, length us, event | category | flops | bytes accessed | tf_op | source)
XLA Modules:
  0.0 196.4 jit_solution(9338886439313158899)
XLA Ops:
  4.7 7.0 %collective-permute-start.1 = (bf16[2,128,512]{1,2,0:T(8,128)(2,1)S(1)}, bf16[2,128,512]{1,2,0:T(8,128)(2,1)}, u32[]{:S(2)}, u32[]{:S(2)}) collective-permute-start(bf16[2,128,512]{1,2,0:T(8,128)(2,1)S(1)} %bitcast.276), channel_id=1, source_target_pairs={{0,12},{4,0},{8,4},{12,8},{16,28},{20,16},{24,20},{28,24}} | collective-permute-start | bytes 786440 | tf_op jit(solution)/shard_map/ppermute | solution.py:120
  12.5 1.9 collective-permute-start
  16.5 6.4 %collective-permute-done = bf16[2,128,512]{1,2,0:T(8,128)(2,1)} collective-permute-done((bf16[2,128,512]{1,2,0:T(8,128)(2,1)}, bf16[2,128,512]{1,2,0:T(8,128)(2,1)}, u32[]{:S(2)}, u32[]{:S(2)}) %collective-permute-start) | collective-permute-done | bytes 262176 | tf_op jit(solution)/shard_map/ppermute | solution.py:119
  22.9 1.8 convolution_bitcast_fusion.7
  32.1 2.6 %collective-permute-done.4 = bf16[2,128,512]{2,1,0:T(8,128)(2,1)S(1)} collective-permute-done((bf16[2,128,512]{2,1,0:T(8,128)(2,1)S(1)}, bf16[2,128,512]{2,1,0:T(8,128)(2,1)S(1)}, u32[]{:S(2)}, u32[]{:S(2)}) %collective-permute-start.4) | collective-permute-done | bytes 262176 | tf_op jit(solution)/shard_map/ppermute | solution.py:139
  34.7 2.8 %collective-permute-done.3 = bf16[2,128,512]{2,1,0:T(8,128)(2,1)S(1)} collective-permute-done((bf16[2,128,512]{2,1,0:T(8,128)(2,1)S(1)}, bf16[2,128,512]{2,1,0:T(8,128)(2,1)S(1)}, u32[]{:S(2)}, u32[]{:S(2)}) %collective-permute-start.3) | collective-permute-done | bytes 262176 | tf_op jit(solution)/shard_map/ppermute | solution.py:138
  46.9 1.5 collective-permute-start.8
  51.9 2.0 %convolution_bitcast_fusion = f32[2,512,512]{2,1,0:T(8,128)S(1)} fusion(bf16[2,128,512]{2,1,0:T(8,128)(2,1)} %collective-permute-done.10, bf16[2,256,512]{2,1,0:T(8,128)(2,1)} %collective-permute-done.8, bf16[2,128,512]{2,1,0:T(8,128)(2,1)} %collective-permute-done.9, bf16[256,512]{1,0:T(8,128)(2,1)S(1)} %fusion.101, bf16[256,512]{1,0:T(8,128)(2,1)S(1)} %bitcast.250), kind=kOutput, calls=%fused_computation.6 | convolution fusion | flops 541065216 | bytes 3670016 | tf_op jit(solution)/shard_map/ij,sjd->sid/dot_general | solution.py:106
  54.4 3.4 %select_select_fusion.2 = (bf16[2,256,512]{2,1,0:T(8,128)(2,1)}, bf16[2,256,512]{2,1,0:T(8,128)(2,1)S(1)}) fusion(pred[]{:T(512)S(6)} %eq.133, pred[]{:T(512)S(6)} %eq.132, pred[]{:T(512)S(6)} %eq.121, f32[2,512,512]{2,1,0:T(8,128)S(1)} %convolution_bitcast_fusion, f32[2,512,512]{2,1,0:T(8,128)} %copy-done.19, f32[2,512,512]{2,1,0:T(8,128)S(1)} %copy-done.18, ...), kind=kLoop, calls=%fused_computation.220 | loop fusion | flops 2883584 | bytes 9437187 | tf_op jit(solution)/shard_map/jit(_where)/select_n | solution.py:133
  59.4 1.5 select_select_fusion
  77.6 1.8 fusion.203
  85.8 2.8 %select_select_fusion.3 = (bf16[2,256,512]{2,1,0:T(8,128)(2,1)S(1)}, bf16[1,2,256,512]{3,2,1,0:T(8,128)(2,1)}) fusion(bf16[2,256,512]{2,1,0:T(8,128)(2,1)} %collective-permute-done.8, bf16[2,256,512]{2,1,0:T(8,128)(2,1)} %copy-done.31, bf16[2,256,512]{2,1,0:T(8,128)(2,1)} %copy-done.30, bf16[2,256,512]{2,1,0:T(8,128)(2,1)S(1)} %copy-done.5, pred[]{:T(512)S(6)} %eq.133, ...), kind=kLoop, calls=%fused_computation.221 | loop fusion | flops 3145728 | bytes 5773315 | tf_op jit(solution)/shard_map/jit(_where)/select_n | solution.py:133
  88.6 50.0 %collective-permute-done.19 = bf16[2,128,512]{2,1,0:T(8,128)(2,1)S(1)} collective-permute-done((bf16[2,128,512]{2,1,0:T(8,128)(2,1)S(1)}, bf16[2,128,512]{2,1,0:T(8,128)(2,1)S(1)}, u32[]{:S(2)}, u32[]{:S(2)}) %collective-permute-start.19) | collective-permute-done | bytes 262176 | tf_op jit(solution)/shard_map/ppermute | solution.py:189
  138.7 2.1 %collective-permute-done.18 = bf16[2,128,512]{2,1,0:T(8,128)(2,1)S(1)} collective-permute-done((bf16[2,128,512]{2,1,0:T(8,128)(2,1)S(1)}, bf16[2,128,512]{2,1,0:T(8,128)(2,1)S(1)}, u32[]{:S(2)}, u32[]{:S(2)}) %collective-permute-start.18) | collective-permute-done | bytes 262176 | tf_op jit(solution)/shard_map/ppermute | solution.py:188
  140.9 2.0 %fusion.48 = (bf16[512]{0:T(512)(128)(2,1)S(1)}, f32[2,256]{1,0:T(2,128)S(1)}, f32[2,256]{1,0:T(2,128)S(1)}, bf16[2,256,512]{2,1,0:T(8,128)(2,1)S(1)}) fusion(f32[2,256,512]{2,1,0:T(8,128)S(1)} %get-tuple-element.21, f32[512]{0:T(512)S(1)} %bitcast.273, f32[2,128,512]{2,1,0:T(8,128)S(1)} %convert_element_type.247, ...), kind=kLoop, calls=%fused_computation.86 | loop fusion | flops 3144192 | bytes 3677696 | tf_op jit(solution)/shard_map/reduce_sum | solution.py:155
  148.8 1.7 copy-done.3
  154.9 1.5 convolution_convert_fusion
  157.2 3.4 %collective-permute-start.21 = (bf16[2,128,512]{2,1,0:T(8,128)(2,1)S(1)}, bf16[2,128,512]{2,1,0:T(8,128)(2,1)S(1)}, u32[]{:S(2)}, u32[]{:S(2)}) collective-permute-start(bf16[2,128,512]{2,1,0:T(8,128)(2,1)S(1)} %get-tuple-element.24), channel_id=1, source_target_pairs={{0,4},{4,8},{8,12},{12,0},{16,20},{20,24},{24,28},{28,16}} | collective-permute-start | bytes 786440 | tf_op jit(solution)/shard_map/ppermute | solution.py:196
  160.7 9.2 %collective-permute-done.25 = bf16[2,400,512]{2,1,0:T(8,128)(2,1)} collective-permute-done((bf16[2,400,512]{2,1,0:T(8,128)(2,1)}, bf16[2,400,512]{2,1,0:T(8,128)(2,1)}, u32[]{:S(2)}, u32[]{:S(2)}) %collective-permute-start.25) | collective-permute-done | bytes 819232 | tf_op jit(solution)/shard_map/ppermute | solution.py:41
  169.9 4.2 %collective-permute-start.20 = (bf16[2,128,512]{2,1,0:T(8,128)(2,1)S(1)}, bf16[2,128,512]{2,1,0:T(8,128)(2,1)S(1)}, u32[]{:S(2)}, u32[]{:S(2)}) collective-permute-start(bf16[2,128,512]{2,1,0:T(8,128)(2,1)S(1)} %get-tuple-element.23), channel_id=1, source_target_pairs={{0,12},{4,0},{8,4},{12,8},{16,28},{20,16},{24,20},{28,24}} | collective-permute-start | bytes 786440 | tf_op jit(solution)/shard_map/ppermute | solution.py:195
  174.1 1.6 fusion
  177.0 2.1 %collective-permute-done.20 = bf16[2,128,512]{2,1,0:T(8,128)(2,1)S(1)} collective-permute-done((bf16[2,128,512]{2,1,0:T(8,128)(2,1)S(1)}, bf16[2,128,512]{2,1,0:T(8,128)(2,1)S(1)}, u32[]{:S(2)}, u32[]{:S(2)}) %collective-permute-start.20) | collective-permute-done | bytes 262176 | tf_op jit(solution)/shard_map/ppermute | solution.py:195
  179.4 1.6 fusion.28
  181.0 13.2 %collective-permute-done.26 = bf16[1,400,512]{2,1,0:T(8,128)(2,1)S(1)} collective-permute-done((bf16[1,400,512]{2,1,0:T(8,128)(2,1)S(1)}, bf16[1,400,512]{2,1,0:T(8,128)(2,1)S(1)}, u32[]{:S(2)}, u32[]{:S(2)}) %collective-permute-start.26) | collective-permute-done | bytes 409632 | tf_op jit(solution)/shard_map/ppermute | solution.py:41
  (268 shorter events, 64.1 us)
Async XLA Ops:
  4.7 11.8 %collective-permute-start.1 = (bf16[2,128,512]{1,2,0:T(8,128)(2,1)S(1)}, bf16[2,128,512]{1,2,0:T(8,128)(2,1)}, u32[]{:S(2)}, u32[]{:S(2)}) collective-permute-start(bf16[2,128,512]{1,2,0:T(8,128)(2,1)S(1)} %bitcast.276), channel_id=1, source_target_pairs={{0,12},{4,0},{8,4},{12,8},{16,28},{20,16},{24,20},{28,24}} | collective-permute-start | bytes 786440 | tf_op jit(solution)/shard_map/ppermute | solution.py:120
  12.5 10.4 %collective-permute-start = (bf16[2,128,512]{1,2,0:T(8,128)(2,1)}, bf16[2,128,512]{1,2,0:T(8,128)(2,1)}, u32[]{:S(2)}, u32[]{:S(2)}) collective-permute-start(bf16[2,128,512]{1,2,0:T(8,128)(2,1)} %bitcast.3), channel_id=1, source_target_pairs={{0,4},{4,8},{8,12},{12,0},{16,20},{20,24},{24,28},{28,16}} | collective-permute-start | bytes 786440 | tf_op jit(solution)/shard_map/ppermute | solution.py:119
  28.0 9.4 %collective-permute-start.2 = (bf16[2,256,512]{2,1,0:T(8,128)(2,1)S(1)}, bf16[2,256,512]{2,1,0:T(8,128)(2,1)S(1)}, u32[]{:S(2)}, u32[]{:S(2)}) collective-permute-start(bf16[2,256,512]{2,1,0:T(8,128)(2,1)S(1)} %add_convert_fusion.3), channel_id=1, source_target_pairs={{0,1},{4,5},{8,9},{12,13},{16,17},{20,21},{24,25},{28,29}} | collective-permute-start | bytes 1572872 | tf_op jit(solution)/shard_map/ppermute | solution.py:137
  29.4 5.2 %collective-permute-start.4 = (bf16[2,128,512]{2,1,0:T(8,128)(2,1)S(1)}, bf16[2,128,512]{2,1,0:T(8,128)(2,1)S(1)}, u32[]{:S(2)}, u32[]{:S(2)}) collective-permute-start(bf16[2,128,512]{2,1,0:T(8,128)(2,1)S(1)} %get-tuple-element.38), channel_id=1, source_target_pairs={{0,13},{4,1},{8,5},{12,9},{16,29},{20,17},{24,21},{28,25}} | collective-permute-start | bytes 786440 | tf_op jit(solution)/shard_map/ppermute | solution.py:139
  30.7 6.7 %collective-permute-start.3 = (bf16[2,128,512]{2,1,0:T(8,128)(2,1)S(1)}, bf16[2,128,512]{2,1,0:T(8,128)(2,1)S(1)}, u32[]{:S(2)}, u32[]{:S(2)}) collective-permute-start(bf16[2,128,512]{2,1,0:T(8,128)(2,1)S(1)} %get-tuple-element.37), channel_id=1, source_target_pairs={{0,5},{4,9},{8,13},{12,1},{16,21},{20,25},{24,29},{28,17}} | collective-permute-start | bytes 786440 | tf_op jit(solution)/shard_map/ppermute | solution.py:138
  41.1 2.2 %collective-permute-start.5 = (bf16[2,256,512]{2,1,0:T(8,128)(2,1)S(1)}, bf16[2,256,512]{2,1,0:T(8,128)(2,1)S(1)}, u32[]{:S(2)}, u32[]{:S(2)}) collective-permute-start(bf16[2,256,512]{2,1,0:T(8,128)(2,1)S(1)} %add_convert_fusion.2), channel_id=1, source_target_pairs={{1,2},{5,6},{9,10},{13,14},{17,18},{21,22},{25,26},{29,30}} | collective-permute-start | bytes 1572872 | tf_op jit(solution)/shard_map/ppermute | solution.py:137
  41.9 1.4 collective-permute-start.7
  46.9 4.9 %collective-permute-start.8 = (bf16[2,256,512]{2,1,0:T(8,128)(2,1)S(1)}, bf16[2,256,512]{2,1,0:T(8,128)(2,1)}, u32[]{:S(2)}, u32[]{:S(2)}) collective-permute-start(bf16[2,256,512]{2,1,0:T(8,128)(2,1)S(1)} %add_convert_fusion.1), channel_id=1, source_target_pairs={{2,3},{6,7},{10,11},{14,15},{18,19},{22,23},{26,27},{30,31}} | collective-permute-start | bytes 1572872 | tf_op jit(solution)/shard_map/ppermute | solution.py:137
  49.1 2.7 %collective-permute-start.10 = (bf16[2,128,512]{2,1,0:T(8,128)(2,1)}, bf16[2,128,512]{2,1,0:T(8,128)(2,1)}, u32[]{:S(2)}, u32[]{:S(2)}) collective-permute-start(bf16[2,128,512]{2,1,0:T(8,128)(2,1)} %get-tuple-element.34), channel_id=1, source_target_pairs={{2,15},{6,3},{10,7},{14,11},{18,31},{22,19},{26,23},{30,27}} | collective-permute-start | bytes 786440 | tf_op jit(solution)/shard_map/ppermute | solution.py:139
  50.5 1.4 collective-permute-start.9
  66.0 2.6 %collective-permute-start.11 = (f32[2,256,512]{2,1,0:T(8,128)S(1)}, f32[2,256,512]{2,1,0:T(8,128)S(1)}, u32[]{:S(2)}, u32[]{:S(2)}) collective-permute-start(f32[2,256,512]{2,1,0:T(8,128)S(1)} %fusion.21), channel_id=1, source_target_pairs={{3,2},{7,6},{11,10},{15,14},{19,18},{23,22},{27,26},{31,30}} | collective-permute-start | bytes 3145736 | tf_op jit(solution)/shard_map/ppermute | solution.py:187
  67.0 1.5 collective-permute-start.13
  72.7 2.5 %collective-permute-start.14 = (f32[2,256,512]{2,1,0:T(8,128)S(1)}, f32[2,256,512]{2,1,0:T(8,128)S(1)}, u32[]{:S(2)}, u32[]{:S(2)}) collective-permute-start(f32[2,256,512]{2,1,0:T(8,128)S(1)} %fusion.19), channel_id=1, source_target_pairs={{2,1},{6,5},{10,9},{14,13},{18,17},{22,21},{26,25},{30,29}} | collective-permute-start | bytes 3145736 | tf_op jit(solution)/shard_map/ppermute | solution.py:187
  73.5 1.6 collective-permute-start.16
  80.8 60.1 %collective-permute-start.17 = (f32[2,256,512]{2,1,0:T(8,128)}, f32[2,256,512]{2,1,0:T(8,128)}, u32[]{:S(2)}, u32[]{:S(2)}) collective-permute-start(f32[2,256,512]{2,1,0:T(8,128)} %fusion.17), channel_id=1, source_target_pairs={{1,0},{5,4},{9,8},{13,12},{17,16},{21,20},{25,24},{29,28}} | collective-permute-start | bytes 3145736 | tf_op jit(solution)/shard_map/ppermute | solution.py:187
  83.2 55.5 %collective-permute-start.19 = (bf16[2,128,512]{2,1,0:T(8,128)(2,1)S(1)}, bf16[2,128,512]{2,1,0:T(8,128)(2,1)S(1)}, u32[]{:S(2)}, u32[]{:S(2)}) collective-permute-start(bf16[2,128,512]{2,1,0:T(8,128)(2,1)S(1)} %get-tuple-element.26), channel_id=1, source_target_pairs={{1,4},{5,8},{9,12},{13,0},{17,20},{21,24},{25,28},{29,16}} | collective-permute-start | bytes 786440 | tf_op jit(solution)/shard_map/ppermute | solution.py:189
  84.5 56.4 %collective-permute-start.18 = (bf16[2,128,512]{2,1,0:T(8,128)(2,1)S(1)}, bf16[2,128,512]{2,1,0:T(8,128)(2,1)S(1)}, u32[]{:S(2)}, u32[]{:S(2)}) collective-permute-start(bf16[2,128,512]{2,1,0:T(8,128)(2,1)S(1)} %get-tuple-element.25), channel_id=1, source_target_pairs={{1,12},{5,0},{9,4},{13,8},{17,28},{21,16},{25,20},{29,24}} | collective-permute-start | bytes 786440 | tf_op jit(solution)/shard_map/ppermute | solution.py:188
  151.5 18.4 %collective-permute-start.25 = (bf16[2,400,512]{2,1,0:T(8,128)(2,1)}, bf16[2,400,512]{2,1,0:T(8,128)(2,1)}, u32[]{:S(2)}, u32[]{:S(2)}) collective-permute-start(bf16[2,400,512]{2,1,0:T(8,128)(2,1)} %fusion.97), channel_id=1, source_target_pairs={{0,4},{4,0},{8,12},{12,8},{1,5},{5,1},{9,13},{13,9},{2,6},{6,2},{1... | collective-permute-start | bytes 2457608 | tf_op jit(solution)/shard_map/ppermute | solution.py:41
  152.1 27.3 %collective-permute-start.24 = (bf16[2,256,512]{2,1,0:T(8,128)(2,1)S(1)}, bf16[2,256,512]{2,1,0:T(8,128)(2,1)S(1)}, u32[]{:S(2)}, u32[]{:S(2)}) collective-permute-start(bf16[2,256,512]{2,1,0:T(8,128)(2,1)S(1)} %copy-done.22), channel_id=1, source_target_pairs={{2,3},{6,7},{10,11},{14,15},{18,19},{22,23},{26,27},{30,31}} | collective-permute-start | bytes 1572872 | tf_op jit(solution)/shard_map/ppermute | solution.py:191
  152.8 26.6 %collective-permute-start.23 = (bf16[2,256,512]{2,1,0:T(8,128)(2,1)S(1)}, bf16[2,256,512]{2,1,0:T(8,128)(2,1)S(1)}, u32[]{:S(2)}, u32[]{:S(2)}) collective-permute-start(bf16[2,256,512]{2,1,0:T(8,128)(2,1)S(1)} %copy-done.24), channel_id=1, source_target_pairs={{1,2},{5,6},{9,10},{13,14},{17,18},{21,22},{25,26},{29,30}} | collective-permute-start | bytes 1572872 | tf_op jit(solution)/shard_map/ppermute | solution.py:191
  153.5 25.9 %collective-permute-start.22 = (bf16[2,256,512]{2,1,0:T(8,128)(2,1)}, bf16[2,256,512]{2,1,0:T(8,128)(2,1)S(1)}, u32[]{:S(2)}, u32[]{:S(2)}) collective-permute-start(bf16[2,256,512]{2,1,0:T(8,128)(2,1)} %copy-done.25), channel_id=1, source_target_pairs={{0,1},{4,5},{8,9},{12,13},{16,17},{20,21},{24,25},{28,29}} | collective-permute-start | bytes 1572872 | tf_op jit(solution)/shard_map/ppermute | solution.py:191
  157.2 18.6 %collective-permute-start.21 = (bf16[2,128,512]{2,1,0:T(8,128)(2,1)S(1)}, bf16[2,128,512]{2,1,0:T(8,128)(2,1)S(1)}, u32[]{:S(2)}, u32[]{:S(2)}) collective-permute-start(bf16[2,128,512]{2,1,0:T(8,128)(2,1)S(1)} %get-tuple-element.24), channel_id=1, source_target_pairs={{0,4},{4,8},{8,12},{12,0},{16,20},{20,24},{24,28},{28,16}} | collective-permute-start | bytes 786440 | tf_op jit(solution)/shard_map/ppermute | solution.py:196
  169.9 9.2 %collective-permute-start.20 = (bf16[2,128,512]{2,1,0:T(8,128)(2,1)S(1)}, bf16[2,128,512]{2,1,0:T(8,128)(2,1)S(1)}, u32[]{:S(2)}, u32[]{:S(2)}) collective-permute-start(bf16[2,128,512]{2,1,0:T(8,128)(2,1)S(1)} %get-tuple-element.23), channel_id=1, source_target_pairs={{0,12},{4,0},{8,4},{12,8},{16,28},{20,16},{24,20},{28,24}} | collective-permute-start | bytes 786440 | tf_op jit(solution)/shard_map/ppermute | solution.py:195
  175.8 18.3 %collective-permute-start.26 = (bf16[1,400,512]{2,1,0:T(8,128)(2,1)S(1)}, bf16[1,400,512]{2,1,0:T(8,128)(2,1)S(1)}, u32[]{:S(2)}, u32[]{:S(2)}) collective-permute-start(bf16[1,400,512]{2,1,0:T(8,128)(2,1)S(1)} %fusion.155), channel_id=1, source_target_pairs={{0,8},{4,12},{8,0},{12,4},{1,9},{5,13},{9,1},{13,5},{2,10},{6,14},... | collective-permute-start | bytes 1228808 | tf_op jit(solution)/shard_map/ppermute | solution.py:41
  (67 other events, 298.0 us)

commit v6 on v5

--- a/solution.py
+++ b/solution.py
@@ -184,7 +184,7 @@
         mine = section_index == active
         if tick + 1 < sections:
             g = finish(
-                lax.ppermute(own, both, route(active, active - 1, 0)),
+                lax.ppermute(own.astype(BF16), both, route(active, active - 1, 0)),
                 lax.ppermute(left_grad, both, route(active, active - 1, -1)),
                 lax.ppermute(right_grad, both, route(active, active - 1, 1)),
             )

time: 197 us -> 187 us (0.949)
  waiting for transfers between devices: 88.6 us -> 77 us
    ppermute x3, waiting for transfers between devices: 50.1 us -> 4.45 us  [shards(): lax.ppermute(right_grad, both, route(active, active - 1, 1))]
    ppermute x3, waiting for transfers between devices: 2.15 us -> 40 us  [shards(): lax.ppermute(left_grad, both, route(active, active - 1, -1))]
    ppermute x1, waiting for transfers between devices: 6.41 us -> 0.01 us  [shards(): lax.ppermute(pick_blocks(in_blocks, send_right, hs), both, route(0, 0, 1))]
    ppermute x1, waiting for transfers between devices: 0.01 us -> 5.76 us  [shards(): lax.ppermute(right_grad, both, route(active, active, 1))]
    ppermute x2, waiting for transfers between devices: 22.4 us -> 18.8 us  [halving_reduce_scatter(): recv = lax.ppermute(send, axis, pairs)]
    ppermute x1, starting transfers between devices: 6.99 us -> 3.94 us  [shards(): lax.ppermute(pick_blocks(in_blocks, send_left, hs), both, route(0, 0, -1))]
    ppermute x1, starting transfers between devices: 1.91 us -> 4.96 us  [shards(): lax.ppermute(pick_blocks(in_blocks, send_right, hs), both, route(0, 0, 1))]
    ppermute x1, waiting for transfers between devices: 0.01 us -> 2.59 us  [shards(): lax.ppermute(pick_blocks(in_blocks, send_left, hs), both, route(0, 0, -1))]
  transfers between devices with their start and end apart: 27 -> 27, of which waited for: 8 -> 8; matrix products, arithmetic and copies ran while one was open for 7% -> 8% of each run, Pallas kernels for 0% -> 0%
where the time goes in v6:
time: 187 us; the launch traced here: 186 us
  waiting for transfers between devices  77 us (41%)
  starting transfers between devices  41.1 us (22%)
  matrix products  27.2 us (15%)
  other arithmetic  20.9 us (11%)
  local copies, waits for them, and re-layouts  15.9 us (9%)
  between operations  4.13 us (2%)
    ppermute x3, waiting for transfers between devices, shards(): lax.ppermute(left_grad, both, route(active, active - 1, -1))  40 us
    ppermute x2, waiting for transfers between devices, halving_reduce_scatter(): recv = lax.ppermute(send, axis, pairs)  18.8 us
    unnamed x137, local copies, waits for them, and re-layouts  10.8 us
    select_n x3, other arithmetic, shards(): saved = tuple((jnp.where(mine, a, b) for a, b in zip(res, saved)))  5.89 us
    ppermute x1, waiting for transfers between devices, shards(): lax.ppermute(right_grad, both, route(active, active, 1))  5.76 us
    dot_general x4, matrix products, forward_layer(): agg2 = jnp.einsum('ij,sjd->sid', adj2, h_ext, preferred_element_type=F32)  5.24 us
    ppermute x1, starting transfers between devices, shards(): lax.ppermute(pick_blocks(in_blocks, send_right, hs), both, route(0, 0, 1))  4.96 us
    ppermute x3, waiting for transfers between devices, shards(): lax.ppermute(right_grad, both, route(active, active - 1, 1))  4.45 us
  transfers between devices with their start and end apart: 27, of which 8 were waited for; matrix products, arithmetic and copies ran while one was open for 8% of the time, Pallas kernels for 0%

profile of v6, /device:TPU:0, one launch (start us, length us, event | category | flops | bytes accessed | tf_op | source)
XLA Modules:
  0.0 186.2 jit_solution(18139556932834134190)
XLA Ops:
  4.7 5.0 %collective-permute-start = (bf16[2,128,512]{1,2,0:T(8,128)(2,1)S(1)}, bf16[2,128,512]{1,2,0:T(8,128)(2,1)}, u32[]{:S(2)}, u32[]{:S(2)}) collective-permute-start(bf16[2,128,512]{1,2,0:T(8,128)(2,1)S(1)} %bitcast.276), channel_id=1, source_target_pairs={{0,4},{4,8},{8,12},{12,0},{16,20},{20,24},{24,28},{28,16}} | collective-permute-start | bytes 786440 | tf_op jit(solution)/shard_map/ppermute | solution.py:119
  10.5 3.9 %collective-permute-start.1 = (bf16[2,128,512]{1,2,0:T(8,128)(2,1)}, bf16[2,128,512]{1,2,0:T(8,128)(2,1)}, u32[]{:S(2)}, u32[]{:S(2)}) collective-permute-start(bf16[2,128,512]{1,2,0:T(8,128)(2,1)} %bitcast.4), channel_id=1, source_target_pairs={{0,12},{4,0},{8,4},{12,8},{16,28},{20,16},{24,20},{28,24}} | collective-permute-start | bytes 786440 | tf_op jit(solution)/shard_map/ppermute | solution.py:120
  16.5 2.6 %collective-permute-done.1 = bf16[2,128,512]{1,2,0:T(8,128)(2,1)} collective-permute-done((bf16[2,128,512]{1,2,0:T(8,128)(2,1)}, bf16[2,128,512]{1,2,0:T(8,128)(2,1)}, u32[]{:S(2)}, u32[]{:S(2)}) %collective-permute-start.1) | collective-permute-done | bytes 262176 | tf_op jit(solution)/shard_map/ppermute | solution.py:120
  19.1 1.8 convolution_bitcast_fusion.7
  28.2 2.5 %collective-permute-done.3 = bf16[2,128,512]{2,1,0:T(8,128)(2,1)S(1)} collective-permute-done((bf16[2,128,512]{2,1,0:T(8,128)(2,1)S(1)}, bf16[2,128,512]{2,1,0:T(8,128)(2,1)S(1)}, u32[]{:S(2)}, u32[]{:S(2)}) %collective-permute-start.3) | collective-permute-done | bytes 262176 | tf_op jit(solution)/shard_map/ppermute | solution.py:138
  30.7 2.9 %collective-permute-done.4 = bf16[2,128,512]{2,1,0:T(8,128)(2,1)S(1)} collective-permute-done((bf16[2,128,512]{2,1,0:T(8,128)(2,1)S(1)}, bf16[2,128,512]{2,1,0:T(8,128)(2,1)S(1)}, u32[]{:S(2)}, u32[]{:S(2)}) %collective-permute-start.4) | collective-permute-done | bytes 262176 | tf_op jit(solution)/shard_map/ppermute | solution.py:139
  43.1 1.5 collective-permute-start.8
  48.1 2.0 %convolution_bitcast_fusion = f32[2,512,512]{2,1,0:T(8,128)S(1)} fusion(bf16[2,128,512]{2,1,0:T(8,128)(2,1)} %collective-permute-done.10, bf16[2,256,512]{2,1,0:T(8,128)(2,1)} %collective-permute-done.8, bf16[2,128,512]{2,1,0:T(8,128)(2,1)} %collective-permute-done.9, bf16[256,512]{1,0:T(8,128)(2,1)S(1)} %fusion.104, bf16[256,512]{1,0:T(8,128)(2,1)S(1)} %bitcast.250), kind=kOutput, calls=%fused_computation.6 | convolution fusion | flops 541065216 | bytes 3670016 | tf_op jit(solution)/shard_map/ij,sjd->sid/dot_general | solution.py:106
  50.7 3.4 %select_select_fusion.2 = (bf16[2,256,512]{2,1,0:T(8,128)(2,1)}, bf16[2,256,512]{2,1,0:T(8,128)(2,1)S(1)}) fusion(pred[]{:T(512)S(6)} %eq.133, pred[]{:T(512)S(6)} %eq.132, pred[]{:T(512)S(6)} %eq.121, f32[2,512,512]{2,1,0:T(8,128)S(1)} %convolution_bitcast_fusion, f32[2,512,512]{2,1,0:T(8,128)} %copy-done.21, f32[2,512,512]{2,1,0:T(8,128)S(1)} %copy-done.20, ...), kind=kLoop, calls=%fused_computation.223 | loop fusion | flops 2883584 | bytes 9437187 | tf_op jit(solution)/shard_map/jit(_where)/select_n | solution.py:133
  55.6 1.6 select_select_fusion
  69.7 1.4 collective-permute-start.14
  76.7 1.8 fusion.50
  85.5 2.5 %select_select_fusion.3 = (bf16[2,256,512]{2,1,0:T(8,128)(2,1)S(1)}, bf16[1,2,256,512]{3,2,1,0:T(8,128)(2,1)}) fusion(bf16[2,256,512]{2,1,0:T(8,128)(2,1)} %collective-permute-done.8, bf16[2,256,512]{2,1,0:T(8,128)(2,1)S(1)} %copy-done.36, bf16[2,256,512]{2,1,0:T(8,128)(2,1)S(1)} %copy-done.34, bf16[2,256,512]{2,1,0:T(8,128)(2,1)S(1)} %copy-done.6, ...), kind=kLoop, calls=%fused_computation.224 | loop fusion | flops 3145728 | bytes 5773315 | tf_op jit(solution)/shard_map/jit(_where)/select_n | solution.py:133
  88.0 40.0 %collective-permute-done.18 = bf16[2,128,512]{2,1,0:T(8,128)(2,1)S(1)} collective-permute-done((bf16[2,128,512]{2,1,0:T(8,128)(2,1)S(1)}, bf16[2,128,512]{2,1,0:T(8,128)(2,1)S(1)}, u32[]{:S(2)}, u32[]{:S(2)}) %collective-permute-start.18) | collective-permute-done | bytes 262176 | tf_op jit(solution)/shard_map/ppermute | solution.py:188
  128.0 4.4 %collective-permute-done.19 = bf16[2,128,512]{2,1,0:T(8,128)(2,1)S(1)} collective-permute-done((bf16[2,128,512]{2,1,0:T(8,128)(2,1)S(1)}, bf16[2,128,512]{2,1,0:T(8,128)(2,1)S(1)}, u32[]{:S(2)}, u32[]{:S(2)}) %collective-permute-start.19) | collective-permute-done | bytes 262176 | tf_op jit(solution)/shard_map/ppermute | solution.py:189
  138.8 1.7 copy-done.4
  144.7 1.5 convolution_convert_fusion
  147.0 4.2 %collective-permute-start.20 = (bf16[2,128,512]{2,1,0:T(8,128)(2,1)S(1)}, bf16[2,128,512]{2,1,0:T(8,128)(2,1)S(1)}, u32[]{:S(2)}, u32[]{:S(2)}) collective-permute-start(bf16[2,128,512]{2,1,0:T(8,128)(2,1)S(1)} %get-tuple-element.23), channel_id=1, source_target_pairs={{0,12},{4,0},{8,4},{12,8},{16,28},{20,16},{24,20},{28,24}} | collective-permute-start | bytes 786440 | tf_op jit(solution)/shard_map/ppermute | solution.py:195
  151.3 8.8 %collective-permute-done.25 = bf16[2,400,512]{2,1,0:T(8,128)(2,1)} collective-permute-done((bf16[2,400,512]{2,1,0:T(8,128)(2,1)}, bf16[2,400,512]{2,1,0:T(8,128)(2,1)}, u32[]{:S(2)}, u32[]{:S(2)}) %collective-permute-start.25) | collective-permute-done | bytes 819232 | tf_op jit(solution)/shard_map/ppermute | solution.py:41
  160.0 3.2 %collective-permute-start.21 = (bf16[2,128,512]{2,1,0:T(8,128)(2,1)S(1)}, bf16[2,128,512]{2,1,0:T(8,128)(2,1)S(1)}, u32[]{:S(2)}, u32[]{:S(2)}) collective-permute-start(bf16[2,128,512]{2,1,0:T(8,128)(2,1)S(1)} %get-tuple-element.24), channel_id=1, source_target_pairs={{0,4},{4,8},{8,12},{12,0},{16,20},{20,24},{24,28},{28,16}} | collective-permute-start | bytes 786440 | tf_op jit(solution)/shard_map/ppermute | solution.py:196
  163.2 1.6 fusion
  166.3 5.8 %collective-permute-done.21 = bf16[2,128,512]{2,1,0:T(8,128)(2,1)S(1)} collective-permute-done((bf16[2,128,512]{2,1,0:T(8,128)(2,1)S(1)}, bf16[2,128,512]{2,1,0:T(8,128)(2,1)S(1)}, u32[]{:S(2)}, u32[]{:S(2)}) %collective-permute-start.21) | collective-permute-done | bytes 262176 | tf_op jit(solution)/shard_map/ppermute | solution.py:196
  172.3 1.6 fusion.31
  173.9 10.0 %collective-permute-done.26 = bf16[1,400,512]{2,1,0:T(8,128)(2,1)S(1)} collective-permute-done((bf16[1,400,512]{2,1,0:T(8,128)(2,1)S(1)}, bf16[1,400,512]{2,1,0:T(8,128)(2,1)S(1)}, u32[]{:S(2)}, u32[]{:S(2)}) %collective-permute-start.26) | collective-permute-done | bytes 409632 | tf_op jit(solution)/shard_map/ppermute | solution.py:41
  (272 shorter events, 66.4 us)
Async XLA Ops:
  4.7 11.8 %collective-permute-start = (bf16[2,128,512]{1,2,0:T(8,128)(2,1)S(1)}, bf16[2,128,512]{1,2,0:T(8,128)(2,1)}, u32[]{:S(2)}, u32[]{:S(2)}) collective-permute-start(bf16[2,128,512]{1,2,0:T(8,128)(2,1)S(1)} %bitcast.276), channel_id=1, source_target_pairs={{0,4},{4,8},{8,12},{12,0},{16,20},{20,24},{24,28},{28,16}} | collective-permute-start | bytes 786440 | tf_op jit(solution)/shard_map/ppermute | solution.py:119
  10.5 8.6 %collective-permute-start.1 = (bf16[2,128,512]{1,2,0:T(8,128)(2,1)}, bf16[2,128,512]{1,2,0:T(8,128)(2,1)}, u32[]{:S(2)}, u32[]{:S(2)}) collective-permute-start(bf16[2,128,512]{1,2,0:T(8,128)(2,1)} %bitcast.4), channel_id=1, source_target_pairs={{0,12},{4,0},{8,4},{12,8},{16,28},{20,16},{24,20},{28,24}} | collective-permute-start | bytes 786440 | tf_op jit(solution)/shard_map/ppermute | solution.py:120
  24.2 9.4 %collective-permute-start.2 = (bf16[2,256,512]{2,1,0:T(8,128)(2,1)S(1)}, bf16[2,256,512]{2,1,0:T(8,128)(2,1)S(1)}, u32[]{:S(2)}, u32[]{:S(2)}) collective-permute-start(bf16[2,256,512]{2,1,0:T(8,128)(2,1)S(1)} %add_convert_fusion.3), channel_id=1, source_target_pairs={{0,1},{4,5},{8,9},{12,13},{16,17},{20,21},{24,25},{28,29}} | collective-permute-start | bytes 1572872 | tf_op jit(solution)/shard_map/ppermute | solution.py:137
  25.6 5.2 %collective-permute-start.3 = (bf16[2,128,512]{2,1,0:T(8,128)(2,1)S(1)}, bf16[2,128,512]{2,1,0:T(8,128)(2,1)S(1)}, u32[]{:S(2)}, u32[]{:S(2)}) collective-permute-start(bf16[2,128,512]{2,1,0:T(8,128)(2,1)S(1)} %get-tuple-element.37), channel_id=1, source_target_pairs={{0,5},{4,9},{8,13},{12,1},{16,21},{20,25},{24,29},{28,17}} | collective-permute-start | bytes 786440 | tf_op jit(solution)/shard_map/ppermute | solution.py:138
  26.9 6.7 %collective-permute-start.4 = (bf16[2,128,512]{2,1,0:T(8,128)(2,1)S(1)}, bf16[2,128,512]{2,1,0:T(8,128)(2,1)S(1)}, u32[]{:S(2)}, u32[]{:S(2)}) collective-permute-start(bf16[2,128,512]{2,1,0:T(8,128)(2,1)S(1)} %get-tuple-element.38), channel_id=1, source_target_pairs={{0,13},{4,1},{8,5},{12,9},{16,29},{20,17},{24,21},{28,25}} | collective-permute-start | bytes 786440 | tf_op jit(solution)/shard_map/ppermute | solution.py:139
  37.3 2.2 %collective-permute-start.5 = (bf16[2,256,512]{2,1,0:T(8,128)(2,1)S(1)}, bf16[2,256,512]{2,1,0:T(8,128)(2,1)S(1)}, u32[]{:S(2)}, u32[]{:S(2)}) collective-permute-start(bf16[2,256,512]{2,1,0:T(8,128)(2,1)S(1)} %add_convert_fusion.2), channel_id=1, source_target_pairs={{1,2},{5,6},{9,10},{13,14},{17,18},{21,22},{25,26},{29,30}} | collective-permute-start | bytes 1572872 | tf_op jit(solution)/shard_map/ppermute | solution.py:137
  43.1 5.1 %collective-permute-start.8 = (bf16[2,256,512]{2,1,0:T(8,128)(2,1)S(1)}, bf16[2,256,512]{2,1,0:T(8,128)(2,1)}, u32[]{:S(2)}, u32[]{:S(2)}) collective-permute-start(bf16[2,256,512]{2,1,0:T(8,128)(2,1)S(1)} %add_convert_fusion.1), channel_id=1, source_target_pairs={{2,3},{6,7},{10,11},{14,15},{18,19},{22,23},{26,27},{30,31}} | collective-permute-start | bytes 1572872 | tf_op jit(solution)/shard_map/ppermute | solution.py:137
  45.3 2.8 %collective-permute-start.10 = (bf16[2,128,512]{2,1,0:T(8,128)(2,1)}, bf16[2,128,512]{2,1,0:T(8,128)(2,1)}, u32[]{:S(2)}, u32[]{:S(2)}) collective-permute-start(bf16[2,128,512]{2,1,0:T(8,128)(2,1)} %get-tuple-element.34), channel_id=1, source_target_pairs={{2,15},{6,3},{10,7},{14,11},{18,31},{22,19},{26,23},{30,27}} | collective-permute-start | bytes 786440 | tf_op jit(solution)/shard_map/ppermute | solution.py:139
  46.7 1.5 collective-permute-start.9
  62.2 2.5 %collective-permute-start.11 = (bf16[2,256,512]{2,1,0:T(8,128)(2,1)S(1)}, bf16[2,256,512]{2,1,0:T(8,128)(2,1)S(1)}, u32[]{:S(2)}, u32[]{:S(2)}) collective-permute-start(bf16[2,256,512]{2,1,0:T(8,128)(2,1)S(1)} %fusion.22), channel_id=1, source_target_pairs={{3,2},{7,6},{11,10},{15,14},{19,18},{23,22},{27,26},{31,30}} | collective-permute-start | bytes 1572872 | tf_op jit(solution)/shard_map/ppermute | solution.py:187
  63.1 1.5 collective-permute-start.12
  69.7 7.1 %collective-permute-start.14 = (bf16[2,256,512]{2,1,0:T(8,128)(2,1)}, bf16[2,256,512]{2,1,0:T(8,128)(2,1)}, u32[]{:S(2)}, u32[]{:S(2)}) collective-permute-start(bf16[2,256,512]{2,1,0:T(8,128)(2,1)} %fusion.24), channel_id=1, source_target_pairs={{2,1},{6,5},{10,9},{14,13},{18,17},{22,21},{26,25},{30,29}} | collective-permute-start | bytes 1572872 | tf_op jit(solution)/shard_map/ppermute | solution.py:187
  72.0 2.7 %collective-permute-start.15 = (bf16[2,128,512]{2,1,0:T(8,128)(2,1)}, bf16[2,128,512]{2,1,0:T(8,128)(2,1)}, u32[]{:S(2)}, u32[]{:S(2)}) collective-permute-start(bf16[2,128,512]{2,1,0:T(8,128)(2,1)} %get-tuple-element.27), channel_id=1, source_target_pairs={{2,13},{6,1},{10,5},{14,9},{18,29},{22,17},{26,21},{30,25}} | collective-permute-start | bytes 786440 | tf_op jit(solution)/shard_map/ppermute | solution.py:188
  73.3 2.4 %collective-permute-start.16 = (bf16[2,128,512]{2,1,0:T(8,128)(2,1)}, bf16[2,128,512]{2,1,0:T(8,128)(2,1)}, u32[]{:S(2)}, u32[]{:S(2)}) collective-permute-start(bf16[2,128,512]{2,1,0:T(8,128)(2,1)} %get-tuple-element.28), channel_id=1, source_target_pairs={{2,5},{6,9},{10,13},{14,1},{18,21},{22,25},{26,29},{30,17}} | collective-permute-start | bytes 786440 | tf_op jit(solution)/shard_map/ppermute | solution.py:189
  81.4 51.2 %collective-permute-start.17 = (bf16[2,256,512]{2,1,0:T(8,128)(2,1)S(1)}, bf16[2,256,512]{2,1,0:T(8,128)(2,1)S(1)}, u32[]{:S(2)}, u32[]{:S(2)}) collective-permute-start(bf16[2,256,512]{2,1,0:T(8,128)(2,1)S(1)} %fusion.26), channel_id=1, source_target_pairs={{1,0},{5,4},{9,8},{13,12},{17,16},{21,20},{25,24},{29,28}} | collective-permute-start | bytes 1572872 | tf_op jit(solution)/shard_map/ppermute | solution.py:187
  82.8 45.1 %collective-permute-start.18 = (bf16[2,128,512]{2,1,0:T(8,128)(2,1)S(1)}, bf16[2,128,512]{2,1,0:T(8,128)(2,1)S(1)}, u32[]{:S(2)}, u32[]{:S(2)}) collective-permute-start(bf16[2,128,512]{2,1,0:T(8,128)(2,1)S(1)} %get-tuple-element.25), channel_id=1, source_target_pairs={{1,12},{5,0},{9,4},{13,8},{17,28},{21,16},{25,20},{29,24}} | collective-permute-start | bytes 786440 | tf_op jit(solution)/shard_map/ppermute | solution.py:188
  84.1 48.3 %collective-permute-start.19 = (bf16[2,128,512]{2,1,0:T(8,128)(2,1)S(1)}, bf16[2,128,512]{2,1,0:T(8,128)(2,1)S(1)}, u32[]{:S(2)}, u32[]{:S(2)}) collective-permute-start(bf16[2,128,512]{2,1,0:T(8,128)(2,1)S(1)} %get-tuple-element.26), channel_id=1, source_target_pairs={{1,4},{5,8},{9,12},{13,0},{17,20},{21,24},{25,28},{29,16}} | collective-permute-start | bytes 786440 | tf_op jit(solution)/shard_map/ppermute | solution.py:189
  141.6 18.4 %collective-permute-start.25 = (bf16[2,400,512]{2,1,0:T(8,128)(2,1)}, bf16[2,400,512]{2,1,0:T(8,128)(2,1)}, u32[]{:S(2)}, u32[]{:S(2)}) collective-permute-start(bf16[2,400,512]{2,1,0:T(8,128)(2,1)} %fusion.100), channel_id=1, source_target_pairs={{0,4},{4,0},{8,12},{12,8},{1,5},{5,1},{9,13},{13,9},{2,6},{6,2},{1... | collective-permute-start | bytes 2457608 | tf_op jit(solution)/shard_map/ppermute | solution.py:41
  141.9 30.4 %collective-permute-start.24 = (bf16[2,256,512]{2,1,0:T(8,128)(2,1)S(1)}, bf16[2,256,512]{2,1,0:T(8,128)(2,1)S(1)}, u32[]{:S(2)}, u32[]{:S(2)}) collective-permute-start(bf16[2,256,512]{2,1,0:T(8,128)(2,1)S(1)} %copy-done.26), channel_id=1, source_target_pairs={{2,3},{6,7},{10,11},{14,15},{18,19},{22,23},{26,27},{30,31}} | collective-permute-start | bytes 1572872 | tf_op jit(solution)/shard_map/ppermute | solution.py:191
  142.6 29.7 %collective-permute-start.23 = (bf16[2,256,512]{2,1,0:T(8,128)(2,1)}, bf16[2,256,512]{2,1,0:T(8,128)(2,1)S(1)}, u32[]{:S(2)}, u32[]{:S(2)}) collective-permute-start(bf16[2,256,512]{2,1,0:T(8,128)(2,1)} %copy-done.37), channel_id=1, source_target_pairs={{1,2},{5,6},{9,10},{13,14},{17,18},{21,22},{25,26},{29,30}} | collective-permute-start | bytes 1572872 | tf_op jit(solution)/shard_map/ppermute | solution.py:191
  143.3 29.0 %collective-permute-start.22 = (bf16[2,256,512]{2,1,0:T(8,128)(2,1)S(1)}, bf16[2,256,512]{2,1,0:T(8,128)(2,1)S(1)}, u32[]{:S(2)}, u32[]{:S(2)}) collective-permute-start(bf16[2,256,512]{2,1,0:T(8,128)(2,1)S(1)} %copy-done.32), channel_id=1, source_target_pairs={{0,1},{4,5},{8,9},{12,13},{16,17},{20,21},{24,25},{28,29}} | collective-permute-start | bytes 1572872 | tf_op jit(solution)/shard_map/ppermute | solution.py:191
  147.0 17.9 %collective-permute-start.20 = (bf16[2,128,512]{2,1,0:T(8,128)(2,1)S(1)}, bf16[2,128,512]{2,1,0:T(8,128)(2,1)S(1)}, u32[]{:S(2)}, u32[]{:S(2)}) collective-permute-start(bf16[2,128,512]{2,1,0:T(8,128)(2,1)S(1)} %get-tuple-element.23), channel_id=1, source_target_pairs={{0,12},{4,0},{8,4},{12,8},{16,28},{20,16},{24,20},{28,24}} | collective-permute-start | bytes 786440 | tf_op jit(solution)/shard_map/ppermute | solution.py:195
  160.0 12.0 %collective-permute-start.21 = (bf16[2,128,512]{2,1,0:T(8,128)(2,1)S(1)}, bf16[2,128,512]{2,1,0:T(8,128)(2,1)S(1)}, u32[]{:S(2)}, u32[]{:S(2)}) collective-permute-start(bf16[2,128,512]{2,1,0:T(8,128)(2,1)S(1)} %get-tuple-element.24), channel_id=1, source_target_pairs={{0,4},{4,8},{8,12},{12,0},{16,20},{20,24},{24,28},{28,16}} | collective-permute-start | bytes 786440 | tf_op jit(solution)/shard_map/ppermute | solution.py:196
  164.9 19.0 %collective-permute-start.26 = (bf16[1,400,512]{2,1,0:T(8,128)(2,1)S(1)}, bf16[1,400,512]{2,1,0:T(8,128)(2,1)S(1)}, u32[]{:S(2)}, u32[]{:S(2)}) collective-permute-start(bf16[1,400,512]{2,1,0:T(8,128)(2,1)S(1)} %fusion.158), channel_id=1, source_target_pairs={{0,8},{4,12},{8,0},{12,4},{1,9},{5,13},{9,1},{13,5},{2,10},{6,14},... | collective-permute-start | bytes 1228808 | tf_op jit(solution)/shard_map/ppermute | solution.py:41
  (69 other events, 304.5 us)

commit v7 on v6

--- a/solution.py
+++ b/solution.py
@@ -25,9 +25,7 @@
     return blocks
 
 
-def halving_reduce_scatter(x, axis, devices, index):
-    if devices & (devices - 1):
-        return lax.psum_scatter(x, axis, scatter_dimension=0, tiled=True)
+def halving_reduce_scatter(x, axis, devices, index, pairs_of):
     rows = x.shape[0] // devices
     cur = x.reshape(devices, rows, x.shape[1]).astype(F32)
     dist = 1
@@ -37,8 +35,7 @@
         low, high = cur[:, 0], cur[:, 1]
         keep = jnp.where(bit == 0, low, high)
         send = jnp.where(bit == 0, high, low).astype(x.dtype)
-        pairs = [(i, i ^ dist) for i in range(devices)]
-        recv = lax.ppermute(send, axis, pairs)
+        recv = lax.ppermute(send, axis, pairs_of(dist))
         cur = keep + recv.astype(F32)
         dist *= 2
     return cur[0]
@@ -141,6 +138,29 @@
     h_in, agg, pre, act, normed, rstd = saved
     _, _, pre_last, _, normed_last, rstd_last = last_res
 
+    norm_factor = 1.0 / math.sqrt(samples * node_rows * domains)
+    stacked = jnp.concatenate([h_in, agg], axis=2)
+    r1 = 2 * width // domains
+    r2 = width // domains
+    r3 = width // domains
+    pad_rows = 16
+
+    def reduce_sections(dpre_s, dout_s, gain_s, members):
+        gw1 = jnp.einsum("via,vid->ad", stacked, dpre_s, preferred_element_type=F32)
+        gw2 = jnp.einsum("via,vid->ad", act, dout_s, preferred_element_type=F32)
+        gain_rows = jnp.pad(gain_s.reshape(domains, 1, r3), ((0, 0), (0, pad_rows - 1), (0, width - r3)))
+        packed = jnp.concatenate(
+            [gw1.reshape(domains, r1, width), gw2.reshape(domains, r2, width), gain_rows], axis=1
+        ).astype(BF16)
+        packed = packed.reshape(domains * (r1 + r2 + pad_rows), width)
+        if domains & (domains - 1):
+            return lax.psum_scatter(packed, "dom", scatter_dimension=0, tiled=True).astype(F32)
+
+        def pairs_of(dist):
+            return [(linear(d, s), linear(d ^ dist, s)) for d in range(domains) for s in members]
+
+        return halving_reduce_scatter(packed, both, domains, domain_index, pairs_of)
+
     g = cotangent
     grad_in = None
     dpre_keep = None
@@ -203,27 +223,13 @@
             dpre_keep = jnp.where(mine, dpre, dpre_keep)
             dout_keep = jnp.where(mine, dout, dout_keep)
             gain_keep = jnp.where(mine, gain_term, gain_keep)
-
-    norm_factor = 1.0 / math.sqrt(samples * node_rows * domains)
-    stacked = jnp.concatenate([h_in, agg], axis=2)
-    gw1 = jnp.einsum("via,vid->ad", stacked, dpre_keep, preferred_element_type=F32)
-    gw2 = jnp.einsum("via,vid->ad", act, dout_keep, preferred_element_type=F32)
-    r1 = gw1.shape[0] // domains
-    r2 = gw2.shape[0] // domains
-    r3 = gain_keep.shape[0] // domains
-    pad_rows = 16
-    gain_rows = jnp.pad(gain_keep.reshape(domains, 1, r3), ((0, 0), (0, pad_rows - 1), (0, width - r3)))
-    packed = jnp.concatenate(
-        [
-            gw1.reshape(domains, r1, width),
-            gw2.reshape(domains, r2, width),
-            gain_rows,
-        ],
-        axis=1,
-    ).astype(BF16)
-    packed = packed.reshape(domains * (r1 + r2 + pad_rows), width)
-    reduced = halving_reduce_scatter(packed, "dom", domains, domain_index)
-    reduced = reduced.astype(F32) * norm_factor
+        if tick == sections - 2:
+            early = reduce_sections(dpre_keep, dout_keep, gain_keep, tuple(range(1, sections)))
+
+    reduced = reduce_sections(dpre, dout, gain_term, (0,))
+    if early is not None:
+        reduced = jnp.where(section_index == 0, reduced, early)
+    reduced = reduced * norm_factor
     g1 = reduced[:r1]
     g2 = reduced[r1 : r1 + r2]
     g3 = reduced[r1 + r2, :r3]

time: 187 us -> 190 us (1.016)
  waiting for transfers between devices: 77 us -> 65 us
  starting transfers between devices: 41.1 us -> 49.7 us
  other arithmetic: 20.9 us -> 27.5 us
  matrix products: 27.2 us -> 30.6 us
  local copies, waits for them, and re-layouts: 15.9 us -> 12.6 us
    ppermute x2 -> x4, starting transfers between devices: 1.49 us -> 9.8 us  [halving_reduce_scatter(): recv = lax.ppermute(send, axis, pairs_of(dist))]
    ppermute x2 -> x4, waiting for transfers between devices: 18.8 us -> 10.5 us  [halving_reduce_scatter(): recv = lax.ppermute(send, axis, pairs_of(dist))]
    unnamed x137 -> x84, local copies, waits for them, and re-layouts: 10.8 us -> 7.15 us
    ppermute x1, waiting for transfers between devices: 5.76 us -> 2.11 us  [shards(): lax.ppermute(right_grad, both, route(active, active, 1))]
    convert_element_type x4, other arithmetic: 1.22 us -> 4.36 us  [shards(): dout = (rstd_t * (dn - jnp.mean(dn, axis=-1, keepdims=True) - normed_t *...]
    dot_general x4, matrix products: 3.8 us -> 6.54 us  [shards(): jnp.einsum('sip,vp->siv', dpre, w_a, preferred_element_type=F32)]
    ppermute x3, starting transfers between devices: 2.7 us -> 5.05 us  [shards(): g_new = lax.ppermute(g, both, route(active - 1, active, 0))]
    select_n x3 -> x4, other arithmetic: 5.89 us -> 6.23 us  [shards(): saved = tuple((jnp.where(mine, a, b) for a, b in zip(res, saved)))]
  transfers between devices with their start and end apart: 27 -> 29, of which waited for: 8 -> 8; matrix products, arithmetic and copies ran while one was open for 8% -> 16% of each run, Pallas kernels for 0% -> 0%
where the time goes in v7:
time: 190 us; the launch traced here: 189 us
  waiting for transfers between devices  65 us (34%)
  starting transfers between devices  49.7 us (26%)
  matrix products  30.6 us (16%)
  other arithmetic  27.5 us (14%)
  local copies, waits for them, and re-layouts  12.6 us (7%)
  between operations  3.89 us (2%)
    ppermute x3, waiting for transfers between devices, shards(): lax.ppermute(left_grad, both, route(active, active - 1, -1))  40.5 us
    ppermute x4, waiting for transfers between devices, halving_reduce_scatter(): recv = lax.ppermute(send, axis, pairs_of(dist))  10.5 us
    ppermute x4, starting transfers between devices, halving_reduce_scatter(): recv = lax.ppermute(send, axis, pairs_of(dist))  9.8 us
    unnamed x84, local copies, waits for them, and re-layouts  7.15 us
    dot_general x4, matrix products, shards(): jnp.einsum('sip,vp->siv', dpre, w_a, preferred_element_type=F32)  6.54 us
    select_n x4, other arithmetic, shards(): saved = tuple((jnp.where(mine, a, b) for a, b in zip(res, saved)))  6.23 us
    reduce_sum x4, other arithmetic, shards(): gain_term = jnp.sum(gf * normed_t, axis=(0, 1))  5.51 us
    dot_general x4, matrix products, forward_layer(): agg2 = jnp.einsum('ij,sjd->sid', adj2, h_ext, preferred_element_type=F32)  5.32 us
  transfers between devices with their start and end apart: 29, of which 8 were waited for; matrix products, arithmetic and copies ran while one was open for 16% of the time, Pallas kernels for 0%

profile of v7, /device:TPU:0, one launch (start us, length us, event | category | flops | bytes accessed | tf_op | source)
XLA Modules:
  0.0 189.3 jit_solution(16065936593798652918)
XLA Ops:
  5.4 4.9 %collective-permute-start = (bf16[2,128,512]{1,2,0:T(8,128)(2,1)}, bf16[2,128,512]{1,2,0:T(8,128)(2,1)}, u32[]{:S(2)}, u32[]{:S(2)}) collective-permute-start(bf16[2,128,512]{1,2,0:T(8,128)(2,1)} %bitcast.3), channel_id=1, source_target_pairs={{0,4},{4,8},{8,12},{12,0},{16,20},{20,24},{24,28},{28,16}} | collective-permute-start | bytes 786440 | tf_op jit(solution)/shard_map/ppermute | solution.py:116
  11.1 3.9 %collective-permute-start.1 = (bf16[2,128,512]{1,2,0:T(8,128)(2,1)}, bf16[2,128,512]{1,2,0:T(8,128)(2,1)}, u32[]{:S(2)}, u32[]{:S(2)}) collective-permute-start(bf16[2,128,512]{1,2,0:T(8,128)(2,1)} %bitcast.4), channel_id=1, source_target_pairs={{0,12},{4,0},{8,4},{12,8},{16,28},{20,16},{24,20},{28,24}} | collective-permute-start | bytes 786440 | tf_op jit(solution)/shard_map/ppermute | solution.py:117
  17.1 2.6 %collective-permute-done.1 = bf16[2,128,512]{1,2,0:T(8,128)(2,1)} collective-permute-done((bf16[2,128,512]{1,2,0:T(8,128)(2,1)}, bf16[2,128,512]{1,2,0:T(8,128)(2,1)}, u32[]{:S(2)}, u32[]{:S(2)}) %collective-permute-start.1) | collective-permute-done | bytes 262176 | tf_op jit(solution)/shard_map/ppermute | solution.py:117
  19.8 1.8 convolution_bitcast_fusion.7
  27.8 2.5 %collective-permute-done.3 = bf16[2,128,512]{2,1,0:T(8,128)(2,1)S(1)} collective-permute-done((bf16[2,128,512]{2,1,0:T(8,128)(2,1)S(1)}, bf16[2,128,512]{2,1,0:T(8,128)(2,1)S(1)}, u32[]{:S(2)}, u32[]{:S(2)}) %collective-permute-start.3) | collective-permute-done | bytes 262176 | tf_op jit(solution)/shard_map/ppermute | solution.py:135
  30.4 2.8 %collective-permute-done.4 = bf16[2,128,512]{2,1,0:T(8,128)(2,1)S(1)} collective-permute-done((bf16[2,128,512]{2,1,0:T(8,128)(2,1)S(1)}, bf16[2,128,512]{2,1,0:T(8,128)(2,1)S(1)}, u32[]{:S(2)}, u32[]{:S(2)}) %collective-permute-start.4) | collective-permute-done | bytes 262176 | tf_op jit(solution)/shard_map/ppermute | solution.py:136
  44.6 1.9 dynamic-slice_bitcast_fusion.1
  49.3 2.1 %convolution_bitcast_fusion = f32[2,512,512]{2,1,0:T(8,128)S(1)} fusion(bf16[2,128,512]{2,1,0:T(8,128)(2,1)} %collective-permute-done.10, bf16[2,256,512]{2,1,0:T(8,128)(2,1)} %collective-permute-done.8, bf16[2,128,512]{2,1,0:T(8,128)(2,1)} %collective-permute-done.9, bf16[256,512]{1,0:T(8,128)(2,1)} %copy-done.15, bf16[256,512]{1,0:T(8,128)(2,1)S(1)} %bitcast.282), kind=kOutput, calls=%fused_computation.12 | convolution fusion | flops 541065216 | bytes 3670016 | tf_op jit(solution)/shard_map/ij,sjd->sid/dot_general | solution.py:103
  51.9 2.6 %select_select_fusion.3 = (bf16[2,256,512]{2,1,0:T(8,128)(2,1)S(1)}, bf16[2,256,512]{2,1,0:T(8,128)(2,1)S(1)}) fusion(pred[]{:T(512)S(6)} %eq.140, pred[]{:T(512)S(6)} %eq.139, pred[]{:T(512)S(6)} %eq.128, f32[2,512,512]{2,1,0:T(8,128)S(1)} %convolution_bitcast_fusion, f32[2,512,512]{2,1,0:T(8,128)} %copy-done.22, f32[2,512,512]{2,1,0:T(8,128)S(1)} %copy-done.21, ...), kind=kLoop, calls=%fused_computation.229 | loop fusion | flops 2883584 | bytes 9437187 | tf_op jit(solution)/shard_map/jit(_where)/select_n | solution.py:130
  65.7 2.1 %fusion.51 = (bf16[512]{0:T(512)(128)(2,1)S(1)}, f32[2,256]{1,0:T(2,128)S(1)}, f32[2,256]{1,0:T(2,128)S(1)}, f32[2,256,512]{2,1,0:T(8,128)S(1)}, bf16[2,256,512]{2,1,0:T(8,128)(2,1)}) fusion(f32[512]{0:T(512)S(1)} %bitcast.301, f32[2,256]{1,0:T(2,128)S(1)} %add_rsqrt_fusion.3, f32[2,256,512]{2,1,0:T(8,128)S(1)} %get-tuple-element.44, ...), kind=kLoop, calls=%fused_computation.95 | loop fusion | flops 6289920 | bytes 7364099 | tf_op jit(solution)/shard_map/reduce_sum | solution.py:175
  71.1 1.7 fusion.25
  74.9 2.5 %select_select_fusion.4 = (bf16[2,256,512]{2,1,0:T(8,128)(2,1)S(1)}, bf16[1,2,256,512]{3,2,1,0:T(8,128)(2,1)}) fusion(bf16[2,256,512]{2,1,0:T(8,128)(2,1)} %collective-permute-done.8, bf16[2,256,512]{2,1,0:T(8,128)(2,1)S(1)} %copy-done.32, bf16[2,256,512]{2,1,0:T(8,128)(2,1)S(1)} %copy-done.30, bf16[2,256,512]{2,1,0:T(8,128)(2,1)S(1)} %copy-done.2, ...), kind=kLoop, calls=%fused_computation.230 | loop fusion | flops 3145728 | bytes 5773315 | tf_op jit(solution)/shard_map/jit(_where)/select_n | solution.py:130
  92.5 40.5 %collective-permute-done.18 = bf16[2,128,512]{2,1,0:T(8,128)(2,1)S(1)} collective-permute-done((bf16[2,128,512]{2,1,0:T(8,128)(2,1)S(1)}, bf16[2,128,512]{2,1,0:T(8,128)(2,1)S(1)}, u32[]{:S(2)}, u32[]{:S(2)}) %collective-permute-start.18) | collective-permute-done | bytes 262176 | tf_op jit(solution)/shard_map/ppermute | solution.py:208
  133.8 3.8 %collective-permute-done.19 = bf16[2,128,512]{2,1,0:T(8,128)(2,1)S(1)} collective-permute-done((bf16[2,128,512]{2,1,0:T(8,128)(2,1)S(1)}, bf16[2,128,512]{2,1,0:T(8,128)(2,1)S(1)}, u32[]{:S(2)}, u32[]{:S(2)}) %collective-permute-start.19) | collective-permute-done | bytes 262176 | tf_op jit(solution)/shard_map/ppermute | solution.py:209
  141.6 2.1 %collective-permute-start.22 = (bf16[2,256,512]{2,1,0:T(8,128)(2,1)}, bf16[2,256,512]{2,1,0:T(8,128)(2,1)}, u32[]{:S(2)}, u32[]{:S(2)}) collective-permute-start(bf16[2,256,512]{2,1,0:T(8,128)(2,1)} %get-tuple-element.19), channel_id=1, source_target_pairs={{0,1},{4,5},{8,9},{12,13},{16,17},{20,21},{24,25},{28,29}} | collective-permute-start | bytes 1572872 | tf_op jit(solution)/shard_map/ppermute | solution.py:211
  145.1 2.8 %collective-permute-start.25 = (bf16[2,400,512]{2,1,0:T(8,128)(2,1)S(1)}, bf16[2,400,512]{2,1,0:T(8,128)(2,1)S(1)}, u32[]{:S(2)}, u32[]{:S(2)}) collective-permute-start(bf16[2,400,512]{2,1,0:T(8,128)(2,1)S(1)} %fusion.99), channel_id=1, source_target_pairs={{0,4},{4,0},{8,12},{12,8},{16,20},{20,16},{24,28},{28,24}} | collective-permute-start | bytes 2457608 | tf_op jit(solution)/shard_map/ppermute | solution.py:38
  148.4 2.1 %fusion.202 = (bf16[2,512,512]{2,1,0:T(8,128)(2,1)S(1)}, f32[2,512,512]{2,1,0:T(8,128)}) fusion(bf16[256,512]{1,0:T(8,128)(2,1)S(1)} %copy-done.17, bf16[256,512]{1,0:T(8,128)(2,1)S(1)} %bitcast.286, bf16[2,256,512]{1,2,0:T(8,128)(2,1)S(1)} %convolution_convert_fusion), kind=kOutput, calls=%fused_computation.318 | convolution fusion | flops 540540928 | bytes 4194304 | tf_op jit(solution)/shard_map/ij,sid->sjd/dot_general | solution.py:190
  150.5 3.4 %collective-permute-start.20 = (bf16[2,128,512]{2,1,0:T(8,128)(2,1)S(1)}, bf16[2,128,512]{2,1,0:T(8,128)(2,1)S(1)}, u32[]{:S(2)}, u32[]{:S(2)}) collective-permute-start(bf16[2,128,512]{2,1,0:T(8,128)(2,1)S(1)} %get-tuple-element.23), channel_id=1, source_target_pairs={{0,12},{4,0},{8,4},{12,8},{16,28},{20,16},{24,20},{28,24}} | collective-permute-start | bytes 786440 | tf_op jit(solution)/shard_map/ppermute | solution.py:215
  155.3 4.6 %collective-permute-done.25 = bf16[2,400,512]{2,1,0:T(8,128)(2,1)S(1)} collective-permute-done((bf16[2,400,512]{2,1,0:T(8,128)(2,1)S(1)}, bf16[2,400,512]{2,1,0:T(8,128)(2,1)S(1)}, u32[]{:S(2)}, u32[]{:S(2)}) %collective-permute-start.25) | collective-permute-done | bytes 819232 | tf_op jit(solution)/shard_map/ppermute | solution.py:38
  159.8 4.3 %collective-permute-start.21 = (bf16[2,128,512]{2,1,0:T(8,128)(2,1)S(1)}, bf16[2,128,512]{2,1,0:T(8,128)(2,1)}, u32[]{:S(2)}, u32[]{:S(2)}) collective-permute-start(bf16[2,128,512]{2,1,0:T(8,128)(2,1)S(1)} %get-tuple-element.24), channel_id=1, source_target_pairs={{0,4},{4,8},{8,12},{12,0},{16,20},{20,24},{24,28},{28,16}} | collective-permute-start | bytes 786440 | tf_op jit(solution)/shard_map/ppermute | solution.py:216
  168.0 2.1 %collective-permute-done.21 = bf16[2,128,512]{2,1,0:T(8,128)(2,1)} collective-permute-done((bf16[2,128,512]{2,1,0:T(8,128)(2,1)S(1)}, bf16[2,128,512]{2,1,0:T(8,128)(2,1)}, u32[]{:S(2)}, u32[]{:S(2)}) %collective-permute-start.21) | collective-permute-done | bytes 262176 | tf_op jit(solution)/shard_map/ppermute | solution.py:216
  170.1 4.9 %collective-permute-start.26 = (bf16[1,400,512]{2,1,0:T(8,128)(2,1)}, bf16[1,400,512]{2,1,0:T(8,128)(2,1)}, u32[]{:S(2)}, u32[]{:S(2)}) collective-permute-start(bf16[1,400,512]{2,1,0:T(8,128)(2,1)} %fusion.151), channel_id=1, source_target_pairs={{0,8},{4,12},{8,0},{12,4},{16,24},{20,28},{24,16},{28,20}} | collective-permute-start | bytes 1228808 | tf_op jit(solution)/shard_map/ppermute | solution.py:38
  176.8 2.9 %fusion.33 = bf16[1,2,256,512]{3,2,1,0:T(8,128)(2,1)} fusion(f32[2,256,512]{2,1,0:T(8,128)S(1)} %bitcast_select_fusion, f32[2,256,512]{2,1,0:T(8,128)S(1)} %bitcast_select_fusion.1, bf16[2,256,512]{2,1,0:T(8,128)(2,1)S(1)} %copy-done.35, bf16[2,256,512]{2,1,0:T(8,128)(2,1)} %get-tuple-element.19, f32[2,512,512]{2,1,0:T(8,128)S(1)} %copy-done.24, ...), kind=kOutput, calls=%fused_computation.77 | convolution fusion | flops 270794752 | bytes 6815747 | tf_op jit(solution)/shard_map/sip,vp->siv/dot_general | solution.py:188
  179.7 5.9 %collective-permute-done.26 = bf16[1,400,512]{2,1,0:T(8,128)(2,1)} collective-permute-done((bf16[1,400,512]{2,1,0:T(8,128)(2,1)}, bf16[1,400,512]{2,1,0:T(8,128)(2,1)}, u32[]{:S(2)}, u32[]{:S(2)}) %collective-permute-start.26) | collective-permute-done | bytes 409632 | tf_op jit(solution)/shard_map/ppermute | solution.py:38
  (231 shorter events, 74.5 us)
Async XLA Ops:
  5.4 11.7 %collective-permute-start = (bf16[2,128,512]{1,2,0:T(8,128)(2,1)}, bf16[2,128,512]{1,2,0:T(8,128)(2,1)}, u32[]{:S(2)}, u32[]{:S(2)}) collective-permute-start(bf16[2,128,512]{1,2,0:T(8,128)(2,1)} %bitcast.3), channel_id=1, source_target_pairs={{0,4},{4,8},{8,12},{12,0},{16,20},{20,24},{24,28},{28,16}} | collective-permute-start | bytes 786440 | tf_op jit(solution)/shard_map/ppermute | solution.py:116
  11.1 8.6 %collective-permute-start.1 = (bf16[2,128,512]{1,2,0:T(8,128)(2,1)}, bf16[2,128,512]{1,2,0:T(8,128)(2,1)}, u32[]{:S(2)}, u32[]{:S(2)}) collective-permute-start(bf16[2,128,512]{1,2,0:T(8,128)(2,1)} %bitcast.4), channel_id=1, source_target_pairs={{0,12},{4,0},{8,4},{12,8},{16,28},{20,16},{24,20},{28,24}} | collective-permute-start | bytes 786440 | tf_op jit(solution)/shard_map/ppermute | solution.py:117
  23.8 9.4 %collective-permute-start.2 = (bf16[2,256,512]{2,1,0:T(8,128)(2,1)S(1)}, bf16[2,256,512]{2,1,0:T(8,128)(2,1)S(1)}, u32[]{:S(2)}, u32[]{:S(2)}) collective-permute-start(bf16[2,256,512]{2,1,0:T(8,128)(2,1)S(1)} %add_convert_fusion.3), channel_id=1, source_target_pairs={{0,1},{4,5},{8,9},{12,13},{16,17},{20,21},{24,25},{28,29}} | collective-permute-start | bytes 1572872 | tf_op jit(solution)/shard_map/ppermute | solution.py:134
  25.2 5.2 %collective-permute-start.3 = (bf16[2,128,512]{2,1,0:T(8,128)(2,1)S(1)}, bf16[2,128,512]{2,1,0:T(8,128)(2,1)S(1)}, u32[]{:S(2)}, u32[]{:S(2)}) collective-permute-start(bf16[2,128,512]{2,1,0:T(8,128)(2,1)S(1)} %get-tuple-element.37), channel_id=1, source_target_pairs={{0,5},{4,9},{8,13},{12,1},{16,21},{20,25},{24,29},{28,17}} | collective-permute-start | bytes 786440 | tf_op jit(solution)/shard_map/ppermute | solution.py:135
  26.5 6.7 %collective-permute-start.4 = (bf16[2,128,512]{2,1,0:T(8,128)(2,1)S(1)}, bf16[2,128,512]{2,1,0:T(8,128)(2,1)S(1)}, u32[]{:S(2)}, u32[]{:S(2)}) collective-permute-start(bf16[2,128,512]{2,1,0:T(8,128)(2,1)S(1)} %get-tuple-element.38), channel_id=1, source_target_pairs={{0,13},{4,1},{8,5},{12,9},{16,29},{20,17},{24,21},{28,25}} | collective-permute-start | bytes 786440 | tf_op jit(solution)/shard_map/ppermute | solution.py:136
  43.0 6.3 %collective-permute-start.8 = (bf16[2,256,512]{2,1,0:T(8,128)(2,1)}, bf16[2,256,512]{2,1,0:T(8,128)(2,1)}, u32[]{:S(2)}, u32[]{:S(2)}) collective-permute-start(bf16[2,256,512]{2,1,0:T(8,128)(2,1)} %add_convert_fusion.1), channel_id=1, source_target_pairs={{2,3},{6,7},{10,11},{14,15},{18,19},{22,23},{26,27},{30,31}} | collective-permute-start | bytes 1572872 | tf_op jit(solution)/shard_map/ppermute | solution.py:134
  46.5 2.8 %collective-permute-start.10 = (bf16[2,128,512]{2,1,0:T(8,128)(2,1)}, bf16[2,128,512]{2,1,0:T(8,128)(2,1)}, u32[]{:S(2)}, u32[]{:S(2)}) collective-permute-start(bf16[2,128,512]{2,1,0:T(8,128)(2,1)} %get-tuple-element.34), channel_id=1, source_target_pairs={{2,15},{6,3},{10,7},{14,11},{18,31},{22,19},{26,23},{30,27}} | collective-permute-start | bytes 786440 | tf_op jit(solution)/shard_map/ppermute | solution.py:136
  62.1 3.5 %collective-permute-start.11 = (bf16[2,256,512]{2,1,0:T(8,128)(2,1)S(1)}, bf16[2,256,512]{2,1,0:T(8,128)(2,1)S(1)}, u32[]{:S(2)}, u32[]{:S(2)}) collective-permute-start(bf16[2,256,512]{2,1,0:T(8,128)(2,1)S(1)} %fusion.23), channel_id=1, source_target_pairs={{3,2},{7,6},{11,10},{15,14},{19,18},{23,22},{27,26},{31,30}} | collective-permute-start | bytes 1572872 | tf_op jit(solution)/shard_map/ppermute | solution.py:207
  62.9 2.6 %collective-permute-start.12 = (bf16[2,128,512]{2,1,0:T(8,128)(2,1)S(1)}, bf16[2,128,512]{2,1,0:T(8,128)(2,1)S(1)}, u32[]{:S(2)}, u32[]{:S(2)}) collective-permute-start(bf16[2,128,512]{2,1,0:T(8,128)(2,1)S(1)} %get-tuple-element.29), channel_id=1, source_target_pairs={{3,14},{7,2},{11,6},{15,10},{19,30},{23,18},{27,22},{31,26}} | collective-permute-start | bytes 786440 | tf_op jit(solution)/shard_map/ppermute | solution.py:208
  72.7 6.3 %collective-permute-start.14 = (bf16[2,256,512]{2,1,0:T(8,128)(2,1)S(1)}, bf16[2,256,512]{2,1,0:T(8,128)(2,1)S(1)}, u32[]{:S(2)}, u32[]{:S(2)}) collective-permute-start(bf16[2,256,512]{2,1,0:T(8,128)(2,1)S(1)} %fusion.25), channel_id=1, source_target_pairs={{2,1},{6,5},{10,9},{14,13},{18,17},{22,21},{26,25},{30,29}} | collective-permute-start | bytes 1572872 | tf_op jit(solution)/shard_map/ppermute | solution.py:207
  73.5 5.4 %collective-permute-start.15 = (bf16[2,128,512]{2,1,0:T(8,128)(2,1)S(1)}, bf16[2,128,512]{2,1,0:T(8,128)(2,1)S(1)}, u32[]{:S(2)}, u32[]{:S(2)}) collective-permute-start(bf16[2,128,512]{2,1,0:T(8,128)(2,1)S(1)} %get-tuple-element.27), channel_id=1, source_target_pairs={{2,13},{6,1},{10,5},{14,9},{18,29},{22,17},{26,21},{30,25}} | collective-permute-start | bytes 786440 | tf_op jit(solution)/shard_map/ppermute | solution.py:208
  74.2 4.8 %collective-permute-start.16 = (bf16[2,128,512]{2,1,0:T(8,128)(2,1)S(1)}, bf16[2,128,512]{2,1,0:T(8,128)(2,1)S(1)}, u32[]{:S(2)}, u32[]{:S(2)}) collective-permute-start(bf16[2,128,512]{2,1,0:T(8,128)(2,1)S(1)} %get-tuple-element.28), channel_id=1, source_target_pairs={{2,5},{6,9},{10,13},{14,1},{18,21},{22,25},{26,29},{30,17}} | collective-permute-start | bytes 786440 | tf_op jit(solution)/shard_map/ppermute | solution.py:209
  77.4 99.2 %collective-permute-start.24 = (bf16[2,256,512]{2,1,0:T(8,128)(2,1)}, bf16[2,256,512]{2,1,0:T(8,128)(2,1)}, u32[]{:S(2)}, u32[]{:S(2)}) collective-permute-start(bf16[2,256,512]{2,1,0:T(8,128)(2,1)} %get-tuple-element.22), channel_id=1, source_target_pairs={{2,3},{6,7},{10,11},{14,15},{18,19},{22,23},{26,27},{30,31}} | collective-permute-start | bytes 1572872 | tf_op jit(solution)/shard_map/ppermute | solution.py:211
  80.4 96.2 %collective-permute-start.23 = (bf16[2,256,512]{2,1,0:T(8,128)(2,1)}, bf16[2,256,512]{2,1,0:T(8,128)(2,1)}, u32[]{:S(2)}, u32[]{:S(2)}) collective-permute-start(bf16[2,256,512]{2,1,0:T(8,128)(2,1)} %get-tuple-element.20), channel_id=1, source_target_pairs={{1,2},{5,6},{9,10},{13,14},{17,18},{21,22},{25,26},{29,30}} | collective-permute-start | bytes 1572872 | tf_op jit(solution)/shard_map/ppermute | solution.py:211
  86.6 51.0 %collective-permute-start.17 = (bf16[2,256,512]{2,1,0:T(8,128)(2,1)S(1)}, bf16[2,256,512]{2,1,0:T(8,128)(2,1)S(1)}, u32[]{:S(2)}, u32[]{:S(2)}) collective-permute-start(bf16[2,256,512]{2,1,0:T(8,128)(2,1)S(1)} %fusion.27), channel_id=1, source_target_pairs={{1,0},{5,4},{9,8},{13,12},{17,16},{21,20},{25,24},{29,28}} | collective-permute-start | bytes 1572872 | tf_op jit(solution)/shard_map/ppermute | solution.py:207
  88.0 45.0 %collective-permute-start.18 = (bf16[2,128,512]{2,1,0:T(8,128)(2,1)S(1)}, bf16[2,128,512]{2,1,0:T(8,128)(2,1)S(1)}, u32[]{:S(2)}, u32[]{:S(2)}) collective-permute-start(bf16[2,128,512]{2,1,0:T(8,128)(2,1)S(1)} %get-tuple-element.25), channel_id=1, source_target_pairs={{1,12},{5,0},{9,4},{13,8},{17,28},{21,16},{25,20},{29,24}} | collective-permute-start | bytes 786440 | tf_op jit(solution)/shard_map/ppermute | solution.py:208
  89.3 48.3 %collective-permute-start.19 = (bf16[2,128,512]{2,1,0:T(8,128)(2,1)S(1)}, bf16[2,128,512]{2,1,0:T(8,128)(2,1)S(1)}, u32[]{:S(2)}, u32[]{:S(2)}) collective-permute-start(bf16[2,128,512]{2,1,0:T(8,128)(2,1)S(1)} %get-tuple-element.26), channel_id=1, source_target_pairs={{1,4},{5,8},{9,12},{13,0},{17,20},{21,24},{25,28},{29,16}} | collective-permute-start | bytes 786440 | tf_op jit(solution)/shard_map/ppermute | solution.py:209
  133.0 17.5 %collective-permute-start.27 = (bf16[2,400,512]{2,1,0:T(8,128)(2,1)S(1)}, bf16[2,400,512]{2,1,0:T(8,128)(2,1)S(1)}, u32[]{:S(2)}, u32[]{:S(2)}) collective-permute-start(bf16[2,400,512]{2,1,0:T(8,128)(2,1)S(1)} %fusion.100), channel_id=1, source_target_pairs={{1,5},{2,6},{3,7},{5,1},{6,2},{7,3},{9,13},{10,14},{11,15},{13,9},... | collective-permute-start | bytes 2457608 | tf_op jit(solution)/shard_map/ppermute | solution.py:38
  141.6 35.0 %collective-permute-start.22 = (bf16[2,256,512]{2,1,0:T(8,128)(2,1)}, bf16[2,256,512]{2,1,0:T(8,128)(2,1)}, u32[]{:S(2)}, u32[]{:S(2)}) collective-permute-start(bf16[2,256,512]{2,1,0:T(8,128)(2,1)} %get-tuple-element.19), channel_id=1, source_target_pairs={{0,1},{4,5},{8,9},{12,13},{16,17},{20,21},{24,25},{28,29}} | collective-permute-start | bytes 1572872 | tf_op jit(solution)/shard_map/ppermute | solution.py:211
  145.1 14.8 %collective-permute-start.25 = (bf16[2,400,512]{2,1,0:T(8,128)(2,1)S(1)}, bf16[2,400,512]{2,1,0:T(8,128)(2,1)S(1)}, u32[]{:S(2)}, u32[]{:S(2)}) collective-permute-start(bf16[2,400,512]{2,1,0:T(8,128)(2,1)S(1)} %fusion.99), channel_id=1, source_target_pairs={{0,4},{4,0},{8,12},{12,8},{16,20},{20,16},{24,28},{28,24}} | collective-permute-start | bytes 2457608 | tf_op jit(solution)/shard_map/ppermute | solution.py:38
  150.5 16.1 %collective-permute-start.20 = (bf16[2,128,512]{2,1,0:T(8,128)(2,1)S(1)}, bf16[2,128,512]{2,1,0:T(8,128)(2,1)S(1)}, u32[]{:S(2)}, u32[]{:S(2)}) collective-permute-start(bf16[2,128,512]{2,1,0:T(8,128)(2,1)S(1)} %get-tuple-element.23), channel_id=1, source_target_pairs={{0,12},{4,0},{8,4},{12,8},{16,28},{20,16},{24,20},{28,24}} | collective-permute-start | bytes 786440 | tf_op jit(solution)/shard_map/ppermute | solution.py:215
  159.8 10.3 %collective-permute-start.21 = (bf16[2,128,512]{2,1,0:T(8,128)(2,1)S(1)}, bf16[2,128,512]{2,1,0:T(8,128)(2,1)}, u32[]{:S(2)}, u32[]{:S(2)}) collective-permute-start(bf16[2,128,512]{2,1,0:T(8,128)(2,1)S(1)} %get-tuple-element.24), channel_id=1, source_target_pairs={{0,4},{4,8},{8,12},{12,0},{16,20},{20,24},{24,28},{28,16}} | collective-permute-start | bytes 786440 | tf_op jit(solution)/shard_map/ppermute | solution.py:216
  166.6 13.1 %collective-permute-start.28 = (bf16[1,400,512]{2,1,0:T(8,128)(2,1)}, bf16[1,400,512]{2,1,0:T(8,128)(2,1)}, u32[]{:S(2)}, u32[]{:S(2)}) collective-permute-start(bf16[1,400,512]{2,1,0:T(8,128)(2,1)} %fusion.152), channel_id=1, source_target_pairs={{1,9},{2,10},{3,11},{5,13},{6,14},{7,15},{9,1},{10,2},{11,3},{13,5... | collective-permute-start | bytes 1228808 | tf_op jit(solution)/shard_map/ppermute | solution.py:38
  170.1 15.5 %collective-permute-start.26 = (bf16[1,400,512]{2,1,0:T(8,128)(2,1)}, bf16[1,400,512]{2,1,0:T(8,128)(2,1)}, u32[]{:S(2)}, u32[]{:S(2)}) collective-permute-start(bf16[1,400,512]{2,1,0:T(8,128)(2,1)} %fusion.151), channel_id=1, source_target_pairs={{0,8},{4,12},{8,0},{12,4},{16,24},{20,28},{24,16},{28,20}} | collective-permute-start | bytes 1228808 | tf_op jit(solution)/shard_map/ppermute | solution.py:38
  (44 other events, 193.8 us)

commit v8 on v6

--- a/solution.py
+++ b/solution.py
@@ -125,10 +125,11 @@
     for tick in range(sections):
         out, res = forward_layer(h, left, right)
         last_res = res
+        last_out = out
         if saved is None:
             saved = res
             saved_out = out
-        else:
+        elif tick + 1 < sections:
             mine = section_index == tick
             saved = tuple(jnp.where(mine, a, b) for a, b in zip(res, saved))
             saved_out = jnp.where(mine, out, saved_out)
@@ -138,11 +139,14 @@
             left = lax.ppermute(pick_blocks(out_blocks, send_right, hs), both, route(tick, tick + 1, 1))
             right = lax.ppermute(pick_blocks(out_blocks, send_left, hs), both, route(tick, tick + 1, -1))
 
-    h_in, agg, pre, act, normed, rstd = saved
+    _, _, pre, _, normed, rstd = saved
     _, _, pre_last, _, normed_last, rstd_last = last_res
+    is_last = section_index == sections - 1
+    h_in, agg, act = (jnp.where(is_last, last_res[i], saved[i]) for i in (0, 1, 3))
+    saved_out = jnp.where(is_last, last_out, saved_out)
 
     g = cotangent
-    grad_in = None
+    formed = []
     dpre_keep = None
     dout_keep = None
     gain_keep = None
@@ -188,18 +192,18 @@
                 lax.ppermute(left_grad, both, route(active, active - 1, -1)),
                 lax.ppermute(right_grad, both, route(active, active - 1, 1)),
             )
-            g_new = lax.ppermute(g, both, route(active - 1, active, 0))
+            formed.append(g)
+            g_new = None
         else:
             g_new = finish(
                 own,
                 lax.ppermute(left_grad, both, route(active, active, -1)),
                 lax.ppermute(right_grad, both, route(active, active, 1)),
             )
-        if grad_in is None:
-            grad_in, dpre_keep, dout_keep = g_new, dpre, dout
+        if dpre_keep is None:
+            dpre_keep, dout_keep = dpre, dout
             gain_keep = gain_term
         else:
-            grad_in = jnp.where(mine, g_new, grad_in)
             dpre_keep = jnp.where(mine, dpre, dpre_keep)
             dout_keep = jnp.where(mine, dout, dout_keep)
             gain_keep = jnp.where(mine, gain_term, gain_keep)
@@ -227,6 +231,15 @@
     g1 = reduced[:r1]
     g2 = reduced[r1 : r1 + r2]
     g3 = reduced[r1 + r2, :r3]
+    if formed:
+        mine_formed = lax.select_n(
+            jnp.clip(sections - 2 - section_index, 0, len(formed) - 1), *formed
+        )
+        back_pairs = [(linear(d, s), linear(d, s + 1)) for d in range(domains) for s in range(sections - 1)]
+        g_back = lax.ppermute(mine_formed, both, back_pairs)
+        grad_in = jnp.where(section_index == 0, g_new, g_back)
+    else:
+        grad_in = g_new
     return (
         saved_out[None],
         grad_in[None],

time: 187 us -> 190 us (1.016)
  matrix products: 27.2 us -> 30 us
  starting transfers between devices: 41.1 us -> 38.9 us
    select_n x3 -> x1, other arithmetic: 5.89 us -> 0.01 us  [shards(): saved = tuple((jnp.where(mine, a, b) for a, b in zip(res, saved)))]
    select_n x0 -> x3, other arithmetic: none -> 5.82 us  [the longest x2 5.74 us: shards(): jnp.where(is_last, last_res[i], saved[i])]
    convert_element_type x3, other arithmetic: 0.8 us -> 3.5 us  [forward_layer(): out = (h.astype(F32) + normed * gain_row).astype(BF16)]
    ppermute x1, waiting for transfers between devices: 0.01 us -> 2.4 us  [shards(): lax.ppermute(left_grad, both, route(active, active, -1))]
    squeeze x3, local copies, waits for them, and re-layouts: 0.84 us -> 2.97 us  [pick_blocks(): lax.dynamic_index_in_dim(blocks, index[i], axis=1, keepdims=False)]
    dot_general x4, matrix products: 2.9 us -> 4.87 us  [forward_layer(): pre = jnp.einsum('sic,ct->sit', h, w_a, preferred_element_type=F32)]
    unnamed x137 -> x107, local copies, waits for them, and re-layouts: 10.8 us -> 9.54 us
  transfers between devices with their start and end apart: 27 -> 25, of which waited for: 8 -> 9; matrix products, arithmetic and copies ran while one was open for 8% -> 8% of each run, Pallas kernels for 0% -> 0%
where the time goes in v8:
time: 190 us; the launch traced here: 189 us
  waiting for transfers between devices  77.9 us (41%)
  starting transfers between devices  38.9 us (20%)
  matrix products  30 us (16%)
  other arithmetic  21.2 us (11%)
  local copies, waits for them, and re-layouts  16.7 us (9%)
  between operations  3.95 us (2%)
    ppermute x3, waiting for transfers between devices, shards(): lax.ppermute(left_grad, both, route(active, active - 1, -1))  39.9 us
    ppermute x2, waiting for transfers between devices, halving_reduce_scatter(): recv = lax.ppermute(send, axis, pairs)  17.9 us
    unnamed x107, local copies, waits for them, and re-layouts  9.54 us
    dot_general x4, matrix products, forward_layer(): agg2 = jnp.einsum('ij,sjd->sid', adj2, h_ext, preferred_element_type=F32)  6.29 us
    ppermute x1, waiting for transfers between devices, shards(): lax.ppermute(right_grad, both, route(active, active, 1))  6.21 us
    select_n x2, other arithmetic, shards(): jnp.where(is_last, last_res[i], saved[i])  5.74 us
    ppermute x1, starting transfers between devices, shards(): lax.ppermute(pick_blocks(in_blocks, send_right, hs), both, route(0, 0, 1))  4.96 us
    dot_general x4, matrix products, forward_layer(): pre = jnp.einsum('sic,ct->sit', h, w_a, preferred_element_type=F32)  4.87 us
  transfers between devices with their start and end apart: 25, of which 9 were waited for; matrix products, arithmetic and copies ran while one was open for 8% of the time, Pallas kernels for 0%

profile of v8, /device:TPU:0, one launch (start us, length us, event | category | flops | bytes accessed | tf_op | source)
XLA Modules:
  0.0 188.7 jit_solution(17407528253852452927)
XLA Ops:
  4.6 5.0 %collective-permute-start = (bf16[2,128,512]{1,2,0:T(8,128)(2,1)S(1)}, bf16[2,128,512]{1,2,0:T(8,128)(2,1)}, u32[]{:S(2)}, u32[]{:S(2)}) collective-permute-start(bf16[2,128,512]{1,2,0:T(8,128)(2,1)S(1)} %bitcast.282), channel_id=1, source_target_pairs={{0,4},{4,8},{8,12},{12,0},{16,20},{20,24},{24,28},{28,16}} | collective-permute-start | bytes 786440 | tf_op jit(solution)/shard_map/ppermute | solution.py:119
  10.5 3.9 %collective-permute-start.1 = (bf16[2,128,512]{1,2,0:T(8,128)(2,1)}, bf16[2,128,512]{1,2,0:T(8,128)(2,1)}, u32[]{:S(2)}, u32[]{:S(2)}) collective-permute-start(bf16[2,128,512]{1,2,0:T(8,128)(2,1)} %bitcast.4), channel_id=1, source_target_pairs={{0,12},{4,0},{8,4},{12,8},{16,28},{20,16},{24,20},{28,24}} | collective-permute-start | bytes 786440 | tf_op jit(solution)/shard_map/ppermute | solution.py:120
  17.4 1.6 collective-permute-done.1
  19.0 1.8 convolution_bitcast_fusion.7
  27.1 2.5 %collective-permute-done.3 = bf16[2,128,512]{2,1,0:T(8,128)(2,1)S(1)} collective-permute-done((bf16[2,128,512]{2,1,0:T(8,128)(2,1)S(1)}, bf16[2,128,512]{2,1,0:T(8,128)(2,1)S(1)}, u32[]{:S(2)}, u32[]{:S(2)}) %collective-permute-start.3) | collective-permute-done | bytes 262176 | tf_op jit(solution)/shard_map/ppermute | solution.py:139
  29.6 2.9 %collective-permute-done.4 = bf16[2,128,512]{2,1,0:T(8,128)(2,1)S(1)} collective-permute-done((bf16[2,128,512]{2,1,0:T(8,128)(2,1)S(1)}, bf16[2,128,512]{2,1,0:T(8,128)(2,1)S(1)}, u32[]{:S(2)}, u32[]{:S(2)}) %collective-permute-start.4) | collective-permute-done | bytes 262176 | tf_op jit(solution)/shard_map/ppermute | solution.py:140
  40.9 1.8 convolution_bitcast_fusion.1
  43.3 1.5 copy-done.28
  45.1 2.5 %select_select_fusion = (f32[2,256,512]{2,1,0:T(8,128)}, f32[2,256,512]{2,1,0:T(8,128)S(1)}) fusion(f32[2,256,512]{2,1,0:T(8,128)S(1)} %copy-done.31, f32[2,256,512]{2,1,0:T(8,128)S(1)} %copy-done.28, pred[]{:T(512)S(6)} %eq.134, pred[]{:T(512)S(6)} %eq.133, f32[2,256,512]{2,1,0:T(8,128)S(1)} %fusion.125, bf16[2,256,512]{2,1,0:T(8,128)(2,1)} %collective-permute-done.5, ...), kind=kOutput, calls=%fused_computation.152 | convolution fusion | flops 269221888 | bytes 6291458 | tf_op jit(solution)/shard_map/sic,ct->sit/dot_general | solution.py:108
  48.9 2.2 %add_convert_fusion.1 = bf16[2,256,512]{2,1,0:T(8,128)(2,1)} fusion(bf16[2,256,512]{2,1,0:T(8,128)(2,1)} %collective-permute-done.5, f32[2,256,512]{2,1,0:T(8,128)S(1)} %get-tuple-element.48, f32[2,256]{1,0:T(2,128)S(1)} %get-tuple-element.42, f32[2,256]{1,0:T(2,128)S(1)} %broadcast_multiply_fusion.9, f32[512]{0:T(512)S(1)} %bitcast.271), kind=kLoop, calls=%fused_computation.159 | loop fusion | flops 1572864 | bytes 2103296 | tf_op jit(solution)/shard_map/convert_element_type | solution.py:115
  52.6 1.9 dynamic-slice_bitcast_fusion.1
  56.1 2.0 %convolution_bitcast_fusion = f32[2,512,512]{2,1,0:T(8,128)S(1)} fusion(bf16[2,128,512]{2,1,0:T(8,128)(2,1)S(1)} %collective-permute-done.10, bf16[2,256,512]{2,1,0:T(8,128)(2,1)} %collective-permute-done.8, bf16[2,128,512]{2,1,0:T(8,128)(2,1)S(1)} %collective-permute-done.9, bf16[256,512]{1,0:T(8,128)(2,1)} %copy-done.13, bf16[256,512]{1,0:T(8,128)(2,1)S(1)} %bitcast.258), kind=kOutput, calls=%fused_computation.6 | convolution fusion | flops 541065216 | bytes 3670016 | tf_op jit(solution)/shard_map/ij,sjd->sid/dot_general | solution.py:106
  58.5 3.3 %select_select_fusion.2 = (bf16[2,256,512]{2,1,0:T(8,128)(2,1)}, bf16[2,256,512]{2,1,0:T(8,128)(2,1)S(1)}) fusion(pred[]{:T(512)S(6)} %eq.134, pred[]{:T(512)S(6)} %eq.133, pred[]{:T(512)S(6)} %eq.122, f32[2,512,512]{2,1,0:T(8,128)S(1)} %convolution_bitcast_fusion, f32[2,512,512]{2,1,0:T(8,128)} %copy-done.21, f32[2,512,512]{2,1,0:T(8,128)S(1)} %copy-done.20, ...), kind=kLoop, calls=%fused_computation.223 | loop fusion | flops 2883584 | bytes 9437187 | tf_op jit(solution)/shard_map/jit(_where)/select_n | solution.py:145
  84.2 1.8 fusion.50
  92.9 2.4 %select_select_fusion.3 = (bf16[2,256,512]{2,1,0:T(8,128)(2,1)S(1)}, bf16[1,2,256,512]{3,2,1,0:T(8,128)(2,1)}) fusion(bf16[2,256,512]{2,1,0:T(8,128)(2,1)} %collective-permute-done.8, bf16[2,256,512]{2,1,0:T(8,128)(2,1)} %collective-permute-done.5, bf16[2,256,512]{2,1,0:T(8,128)(2,1)S(1)} %copy-done.26, bf16[2,256,512]{2,1,0:T(8,128)(2,1)S(1)} %copy-done.4, ...), kind=kLoop, calls=%fused_computation.224 | loop fusion | flops 3145728 | bytes 5773315 | tf_op jit(solution)/shard_map/jit(_where)/select_n | solution.py:145
  95.3 39.9 %collective-permute-done.18 = bf16[2,128,512]{2,1,0:T(8,128)(2,1)S(1)} collective-permute-done((bf16[2,128,512]{2,1,0:T(8,128)(2,1)S(1)}, bf16[2,128,512]{2,1,0:T(8,128)(2,1)S(1)}, u32[]{:S(2)}, u32[]{:S(2)}) %collective-permute-start.18) | collective-permute-done | bytes 262176 | tf_op jit(solution)/shard_map/ppermute | solution.py:192
  135.2 4.4 %collective-permute-done.19 = bf16[2,128,512]{2,1,0:T(8,128)(2,1)S(1)} collective-permute-done((bf16[2,128,512]{2,1,0:T(8,128)(2,1)S(1)}, bf16[2,128,512]{2,1,0:T(8,128)(2,1)S(1)}, u32[]{:S(2)}, u32[]{:S(2)}) %collective-permute-start.19) | collective-permute-done | bytes 262176 | tf_op jit(solution)/shard_map/ppermute | solution.py:193
  147.9 4.1 %collective-permute-start.20 = (bf16[2,128,512]{2,1,0:T(8,128)(2,1)S(1)}, bf16[2,128,512]{2,1,0:T(8,128)(2,1)S(1)}, u32[]{:S(2)}, u32[]{:S(2)}) collective-permute-start(bf16[2,128,512]{2,1,0:T(8,128)(2,1)S(1)} %get-tuple-element.23), channel_id=1, source_target_pairs={{0,12},{4,0},{8,4},{12,8},{16,28},{20,16},{24,20},{28,24}} | collective-permute-start | bytes 786440 | tf_op jit(solution)/shard_map/ppermute | solution.py:200
  152.0 1.9 %collective-permute-start.21 = (bf16[2,128,512]{2,1,0:T(8,128)(2,1)S(1)}, bf16[2,128,512]{2,1,0:T(8,128)(2,1)S(1)}, u32[]{:S(2)}, u32[]{:S(2)}) collective-permute-start(bf16[2,128,512]{2,1,0:T(8,128)(2,1)S(1)} %get-tuple-element.24), channel_id=1, source_target_pairs={{0,4},{4,8},{8,12},{12,0},{16,20},{20,24},{24,28},{28,16}} | collective-permute-start | bytes 786440 | tf_op jit(solution)/shard_map/ppermute | solution.py:201
  155.3 9.0 %collective-permute-done.23 = bf16[2,400,512]{2,1,0:T(8,128)(2,1)S(1)} collective-permute-done((bf16[2,400,512]{2,1,0:T(8,128)(2,1)S(1)}, bf16[2,400,512]{2,1,0:T(8,128)(2,1)S(1)}, u32[]{:S(2)}, u32[]{:S(2)}) %collective-permute-start.23) | collective-permute-done | bytes 819232 | tf_op jit(solution)/shard_map/ppermute | solution.py:41
  164.9 2.1 %collective-permute-start.24 = (bf16[1,400,512]{2,1,0:T(8,128)(2,1)S(1)}, bf16[1,400,512]{2,1,0:T(8,128)(2,1)S(1)}, u32[]{:S(2)}, u32[]{:S(2)}) collective-permute-start(bf16[1,400,512]{2,1,0:T(8,128)(2,1)S(1)} %fusion.158), channel_id=1, source_target_pairs={{0,8},{4,12},{8,0},{12,4},{1,9},{5,13},{9,1},{13,5},{2,10},{6,14},... | collective-permute-start | bytes 1228808 | tf_op jit(solution)/shard_map/ppermute | solution.py:41
  167.0 2.4 %collective-permute-done.20 = bf16[2,128,512]{2,1,0:T(8,128)(2,1)S(1)} collective-permute-done((bf16[2,128,512]{2,1,0:T(8,128)(2,1)S(1)}, bf16[2,128,512]{2,1,0:T(8,128)(2,1)S(1)}, u32[]{:S(2)}, u32[]{:S(2)}) %collective-permute-start.20) | collective-permute-done | bytes 262176 | tf_op jit(solution)/shard_map/ppermute | solution.py:200
  169.6 6.2 %collective-permute-done.21 = bf16[2,128,512]{2,1,0:T(8,128)(2,1)S(1)} collective-permute-done((bf16[2,128,512]{2,1,0:T(8,128)(2,1)S(1)}, bf16[2,128,512]{2,1,0:T(8,128)(2,1)S(1)}, u32[]{:S(2)}, u32[]{:S(2)}) %collective-permute-start.21) | collective-permute-done | bytes 262176 | tf_op jit(solution)/shard_map/ppermute | solution.py:201
  177.6 8.8 %collective-permute-done.24 = bf16[1,400,512]{2,1,0:T(8,128)(2,1)S(1)} collective-permute-done((bf16[1,400,512]{2,1,0:T(8,128)(2,1)S(1)}, bf16[1,400,512]{2,1,0:T(8,128)(2,1)S(1)}, u32[]{:S(2)}, u32[]{:S(2)}) %collective-permute-start.24) | collective-permute-done | bytes 409632 | tf_op jit(solution)/shard_map/ppermute | solution.py:41
  (239 shorter events, 68.7 us)
Async XLA Ops:
  4.6 12.8 %collective-permute-start = (bf16[2,128,512]{1,2,0:T(8,128)(2,1)S(1)}, bf16[2,128,512]{1,2,0:T(8,128)(2,1)}, u32[]{:S(2)}, u32[]{:S(2)}) collective-permute-start(bf16[2,128,512]{1,2,0:T(8,128)(2,1)S(1)} %bitcast.282), channel_id=1, source_target_pairs={{0,4},{4,8},{8,12},{12,0},{16,20},{20,24},{24,28},{28,16}} | collective-permute-start | bytes 786440 | tf_op jit(solution)/shard_map/ppermute | solution.py:119
  10.5 8.6 %collective-permute-start.1 = (bf16[2,128,512]{1,2,0:T(8,128)(2,1)}, bf16[2,128,512]{1,2,0:T(8,128)(2,1)}, u32[]{:S(2)}, u32[]{:S(2)}) collective-permute-start(bf16[2,128,512]{1,2,0:T(8,128)(2,1)} %bitcast.4), channel_id=1, source_target_pairs={{0,12},{4,0},{8,4},{12,8},{16,28},{20,16},{24,20},{28,24}} | collective-permute-start | bytes 786440 | tf_op jit(solution)/shard_map/ppermute | solution.py:120
  23.1 9.4 %collective-permute-start.2 = (bf16[2,256,512]{2,1,0:T(8,128)(2,1)S(1)}, bf16[2,256,512]{2,1,0:T(8,128)(2,1)S(1)}, u32[]{:S(2)}, u32[]{:S(2)}) collective-permute-start(bf16[2,256,512]{2,1,0:T(8,128)(2,1)S(1)} %add_convert_fusion.3), channel_id=1, source_target_pairs={{0,1},{4,5},{8,9},{12,13},{16,17},{20,21},{24,25},{28,29}} | collective-permute-start | bytes 1572872 | tf_op jit(solution)/shard_map/ppermute | solution.py:138
  24.5 5.2 %collective-permute-start.3 = (bf16[2,128,512]{2,1,0:T(8,128)(2,1)S(1)}, bf16[2,128,512]{2,1,0:T(8,128)(2,1)S(1)}, u32[]{:S(2)}, u32[]{:S(2)}) collective-permute-start(bf16[2,128,512]{2,1,0:T(8,128)(2,1)S(1)} %get-tuple-element.37), channel_id=1, source_target_pairs={{0,5},{4,9},{8,13},{12,1},{16,21},{20,25},{24,29},{28,17}} | collective-permute-start | bytes 786440 | tf_op jit(solution)/shard_map/ppermute | solution.py:139
  25.8 6.7 %collective-permute-start.4 = (bf16[2,128,512]{2,1,0:T(8,128)(2,1)S(1)}, bf16[2,128,512]{2,1,0:T(8,128)(2,1)S(1)}, u32[]{:S(2)}, u32[]{:S(2)}) collective-permute-start(bf16[2,128,512]{2,1,0:T(8,128)(2,1)S(1)} %get-tuple-element.38), channel_id=1, source_target_pairs={{0,13},{4,1},{8,5},{12,9},{16,29},{20,17},{24,21},{28,25}} | collective-permute-start | bytes 786440 | tf_op jit(solution)/shard_map/ppermute | solution.py:140
  37.0 4.0 %collective-permute-start.5 = (bf16[2,256,512]{2,1,0:T(8,128)(2,1)}, bf16[2,256,512]{2,1,0:T(8,128)(2,1)}, u32[]{:S(2)}, u32[]{:S(2)}) collective-permute-start(bf16[2,256,512]{2,1,0:T(8,128)(2,1)} %add_convert_fusion.2), channel_id=1, source_target_pairs={{1,2},{5,6},{9,10},{13,14},{17,18},{21,22},{25,26},{29,30}} | collective-permute-start | bytes 1572872 | tf_op jit(solution)/shard_map/ppermute | solution.py:138
  39.5 1.4 collective-permute-start.6
  51.1 5.0 %collective-permute-start.8 = (bf16[2,256,512]{2,1,0:T(8,128)(2,1)}, bf16[2,256,512]{2,1,0:T(8,128)(2,1)}, u32[]{:S(2)}, u32[]{:S(2)}) collective-permute-start(bf16[2,256,512]{2,1,0:T(8,128)(2,1)} %add_convert_fusion.1), channel_id=1, source_target_pairs={{2,3},{6,7},{10,11},{14,15},{18,19},{22,23},{26,27},{30,31}} | collective-permute-start | bytes 1572872 | tf_op jit(solution)/shard_map/ppermute | solution.py:138
  54.4 1.6 collective-permute-start.10
  55.1 1.0 collective-permute-start.9
  68.8 2.5 %collective-permute-start.11 = (bf16[2,256,512]{2,1,0:T(8,128)(2,1)S(1)}, bf16[2,256,512]{2,1,0:T(8,128)(2,1)S(1)}, u32[]{:S(2)}, u32[]{:S(2)}) collective-permute-start(bf16[2,256,512]{2,1,0:T(8,128)(2,1)S(1)} %fusion.22), channel_id=1, source_target_pairs={{3,2},{7,6},{11,10},{15,14},{19,18},{23,22},{27,26},{31,30}} | collective-permute-start | bytes 1572872 | tf_op jit(solution)/shard_map/ppermute | solution.py:191
  69.7 1.5 collective-permute-start.12
  70.4 0.8 collective-permute-start.13
  77.2 7.0 %collective-permute-start.14 = (bf16[2,256,512]{2,1,0:T(8,128)(2,1)}, bf16[2,256,512]{2,1,0:T(8,128)(2,1)}, u32[]{:S(2)}, u32[]{:S(2)}) collective-permute-start(bf16[2,256,512]{2,1,0:T(8,128)(2,1)} %fusion.24), channel_id=1, source_target_pairs={{2,1},{6,5},{10,9},{14,13},{18,17},{22,21},{26,25},{30,29}} | collective-permute-start | bytes 1572872 | tf_op jit(solution)/shard_map/ppermute | solution.py:191
  79.4 2.7 %collective-permute-start.15 = (bf16[2,128,512]{2,1,0:T(8,128)(2,1)}, bf16[2,128,512]{2,1,0:T(8,128)(2,1)}, u32[]{:S(2)}, u32[]{:S(2)}) collective-permute-start(bf16[2,128,512]{2,1,0:T(8,128)(2,1)} %get-tuple-element.27), channel_id=1, source_target_pairs={{2,13},{6,1},{10,5},{14,9},{18,29},{22,17},{26,21},{30,25}} | collective-permute-start | bytes 786440 | tf_op jit(solution)/shard_map/ppermute | solution.py:192
  80.8 2.4 %collective-permute-start.16 = (bf16[2,128,512]{2,1,0:T(8,128)(2,1)}, bf16[2,128,512]{2,1,0:T(8,128)(2,1)}, u32[]{:S(2)}, u32[]{:S(2)}) collective-permute-start(bf16[2,128,512]{2,1,0:T(8,128)(2,1)} %get-tuple-element.28), channel_id=1, source_target_pairs={{2,5},{6,9},{10,13},{14,1},{18,21},{22,25},{26,29},{30,17}} | collective-permute-start | bytes 786440 | tf_op jit(solution)/shard_map/ppermute | solution.py:193
  88.8 51.0 %collective-permute-start.17 = (bf16[2,256,512]{2,1,0:T(8,128)(2,1)S(1)}, bf16[2,256,512]{2,1,0:T(8,128)(2,1)S(1)}, u32[]{:S(2)}, u32[]{:S(2)}) collective-permute-start(bf16[2,256,512]{2,1,0:T(8,128)(2,1)S(1)} %fusion.26), channel_id=1, source_target_pairs={{1,0},{5,4},{9,8},{13,12},{17,16},{21,20},{25,24},{29,28}} | collective-permute-start | bytes 1572872 | tf_op jit(solution)/shard_map/ppermute | solution.py:191
  90.2 44.9 %collective-permute-start.18 = (bf16[2,128,512]{2,1,0:T(8,128)(2,1)S(1)}, bf16[2,128,512]{2,1,0:T(8,128)(2,1)S(1)}, u32[]{:S(2)}, u32[]{:S(2)}) collective-permute-start(bf16[2,128,512]{2,1,0:T(8,128)(2,1)S(1)} %get-tuple-element.25), channel_id=1, source_target_pairs={{1,12},{5,0},{9,4},{13,8},{17,28},{21,16},{25,20},{29,24}} | collective-permute-start | bytes 786440 | tf_op jit(solution)/shard_map/ppermute | solution.py:192
  91.5 48.1 %collective-permute-start.19 = (bf16[2,128,512]{2,1,0:T(8,128)(2,1)S(1)}, bf16[2,128,512]{2,1,0:T(8,128)(2,1)S(1)}, u32[]{:S(2)}, u32[]{:S(2)}) collective-permute-start(bf16[2,128,512]{2,1,0:T(8,128)(2,1)S(1)} %get-tuple-element.26), channel_id=1, source_target_pairs={{1,4},{5,8},{9,12},{13,0},{17,20},{21,24},{25,28},{29,16}} | collective-permute-start | bytes 786440 | tf_op jit(solution)/shard_map/ppermute | solution.py:193
  146.1 18.2 %collective-permute-start.23 = (bf16[2,400,512]{2,1,0:T(8,128)(2,1)S(1)}, bf16[2,400,512]{2,1,0:T(8,128)(2,1)S(1)}, u32[]{:S(2)}, u32[]{:S(2)}) collective-permute-start(bf16[2,400,512]{2,1,0:T(8,128)(2,1)S(1)} %fusion.100), channel_id=1, source_target_pairs={{0,4},{4,0},{8,12},{12,8},{1,5},{5,1},{9,13},{13,9},{2,6},{6,2},{1... | collective-permute-start | bytes 2457608 | tf_op jit(solution)/shard_map/ppermute | solution.py:41
  147.9 21.6 %collective-permute-start.20 = (bf16[2,128,512]{2,1,0:T(8,128)(2,1)S(1)}, bf16[2,128,512]{2,1,0:T(8,128)(2,1)S(1)}, u32[]{:S(2)}, u32[]{:S(2)}) collective-permute-start(bf16[2,128,512]{2,1,0:T(8,128)(2,1)S(1)} %get-tuple-element.23), channel_id=1, source_target_pairs={{0,12},{4,0},{8,4},{12,8},{16,28},{20,16},{24,20},{28,24}} | collective-permute-start | bytes 786440 | tf_op jit(solution)/shard_map/ppermute | solution.py:200
  152.0 23.9 %collective-permute-start.21 = (bf16[2,128,512]{2,1,0:T(8,128)(2,1)S(1)}, bf16[2,128,512]{2,1,0:T(8,128)(2,1)S(1)}, u32[]{:S(2)}, u32[]{:S(2)}) collective-permute-start(bf16[2,128,512]{2,1,0:T(8,128)(2,1)S(1)} %get-tuple-element.24), channel_id=1, source_target_pairs={{0,4},{4,8},{8,12},{12,0},{16,20},{20,24},{24,28},{28,16}} | collective-permute-start | bytes 786440 | tf_op jit(solution)/shard_map/ppermute | solution.py:201
  154.0 22.1 %collective-permute-start.22 = (bf16[2,256,512]{2,1,0:T(8,128)(2,1)S(1)}, bf16[2,256,512]{2,1,0:T(8,128)(2,1)S(1)}, u32[]{:S(2)}, u32[]{:S(2)}) collective-permute-start(bf16[2,256,512]{2,1,0:T(8,128)(2,1)S(1)} %select_select_fusion.4), channel_id=1, source_target_pairs={{0,1},{1,2},{2,3},{4,5},{5,6},{6,7},{8,9},{9,10},{10,11},{12,13},{... | collective-permute-start | bytes 1572872 | tf_op jit(solution)/shard_map/ppermute | solution.py:239
  164.9 21.5 %collective-permute-start.24 = (bf16[1,400,512]{2,1,0:T(8,128)(2,1)S(1)}, bf16[1,400,512]{2,1,0:T(8,128)(2,1)S(1)}, u32[]{:S(2)}, u32[]{:S(2)}) collective-permute-start(bf16[1,400,512]{2,1,0:T(8,128)(2,1)S(1)} %fusion.158), channel_id=1, source_target_pairs={{0,8},{4,12},{8,0},{12,4},{1,9},{5,13},{9,1},{13,5},{2,10},{6,14},... | collective-permute-start | bytes 1228808 | tf_op jit(solution)/shard_map/ppermute | solution.py:41
  (52 other events, 195.3 us)

commit v9 on v8

--- a/solution.py
+++ b/solution.py
@@ -119,42 +119,25 @@
     left = lax.ppermute(pick_blocks(in_blocks, send_right, hs), both, route(0, 0, 1))
     right = lax.ppermute(pick_blocks(in_blocks, send_left, hs), both, route(0, 0, -1))
     h = node_input
-    saved = None
-    saved_out = None
-    last_res = None
+    res_list = []
+    out_list = []
     for tick in range(sections):
         out, res = forward_layer(h, left, right)
-        last_res = res
-        last_out = out
-        if saved is None:
-            saved = res
-            saved_out = out
-        elif tick + 1 < sections:
-            mine = section_index == tick
-            saved = tuple(jnp.where(mine, a, b) for a, b in zip(res, saved))
-            saved_out = jnp.where(mine, out, saved_out)
+        res_list.append(res)
+        out_list.append(out)
         if tick + 1 < sections:
             out_blocks = out.reshape(samples, nb, blk, width)
             h = lax.ppermute(out, both, route(tick, tick + 1, 0))
             left = lax.ppermute(pick_blocks(out_blocks, send_right, hs), both, route(tick, tick + 1, 1))
             right = lax.ppermute(pick_blocks(out_blocks, send_left, hs), both, route(tick, tick + 1, -1))
 
-    _, _, pre, _, normed, rstd = saved
-    _, _, pre_last, _, normed_last, rstd_last = last_res
-    is_last = section_index == sections - 1
-    h_in, agg, act = (jnp.where(is_last, last_res[i], saved[i]) for i in (0, 1, 3))
-    saved_out = jnp.where(is_last, last_out, saved_out)
-
     g = cotangent
     formed = []
-    dpre_keep = None
-    dout_keep = None
-    gain_keep = None
+    dpre_list = []
+    dout_list = []
+    gain_list = []
     for tick in range(sections):
-        if tick == 0:
-            pre_t, normed_t, rstd_t = pre_last, normed_last, rstd_last
-        else:
-            pre_t, normed_t, rstd_t = pre, normed, rstd
+        _, _, pre_t, _, normed_t, rstd_t = res_list[sections - 1 - tick]
         gf = g.astype(F32)
         gain_term = jnp.sum(gf * normed_t, axis=(0, 1))
         dn = gf * gain_row
@@ -200,13 +183,21 @@
                 lax.ppermute(left_grad, both, route(active, active, -1)),
                 lax.ppermute(right_grad, both, route(active, active, 1)),
             )
-        if dpre_keep is None:
-            dpre_keep, dout_keep = dpre, dout
-            gain_keep = gain_term
-        else:
-            dpre_keep = jnp.where(mine, dpre, dpre_keep)
-            dout_keep = jnp.where(mine, dout, dout_keep)
-            gain_keep = jnp.where(mine, gain_term, gain_keep)
+        dpre_list.append(dpre)
+        dout_list.append(dout)
+        gain_list.append(gain_term)
+
+    def own_forward(i):
+        return lax.select_n(section_index, *[r[i] for r in res_list])
+
+    def own_backward(values):
+        return lax.select_n(sections - 1 - section_index, *values)
+
+    h_in, agg, act = own_forward(0), own_forward(1), own_forward(3)
+    saved_out = lax.select_n(section_index, *out_list)
+    dpre_keep = own_backward(dpre_list)
+    dout_keep = own_backward(dout_list)
+    gain_keep = own_backward(gain_list)
 
     norm_factor = 1.0 / math.sqrt(samples * node_rows * domains)
     stacked = jnp.concatenate([h_in, agg], axis=2)

time: 190 us -> 184 us (0.968)
  waiting for transfers between devices: 77.9 us -> 72.5 us
  other arithmetic: 21.2 us -> 24.3 us
  local copies, waits for them, and re-layouts: 16.7 us -> 13.6 us
    unnamed x107 -> x115, local copies, waits for them, and re-layouts: 9.54 us -> 6.56 us
    ppermute x2, waiting for transfers between devices: 17.9 us -> 15.2 us  [halving_reduce_scatter(): recv = lax.ppermute(send, axis, pairs)]
    dot_general x4, matrix products: 4.87 us -> 2.8 us  [forward_layer(): pre = jnp.einsum('sic,ct->sit', h, w_a, preferred_element_type=F32)]
    convert_element_type x8, other arithmetic: 2.3 us -> 4.29 us  [add_blocks(): values = values.reshape(samples, count, blk, width).astype(F32)]
    select_n x4 -> x3, other arithmetic: 5.76 us -> 6.01 us  [the longest x2 6.01 us: own_forward(): return lax.select_n(section_index, *[r[i] for r in res_list])]
  transfers between devices with their start and end apart: 25 -> 25, of which waited for: 9 -> 9; matrix products, arithmetic and copies ran while one was open for 8% -> 11% of each run, Pallas kernels for 0% -> 0%
where the time goes in v9:
time: 184 us; the launch traced here: 183 us
  waiting for transfers between devices  72.5 us (39%)
  starting transfers between devices  40 us (22%)
  matrix products  28.3 us (15%)
  other arithmetic  24.3 us (13%)
  local copies, waits for them, and re-layouts  13.6 us (7%)
  between operations  3.95 us (2%)
    ppermute x3, waiting for transfers between devices, shards(): lax.ppermute(left_grad, both, route(active, active - 1, -1))  39.9 us
    ppermute x2, waiting for transfers between devices, halving_reduce_scatter(): recv = lax.ppermute(send, axis, pairs)  15.2 us
    unnamed x115, local copies, waits for them, and re-layouts  6.56 us
    select_n x2, other arithmetic, own_forward(): return lax.select_n(section_index, *[r[i] for r in res_list])  6.01 us
    dot_general x4, matrix products, forward_layer(): agg2 = jnp.einsum('ij,sjd->sid', adj2, h_ext, preferred_element_type=F32)  5.32 us
    ppermute x1, starting transfers between devices, shards(): lax.ppermute(pick_blocks(in_blocks, send_right, hs), both, route(0, 0, 1))  4.96 us
    ppermute x1, waiting for transfers between devices, shards(): lax.ppermute(right_grad, both, route(active, active, 1))  4.86 us
    dot_general x4, matrix products, shards(): jnp.einsum('ij,sid->sjd', adj2, jnp.concatenate([dagg, dagg], axis=1), pr...  4.41 us
  transfers between devices with their start and end apart: 25, of which 9 were waited for; matrix products, arithmetic and copies ran while one was open for 11% of the time, Pallas kernels for 0%

profile of v9, /device:TPU:0, one launch (start us, length us, event | category | flops | bytes accessed | tf_op | source)
XLA Modules:
  0.0 182.6 jit_solution(17470097346601052239)
XLA Ops:
  4.7 5.0 %collective-permute-start = (bf16[2,128,512]{1,2,0:T(8,128)(2,1)S(1)}, bf16[2,128,512]{1,2,0:T(8,128)(2,1)}, u32[]{:S(2)}, u32[]{:S(2)}) collective-permute-start(bf16[2,128,512]{1,2,0:T(8,128)(2,1)S(1)} %bitcast.285), channel_id=1, source_target_pairs={{0,4},{4,8},{8,12},{12,0},{16,20},{20,24},{24,28},{28,16}} | collective-permute-start | bytes 786440 | tf_op jit(solution)/shard_map/ppermute | solution.py:119
  10.5 3.9 %collective-permute-start.1 = (bf16[2,128,512]{1,2,0:T(8,128)(2,1)}, bf16[2,128,512]{1,2,0:T(8,128)(2,1)}, u32[]{:S(2)}, u32[]{:S(2)}) collective-permute-start(bf16[2,128,512]{1,2,0:T(8,128)(2,1)} %bitcast.4), channel_id=1, source_target_pairs={{0,12},{4,0},{8,4},{12,8},{16,28},{20,16},{24,20},{28,24}} | collective-permute-start | bytes 786440 | tf_op jit(solution)/shard_map/ppermute | solution.py:120
  15.1 1.5 fusion.131
  17.4 1.7 collective-permute-done.1
  19.1 1.8 convolution_bitcast_fusion.7
  27.1 2.5 %collective-permute-done.3 = bf16[2,128,512]{2,1,0:T(8,128)(2,1)S(1)} collective-permute-done((bf16[2,128,512]{2,1,0:T(8,128)(2,1)S(1)}, bf16[2,128,512]{2,1,0:T(8,128)(2,1)S(1)}, u32[]{:S(2)}, u32[]{:S(2)}) %collective-permute-start.3) | collective-permute-done | bytes 262176 | tf_op jit(solution)/shard_map/ppermute | solution.py:131
  29.7 2.8 %collective-permute-done.4 = bf16[2,128,512]{2,1,0:T(8,128)(2,1)S(1)} collective-permute-done((bf16[2,128,512]{2,1,0:T(8,128)(2,1)S(1)}, bf16[2,128,512]{2,1,0:T(8,128)(2,1)S(1)}, u32[]{:S(2)}, u32[]{:S(2)}) %collective-permute-start.4) | collective-permute-done | bytes 262176 | tf_op jit(solution)/shard_map/ppermute | solution.py:132
  42.9 1.5 collective-permute-start.8
  44.4 1.9 %dynamic-slice_bitcast_fusion.1 = (bf16[2,128,512]{2,1,0:T(8,128)(2,1)}, bf16[2,128,512]{2,1,0:T(8,128)(2,1)}) fusion(bf16[2,2,128,512]{3,2,1,0:T(8,128)(2,1)} %bitcast.28, s32[]{:T(128)S(6)} %select_n.318, s32[]{:T(128)S(6)} %select_n.321), kind=kLoop, calls=%fused_computation.238 | loop fusion | bytes 1048584 | tf_op jit(solution)/shard_map/jit(dynamic_index_in_dim)/squeeze | solution.py:15
  49.1 2.1 %convolution_bitcast_fusion = f32[2,512,512]{2,1,0:T(8,128)S(1)} fusion(bf16[2,128,512]{2,1,0:T(8,128)(2,1)} %collective-permute-done.10, bf16[2,256,512]{2,1,0:T(8,128)(2,1)} %collective-permute-done.8, bf16[2,128,512]{2,1,0:T(8,128)(2,1)} %collective-permute-done.9, bf16[256,512]{1,0:T(8,128)(2,1)} %copy-done.13, bf16[256,512]{1,0:T(8,128)(2,1)S(1)} %bitcast.260), kind=kOutput, calls=%fused_computation.6 | convolution fusion | flops 541065216 | bytes 3670016 | tf_op jit(solution)/shard_map/ij,sjd->sid/dot_general | solution.py:106
  51.7 3.3 %select_select_fusion = (bf16[2,256,512]{2,1,0:T(8,128)(2,1)}, bf16[2,256,512]{2,1,0:T(8,128)(2,1)S(1)}) fusion(pred[]{:T(512)S(6)} %select_n.323, pred[]{:T(512)S(6)} %select_n.314, pred[]{:T(512)S(6)} %select_n.312, f32[2,512,512]{2,1,0:T(8,128)S(1)} %convolution_bitcast_fusion, f32[2,512,512]{2,1,0:T(8,128)} %copy-done.21, ...), kind=kLoop, calls=%fused_computation.224 | loop fusion | flops 2883584 | bytes 9437187 | tf_op jit(solution)/shard_map/select_n | solution.py:191
  55.4 1.5 convolution_add_fusion
  76.1 1.9 %fusion.46 = (bf16[512]{0:T(512)(128)(2,1)S(1)}, f32[2,256]{1,0:T(2,128)S(1)}, f32[2,256]{1,0:T(2,128)S(1)}, bf16[2,256,512]{2,1,0:T(8,128)(2,1)S(1)}) fusion(f32[2,256,512]{2,1,0:T(8,128)S(1)} %copy-done.3, f32[2,256]{1,0:T(2,128)S(1)} %add_rsqrt_fusion.2, f32[2,256]{1,0:T(2,128)S(1)} %broadcast_multiply_fusion.10, f32[512]{0:T(512)S(1)} %bitcast.279, ...), kind=kLoop, calls=%fused_computation.84 | loop fusion | flops 3930624 | bytes 3157504 | tf_op jit(solution)/shard_map/reduce_sum | solution.py:142
  85.0 2.7 %select_select_fusion.1 = (bf16[2,256,512]{2,1,0:T(8,128)(2,1)S(1)}, bf16[1,2,256,512]{3,2,1,0:T(8,128)(2,1)}) fusion(bf16[2,256,512]{2,1,0:T(8,128)(2,1)S(1)} %copy-done.31, bf16[2,256,512]{2,1,0:T(8,128)(2,1)} %collective-permute-done.8, bf16[2,256,512]{2,1,0:T(8,128)(2,1)S(1)} %copy-done.8, bf16[2,256,512]{2,1,0:T(8,128)(2,1)S(1)} %copy-done.29, ...), kind=kLoop, calls=%fused_computation.225 | loop fusion | flops 3145728 | bytes 5773315 | tf_op jit(solution)/shard_map/select_n | solution.py:191
  87.7 39.9 %collective-permute-done.18 = bf16[2,128,512]{2,1,0:T(8,128)(2,1)S(1)} collective-permute-done((bf16[2,128,512]{2,1,0:T(8,128)(2,1)S(1)}, bf16[2,128,512]{2,1,0:T(8,128)(2,1)S(1)}, u32[]{:S(2)}, u32[]{:S(2)}) %collective-permute-start.18) | collective-permute-done | bytes 262176 | tf_op jit(solution)/shard_map/ppermute | solution.py:175
  127.6 4.4 %collective-permute-done.19 = bf16[2,128,512]{2,1,0:T(8,128)(2,1)S(1)} collective-permute-done((bf16[2,128,512]{2,1,0:T(8,128)(2,1)S(1)}, bf16[2,128,512]{2,1,0:T(8,128)(2,1)S(1)}, u32[]{:S(2)}, u32[]{:S(2)}) %collective-permute-start.19) | collective-permute-done | bytes 262176 | tf_op jit(solution)/shard_map/ppermute | solution.py:176
  139.0 2.1 %fusion.210 = (bf16[2,512,512]{2,1,0:T(8,128)(2,1)S(1)}, f32[2,512,512]{2,1,0:T(8,128)}) fusion(bf16[256,512]{1,0:T(8,128)(2,1)S(1)} %copy-done.16, bf16[256,512]{1,0:T(8,128)(2,1)S(1)} %bitcast.264, bf16[2,256,512]{1,2,0:T(8,128)(2,1)S(1)} %convolution_convert_fusion), kind=kOutput, calls=%fused_computation.315 | convolution fusion | flops 540540928 | bytes 4194304 | tf_op jit(solution)/shard_map/ij,sid->sjd/dot_general | solution.py:157
  141.9 4.1 %collective-permute-start.20 = (bf16[2,128,512]{2,1,0:T(8,128)(2,1)}, bf16[2,128,512]{2,1,0:T(8,128)(2,1)}, u32[]{:S(2)}, u32[]{:S(2)}) collective-permute-start(bf16[2,128,512]{2,1,0:T(8,128)(2,1)} %get-tuple-element.22), channel_id=1, source_target_pairs={{0,12},{4,0},{8,4},{12,8},{16,28},{20,16},{24,20},{28,24}} | collective-permute-start | bytes 786440 | tf_op jit(solution)/shard_map/ppermute | solution.py:183
  146.1 1.9 %collective-permute-start.21 = (bf16[2,128,512]{2,1,0:T(8,128)(2,1)}, bf16[2,128,512]{2,1,0:T(8,128)(2,1)}, u32[]{:S(2)}, u32[]{:S(2)}) collective-permute-start(bf16[2,128,512]{2,1,0:T(8,128)(2,1)} %get-tuple-element.23), channel_id=1, source_target_pairs={{0,4},{4,8},{8,12},{12,0},{16,20},{20,24},{24,28},{28,16}} | collective-permute-start | bytes 786440 | tf_op jit(solution)/shard_map/ppermute | solution.py:184
  148.9 2.1 %collective-permute-start.22 = (bf16[2,256,512]{2,1,0:T(8,128)(2,1)}, bf16[2,256,512]{2,1,0:T(8,128)(2,1)}, u32[]{:S(2)}, u32[]{:S(2)}) collective-permute-start(bf16[2,256,512]{2,1,0:T(8,128)(2,1)} %select_select_fusion.2), channel_id=1, source_target_pairs={{0,1},{1,2},{2,3},{4,5},{5,6},{6,7},{8,9},{9,10},{10,11},{12,13},{... | collective-permute-start | bytes 1572872 | tf_op jit(solution)/shard_map/ppermute | solution.py:230
  151.0 5.4 %collective-permute-done.23 = bf16[2,400,512]{2,1,0:T(8,128)(2,1)S(1)} collective-permute-done((bf16[2,400,512]{2,1,0:T(8,128)(2,1)S(1)}, bf16[2,400,512]{2,1,0:T(8,128)(2,1)S(1)}, u32[]{:S(2)}, u32[]{:S(2)}) %collective-permute-start.23) | collective-permute-done | bytes 819232 | tf_op jit(solution)/shard_map/ppermute | solution.py:41
  157.6 2.0 %collective-permute-start.24 = (bf16[1,400,512]{2,1,0:T(8,128)(2,1)}, bf16[1,400,512]{2,1,0:T(8,128)(2,1)}, u32[]{:S(2)}, u32[]{:S(2)}) collective-permute-start(bf16[1,400,512]{2,1,0:T(8,128)(2,1)} %fusion.161), channel_id=1, source_target_pairs={{0,8},{4,12},{8,0},{12,4},{1,9},{5,13},{9,1},{13,5},{2,10},{6,14},... | collective-permute-start | bytes 1228808 | tf_op jit(solution)/shard_map/ppermute | solution.py:41
  162.0 4.9 %collective-permute-done.21 = bf16[2,128,512]{2,1,0:T(8,128)(2,1)} collective-permute-done((bf16[2,128,512]{2,1,0:T(8,128)(2,1)}, bf16[2,128,512]{2,1,0:T(8,128)(2,1)}, u32[]{:S(2)}, u32[]{:S(2)}) %collective-permute-start.21) | collective-permute-done | bytes 262176 | tf_op jit(solution)/shard_map/ppermute | solution.py:184
  169.5 9.8 %collective-permute-done.24 = bf16[1,400,512]{2,1,0:T(8,128)(2,1)} collective-permute-done((bf16[1,400,512]{2,1,0:T(8,128)(2,1)}, bf16[1,400,512]{2,1,0:T(8,128)(2,1)}, u32[]{:S(2)}, u32[]{:S(2)}) %collective-permute-start.24) | collective-permute-done | bytes 409632 | tf_op jit(solution)/shard_map/ppermute | solution.py:41
  (247 shorter events, 68.1 us)
Async XLA Ops:
  4.7 12.7 %collective-permute-start = (bf16[2,128,512]{1,2,0:T(8,128)(2,1)S(1)}, bf16[2,128,512]{1,2,0:T(8,128)(2,1)}, u32[]{:S(2)}, u32[]{:S(2)}) collective-permute-start(bf16[2,128,512]{1,2,0:T(8,128)(2,1)S(1)} %bitcast.285), channel_id=1, source_target_pairs={{0,4},{4,8},{8,12},{12,0},{16,20},{20,24},{24,28},{28,16}} | collective-permute-start | bytes 786440 | tf_op jit(solution)/shard_map/ppermute | solution.py:119
  10.5 8.6 %collective-permute-start.1 = (bf16[2,128,512]{1,2,0:T(8,128)(2,1)}, bf16[2,128,512]{1,2,0:T(8,128)(2,1)}, u32[]{:S(2)}, u32[]{:S(2)}) collective-permute-start(bf16[2,128,512]{1,2,0:T(8,128)(2,1)} %bitcast.4), channel_id=1, source_target_pairs={{0,12},{4,0},{8,4},{12,8},{16,28},{20,16},{24,20},{28,24}} | collective-permute-start | bytes 786440 | tf_op jit(solution)/shard_map/ppermute | solution.py:120
  23.1 9.4 %collective-permute-start.2 = (bf16[2,256,512]{2,1,0:T(8,128)(2,1)S(1)}, bf16[2,256,512]{2,1,0:T(8,128)(2,1)S(1)}, u32[]{:S(2)}, u32[]{:S(2)}) collective-permute-start(bf16[2,256,512]{2,1,0:T(8,128)(2,1)S(1)} %add_convert_fusion.3), channel_id=1, source_target_pairs={{0,1},{4,5},{8,9},{12,13},{16,17},{20,21},{24,25},{28,29}} | collective-permute-start | bytes 1572872 | tf_op jit(solution)/shard_map/ppermute | solution.py:130
  24.5 5.2 %collective-permute-start.3 = (bf16[2,128,512]{2,1,0:T(8,128)(2,1)S(1)}, bf16[2,128,512]{2,1,0:T(8,128)(2,1)S(1)}, u32[]{:S(2)}, u32[]{:S(2)}) collective-permute-start(bf16[2,128,512]{2,1,0:T(8,128)(2,1)S(1)} %get-tuple-element.36), channel_id=1, source_target_pairs={{0,5},{4,9},{8,13},{12,1},{16,21},{20,25},{24,29},{28,17}} | collective-permute-start | bytes 786440 | tf_op jit(solution)/shard_map/ppermute | solution.py:131
  25.8 6.7 %collective-permute-start.4 = (bf16[2,128,512]{2,1,0:T(8,128)(2,1)S(1)}, bf16[2,128,512]{2,1,0:T(8,128)(2,1)S(1)}, u32[]{:S(2)}, u32[]{:S(2)}) collective-permute-start(bf16[2,128,512]{2,1,0:T(8,128)(2,1)S(1)} %get-tuple-element.37), channel_id=1, source_target_pairs={{0,13},{4,1},{8,5},{12,9},{16,29},{20,17},{24,21},{28,25}} | collective-permute-start | bytes 786440 | tf_op jit(solution)/shard_map/ppermute | solution.py:132
  36.2 2.2 %collective-permute-start.5 = (bf16[2,256,512]{2,1,0:T(8,128)(2,1)S(1)}, bf16[2,256,512]{2,1,0:T(8,128)(2,1)S(1)}, u32[]{:S(2)}, u32[]{:S(2)}) collective-permute-start(bf16[2,256,512]{2,1,0:T(8,128)(2,1)S(1)} %add_convert_fusion.2), channel_id=1, source_target_pairs={{1,2},{5,6},{9,10},{13,14},{17,18},{21,22},{25,26},{29,30}} | collective-permute-start | bytes 1572872 | tf_op jit(solution)/shard_map/ppermute | solution.py:130
  36.9 1.4 collective-permute-start.6
  42.9 6.2 %collective-permute-start.8 = (bf16[2,256,512]{2,1,0:T(8,128)(2,1)}, bf16[2,256,512]{2,1,0:T(8,128)(2,1)}, u32[]{:S(2)}, u32[]{:S(2)}) collective-permute-start(bf16[2,256,512]{2,1,0:T(8,128)(2,1)} %add_convert_fusion.1), channel_id=1, source_target_pairs={{2,3},{6,7},{10,11},{14,15},{18,19},{22,23},{26,27},{30,31}} | collective-permute-start | bytes 1572872 | tf_op jit(solution)/shard_map/ppermute | solution.py:130
  46.3 2.8 %collective-permute-start.10 = (bf16[2,128,512]{2,1,0:T(8,128)(2,1)}, bf16[2,128,512]{2,1,0:T(8,128)(2,1)}, u32[]{:S(2)}, u32[]{:S(2)}) collective-permute-start(bf16[2,128,512]{2,1,0:T(8,128)(2,1)} %get-tuple-element.33), channel_id=1, source_target_pairs={{2,15},{6,3},{10,7},{14,11},{18,31},{22,19},{26,23},{30,27}} | collective-permute-start | bytes 786440 | tf_op jit(solution)/shard_map/ppermute | solution.py:132
  47.6 1.4 collective-permute-start.9
  61.9 2.5 %collective-permute-start.11 = (bf16[2,256,512]{2,1,0:T(8,128)(2,1)S(1)}, bf16[2,256,512]{2,1,0:T(8,128)(2,1)S(1)}, u32[]{:S(2)}, u32[]{:S(2)}) collective-permute-start(bf16[2,256,512]{2,1,0:T(8,128)(2,1)S(1)} %fusion.20), channel_id=1, source_target_pairs={{3,2},{7,6},{11,10},{15,14},{19,18},{23,22},{27,26},{31,30}} | collective-permute-start | bytes 1572872 | tf_op jit(solution)/shard_map/ppermute | solution.py:174
  62.8 1.5 collective-permute-start.12
  63.5 0.8 collective-permute-start.13
  69.0 7.1 %collective-permute-start.14 = (bf16[2,256,512]{2,1,0:T(8,128)(2,1)}, bf16[2,256,512]{2,1,0:T(8,128)(2,1)}, u32[]{:S(2)}, u32[]{:S(2)}) collective-permute-start(bf16[2,256,512]{2,1,0:T(8,128)(2,1)} %fusion.21), channel_id=1, source_target_pairs={{2,1},{6,5},{10,9},{14,13},{18,17},{22,21},{26,25},{30,29}} | collective-permute-start | bytes 1572872 | tf_op jit(solution)/shard_map/ppermute | solution.py:174
  71.3 2.7 %collective-permute-start.15 = (bf16[2,128,512]{2,1,0:T(8,128)(2,1)}, bf16[2,128,512]{2,1,0:T(8,128)(2,1)}, u32[]{:S(2)}, u32[]{:S(2)}) collective-permute-start(bf16[2,128,512]{2,1,0:T(8,128)(2,1)} %get-tuple-element.26), channel_id=1, source_target_pairs={{2,13},{6,1},{10,5},{14,9},{18,29},{22,17},{26,21},{30,25}} | collective-permute-start | bytes 786440 | tf_op jit(solution)/shard_map/ppermute | solution.py:175
  72.6 2.5 %collective-permute-start.16 = (bf16[2,128,512]{2,1,0:T(8,128)(2,1)}, bf16[2,128,512]{2,1,0:T(8,128)(2,1)}, u32[]{:S(2)}, u32[]{:S(2)}) collective-permute-start(bf16[2,128,512]{2,1,0:T(8,128)(2,1)} %get-tuple-element.27), channel_id=1, source_target_pairs={{2,5},{6,9},{10,13},{14,1},{18,21},{22,25},{26,29},{30,17}} | collective-permute-start | bytes 786440 | tf_op jit(solution)/shard_map/ppermute | solution.py:176
  80.9 51.2 %collective-permute-start.17 = (bf16[2,256,512]{2,1,0:T(8,128)(2,1)S(1)}, bf16[2,256,512]{2,1,0:T(8,128)(2,1)S(1)}, u32[]{:S(2)}, u32[]{:S(2)}) collective-permute-start(bf16[2,256,512]{2,1,0:T(8,128)(2,1)S(1)} %fusion.22), channel_id=1, source_target_pairs={{1,0},{5,4},{9,8},{13,12},{17,16},{21,20},{25,24},{29,28}} | collective-permute-start | bytes 1572872 | tf_op jit(solution)/shard_map/ppermute | solution.py:174
  82.4 45.2 %collective-permute-start.18 = (bf16[2,128,512]{2,1,0:T(8,128)(2,1)S(1)}, bf16[2,128,512]{2,1,0:T(8,128)(2,1)S(1)}, u32[]{:S(2)}, u32[]{:S(2)}) collective-permute-start(bf16[2,128,512]{2,1,0:T(8,128)(2,1)S(1)} %get-tuple-element.24), channel_id=1, source_target_pairs={{1,12},{5,0},{9,4},{13,8},{17,28},{21,16},{25,20},{29,24}} | collective-permute-start | bytes 786440 | tf_op jit(solution)/shard_map/ppermute | solution.py:175
  83.7 48.3 %collective-permute-start.19 = (bf16[2,128,512]{2,1,0:T(8,128)(2,1)S(1)}, bf16[2,128,512]{2,1,0:T(8,128)(2,1)S(1)}, u32[]{:S(2)}, u32[]{:S(2)}) collective-permute-start(bf16[2,128,512]{2,1,0:T(8,128)(2,1)S(1)} %get-tuple-element.25), channel_id=1, source_target_pairs={{1,4},{5,8},{9,12},{13,0},{17,20},{21,24},{25,28},{29,16}} | collective-permute-start | bytes 786440 | tf_op jit(solution)/shard_map/ppermute | solution.py:176
  138.1 18.3 %collective-permute-start.23 = (bf16[2,400,512]{2,1,0:T(8,128)(2,1)S(1)}, bf16[2,400,512]{2,1,0:T(8,128)(2,1)S(1)}, u32[]{:S(2)}, u32[]{:S(2)}) collective-permute-start(bf16[2,400,512]{2,1,0:T(8,128)(2,1)S(1)} %fusion.96), channel_id=1, source_target_pairs={{0,4},{4,0},{8,12},{12,8},{1,5},{5,1},{9,13},{13,9},{2,6},{6,2},{1... | collective-permute-start | bytes 2457608 | tf_op jit(solution)/shard_map/ppermute | solution.py:41
  141.9 18.9 %collective-permute-start.20 = (bf16[2,128,512]{2,1,0:T(8,128)(2,1)}, bf16[2,128,512]{2,1,0:T(8,128)(2,1)}, u32[]{:S(2)}, u32[]{:S(2)}) collective-permute-start(bf16[2,128,512]{2,1,0:T(8,128)(2,1)} %get-tuple-element.22), channel_id=1, source_target_pairs={{0,12},{4,0},{8,4},{12,8},{16,28},{20,16},{24,20},{28,24}} | collective-permute-start | bytes 786440 | tf_op jit(solution)/shard_map/ppermute | solution.py:183
  146.1 20.8 %collective-permute-start.21 = (bf16[2,128,512]{2,1,0:T(8,128)(2,1)}, bf16[2,128,512]{2,1,0:T(8,128)(2,1)}, u32[]{:S(2)}, u32[]{:S(2)}) collective-permute-start(bf16[2,128,512]{2,1,0:T(8,128)(2,1)} %get-tuple-element.23), channel_id=1, source_target_pairs={{0,4},{4,8},{8,12},{12,0},{16,20},{20,24},{24,28},{28,16}} | collective-permute-start | bytes 786440 | tf_op jit(solution)/shard_map/ppermute | solution.py:184
  148.9 19.2 %collective-permute-start.22 = (bf16[2,256,512]{2,1,0:T(8,128)(2,1)}, bf16[2,256,512]{2,1,0:T(8,128)(2,1)}, u32[]{:S(2)}, u32[]{:S(2)}) collective-permute-start(bf16[2,256,512]{2,1,0:T(8,128)(2,1)} %select_select_fusion.2), channel_id=1, source_target_pairs={{0,1},{1,2},{2,3},{4,5},{5,6},{6,7},{8,9},{9,10},{10,11},{12,13},{... | collective-permute-start | bytes 1572872 | tf_op jit(solution)/shard_map/ppermute | solution.py:230
  157.6 21.7 %collective-permute-start.24 = (bf16[1,400,512]{2,1,0:T(8,128)(2,1)}, bf16[1,400,512]{2,1,0:T(8,128)(2,1)}, u32[]{:S(2)}, u32[]{:S(2)}) collective-permute-start(bf16[1,400,512]{2,1,0:T(8,128)(2,1)} %fusion.161), channel_id=1, source_target_pairs={{0,8},{4,12},{8,0},{12,4},{1,9},{5,13},{9,1},{13,5},{2,10},{6,14},... | collective-permute-start | bytes 1228808 | tf_op jit(solution)/shard_map/ppermute | solution.py:41
  (56 other events, 226.1 us)

commit v10 on v9

--- a/solution.py
+++ b/solution.py
@@ -187,14 +187,16 @@
         dout_list.append(dout)
         gain_list.append(gain_term)
 
+    late_index, _ = lax.optimization_barrier((section_index, dpre))
+
     def own_forward(i):
-        return lax.select_n(section_index, *[r[i] for r in res_list])
+        return lax.select_n(late_index, *[r[i] for r in res_list])
 
     def own_backward(values):
         return lax.select_n(sections - 1 - section_index, *values)
 
     h_in, agg, act = own_forward(0), own_forward(1), own_forward(3)
-    saved_out = lax.select_n(section_index, *out_list)
+    saved_out = lax.select_n(late_index, *out_list)
     dpre_keep = own_backward(dpre_list)
     dout_keep = own_backward(dout_list)
     gain_keep = own_backward(gain_list)
@@ -224,7 +226,7 @@
     g3 = reduced[r1 + r2, :r3]
     if formed:
         mine_formed = lax.select_n(
-            jnp.clip(sections - 2 - section_index, 0, len(formed) - 1), *formed
+            jnp.clip(sections - 2 - late_index, 0, len(formed) - 1), *formed
         )
         back_pairs = [(linear(d, s), linear(d, s + 1)) for d in range(domains) for s in range(sections - 1)]
         g_back = lax.ppermute(mine_formed, both, back_pairs)

time: 184 us -> 186 us (1.011)
  waiting for transfers between devices: 72.5 us -> 74.9 us
    ppermute x3, waiting for transfers between devices: 39.9 us -> 48.8 us  [shards(): lax.ppermute(left_grad, both, route(active, active - 1, -1))]
    ppermute x1, waiting for transfers between devices: 4.86 us -> 0.01 us  [shards(): lax.ppermute(right_grad, both, route(active, active, 1))]
    unnamed x115 -> x131, local copies, waits for them, and re-layouts: 6.56 us -> 9.04 us
  transfers between devices with their start and end apart: 25 -> 25, of which waited for: 9 -> 8; matrix products, arithmetic and copies ran while one was open for 11% -> 10% of each run, Pallas kernels for 0% -> 0%
where the time goes in v10:
time: 186 us; the launch traced here: 185 us
  waiting for transfers between devices  74.9 us (40%)
  starting transfers between devices  38.2 us (21%)
  matrix products  28.8 us (15%)
  other arithmetic  25.3 us (14%)
  local copies, waits for them, and re-layouts  14.2 us (8%)
  between operations  4.01 us (2%)
    ppermute x3, waiting for transfers between devices, shards(): lax.ppermute(left_grad, both, route(active, active - 1, -1))  48.8 us
    ppermute x2, waiting for transfers between devices, halving_reduce_scatter(): recv = lax.ppermute(send, axis, pairs)  13.9 us
    unnamed x131, local copies, waits for them, and re-layouts  9.04 us
    select_n x2, other arithmetic, own_forward(): return lax.select_n(late_index, *[r[i] for r in res_list])  5.76 us
    dot_general x4, matrix products, shards(): jnp.einsum('ij,sid->sjd', adj2, jnp.concatenate([dagg, dagg], axis=1), pr...  5.75 us
    ppermute x1, starting transfers between devices, shards(): lax.ppermute(pick_blocks(in_blocks, send_right, hs), both, route(0, 0, 1))  5 us
    ppermute x1, starting transfers between devices, shards(): lax.ppermute(left_grad, both, route(active, active, -1))  4.6 us
    convert_element_type x8, other arithmetic, add_blocks(): values = values.reshape(samples, count, blk, width).astype(F32)  4.2 us
  transfers between devices with their start and end apart: 25, of which 8 were waited for; matrix products, arithmetic and copies ran while one was open for 10% of the time, Pallas kernels for 0%

profile of v10, /device:TPU:0, one launch (start us, length us, event | category | flops | bytes accessed | tf_op | source)
XLA Modules:
  0.0 185.3 jit_solution(4132760588418393223)
XLA Ops:
  4.6 5.0 %collective-permute-start = (bf16[2,128,512]{1,2,0:T(8,128)(2,1)S(1)}, bf16[2,128,512]{1,2,0:T(8,128)(2,1)}, u32[]{:S(2)}, u32[]{:S(2)}) collective-permute-start(bf16[2,128,512]{1,2,0:T(8,128)(2,1)S(1)} %bitcast.282), channel_id=1, source_target_pairs={{0,4},{4,8},{8,12},{12,0},{16,20},{20,24},{24,28},{28,16}} | collective-permute-start | bytes 786440 | tf_op jit(solution)/shard_map/ppermute | solution.py:119
  10.5 3.9 %collective-permute-start.1 = (bf16[2,128,512]{1,2,0:T(8,128)(2,1)}, bf16[2,128,512]{1,2,0:T(8,128)(2,1)}, u32[]{:S(2)}, u32[]{:S(2)}) collective-permute-start(bf16[2,128,512]{1,2,0:T(8,128)(2,1)} %bitcast.4), channel_id=1, source_target_pairs={{0,12},{4,0},{8,4},{12,8},{16,28},{20,16},{24,20},{28,24}} | collective-permute-start | bytes 786440 | tf_op jit(solution)/shard_map/ppermute | solution.py:120
  15.1 1.5 fusion.131
  17.4 1.6 collective-permute-done.1
  19.1 1.8 convolution_bitcast_fusion.7
  27.1 2.5 %collective-permute-done.3 = bf16[2,128,512]{2,1,0:T(8,128)(2,1)S(1)} collective-permute-done((bf16[2,128,512]{2,1,0:T(8,128)(2,1)S(1)}, bf16[2,128,512]{2,1,0:T(8,128)(2,1)S(1)}, u32[]{:S(2)}, u32[]{:S(2)}) %collective-permute-start.3) | collective-permute-done | bytes 262176 | tf_op jit(solution)/shard_map/ppermute | solution.py:131
  29.6 2.9 %collective-permute-done.4 = bf16[2,128,512]{2,1,0:T(8,128)(2,1)S(1)} collective-permute-done((bf16[2,128,512]{2,1,0:T(8,128)(2,1)S(1)}, bf16[2,128,512]{2,1,0:T(8,128)(2,1)S(1)}, u32[]{:S(2)}, u32[]{:S(2)}) %collective-permute-start.4) | collective-permute-done | bytes 262176 | tf_op jit(solution)/shard_map/ppermute | solution.py:132
  66.9 1.5 collective-permute-start.19
  68.4 48.8 %collective-permute-done.18 = bf16[2,128,512]{2,1,0:T(8,128)(2,1)} collective-permute-done((bf16[2,128,512]{2,1,0:T(8,128)(2,1)}, bf16[2,128,512]{2,1,0:T(8,128)(2,1)}, u32[]{:S(2)}, u32[]{:S(2)}) %collective-permute-start.18) | collective-permute-done | bytes 262176 | tf_op jit(solution)/shard_map/ppermute | solution.py:175
  118.3 3.6 %collective-permute-done.19 = bf16[2,128,512]{2,1,0:T(8,128)(2,1)} collective-permute-done((bf16[2,128,512]{2,1,0:T(8,128)(2,1)}, bf16[2,128,512]{2,1,0:T(8,128)(2,1)}, u32[]{:S(2)}, u32[]{:S(2)}) %collective-permute-start.19) | collective-permute-done | bytes 262176 | tf_op jit(solution)/shard_map/ppermute | solution.py:176
  122.9 1.9 %fusion.47 = (bf16[512]{0:T(512)(128)(2,1)S(1)}, f32[2,256]{1,0:T(2,128)S(1)}, f32[2,256]{1,0:T(2,128)S(1)}, bf16[2,256,512]{2,1,0:T(8,128)(2,1)S(1)}) fusion(f32[2,256,512]{2,1,0:T(8,128)S(1)} %get-tuple-element.41, f32[2,256]{1,0:T(2,128)S(1)} %add_rsqrt_fusion.3, f32[2,256]{1,0:T(2,128)S(1)} %broadcast_multiply_fusion.11, f32[512]{0:T(512)S(1)} %bitcast.278, ...), kind=kLoop, calls=%fused_computation.85 | loop fusion | flops 3930624 | bytes 3157504 | tf_op jit(solution)/shard_map/reduce_sum | solution.py:142
  126.4 1.4 fusion.23
  127.9 4.5 %select_select_fusion = bf16[2,256,512]{2,1,0:T(8,128)(2,1)S(1)} fusion(pred[]{:T(512)S(6)} %select_n.329, pred[]{:T(512)S(6)} %select_n.326, pred[]{:T(512)S(6)} %select_n.324, f32[2,512,512]{2,1,0:T(8,128)} %copy-done.20, f32[2,512,512]{2,1,0:T(8,128)} %copy-done.19, f32[2,512,512]{2,1,0:T(8,128)} %copy-done.18, f32[2,512,512]{2,1,0:T(8,128)} %copy-done.17), kind=kLoop, calls=%fused_computation.224 | loop fusion | flops 2883584 | bytes 8912899 | tf_op jit(solution)/shard_map/select_n | solution.py:193
  138.2 1.7 copy-done.2
  143.1 3.5 %fusion.209 = (bf16[2,512,512]{2,1,0:T(8,128)(2,1)S(1)}, f32[2,512,512]{2,1,0:T(8,128)}) fusion(bf16[256,512]{1,0:T(8,128)(2,1)S(1)} %copy-done.16, bf16[256,512]{1,0:T(8,128)(2,1)S(1)} %bitcast.260, bf16[2,256,512]{1,2,0:T(8,128)(2,1)} %convolution_convert_fusion), kind=kOutput, calls=%fused_computation.315 | convolution fusion | flops 540540928 | bytes 4194304 | tf_op jit(solution)/shard_map/ij,sid->sjd/dot_general | solution.py:157
  147.4 3.0 %collective-permute-start.21 = (bf16[2,128,512]{2,1,0:T(8,128)(2,1)}, bf16[2,128,512]{2,1,0:T(8,128)(2,1)}, u32[]{:S(2)}, u32[]{:S(2)}) collective-permute-start(bf16[2,128,512]{2,1,0:T(8,128)(2,1)} %get-tuple-element.23), channel_id=1, source_target_pairs={{0,4},{4,8},{8,12},{12,0},{16,20},{20,24},{24,28},{28,16}} | collective-permute-start | bytes 786440 | tf_op jit(solution)/shard_map/ppermute | solution.py:184
  150.4 4.6 %collective-permute-start.20 = (bf16[2,128,512]{2,1,0:T(8,128)(2,1)}, bf16[2,128,512]{2,1,0:T(8,128)(2,1)}, u32[]{:S(2)}, u32[]{:S(2)}) collective-permute-start(bf16[2,128,512]{2,1,0:T(8,128)(2,1)} %get-tuple-element.22), channel_id=1, source_target_pairs={{0,12},{4,0},{8,4},{12,8},{16,28},{20,16},{24,20},{28,24}} | collective-permute-start | bytes 786440 | tf_op jit(solution)/shard_map/ppermute | solution.py:183
  156.0 2.1 %collective-permute-start.22 = (bf16[2,256,512]{2,1,0:T(8,128)(2,1)}, bf16[2,256,512]{2,1,0:T(8,128)(2,1)}, u32[]{:S(2)}, u32[]{:S(2)}) collective-permute-start(bf16[2,256,512]{2,1,0:T(8,128)(2,1)} %select_select_fusion.2), channel_id=1, source_target_pairs={{0,1},{1,2},{2,3},{4,5},{5,6},{6,7},{8,9},{9,10},{10,11},{12,13},{... | collective-permute-start | bytes 1572872 | tf_op jit(solution)/shard_map/ppermute | solution.py:232
  158.1 1.8 collective-permute-done.23
  159.9 1.6 fusion
  162.3 2.2 %collective-permute-start.24 = (bf16[1,400,512]{2,1,0:T(8,128)(2,1)}, bf16[1,400,512]{2,1,0:T(8,128)(2,1)}, u32[]{:S(2)}, u32[]{:S(2)}) collective-permute-start(bf16[1,400,512]{2,1,0:T(8,128)(2,1)} %fusion.161), channel_id=1, source_target_pairs={{0,8},{4,12},{8,0},{12,4},{1,9},{5,13},{9,1},{13,5},{2,10},{6,14},... | collective-permute-start | bytes 1228808 | tf_op jit(solution)/shard_map/ppermute | solution.py:41
  165.8 1.4 collective-permute-done.20
  168.4 1.4 fusion.27
  169.8 12.1 %collective-permute-done.24 = bf16[1,400,512]{2,1,0:T(8,128)(2,1)} collective-permute-done((bf16[1,400,512]{2,1,0:T(8,128)(2,1)}, bf16[1,400,512]{2,1,0:T(8,128)(2,1)}, u32[]{:S(2)}, u32[]{:S(2)}) %collective-permute-start.24) | collective-permute-done | bytes 409632 | tf_op jit(solution)/shard_map/ppermute | solution.py:41
  (263 shorter events, 64.8 us)
Async XLA Ops:
  4.6 12.8 %collective-permute-start = (bf16[2,128,512]{1,2,0:T(8,128)(2,1)S(1)}, bf16[2,128,512]{1,2,0:T(8,128)(2,1)}, u32[]{:S(2)}, u32[]{:S(2)}) collective-permute-start(bf16[2,128,512]{1,2,0:T(8,128)(2,1)S(1)} %bitcast.282), channel_id=1, source_target_pairs={{0,4},{4,8},{8,12},{12,0},{16,20},{20,24},{24,28},{28,16}} | collective-permute-start | bytes 786440 | tf_op jit(solution)/shard_map/ppermute | solution.py:119
  10.5 8.6 %collective-permute-start.1 = (bf16[2,128,512]{1,2,0:T(8,128)(2,1)}, bf16[2,128,512]{1,2,0:T(8,128)(2,1)}, u32[]{:S(2)}, u32[]{:S(2)}) collective-permute-start(bf16[2,128,512]{1,2,0:T(8,128)(2,1)} %bitcast.4), channel_id=1, source_target_pairs={{0,12},{4,0},{8,4},{12,8},{16,28},{20,16},{24,20},{28,24}} | collective-permute-start | bytes 786440 | tf_op jit(solution)/shard_map/ppermute | solution.py:120
  23.0 9.4 %collective-permute-start.2 = (bf16[2,256,512]{2,1,0:T(8,128)(2,1)S(1)}, bf16[2,256,512]{2,1,0:T(8,128)(2,1)S(1)}, u32[]{:S(2)}, u32[]{:S(2)}) collective-permute-start(bf16[2,256,512]{2,1,0:T(8,128)(2,1)S(1)} %add_convert_fusion.3), channel_id=1, source_target_pairs={{0,1},{4,5},{8,9},{12,13},{16,17},{20,21},{24,25},{28,29}} | collective-permute-start | bytes 1572872 | tf_op jit(solution)/shard_map/ppermute | solution.py:130
  24.4 5.2 %collective-permute-start.3 = (bf16[2,128,512]{2,1,0:T(8,128)(2,1)S(1)}, bf16[2,128,512]{2,1,0:T(8,128)(2,1)S(1)}, u32[]{:S(2)}, u32[]{:S(2)}) collective-permute-start(bf16[2,128,512]{2,1,0:T(8,128)(2,1)S(1)} %get-tuple-element.36), channel_id=1, source_target_pairs={{0,5},{4,9},{8,13},{12,1},{16,21},{20,25},{24,29},{28,17}} | collective-permute-start | bytes 786440 | tf_op jit(solution)/shard_map/ppermute | solution.py:131
  25.7 6.7 %collective-permute-start.4 = (bf16[2,128,512]{2,1,0:T(8,128)(2,1)S(1)}, bf16[2,128,512]{2,1,0:T(8,128)(2,1)S(1)}, u32[]{:S(2)}, u32[]{:S(2)}) collective-permute-start(bf16[2,128,512]{2,1,0:T(8,128)(2,1)S(1)} %get-tuple-element.37), channel_id=1, source_target_pairs={{0,13},{4,1},{8,5},{12,9},{16,29},{20,17},{24,21},{28,25}} | collective-permute-start | bytes 786440 | tf_op jit(solution)/shard_map/ppermute | solution.py:132
  35.6 2.2 %collective-permute-start.5 = (bf16[2,256,512]{2,1,0:T(8,128)(2,1)S(1)}, bf16[2,256,512]{2,1,0:T(8,128)(2,1)S(1)}, u32[]{:S(2)}, u32[]{:S(2)}) collective-permute-start(bf16[2,256,512]{2,1,0:T(8,128)(2,1)S(1)} %add_convert_fusion.2), channel_id=1, source_target_pairs={{1,2},{5,6},{9,10},{13,14},{17,18},{21,22},{25,26},{29,30}} | collective-permute-start | bytes 1572872 | tf_op jit(solution)/shard_map/ppermute | solution.py:130
  36.4 1.4 collective-permute-start.6
  41.0 2.4 %collective-permute-start.8 = (bf16[2,256,512]{2,1,0:T(8,128)(2,1)S(1)}, bf16[2,256,512]{2,1,0:T(8,128)(2,1)S(1)}, u32[]{:S(2)}, u32[]{:S(2)}) collective-permute-start(bf16[2,256,512]{2,1,0:T(8,128)(2,1)S(1)} %add_convert_fusion.1), channel_id=1, source_target_pairs={{2,3},{6,7},{10,11},{14,15},{18,19},{22,23},{26,27},{30,31}} | collective-permute-start | bytes 1572872 | tf_op jit(solution)/shard_map/ppermute | solution.py:130
  41.8 1.6 collective-permute-start.10
  42.5 1.0 collective-permute-start.9
  50.5 2.3 %collective-permute-start.11 = (bf16[2,256,512]{2,1,0:T(8,128)(2,1)S(1)}, bf16[2,256,512]{2,1,0:T(8,128)(2,1)S(1)}, u32[]{:S(2)}, u32[]{:S(2)}) collective-permute-start(bf16[2,256,512]{2,1,0:T(8,128)(2,1)S(1)} %fusion.20), channel_id=1, source_target_pairs={{3,2},{7,6},{11,10},{15,14},{19,18},{23,22},{27,26},{31,30}} | collective-permute-start | bytes 1572872 | tf_op jit(solution)/shard_map/ppermute | solution.py:174
  51.3 1.5 collective-permute-start.12
  52.0 0.8 collective-permute-start.13
  56.7 2.3 %collective-permute-start.14 = (bf16[2,256,512]{2,1,0:T(8,128)(2,1)S(1)}, bf16[2,256,512]{2,1,0:T(8,128)(2,1)S(1)}, u32[]{:S(2)}, u32[]{:S(2)}) collective-permute-start(bf16[2,256,512]{2,1,0:T(8,128)(2,1)S(1)} %fusion.21), channel_id=1, source_target_pairs={{2,1},{6,5},{10,9},{14,13},{18,17},{22,21},{26,25},{30,29}} | collective-permute-start | bytes 1572872 | tf_op jit(solution)/shard_map/ppermute | solution.py:174
  57.4 1.4 collective-permute-start.15
  58.1 0.8 collective-permute-start.16
  63.5 59.4 %collective-permute-start.17 = (bf16[2,256,512]{2,1,0:T(8,128)(2,1)}, bf16[2,256,512]{2,1,0:T(8,128)(2,1)}, u32[]{:S(2)}, u32[]{:S(2)}) collective-permute-start(bf16[2,256,512]{2,1,0:T(8,128)(2,1)} %fusion.22), channel_id=1, source_target_pairs={{1,0},{5,4},{9,8},{13,12},{17,16},{21,20},{25,24},{29,28}} | collective-permute-start | bytes 1572872 | tf_op jit(solution)/shard_map/ppermute | solution.py:174
  65.6 51.7 %collective-permute-start.18 = (bf16[2,128,512]{2,1,0:T(8,128)(2,1)}, bf16[2,128,512]{2,1,0:T(8,128)(2,1)}, u32[]{:S(2)}, u32[]{:S(2)}) collective-permute-start(bf16[2,128,512]{2,1,0:T(8,128)(2,1)} %get-tuple-element.24), channel_id=1, source_target_pairs={{1,12},{5,0},{9,4},{13,8},{17,28},{21,16},{25,20},{29,24}} | collective-permute-start | bytes 786440 | tf_op jit(solution)/shard_map/ppermute | solution.py:175
  66.9 55.0 %collective-permute-start.19 = (bf16[2,128,512]{2,1,0:T(8,128)(2,1)}, bf16[2,128,512]{2,1,0:T(8,128)(2,1)}, u32[]{:S(2)}, u32[]{:S(2)}) collective-permute-start(bf16[2,128,512]{2,1,0:T(8,128)(2,1)} %get-tuple-element.25), channel_id=1, source_target_pairs={{1,4},{5,8},{9,12},{13,0},{17,20},{21,24},{25,28},{29,16}} | collective-permute-start | bytes 786440 | tf_op jit(solution)/shard_map/ppermute | solution.py:176
  140.9 19.0 %collective-permute-start.23 = (bf16[2,400,512]{2,1,0:T(8,128)(2,1)}, bf16[2,400,512]{2,1,0:T(8,128)(2,1)}, u32[]{:S(2)}, u32[]{:S(2)}) collective-permute-start(bf16[2,400,512]{2,1,0:T(8,128)(2,1)} %fusion.96), channel_id=1, source_target_pairs={{0,4},{4,0},{8,12},{12,8},{1,5},{5,1},{9,13},{13,9},{2,6},{6,2},{1... | collective-permute-start | bytes 2457608 | tf_op jit(solution)/shard_map/ppermute | solution.py:41
  147.4 17.2 %collective-permute-start.21 = (bf16[2,128,512]{2,1,0:T(8,128)(2,1)}, bf16[2,128,512]{2,1,0:T(8,128)(2,1)}, u32[]{:S(2)}, u32[]{:S(2)}) collective-permute-start(bf16[2,128,512]{2,1,0:T(8,128)(2,1)} %get-tuple-element.23), channel_id=1, source_target_pairs={{0,4},{4,8},{8,12},{12,0},{16,20},{20,24},{24,28},{28,16}} | collective-permute-start | bytes 786440 | tf_op jit(solution)/shard_map/ppermute | solution.py:184
  150.4 16.7 %collective-permute-start.20 = (bf16[2,128,512]{2,1,0:T(8,128)(2,1)}, bf16[2,128,512]{2,1,0:T(8,128)(2,1)}, u32[]{:S(2)}, u32[]{:S(2)}) collective-permute-start(bf16[2,128,512]{2,1,0:T(8,128)(2,1)} %get-tuple-element.22), channel_id=1, source_target_pairs={{0,12},{4,0},{8,4},{12,8},{16,28},{20,16},{24,20},{28,24}} | collective-permute-start | bytes 786440 | tf_op jit(solution)/shard_map/ppermute | solution.py:183
  156.0 12.3 %collective-permute-start.22 = (bf16[2,256,512]{2,1,0:T(8,128)(2,1)}, bf16[2,256,512]{2,1,0:T(8,128)(2,1)}, u32[]{:S(2)}, u32[]{:S(2)}) collective-permute-start(bf16[2,256,512]{2,1,0:T(8,128)(2,1)} %select_select_fusion.2), channel_id=1, source_target_pairs={{0,1},{1,2},{2,3},{4,5},{5,6},{6,7},{8,9},{9,10},{10,11},{12,13},{... | collective-permute-start | bytes 1572872 | tf_op jit(solution)/shard_map/ppermute | solution.py:232
  162.3 19.7 %collective-permute-start.24 = (bf16[1,400,512]{2,1,0:T(8,128)(2,1)}, bf16[1,400,512]{2,1,0:T(8,128)(2,1)}, u32[]{:S(2)}, u32[]{:S(2)}) collective-permute-start(bf16[1,400,512]{2,1,0:T(8,128)(2,1)} %fusion.161), channel_id=1, source_target_pairs={{0,8},{4,12},{8,0},{12,4},{1,9},{5,13},{9,1},{13,5},{2,10},{6,14},... | collective-permute-start | bytes 1228808 | tf_op jit(solution)/shard_map/ppermute | solution.py:41
  (64 other events, 296.5 us)

commit v11 on v9

--- a/solution.py
+++ b/solution.py
@@ -85,8 +85,7 @@
     adj_lo = (adj - adj_hi.astype(F32)).astype(BF16)
     adj2 = jnp.concatenate([adj_hi, adj_lo], axis=0)
 
-    w_a = w_one[0, :width]
-    w_b = w_one[0, width:]
+    w_full = w_one[0]
     w_2 = w_two[0]
     gain_row = gain[0]
 
@@ -105,8 +104,8 @@
         h_ext = jnp.concatenate([left, h, right], axis=1)
         agg2 = jnp.einsum("ij,sjd->sid", adj2, h_ext, preferred_element_type=F32)
         agg = (agg2[:, : nb * blk] + agg2[:, nb * blk :]).astype(BF16)
-        pre = jnp.einsum("sic,ct->sit", h, w_a, preferred_element_type=F32)
-        pre = pre + jnp.einsum("sic,ct->sit", agg, w_b, preferred_element_type=F32)
+        pre = jnp.einsum("sic,ct->sit", h, w_full[:width], preferred_element_type=F32)
+        pre = pre + jnp.einsum("sic,ct->sit", agg, w_full[width:], preferred_element_type=F32)
         act = jax.nn.silu(pre).astype(BF16)
         mixed = jnp.einsum("sic,ct->sit", act, w_2, preferred_element_type=F32)
         center = mixed - jnp.mean(mixed, axis=-1, keepdims=True)
@@ -152,8 +151,9 @@
         dact = jnp.einsum("sip,vp->siv", dout, w_2, preferred_element_type=F32)
         sig = jax.nn.sigmoid(pre_t)
         dpre = (dact * sig * (1.0 + pre_t * (1.0 - sig))).astype(BF16)
-        gnode = gf + jnp.einsum("sip,vp->siv", dpre, w_a, preferred_element_type=F32)
-        dagg = jnp.einsum("sip,vp->siv", dpre, w_b, preferred_element_type=F32).astype(BF16)
+        both_grads = jnp.einsum("sip,vp->siv", dpre, w_full, preferred_element_type=F32)
+        gnode = gf + both_grads[:, :, :width]
+        dagg = both_grads[:, :, width:].astype(BF16)
         spread = jnp.einsum(
             "ij,sid->sjd", adj2, jnp.concatenate([dagg, dagg], axis=1), preferred_element_type=F32
         )

time: 184 us -> 194 us (1.054)
  local copies, waits for them, and re-layouts: 13.6 us -> 18.7 us
  other arithmetic: 24.3 us -> 28.9 us
  matrix products: 28.3 us -> 26 us
    ppermute x3, waiting for transfers between devices: 39.9 us -> 2.65 us  [shards(): lax.ppermute(left_grad, both, route(active, active - 1, -1))]
    ppermute x3, waiting for transfers between devices: 4.39 us -> 38.9 us  [shards(): lax.ppermute(right_grad, both, route(active, active - 1, 1))]
    ppermute x1, waiting for transfers between devices: 1.14 us -> 7.43 us  [shards(): lax.ppermute(left_grad, both, route(active, active, -1))]
    ppermute x2, waiting for transfers between devices: 15.2 us -> 9.25 us  [halving_reduce_scatter(): recv = lax.ppermute(send, axis, pairs)]
    ppermute x1, waiting for transfers between devices: 0.01 us -> 5.62 us  [shards(): lax.ppermute(pick_blocks(in_blocks, send_right, hs), both, route(0, 0, 1))]
    unnamed x115 -> x129, local copies, waits for them, and re-layouts: 6.56 us -> 10.2 us
    ppermute x1, starting transfers between devices: 4.96 us -> 1.91 us  [shards(): lax.ppermute(pick_blocks(in_blocks, send_right, hs), both, route(0, 0, 1))]
    ppermute x1, starting transfers between devices: 3.89 us -> 6.93 us  [shards(): lax.ppermute(pick_blocks(in_blocks, send_left, hs), both, route(0, 0, -1))]
  transfers between devices with their start and end apart: 25 -> 25, of which waited for: 9 -> 8; matrix products, arithmetic and copies ran while one was open for 11% -> 13% of each run, Pallas kernels for 0% -> 0%
where the time goes in v11:
time: 194 us; the launch traced here: 193 us
  waiting for transfers between devices  73.9 us (38%)
  starting transfers between devices  41.6 us (21%)
  other arithmetic  28.9 us (15%)
  matrix products  26 us (13%)
  local copies, waits for them, and re-layouts  18.7 us (10%)
  between operations  3.99 us (2%)
    ppermute x3, waiting for transfers between devices, shards(): lax.ppermute(right_grad, both, route(active, active - 1, 1))  38.9 us
    unnamed x129, local copies, waits for them, and re-layouts  10.2 us
    ppermute x2, waiting for transfers between devices, halving_reduce_scatter(): recv = lax.ppermute(send, axis, pairs)  9.25 us
    ppermute x1, waiting for transfers between devices, shards(): lax.ppermute(left_grad, both, route(active, active, -1))  7.43 us
    ppermute x1, starting transfers between devices, shards(): lax.ppermute(pick_blocks(in_blocks, send_left, hs), both, route(0, 0, -1))  6.93 us
    select_n x2, other arithmetic, own_forward(): return lax.select_n(section_index, *[r[i] for r in res_list])  6.01 us
    ppermute x1, waiting for transfers between devices, shards(): lax.ppermute(pick_blocks(in_blocks, send_right, hs), both, route(0, 0, 1))  5.62 us
    dot_general x4, matrix products, forward_layer(): agg2 = jnp.einsum('ij,sjd->sid', adj2, h_ext, preferred_element_type=F32)  5.31 us
  transfers between devices with their start and end apart: 25, of which 8 were waited for; matrix products, arithmetic and copies ran while one was open for 13% of the time, Pallas kernels for 0%

profile of v11, /device:TPU:0, one launch (start us, length us, event | category | flops | bytes accessed | tf_op | source)
XLA Modules:
  0.0 193.2 jit_solution(2581283164940338989)
XLA Ops:
  5.4 6.9 %collective-permute-start.1 = (bf16[2,128,512]{1,2,0:T(8,128)(2,1)}, bf16[2,128,512]{1,2,0:T(8,128)(2,1)}, u32[]{:S(2)}, u32[]{:S(2)}) collective-permute-start(bf16[2,128,512]{1,2,0:T(8,128)(2,1)} %bitcast.4), channel_id=1, source_target_pairs={{0,12},{4,0},{8,4},{12,8},{16,28},{20,16},{24,20},{28,24}} | collective-permute-start | bytes 786440 | tf_op jit(solution)/shard_map/ppermute | solution.py:119
  13.2 1.9 collective-permute-start
  17.9 5.6 %collective-permute-done = bf16[2,128,512]{1,2,0:T(8,128)(2,1)} collective-permute-done((bf16[2,128,512]{1,2,0:T(8,128)(2,1)}, bf16[2,128,512]{1,2,0:T(8,128)(2,1)}, u32[]{:S(2)}, u32[]{:S(2)}) %collective-permute-start) | collective-permute-done | bytes 262176 | tf_op jit(solution)/shard_map/ppermute | solution.py:118
  23.6 1.8 convolution_bitcast_fusion.7
  31.7 2.6 %collective-permute-done.4 = bf16[2,128,512]{2,1,0:T(8,128)(2,1)S(1)} collective-permute-done((bf16[2,128,512]{2,1,0:T(8,128)(2,1)S(1)}, bf16[2,128,512]{2,1,0:T(8,128)(2,1)S(1)}, u32[]{:S(2)}, u32[]{:S(2)}) %collective-permute-start.4) | collective-permute-done | bytes 262176 | tf_op jit(solution)/shard_map/ppermute | solution.py:131
  34.3 2.8 %collective-permute-done.3 = bf16[2,128,512]{2,1,0:T(8,128)(2,1)S(1)} collective-permute-done((bf16[2,128,512]{2,1,0:T(8,128)(2,1)S(1)}, bf16[2,128,512]{2,1,0:T(8,128)(2,1)S(1)}, u32[]{:S(2)}, u32[]{:S(2)}) %collective-permute-start.3) | collective-permute-done | bytes 262176 | tf_op jit(solution)/shard_map/ppermute | solution.py:130
  48.4 1.9 dynamic-slice_bitcast_fusion.1
  53.2 2.1 %convolution_bitcast_fusion = f32[2,512,512]{2,1,0:T(8,128)S(1)} fusion(bf16[2,128,512]{2,1,0:T(8,128)(2,1)} %collective-permute-done.10, bf16[2,256,512]{2,1,0:T(8,128)(2,1)} %collective-permute-done.8, bf16[2,128,512]{2,1,0:T(8,128)(2,1)} %collective-permute-done.9, bf16[256,512]{1,0:T(8,128)(2,1)S(1)} %fusion.108, bf16[256,512]{1,0:T(8,128)(2,1)} %bitcast.278), kind=kOutput, calls=%fused_computation.6 | convolution fusion | flops 541065216 | bytes 3670016 | tf_op jit(solution)/shard_map/ij,sjd->sid/dot_general | solution.py:105
  55.7 3.3 %select_select_fusion = (bf16[2,256,512]{2,1,0:T(8,128)(2,1)}, bf16[2,256,512]{2,1,0:T(8,128)(2,1)S(1)}) fusion(pred[]{:T(512)S(6)} %select_n.323, pred[]{:T(512)S(6)} %select_n.314, pred[]{:T(512)S(6)} %select_n.312, f32[2,512,512]{2,1,0:T(8,128)S(1)} %convolution_bitcast_fusion, f32[2,512,512]{2,1,0:T(8,128)} %copy-done.19, ...), kind=kLoop, calls=%fused_computation.223 | loop fusion | flops 2883584 | bytes 9437187 | tf_op jit(solution)/shard_map/select_n | solution.py:191
  81.5 1.9 fusion.40
  90.7 2.7 %select_select_fusion.1 = (bf16[2,256,512]{2,1,0:T(8,128)(2,1)S(1)}, bf16[1,2,256,512]{3,2,1,0:T(8,128)(2,1)}) fusion(bf16[2,256,512]{2,1,0:T(8,128)(2,1)S(1)} %copy-done.28, bf16[2,256,512]{2,1,0:T(8,128)(2,1)} %collective-permute-done.8, bf16[2,256,512]{2,1,0:T(8,128)(2,1)S(1)} %copy-done.10, bf16[2,256,512]{2,1,0:T(8,128)(2,1)S(1)} %copy-done.26, ...), kind=kLoop, calls=%fused_computation.224 | loop fusion | flops 3145728 | bytes 5773315 | tf_op jit(solution)/shard_map/select_n | solution.py:191
  93.4 38.9 %collective-permute-done.19 = bf16[2,128,512]{2,1,0:T(8,128)(2,1)S(1)} collective-permute-done((bf16[2,128,512]{2,1,0:T(8,128)(2,1)S(1)}, bf16[2,128,512]{2,1,0:T(8,128)(2,1)S(1)}, u32[]{:S(2)}, u32[]{:S(2)}) %collective-permute-start.19) | collective-permute-done | bytes 262176 | tf_op jit(solution)/shard_map/ppermute | solution.py:176
  132.3 2.6 %collective-permute-done.18 = bf16[2,128,512]{2,1,0:T(8,128)(2,1)S(1)} collective-permute-done((bf16[2,128,512]{2,1,0:T(8,128)(2,1)S(1)}, bf16[2,128,512]{2,1,0:T(8,128)(2,1)S(1)}, u32[]{:S(2)}, u32[]{:S(2)}) %collective-permute-start.18) | collective-permute-done | bytes 262176 | tf_op jit(solution)/shard_map/ppermute | solution.py:175
  140.9 1.7 copy-done.2
  145.1 2.2 %collective-permute-start.22 = (bf16[2,256,512]{2,1,0:T(8,128)(2,1)}, bf16[2,256,512]{2,1,0:T(8,128)(2,1)}, u32[]{:S(2)}, u32[]{:S(2)}) collective-permute-start(bf16[2,256,512]{2,1,0:T(8,128)(2,1)} %select_select_fusion.2), channel_id=1, source_target_pairs={{0,1},{1,2},{2,3},{4,5},{5,6},{6,7},{8,9},{9,10},{10,11},{12,13},{... | collective-permute-start | bytes 1572872 | tf_op jit(solution)/shard_map/ppermute | solution.py:230
  147.3 2.1 %fusion.94 = f32[2,256,1024]{2,1,0:T(8,128)} fusion(bf16[2,256,512]{2,1,0:T(8,128)(2,1)S(1)} %copy-done.49, bf16[1,1024,512]{2,1,0:T(8,128)(2,1)S(1)} %copy-done.1), kind=kOutput, calls=%fused_computation.144 | convolution fusion | flops 536870912 | bytes 3670016 | tf_op jit(solution)/shard_map/sip,vp->siv/dot_general | solution.py:154
  150.8 2.1 %fusion.201 = (bf16[2,512,512]{2,1,0:T(8,128)(2,1)S(1)}, f32[2,512,512]{2,1,0:T(8,128)}) fusion(bf16[256,512]{1,0:T(8,128)(2,1)S(1)} %fusion.108, bf16[256,512]{1,0:T(8,128)(2,1)S(1)} %bitcast.282, bf16[2,256,512]{2,1,0:T(8,128)(2,1)S(1)} %slice.291), kind=kOutput, calls=%fused_computation.306 | convolution fusion | flops 540540928 | bytes 4194304 | tf_op jit(solution)/shard_map/ij,sid->sjd/dot_general | solution.py:157
  152.8 9.2 %collective-permute-done.23 = bf16[2,400,512]{2,1,0:T(8,128)(2,1)} collective-permute-done((bf16[2,400,512]{2,1,0:T(8,128)(2,1)}, bf16[2,400,512]{2,1,0:T(8,128)(2,1)}, u32[]{:S(2)}, u32[]{:S(2)}) %collective-permute-start.23) | collective-permute-done | bytes 819232 | tf_op jit(solution)/shard_map/ppermute | solution.py:41
  163.8 1.8 collective-permute-start.24
  166.4 2.5 %collective-permute-start.21 = (bf16[2,128,512]{2,1,0:T(8,128)(2,1)}, bf16[2,128,512]{2,1,0:T(8,128)(2,1)}, u32[]{:S(2)}, u32[]{:S(2)}) collective-permute-start(bf16[2,128,512]{2,1,0:T(8,128)(2,1)} %get-tuple-element.23), channel_id=1, source_target_pairs={{0,4},{4,8},{8,12},{12,0},{16,20},{20,24},{24,28},{28,16}} | collective-permute-start | bytes 786440 | tf_op jit(solution)/shard_map/ppermute | solution.py:184
  168.9 5.1 %collective-permute-start.20 = (bf16[2,128,512]{2,1,0:T(8,128)(2,1)}, bf16[2,128,512]{2,1,0:T(8,128)(2,1)}, u32[]{:S(2)}, u32[]{:S(2)}) collective-permute-start(bf16[2,128,512]{2,1,0:T(8,128)(2,1)} %get-tuple-element.22), channel_id=1, source_target_pairs={{0,12},{4,0},{8,4},{12,8},{16,28},{20,16},{24,20},{28,24}} | collective-permute-start | bytes 786440 | tf_op jit(solution)/shard_map/ppermute | solution.py:183
  174.0 4.6 %collective-permute-done.21 = bf16[2,128,512]{2,1,0:T(8,128)(2,1)} collective-permute-done((bf16[2,128,512]{2,1,0:T(8,128)(2,1)}, bf16[2,128,512]{2,1,0:T(8,128)(2,1)}, u32[]{:S(2)}, u32[]{:S(2)}) %collective-permute-start.21) | collective-permute-done | bytes 262176 | tf_op jit(solution)/shard_map/ppermute | solution.py:184
  179.6 7.4 %collective-permute-done.20 = bf16[2,128,512]{2,1,0:T(8,128)(2,1)} collective-permute-done((bf16[2,128,512]{2,1,0:T(8,128)(2,1)}, bf16[2,128,512]{2,1,0:T(8,128)(2,1)}, u32[]{:S(2)}, u32[]{:S(2)}) %collective-permute-start.20) | collective-permute-done | bytes 262176 | tf_op jit(solution)/shard_map/ppermute | solution.py:183
  188.1 2.8 %fusion.107 = bf16[2,256,512]{2,1,0:T(8,128)(2,1)} fusion(bf16[2,256,512]{2,1,0:T(8,128)(2,1)} %collective-permute-done.22, f32[2,512,512]{2,1,0:T(8,128)} %get-tuple-element.55, f32[2,256,1024]{2,1,0:T(8,128)} %fusion.94, bf16[2,256,512]{2,1,0:T(8,128)(2,1)S(1)} %get-tuple-element.19, f32[2,128,512]{2,1,0:T(8,128)S(1)} %convert_element_type.269, ...), kind=kLoop, calls=%fused_computation.182 | loop fusion | flops 2359296 | bytes 4719105 | tf_op jit(solution)/shard_map/jit(_where)/select_n | solution.py:231
  (263 shorter events, 72.6 us)
Async XLA Ops:
  5.4 12.5 %collective-permute-start.1 = (bf16[2,128,512]{1,2,0:T(8,128)(2,1)}, bf16[2,128,512]{1,2,0:T(8,128)(2,1)}, u32[]{:S(2)}, u32[]{:S(2)}) collective-permute-start(bf16[2,128,512]{1,2,0:T(8,128)(2,1)} %bitcast.4), channel_id=1, source_target_pairs={{0,12},{4,0},{8,4},{12,8},{16,28},{20,16},{24,20},{28,24}} | collective-permute-start | bytes 786440 | tf_op jit(solution)/shard_map/ppermute | solution.py:119
  13.2 10.4 %collective-permute-start = (bf16[2,128,512]{1,2,0:T(8,128)(2,1)}, bf16[2,128,512]{1,2,0:T(8,128)(2,1)}, u32[]{:S(2)}, u32[]{:S(2)}) collective-permute-start(bf16[2,128,512]{1,2,0:T(8,128)(2,1)} %bitcast.3), channel_id=1, source_target_pairs={{0,4},{4,8},{8,12},{12,0},{16,20},{20,24},{24,28},{28,16}} | collective-permute-start | bytes 786440 | tf_op jit(solution)/shard_map/ppermute | solution.py:118
  27.7 9.4 %collective-permute-start.2 = (bf16[2,256,512]{2,1,0:T(8,128)(2,1)S(1)}, bf16[2,256,512]{2,1,0:T(8,128)(2,1)S(1)}, u32[]{:S(2)}, u32[]{:S(2)}) collective-permute-start(bf16[2,256,512]{2,1,0:T(8,128)(2,1)S(1)} %add_convert_fusion.3), channel_id=1, source_target_pairs={{0,1},{4,5},{8,9},{12,13},{16,17},{20,21},{24,25},{28,29}} | collective-permute-start | bytes 1572872 | tf_op jit(solution)/shard_map/ppermute | solution.py:129
  29.1 5.2 %collective-permute-start.4 = (bf16[2,128,512]{2,1,0:T(8,128)(2,1)S(1)}, bf16[2,128,512]{2,1,0:T(8,128)(2,1)S(1)}, u32[]{:S(2)}, u32[]{:S(2)}) collective-permute-start(bf16[2,128,512]{2,1,0:T(8,128)(2,1)S(1)} %get-tuple-element.37), channel_id=1, source_target_pairs={{0,13},{4,1},{8,5},{12,9},{16,29},{20,17},{24,21},{28,25}} | collective-permute-start | bytes 786440 | tf_op jit(solution)/shard_map/ppermute | solution.py:131
  30.4 6.7 %collective-permute-start.3 = (bf16[2,128,512]{2,1,0:T(8,128)(2,1)S(1)}, bf16[2,128,512]{2,1,0:T(8,128)(2,1)S(1)}, u32[]{:S(2)}, u32[]{:S(2)}) collective-permute-start(bf16[2,128,512]{2,1,0:T(8,128)(2,1)S(1)} %get-tuple-element.36), channel_id=1, source_target_pairs={{0,5},{4,9},{8,13},{12,1},{16,21},{20,25},{24,29},{28,17}} | collective-permute-start | bytes 786440 | tf_op jit(solution)/shard_map/ppermute | solution.py:130
  40.7 2.2 %collective-permute-start.5 = (bf16[2,256,512]{2,1,0:T(8,128)(2,1)S(1)}, bf16[2,256,512]{2,1,0:T(8,128)(2,1)S(1)}, u32[]{:S(2)}, u32[]{:S(2)}) collective-permute-start(bf16[2,256,512]{2,1,0:T(8,128)(2,1)S(1)} %add_convert_fusion.2), channel_id=1, source_target_pairs={{1,2},{5,6},{9,10},{13,14},{17,18},{21,22},{25,26},{29,30}} | collective-permute-start | bytes 1572872 | tf_op jit(solution)/shard_map/ppermute | solution.py:129
  41.4 1.4 collective-permute-start.7
  46.9 6.2 %collective-permute-start.8 = (bf16[2,256,512]{2,1,0:T(8,128)(2,1)}, bf16[2,256,512]{2,1,0:T(8,128)(2,1)}, u32[]{:S(2)}, u32[]{:S(2)}) collective-permute-start(bf16[2,256,512]{2,1,0:T(8,128)(2,1)} %add_convert_fusion.1), channel_id=1, source_target_pairs={{2,3},{6,7},{10,11},{14,15},{18,19},{22,23},{26,27},{30,31}} | collective-permute-start | bytes 1572872 | tf_op jit(solution)/shard_map/ppermute | solution.py:129
  50.3 2.8 %collective-permute-start.10 = (bf16[2,128,512]{2,1,0:T(8,128)(2,1)}, bf16[2,128,512]{2,1,0:T(8,128)(2,1)}, u32[]{:S(2)}, u32[]{:S(2)}) collective-permute-start(bf16[2,128,512]{2,1,0:T(8,128)(2,1)} %get-tuple-element.33), channel_id=1, source_target_pairs={{2,15},{6,3},{10,7},{14,11},{18,31},{22,19},{26,23},{30,27}} | collective-permute-start | bytes 786440 | tf_op jit(solution)/shard_map/ppermute | solution.py:131
  51.7 1.5 collective-permute-start.9
  67.1 2.5 %collective-permute-start.11 = (bf16[2,256,512]{2,1,0:T(8,128)(2,1)S(1)}, bf16[2,256,512]{2,1,0:T(8,128)(2,1)S(1)}, u32[]{:S(2)}, u32[]{:S(2)}) collective-permute-start(bf16[2,256,512]{2,1,0:T(8,128)(2,1)S(1)} %fusion.33), channel_id=1, source_target_pairs={{3,2},{7,6},{11,10},{15,14},{19,18},{23,22},{27,26},{31,30}} | collective-permute-start | bytes 1572872 | tf_op jit(solution)/shard_map/ppermute | solution.py:174
  68.0 1.5 collective-permute-start.13
  68.7 0.8 collective-permute-start.12
  74.4 7.1 %collective-permute-start.14 = (bf16[2,256,512]{2,1,0:T(8,128)(2,1)}, bf16[2,256,512]{2,1,0:T(8,128)(2,1)}, u32[]{:S(2)}, u32[]{:S(2)}) collective-permute-start(bf16[2,256,512]{2,1,0:T(8,128)(2,1)} %fusion.36), channel_id=1, source_target_pairs={{2,1},{6,5},{10,9},{14,13},{18,17},{22,21},{26,25},{30,29}} | collective-permute-start | bytes 1572872 | tf_op jit(solution)/shard_map/ppermute | solution.py:174
  76.6 2.7 %collective-permute-start.16 = (bf16[2,128,512]{2,1,0:T(8,128)(2,1)}, bf16[2,128,512]{2,1,0:T(8,128)(2,1)}, u32[]{:S(2)}, u32[]{:S(2)}) collective-permute-start(bf16[2,128,512]{2,1,0:T(8,128)(2,1)} %get-tuple-element.27), channel_id=1, source_target_pairs={{2,5},{6,9},{10,13},{14,1},{18,21},{22,25},{26,29},{30,17}} | collective-permute-start | bytes 786440 | tf_op jit(solution)/shard_map/ppermute | solution.py:176
  78.0 2.5 %collective-permute-start.15 = (bf16[2,128,512]{2,1,0:T(8,128)(2,1)}, bf16[2,128,512]{2,1,0:T(8,128)(2,1)}, u32[]{:S(2)}, u32[]{:S(2)}) collective-permute-start(bf16[2,128,512]{2,1,0:T(8,128)(2,1)} %get-tuple-element.26), channel_id=1, source_target_pairs={{2,13},{6,1},{10,5},{14,9},{18,29},{22,17},{26,21},{30,25}} | collective-permute-start | bytes 786440 | tf_op jit(solution)/shard_map/ppermute | solution.py:175
  86.6 48.5 %collective-permute-start.17 = (bf16[2,256,512]{2,1,0:T(8,128)(2,1)S(1)}, bf16[2,256,512]{2,1,0:T(8,128)(2,1)S(1)}, u32[]{:S(2)}, u32[]{:S(2)}) collective-permute-start(bf16[2,256,512]{2,1,0:T(8,128)(2,1)S(1)} %fusion.39), channel_id=1, source_target_pairs={{1,0},{5,4},{9,8},{13,12},{17,16},{21,20},{25,24},{29,28}} | collective-permute-start | bytes 1572872 | tf_op jit(solution)/shard_map/ppermute | solution.py:174
  88.1 44.2 %collective-permute-start.19 = (bf16[2,128,512]{2,1,0:T(8,128)(2,1)S(1)}, bf16[2,128,512]{2,1,0:T(8,128)(2,1)S(1)}, u32[]{:S(2)}, u32[]{:S(2)}) collective-permute-start(bf16[2,128,512]{2,1,0:T(8,128)(2,1)S(1)} %get-tuple-element.25), channel_id=1, source_target_pairs={{1,4},{5,8},{9,12},{13,0},{17,20},{21,24},{25,28},{29,16}} | collective-permute-start | bytes 786440 | tf_op jit(solution)/shard_map/ppermute | solution.py:176
  89.4 45.6 %collective-permute-start.18 = (bf16[2,128,512]{2,1,0:T(8,128)(2,1)S(1)}, bf16[2,128,512]{2,1,0:T(8,128)(2,1)S(1)}, u32[]{:S(2)}, u32[]{:S(2)}) collective-permute-start(bf16[2,128,512]{2,1,0:T(8,128)(2,1)S(1)} %get-tuple-element.24), channel_id=1, source_target_pairs={{1,12},{5,0},{9,4},{13,8},{17,28},{21,16},{25,20},{29,24}} | collective-permute-start | bytes 786440 | tf_op jit(solution)/shard_map/ppermute | solution.py:175
  143.7 18.4 %collective-permute-start.23 = (bf16[2,400,512]{2,1,0:T(8,128)(2,1)}, bf16[2,400,512]{2,1,0:T(8,128)(2,1)}, u32[]{:S(2)}, u32[]{:S(2)}) collective-permute-start(bf16[2,400,512]{2,1,0:T(8,128)(2,1)} %fusion.102), channel_id=1, source_target_pairs={{0,4},{4,0},{8,12},{12,8},{1,5},{5,1},{9,13},{13,9},{2,6},{6,2},{1... | collective-permute-start | bytes 2457608 | tf_op jit(solution)/shard_map/ppermute | solution.py:41
  145.1 42.9 %collective-permute-start.22 = (bf16[2,256,512]{2,1,0:T(8,128)(2,1)}, bf16[2,256,512]{2,1,0:T(8,128)(2,1)}, u32[]{:S(2)}, u32[]{:S(2)}) collective-permute-start(bf16[2,256,512]{2,1,0:T(8,128)(2,1)} %select_select_fusion.2), channel_id=1, source_target_pairs={{0,1},{1,2},{2,3},{4,5},{5,6},{6,7},{8,9},{9,10},{10,11},{12,13},{... | collective-permute-start | bytes 1572872 | tf_op jit(solution)/shard_map/ppermute | solution.py:230
  163.8 27.1 %collective-permute-start.24 = (bf16[1,400,512]{2,1,0:T(8,128)(2,1)S(1)}, bf16[1,400,512]{2,1,0:T(8,128)(2,1)S(1)}, u32[]{:S(2)}, u32[]{:S(2)}) collective-permute-start(bf16[1,400,512]{2,1,0:T(8,128)(2,1)S(1)} %fusion.160), channel_id=1, source_target_pairs={{0,8},{4,12},{8,0},{12,4},{1,9},{5,13},{9,1},{13,5},{2,10},{6,14},... | collective-permute-start | bytes 1228808 | tf_op jit(solution)/shard_map/ppermute | solution.py:41
  166.4 12.2 %collective-permute-start.21 = (bf16[2,128,512]{2,1,0:T(8,128)(2,1)}, bf16[2,128,512]{2,1,0:T(8,128)(2,1)}, u32[]{:S(2)}, u32[]{:S(2)}) collective-permute-start(bf16[2,128,512]{2,1,0:T(8,128)(2,1)} %get-tuple-element.23), channel_id=1, source_target_pairs={{0,4},{4,8},{8,12},{12,0},{16,20},{20,24},{24,28},{28,16}} | collective-permute-start | bytes 786440 | tf_op jit(solution)/shard_map/ppermute | solution.py:184
  168.9 18.2 %collective-permute-start.20 = (bf16[2,128,512]{2,1,0:T(8,128)(2,1)}, bf16[2,128,512]{2,1,0:T(8,128)(2,1)}, u32[]{:S(2)}, u32[]{:S(2)}) collective-permute-start(bf16[2,128,512]{2,1,0:T(8,128)(2,1)} %get-tuple-element.22), channel_id=1, source_target_pairs={{0,12},{4,0},{8,4},{12,8},{16,28},{20,16},{24,20},{28,24}} | collective-permute-start | bytes 786440 | tf_op jit(solution)/shard_map/ppermute | solution.py:183
  (63 other events, 445.3 us)

commit v12 on v9

--- a/solution.py
+++ b/solution.py
@@ -101,9 +101,17 @@
             for d in range(domains)
         ]
 
-    def forward_layer(h, left, right):
-        h_ext = jnp.concatenate([left, h, right], axis=1)
-        agg2 = jnp.einsum("ij,sjd->sid", adj2, h_ext, preferred_element_type=F32)
+    def forward_layer(h, left, right, split=False):
+        if split:
+            agg2 = jnp.einsum(
+                "ij,sjd->sid", adj2[:, margin : margin + nb * blk], h, preferred_element_type=F32
+            )
+            halo = jnp.concatenate([left, right], axis=1)
+            adj_halo = jnp.concatenate([adj2[:, :margin], adj2[:, margin + nb * blk :]], axis=1)
+            agg2 = agg2 + jnp.einsum("ij,sjd->sid", adj_halo, halo, preferred_element_type=F32)
+        else:
+            h_ext = jnp.concatenate([left, h, right], axis=1)
+            agg2 = jnp.einsum("ij,sjd->sid", adj2, h_ext, preferred_element_type=F32)
         agg = (agg2[:, : nb * blk] + agg2[:, nb * blk :]).astype(BF16)
         pre = jnp.einsum("sic,ct->sit", h, w_a, preferred_element_type=F32)
         pre = pre + jnp.einsum("sic,ct->sit", agg, w_b, preferred_element_type=F32)
@@ -122,7 +130,7 @@
     res_list = []
     out_list = []
     for tick in range(sections):
-        out, res = forward_layer(h, left, right)
+        out, res = forward_layer(h, left, right, split=tick == 0)
         res_list.append(res)
         out_list.append(out)
         if tick + 1 < sections:

time: 184 us -> 182 us (0.989)
    dot_general x4 -> x3, matrix products: 5.32 us -> 3.55 us  [forward_layer(): agg2 = jnp.einsum('ij,sjd->sid', adj2, h_ext, preferred_element_type=F32)]
    unnamed x115 -> x114, local copies, waits for them, and re-layouts: 6.56 us -> 6.45 us
  transfers between devices with their start and end apart: 25 -> 25, of which waited for: 9 -> 9; matrix products, arithmetic and copies ran while one was open for 11% -> 10% of each run, Pallas kernels for 0% -> 0%
where the time goes in v12:
time: 182 us; the launch traced here: 181 us
  waiting for transfers between devices  73.1 us (40%)
  starting transfers between devices  40.1 us (22%)
  matrix products  26.6 us (15%)
  other arithmetic  23.5 us (13%)
  local copies, waits for them, and re-layouts  13.5 us (7%)
  between operations  3.97 us (2%)
    ppermute x3, waiting for transfers between devices, shards(): lax.ppermute(left_grad, both, route(active, active - 1, -1))  39.2 us
    ppermute x2, waiting for transfers between devices, halving_reduce_scatter(): recv = lax.ppermute(send, axis, pairs)  16.1 us
    unnamed x114, local copies, waits for them, and re-layouts  6.45 us
    select_n x2, other arithmetic, own_forward(): return lax.select_n(section_index, *[r[i] for r in res_list])  6.01 us
    ppermute x1, waiting for transfers between devices, shards(): lax.ppermute(right_grad, both, route(active, active, 1))  5.45 us
    ppermute x1, starting transfers between devices, shards(): lax.ppermute(pick_blocks(in_blocks, send_right, hs), both, route(0, 0, 1))  5.05 us
    ppermute x3, waiting for transfers between devices, shards(): lax.ppermute(right_grad, both, route(active, active - 1, 1))  4.51 us
    dot_general x4, matrix products, shards(): jnp.einsum('ij,sid->sjd', adj2, jnp.concatenate([dagg, dagg], axis=1), pr...  4.43 us
  transfers between devices with their start and end apart: 25, of which 9 were waited for; matrix products, arithmetic and copies ran while one was open for 10% of the time, Pallas kernels for 0%

profile of v12, /device:TPU:0, one launch (start us, length us, event | category | flops | bytes accessed | tf_op | source)
XLA Modules:
  0.0 180.7 jit_solution(13092412894275930923)
XLA Ops:
  4.7 5.1 %collective-permute-start = (bf16[2,128,512]{1,2,0:T(8,128)(2,1)S(1)}, bf16[2,128,512]{1,2,0:T(8,128)(2,1)S(1)}, u32[]{:S(2)}, u32[]{:S(2)}) collective-permute-start(bf16[2,128,512]{1,2,0:T(8,128)(2,1)S(1)} %bitcast.294), channel_id=1, source_target_pairs={{0,4},{4,8},{8,12},{12,0},{16,20},{20,24},{24,28},{28,16}} | collective-permute-start | bytes 786440 | tf_op jit(solution)/shard_map/ppermute | solution.py:127
  9.9 3.9 %collective-permute-start.1 = (bf16[2,128,512]{1,2,0:T(8,128)(2,1)S(1)}, bf16[2,128,512]{1,2,0:T(8,128)(2,1)S(1)}, u32[]{:S(2)}, u32[]{:S(2)}) collective-permute-start(bf16[2,128,512]{1,2,0:T(8,128)(2,1)S(1)} %bitcast.295), channel_id=1, source_target_pairs={{0,12},{4,0},{8,4},{12,8},{16,28},{20,16},{24,20},{28,24}} | collective-permute-start | bytes 786440 | tf_op jit(solution)/shard_map/ppermute | solution.py:128
  17.0 1.9 %collective-permute-done.1 = bf16[2,128,512]{1,2,0:T(8,128)(2,1)S(1)} collective-permute-done((bf16[2,128,512]{1,2,0:T(8,128)(2,1)S(1)}, bf16[2,128,512]{1,2,0:T(8,128)(2,1)S(1)}, u32[]{:S(2)}, u32[]{:S(2)}) %collective-permute-start.1) | collective-permute-done | bytes 262176 | tf_op jit(solution)/shard_map/ppermute | solution.py:128
  25.7 2.5 %collective-permute-done.3 = bf16[2,128,512]{2,1,0:T(8,128)(2,1)S(1)} collective-permute-done((bf16[2,128,512]{2,1,0:T(8,128)(2,1)S(1)}, bf16[2,128,512]{2,1,0:T(8,128)(2,1)S(1)}, u32[]{:S(2)}, u32[]{:S(2)}) %collective-permute-start.3) | collective-permute-done | bytes 262176 | tf_op jit(solution)/shard_map/ppermute | solution.py:139
  28.3 2.8 %collective-permute-done.4 = bf16[2,128,512]{2,1,0:T(8,128)(2,1)S(1)} collective-permute-done((bf16[2,128,512]{2,1,0:T(8,128)(2,1)S(1)}, bf16[2,128,512]{2,1,0:T(8,128)(2,1)S(1)}, u32[]{:S(2)}, u32[]{:S(2)}) %collective-permute-start.4) | collective-permute-done | bytes 262176 | tf_op jit(solution)/shard_map/ppermute | solution.py:140
  41.4 1.5 collective-permute-start.8
  42.9 1.9 %dynamic-slice_bitcast_fusion.1 = (bf16[2,128,512]{2,1,0:T(8,128)(2,1)}, bf16[2,128,512]{2,1,0:T(8,128)(2,1)}) fusion(bf16[2,2,128,512]{3,2,1,0:T(8,128)(2,1)} %bitcast.31, s32[]{:T(128)S(6)} %select_n.318, s32[]{:T(128)S(6)} %select_n.321), kind=kLoop, calls=%fused_computation.249 | loop fusion | bytes 1048584 | tf_op jit(solution)/shard_map/jit(dynamic_index_in_dim)/squeeze | solution.py:15
  47.6 2.1 %convolution_bitcast_fusion = f32[2,512,512]{2,1,0:T(8,128)S(1)} fusion(bf16[2,128,512]{2,1,0:T(8,128)(2,1)} %collective-permute-done.10, bf16[2,256,512]{2,1,0:T(8,128)(2,1)} %collective-permute-done.8, bf16[2,128,512]{2,1,0:T(8,128)(2,1)} %collective-permute-done.9, bf16[256,512]{1,0:T(8,128)(2,1)} %copy-done.11, bf16[256,512]{1,0:T(8,128)(2,1)S(1)} %bitcast.269), kind=kOutput, calls=%fused_computation.7 | convolution fusion | flops 541065216 | bytes 3670016 | tf_op jit(solution)/shard_map/ij,sjd->sid/dot_general | solution.py:114
  50.2 3.3 %select_select_fusion = (bf16[2,256,512]{2,1,0:T(8,128)(2,1)}, bf16[2,256,512]{2,1,0:T(8,128)(2,1)S(1)}) fusion(pred[]{:T(512)S(6)} %select_n.323, pred[]{:T(512)S(6)} %select_n.314, pred[]{:T(512)S(6)} %select_n.312, f32[2,512,512]{2,1,0:T(8,128)S(1)} %convolution_bitcast_fusion, f32[2,512,512]{2,1,0:T(8,128)} %copy-done.20, ...), kind=kLoop, calls=%fused_computation.229 | loop fusion | flops 2883584 | bytes 9437187 | tf_op jit(solution)/shard_map/select_n | solution.py:199
  54.0 1.5 convolution_add_fusion
  67.5 1.5 collective-permute-start.14
  74.7 1.9 %fusion.46 = (bf16[512]{0:T(512)(128)(2,1)S(1)}, f32[2,256]{1,0:T(2,128)S(1)}, f32[2,256]{1,0:T(2,128)S(1)}, bf16[2,256,512]{2,1,0:T(8,128)(2,1)S(1)}) fusion(f32[2,256,512]{2,1,0:T(8,128)S(1)} %copy-done.3, f32[2,256]{1,0:T(2,128)S(1)} %add_rsqrt_fusion.2, f32[2,256]{1,0:T(2,128)S(1)} %broadcast_multiply_fusion.10, f32[512]{0:T(512)S(1)} %bitcast.288, ...), kind=kLoop, calls=%fused_computation.84 | loop fusion | flops 3930624 | bytes 3157504 | tf_op jit(solution)/shard_map/reduce_sum | solution.py:150
  83.6 2.7 %select_select_fusion.1 = (bf16[2,256,512]{2,1,0:T(8,128)(2,1)S(1)}, bf16[1,2,256,512]{3,2,1,0:T(8,128)(2,1)}) fusion(bf16[2,256,512]{2,1,0:T(8,128)(2,1)S(1)} %copy-done.30, bf16[2,256,512]{2,1,0:T(8,128)(2,1)} %collective-permute-done.8, bf16[2,256,512]{2,1,0:T(8,128)(2,1)S(1)} %copy-done.10, bf16[2,256,512]{2,1,0:T(8,128)(2,1)S(1)} %copy-done.28, ...), kind=kLoop, calls=%fused_computation.230 | loop fusion | flops 3145728 | bytes 5773315 | tf_op jit(solution)/shard_map/select_n | solution.py:199
  86.2 39.2 %collective-permute-done.18 = bf16[2,128,512]{2,1,0:T(8,128)(2,1)S(1)} collective-permute-done((bf16[2,128,512]{2,1,0:T(8,128)(2,1)S(1)}, bf16[2,128,512]{2,1,0:T(8,128)(2,1)S(1)}, u32[]{:S(2)}, u32[]{:S(2)}) %collective-permute-start.18) | collective-permute-done | bytes 262176 | tf_op jit(solution)/shard_map/ppermute | solution.py:183
  125.5 4.5 %collective-permute-done.19 = bf16[2,128,512]{2,1,0:T(8,128)(2,1)S(1)} collective-permute-done((bf16[2,128,512]{2,1,0:T(8,128)(2,1)S(1)}, bf16[2,128,512]{2,1,0:T(8,128)(2,1)S(1)}, u32[]{:S(2)}, u32[]{:S(2)}) %collective-permute-start.19) | collective-permute-done | bytes 262176 | tf_op jit(solution)/shard_map/ppermute | solution.py:184
  136.9 2.1 %fusion.225 = (bf16[2,512,512]{2,1,0:T(8,128)(2,1)S(1)}, f32[2,512,512]{2,1,0:T(8,128)}) fusion(bf16[256,512]{1,0:T(8,128)(2,1)S(1)} %copy-done.13, bf16[256,512]{1,0:T(8,128)(2,1)S(1)} %bitcast.273, bf16[2,256,512]{1,2,0:T(8,128)(2,1)S(1)} %convolution_convert_fusion), kind=kOutput, calls=%fused_computation.329 | convolution fusion | flops 540540928 | bytes 4194304 | tf_op jit(solution)/shard_map/ij,sid->sjd/dot_general | solution.py:165
  139.9 4.1 %collective-permute-start.20 = (bf16[2,128,512]{2,1,0:T(8,128)(2,1)}, bf16[2,128,512]{2,1,0:T(8,128)(2,1)}, u32[]{:S(2)}, u32[]{:S(2)}) collective-permute-start(bf16[2,128,512]{2,1,0:T(8,128)(2,1)} %get-tuple-element.22), channel_id=1, source_target_pairs={{0,12},{4,0},{8,4},{12,8},{16,28},{20,16},{24,20},{28,24}} | collective-permute-start | bytes 786440 | tf_op jit(solution)/shard_map/ppermute | solution.py:191
  144.0 1.9 %collective-permute-start.21 = (bf16[2,128,512]{2,1,0:T(8,128)(2,1)}, bf16[2,128,512]{2,1,0:T(8,128)(2,1)S(1)}, u32[]{:S(2)}, u32[]{:S(2)}) collective-permute-start(bf16[2,128,512]{2,1,0:T(8,128)(2,1)} %get-tuple-element.23), channel_id=1, source_target_pairs={{0,4},{4,8},{8,12},{12,0},{16,20},{20,24},{24,28},{28,16}} | collective-permute-start | bytes 786440 | tf_op jit(solution)/shard_map/ppermute | solution.py:192
  146.9 2.1 %collective-permute-start.22 = (bf16[2,256,512]{2,1,0:T(8,128)(2,1)}, bf16[2,256,512]{2,1,0:T(8,128)(2,1)}, u32[]{:S(2)}, u32[]{:S(2)}) collective-permute-start(bf16[2,256,512]{2,1,0:T(8,128)(2,1)} %select_select_fusion.2), channel_id=1, source_target_pairs={{0,1},{1,2},{2,3},{4,5},{5,6},{6,7},{8,9},{9,10},{10,11},{12,13},{... | collective-permute-start | bytes 1572872 | tf_op jit(solution)/shard_map/ppermute | solution.py:238
  149.0 5.3 %collective-permute-done.23 = bf16[2,400,512]{2,1,0:T(8,128)(2,1)S(1)} collective-permute-done((bf16[2,400,512]{2,1,0:T(8,128)(2,1)S(1)}, bf16[2,400,512]{2,1,0:T(8,128)(2,1)S(1)}, u32[]{:S(2)}, u32[]{:S(2)}) %collective-permute-start.23) | collective-permute-done | bytes 819232 | tf_op jit(solution)/shard_map/ppermute | solution.py:41
  155.5 2.1 %collective-permute-start.24 = (bf16[1,400,512]{2,1,0:T(8,128)(2,1)}, bf16[1,400,512]{2,1,0:T(8,128)(2,1)}, u32[]{:S(2)}, u32[]{:S(2)}) collective-permute-start(bf16[1,400,512]{2,1,0:T(8,128)(2,1)} %fusion.160), channel_id=1, source_target_pairs={{0,8},{4,12},{8,0},{12,4},{1,9},{5,13},{9,1},{13,5},{2,10},{6,14},... | collective-permute-start | bytes 1228808 | tf_op jit(solution)/shard_map/ppermute | solution.py:41
  159.4 5.4 %collective-permute-done.21 = bf16[2,128,512]{2,1,0:T(8,128)(2,1)S(1)} collective-permute-done((bf16[2,128,512]{2,1,0:T(8,128)(2,1)}, bf16[2,128,512]{2,1,0:T(8,128)(2,1)S(1)}, u32[]{:S(2)}, u32[]{:S(2)}) %collective-permute-start.21) | collective-permute-done | bytes 262176 | tf_op jit(solution)/shard_map/ppermute | solution.py:192
  165.2 1.5 fusion.27
  166.6 10.8 %collective-permute-done.24 = bf16[1,400,512]{2,1,0:T(8,128)(2,1)} collective-permute-done((bf16[1,400,512]{2,1,0:T(8,128)(2,1)}, bf16[1,400,512]{2,1,0:T(8,128)(2,1)}, u32[]{:S(2)}, u32[]{:S(2)}) %collective-permute-start.24) | collective-permute-done | bytes 409632 | tf_op jit(solution)/shard_map/ppermute | solution.py:41
  (248 shorter events, 65.1 us)
Async XLA Ops:
  4.7 12.3 %collective-permute-start = (bf16[2,128,512]{1,2,0:T(8,128)(2,1)S(1)}, bf16[2,128,512]{1,2,0:T(8,128)(2,1)S(1)}, u32[]{:S(2)}, u32[]{:S(2)}) collective-permute-start(bf16[2,128,512]{1,2,0:T(8,128)(2,1)S(1)} %bitcast.294), channel_id=1, source_target_pairs={{0,4},{4,8},{8,12},{12,0},{16,20},{20,24},{24,28},{28,16}} | collective-permute-start | bytes 786440 | tf_op jit(solution)/shard_map/ppermute | solution.py:127
  9.9 9.0 %collective-permute-start.1 = (bf16[2,128,512]{1,2,0:T(8,128)(2,1)S(1)}, bf16[2,128,512]{1,2,0:T(8,128)(2,1)S(1)}, u32[]{:S(2)}, u32[]{:S(2)}) collective-permute-start(bf16[2,128,512]{1,2,0:T(8,128)(2,1)S(1)} %bitcast.295), channel_id=1, source_target_pairs={{0,12},{4,0},{8,4},{12,8},{16,28},{20,16},{24,20},{28,24}} | collective-permute-start | bytes 786440 | tf_op jit(solution)/shard_map/ppermute | solution.py:128
  21.7 9.4 %collective-permute-start.2 = (bf16[2,256,512]{2,1,0:T(8,128)(2,1)S(1)}, bf16[2,256,512]{2,1,0:T(8,128)(2,1)S(1)}, u32[]{:S(2)}, u32[]{:S(2)}) collective-permute-start(bf16[2,256,512]{2,1,0:T(8,128)(2,1)S(1)} %add_convert_fusion.3), channel_id=1, source_target_pairs={{0,1},{4,5},{8,9},{12,13},{16,17},{20,21},{24,25},{28,29}} | collective-permute-start | bytes 1572872 | tf_op jit(solution)/shard_map/ppermute | solution.py:138
  23.1 5.2 %collective-permute-start.3 = (bf16[2,128,512]{2,1,0:T(8,128)(2,1)S(1)}, bf16[2,128,512]{2,1,0:T(8,128)(2,1)S(1)}, u32[]{:S(2)}, u32[]{:S(2)}) collective-permute-start(bf16[2,128,512]{2,1,0:T(8,128)(2,1)S(1)} %get-tuple-element.36), channel_id=1, source_target_pairs={{0,5},{4,9},{8,13},{12,1},{16,21},{20,25},{24,29},{28,17}} | collective-permute-start | bytes 786440 | tf_op jit(solution)/shard_map/ppermute | solution.py:139
  24.4 6.7 %collective-permute-start.4 = (bf16[2,128,512]{2,1,0:T(8,128)(2,1)S(1)}, bf16[2,128,512]{2,1,0:T(8,128)(2,1)S(1)}, u32[]{:S(2)}, u32[]{:S(2)}) collective-permute-start(bf16[2,128,512]{2,1,0:T(8,128)(2,1)S(1)} %get-tuple-element.37), channel_id=1, source_target_pairs={{0,13},{4,1},{8,5},{12,9},{16,29},{20,17},{24,21},{28,25}} | collective-permute-start | bytes 786440 | tf_op jit(solution)/shard_map/ppermute | solution.py:140
  34.7 2.2 %collective-permute-start.5 = (bf16[2,256,512]{2,1,0:T(8,128)(2,1)S(1)}, bf16[2,256,512]{2,1,0:T(8,128)(2,1)S(1)}, u32[]{:S(2)}, u32[]{:S(2)}) collective-permute-start(bf16[2,256,512]{2,1,0:T(8,128)(2,1)S(1)} %add_convert_fusion.2), channel_id=1, source_target_pairs={{1,2},{5,6},{9,10},{13,14},{17,18},{21,22},{25,26},{29,30}} | collective-permute-start | bytes 1572872 | tf_op jit(solution)/shard_map/ppermute | solution.py:138
  35.5 1.4 collective-permute-start.6
  41.4 6.2 %collective-permute-start.8 = (bf16[2,256,512]{2,1,0:T(8,128)(2,1)}, bf16[2,256,512]{2,1,0:T(8,128)(2,1)}, u32[]{:S(2)}, u32[]{:S(2)}) collective-permute-start(bf16[2,256,512]{2,1,0:T(8,128)(2,1)} %add_convert_fusion.1), channel_id=1, source_target_pairs={{2,3},{6,7},{10,11},{14,15},{18,19},{22,23},{26,27},{30,31}} | collective-permute-start | bytes 1572872 | tf_op jit(solution)/shard_map/ppermute | solution.py:138
  44.8 2.8 %collective-permute-start.10 = (bf16[2,128,512]{2,1,0:T(8,128)(2,1)}, bf16[2,128,512]{2,1,0:T(8,128)(2,1)}, u32[]{:S(2)}, u32[]{:S(2)}) collective-permute-start(bf16[2,128,512]{2,1,0:T(8,128)(2,1)} %get-tuple-element.33), channel_id=1, source_target_pairs={{2,15},{6,3},{10,7},{14,11},{18,31},{22,19},{26,23},{30,27}} | collective-permute-start | bytes 786440 | tf_op jit(solution)/shard_map/ppermute | solution.py:140
  46.2 1.4 collective-permute-start.9
  60.5 2.5 %collective-permute-start.11 = (bf16[2,256,512]{2,1,0:T(8,128)(2,1)S(1)}, bf16[2,256,512]{2,1,0:T(8,128)(2,1)S(1)}, u32[]{:S(2)}, u32[]{:S(2)}) collective-permute-start(bf16[2,256,512]{2,1,0:T(8,128)(2,1)S(1)} %fusion.20), channel_id=1, source_target_pairs={{3,2},{7,6},{11,10},{15,14},{19,18},{23,22},{27,26},{31,30}} | collective-permute-start | bytes 1572872 | tf_op jit(solution)/shard_map/ppermute | solution.py:182
  61.3 1.5 collective-permute-start.12
  62.0 0.8 collective-permute-start.13
  67.5 7.1 %collective-permute-start.14 = (bf16[2,256,512]{2,1,0:T(8,128)(2,1)}, bf16[2,256,512]{2,1,0:T(8,128)(2,1)}, u32[]{:S(2)}, u32[]{:S(2)}) collective-permute-start(bf16[2,256,512]{2,1,0:T(8,128)(2,1)} %fusion.21), channel_id=1, source_target_pairs={{2,1},{6,5},{10,9},{14,13},{18,17},{22,21},{26,25},{30,29}} | collective-permute-start | bytes 1572872 | tf_op jit(solution)/shard_map/ppermute | solution.py:182
  69.8 2.7 %collective-permute-start.15 = (bf16[2,128,512]{2,1,0:T(8,128)(2,1)}, bf16[2,128,512]{2,1,0:T(8,128)(2,1)}, u32[]{:S(2)}, u32[]{:S(2)}) collective-permute-start(bf16[2,128,512]{2,1,0:T(8,128)(2,1)} %get-tuple-element.26), channel_id=1, source_target_pairs={{2,13},{6,1},{10,5},{14,9},{18,29},{22,17},{26,21},{30,25}} | collective-permute-start | bytes 786440 | tf_op jit(solution)/shard_map/ppermute | solution.py:183
  71.2 2.5 %collective-permute-start.16 = (bf16[2,128,512]{2,1,0:T(8,128)(2,1)}, bf16[2,128,512]{2,1,0:T(8,128)(2,1)}, u32[]{:S(2)}, u32[]{:S(2)}) collective-permute-start(bf16[2,128,512]{2,1,0:T(8,128)(2,1)} %get-tuple-element.27), channel_id=1, source_target_pairs={{2,5},{6,9},{10,13},{14,1},{18,21},{22,25},{26,29},{30,17}} | collective-permute-start | bytes 786440 | tf_op jit(solution)/shard_map/ppermute | solution.py:184
  79.4 50.6 %collective-permute-start.17 = (bf16[2,256,512]{2,1,0:T(8,128)(2,1)S(1)}, bf16[2,256,512]{2,1,0:T(8,128)(2,1)S(1)}, u32[]{:S(2)}, u32[]{:S(2)}) collective-permute-start(bf16[2,256,512]{2,1,0:T(8,128)(2,1)S(1)} %fusion.22), channel_id=1, source_target_pairs={{1,0},{5,4},{9,8},{13,12},{17,16},{21,20},{25,24},{29,28}} | collective-permute-start | bytes 1572872 | tf_op jit(solution)/shard_map/ppermute | solution.py:182
  80.9 44.5 %collective-permute-start.18 = (bf16[2,128,512]{2,1,0:T(8,128)(2,1)S(1)}, bf16[2,128,512]{2,1,0:T(8,128)(2,1)S(1)}, u32[]{:S(2)}, u32[]{:S(2)}) collective-permute-start(bf16[2,128,512]{2,1,0:T(8,128)(2,1)S(1)} %get-tuple-element.24), channel_id=1, source_target_pairs={{1,12},{5,0},{9,4},{13,8},{17,28},{21,16},{25,20},{29,24}} | collective-permute-start | bytes 786440 | tf_op jit(solution)/shard_map/ppermute | solution.py:183
  82.2 47.8 %collective-permute-start.19 = (bf16[2,128,512]{2,1,0:T(8,128)(2,1)S(1)}, bf16[2,128,512]{2,1,0:T(8,128)(2,1)S(1)}, u32[]{:S(2)}, u32[]{:S(2)}) collective-permute-start(bf16[2,128,512]{2,1,0:T(8,128)(2,1)S(1)} %get-tuple-element.25), channel_id=1, source_target_pairs={{1,4},{5,8},{9,12},{13,0},{17,20},{21,24},{25,28},{29,16}} | collective-permute-start | bytes 786440 | tf_op jit(solution)/shard_map/ppermute | solution.py:184
  136.1 18.2 %collective-permute-start.23 = (bf16[2,400,512]{2,1,0:T(8,128)(2,1)S(1)}, bf16[2,400,512]{2,1,0:T(8,128)(2,1)S(1)}, u32[]{:S(2)}, u32[]{:S(2)}) collective-permute-start(bf16[2,400,512]{2,1,0:T(8,128)(2,1)S(1)} %fusion.91), channel_id=1, source_target_pairs={{0,4},{4,0},{8,12},{12,8},{1,5},{5,1},{9,13},{13,9},{2,6},{6,2},{1... | collective-permute-start | bytes 2457608 | tf_op jit(solution)/shard_map/ppermute | solution.py:41
  139.9 18.4 %collective-permute-start.20 = (bf16[2,128,512]{2,1,0:T(8,128)(2,1)}, bf16[2,128,512]{2,1,0:T(8,128)(2,1)}, u32[]{:S(2)}, u32[]{:S(2)}) collective-permute-start(bf16[2,128,512]{2,1,0:T(8,128)(2,1)} %get-tuple-element.22), channel_id=1, source_target_pairs={{0,12},{4,0},{8,4},{12,8},{16,28},{20,16},{24,20},{28,24}} | collective-permute-start | bytes 786440 | tf_op jit(solution)/shard_map/ppermute | solution.py:191
  144.0 20.9 %collective-permute-start.21 = (bf16[2,128,512]{2,1,0:T(8,128)(2,1)}, bf16[2,128,512]{2,1,0:T(8,128)(2,1)S(1)}, u32[]{:S(2)}, u32[]{:S(2)}) collective-permute-start(bf16[2,128,512]{2,1,0:T(8,128)(2,1)} %get-tuple-element.23), channel_id=1, source_target_pairs={{0,4},{4,8},{8,12},{12,0},{16,20},{20,24},{24,28},{28,16}} | collective-permute-start | bytes 786440 | tf_op jit(solution)/shard_map/ppermute | solution.py:192
  146.9 18.3 %collective-permute-start.22 = (bf16[2,256,512]{2,1,0:T(8,128)(2,1)}, bf16[2,256,512]{2,1,0:T(8,128)(2,1)}, u32[]{:S(2)}, u32[]{:S(2)}) collective-permute-start(bf16[2,256,512]{2,1,0:T(8,128)(2,1)} %select_select_fusion.2), channel_id=1, source_target_pairs={{0,1},{1,2},{2,3},{4,5},{5,6},{6,7},{8,9},{9,10},{10,11},{12,13},{... | collective-permute-start | bytes 1572872 | tf_op jit(solution)/shard_map/ppermute | solution.py:238
  155.5 21.9 %collective-permute-start.24 = (bf16[1,400,512]{2,1,0:T(8,128)(2,1)}, bf16[1,400,512]{2,1,0:T(8,128)(2,1)}, u32[]{:S(2)}, u32[]{:S(2)}) collective-permute-start(bf16[1,400,512]{2,1,0:T(8,128)(2,1)} %fusion.160), channel_id=1, source_target_pairs={{0,8},{4,12},{8,0},{12,4},{1,9},{5,13},{9,1},{13,5},{2,10},{6,14},... | collective-permute-start | bytes 1228808 | tf_op jit(solution)/shard_map/ppermute | solution.py:41
  (56 other events, 236.2 us)

commit v13 on v12

--- a/solution.py
+++ b/solution.py
@@ -130,7 +130,7 @@
     res_list = []
     out_list = []
     for tick in range(sections):
-        out, res = forward_layer(h, left, right, split=tick == 0)
+        out, res = forward_layer(h, left, right, split=True)
         res_list.append(res)
         out_list.append(out)
         if tick + 1 < sections:

time: 182 us -> 207 us (1.14)
  local copies, waits for them, and re-layouts: 13.5 us -> 33 us
  waiting for transfers between devices: 73.1 us -> 65.1 us
  matrix products: 26.6 us -> 34.2 us
  other arithmetic: 23.5 us -> 26.4 us
  starting transfers between devices: 40.1 us -> 42.8 us
    dynamic_slice x1 -> x10, local copies, waits for them, and re-layouts: 1.12 us -> 17.5 us  [pick_blocks(): lax.dynamic_index_in_dim(blocks, index[i], axis=1, keepdims=False)]
    ppermute x3, waiting for transfers between devices: 39.2 us -> 33.8 us  [shards(): lax.ppermute(left_grad, both, route(active, active - 1, -1))]
    dot_general x1 -> x4, matrix products: 0.43 us -> 5.01 us  [forward_layer(): jnp.einsum('ij,sjd->sid', adj2[:, margin:margin + nb * blk], h, preferred...]
    dot_general x1 -> x4, matrix products: 0.48 us -> 5.05 us  [forward_layer(): jnp.einsum('ij,sjd->sid', adj_halo, halo, preferred_element_type=F32)]
    unnamed x114 -> x126, local copies, waits for them, and re-layouts: 6.45 us -> 10.9 us
    convert_element_type x3, other arithmetic: 1.6 us -> 5.25 us  [forward_layer(): out = (h.astype(F32) + normed * gain_row).astype(BF16)]
    dot_general x3 -> x0, matrix products: 3.55 us -> none  [forward_layer(): agg2 = jnp.einsum('ij,sjd->sid', adj2, h_ext, preferred_element_type=F32)]
    ppermute x1, waiting for transfers between devices: 5.45 us -> 2.97 us  [shards(): lax.ppermute(right_grad, both, route(active, active, 1))]
  transfers between devices with their start and end apart: 25 -> 25, of which waited for: 9 -> 9; matrix products, arithmetic and copies ran while one was open for 10% -> 19% of each run, Pallas kernels for 0% -> 0%
where the time goes in v13:
time: 207 us; the launch traced here: 205 us
  waiting for transfers between devices  65.1 us (31%)
  starting transfers between devices  42.8 us (21%)
  matrix products  34.2 us (17%)
  local copies, waits for them, and re-layouts  33 us (16%)
  other arithmetic  26.4 us (13%)
  between operations  3.97 us (2%)
    ppermute x3, waiting for transfers between devices, shards(): lax.ppermute(left_grad, both, route(active, active - 1, -1))  33.8 us
    dynamic_slice x10, local copies, waits for them, and re-layouts, pick_blocks(): lax.dynamic_index_in_dim(blocks, index[i], axis=1, keepdims=False)  17.5 us
    ppermute x2, waiting for transfers between devices, halving_reduce_scatter(): recv = lax.ppermute(send, axis, pairs)  16.5 us
    unnamed x126, local copies, waits for them, and re-layouts  10.9 us
    convert_element_type x3, other arithmetic, forward_layer(): out = (h.astype(F32) + normed * gain_row).astype(BF16)  5.25 us
    ppermute x3, starting transfers between devices, shards(): h = lax.ppermute(out, both, route(tick, tick + 1, 0))  5.05 us
    dot_general x4, matrix products, forward_layer(): jnp.einsum('ij,sjd->sid', adj_halo, halo, preferred_element_type=F32)  5.05 us
    dot_general x4, matrix products, forward_layer(): jnp.einsum('ij,sjd->sid', adj2[:, margin:margin + nb * blk], h, preferred...  5.01 us
  transfers between devices with their start and end apart: 25, of which 9 were waited for; matrix products, arithmetic and copies ran while one was open for 19% of the time, Pallas kernels for 0%

profile of v13, /device:TPU:0, one launch (start us, length us, event | category | flops | bytes accessed | tf_op | source)
XLA Modules:
  0.0 205.4 jit_solution(16934372612667506134)
XLA Ops:
  5.3 4.9 %collective-permute-start = (bf16[2,128,512]{1,2,0:T(8,128)(2,1)}, bf16[2,128,512]{1,2,0:T(8,128)(2,1)S(1)}, u32[]{:S(2)}, u32[]{:S(2)}) collective-permute-start(bf16[2,128,512]{1,2,0:T(8,128)(2,1)} %bitcast.13), channel_id=1, source_target_pairs={{0,4},{4,8},{8,12},{12,0},{16,20},{20,24},{24,28},{28,16}} | collective-permute-start | bytes 786440 | tf_op jit(solution)/shard_map/ppermute | solution.py:127
  11.1 3.9 %collective-permute-start.1 = (bf16[2,128,512]{1,2,0:T(8,128)(2,1)}, bf16[2,128,512]{1,2,0:T(8,128)(2,1)S(1)}, u32[]{:S(2)}, u32[]{:S(2)}) collective-permute-start(bf16[2,128,512]{1,2,0:T(8,128)(2,1)} %bitcast.14), channel_id=1, source_target_pairs={{0,12},{4,0},{8,4},{12,8},{16,28},{20,16},{24,20},{28,24}} | collective-permute-start | bytes 786440 | tf_op jit(solution)/shard_map/ppermute | solution.py:128
  23.8 2.1 %collective-permute-start.2 = (bf16[2,256,512]{2,1,0:T(8,128)(2,1)}, bf16[2,256,512]{2,1,0:T(8,128)(2,1)}, u32[]{:S(2)}, u32[]{:S(2)}) collective-permute-start(bf16[2,256,512]{2,1,0:T(8,128)(2,1)} %add_convert_fusion.3), channel_id=1, source_target_pairs={{0,1},{4,5},{8,9},{12,13},{16,17},{20,21},{24,25},{28,29}} | collective-permute-start | bytes 1572872 | tf_op jit(solution)/shard_map/ppermute | solution.py:138
  25.9 1.9 constant_dynamic-slice_fusion.5
  29.5 2.0 collective-permute-start.3
  35.0 3.9 %collective-permute-done.4 = bf16[2,128,512]{1,2,0:T(8,128)(2,1)S(1)} collective-permute-done((bf16[2,128,512]{1,2,0:T(8,128)(2,1)}, bf16[2,128,512]{1,2,0:T(8,128)(2,1)S(1)}, u32[]{:S(2)}, u32[]{:S(2)}) %collective-permute-start.4) | collective-permute-done | bytes 262176 | tf_op jit(solution)/shard_map/ppermute | solution.py:140
  46.5 2.1 %add_convert_fusion.2 = bf16[2,256,512]{2,1,0:T(8,128)(2,1)} fusion(bf16[2,256,512]{2,1,0:T(8,128)(2,1)} %collective-permute-done.2, f32[2,256,512]{2,1,0:T(8,128)S(1)} %get-tuple-element.45, f32[2,256]{1,0:T(2,128)S(1)} %add_rsqrt_fusion.2, f32[2,256]{1,0:T(2,128)S(1)} %broadcast_multiply_fusion.10, f32[512]{0:T(512)S(1)} %bitcast.269), kind=kLoop, calls=%fused_computation.137 | loop fusion | flops 1572864 | bytes 2103296 | tf_op jit(solution)/shard_map/convert_element_type | solution.py:123
  50.1 1.9 constant_dynamic-slice_fusion.3
  52.0 1.8 copy.57
  65.6 2.1 %add_convert_fusion.1 = bf16[2,256,512]{2,1,0:T(8,128)(2,1)} fusion(bf16[2,256,512]{2,1,0:T(8,128)(2,1)} %collective-permute-done.5, f32[2,256,512]{2,1,0:T(8,128)S(1)} %get-tuple-element.47, f32[2,256]{1,0:T(2,128)S(1)} %add_rsqrt_fusion.1, f32[2,256]{1,0:T(2,128)S(1)} %broadcast_multiply_fusion.9, f32[512]{0:T(512)S(1)} %bitcast.270), kind=kLoop, calls=%fused_computation.133 | loop fusion | flops 1572864 | bytes 2103296 | tf_op jit(solution)/shard_map/convert_element_type | solution.py:123
  69.2 1.9 constant_dynamic-slice_fusion.1
  71.1 1.8 copy.63
  105.9 1.9 fusion.46
  114.6 2.9 %select_select_fusion.1 = (bf16[2,256,512]{2,1,0:T(8,128)(2,1)S(1)}, bf16[1,2,256,512]{3,2,1,0:T(8,128)(2,1)}) fusion(bf16[2,256,512]{2,1,0:T(8,128)(2,1)} %collective-permute-done.5, bf16[2,256,512]{2,1,0:T(8,128)(2,1)} %collective-permute-done.8, bf16[2,256,512]{2,1,0:T(8,128)(2,1)S(1)} %copy-done.14, bf16[2,256,512]{2,1,0:T(8,128)(2,1)} %collective-permute-done.2, ...), kind=kLoop, calls=%fused_computation.227 | loop fusion | flops 3145728 | bytes 5773315 | tf_op jit(solution)/shard_map/select_n | solution.py:199
  117.6 33.8 %collective-permute-done.18 = bf16[2,128,512]{2,1,0:T(8,128)(2,1)S(1)} collective-permute-done((bf16[2,128,512]{2,1,0:T(8,128)(2,1)S(1)}, bf16[2,128,512]{2,1,0:T(8,128)(2,1)S(1)}, u32[]{:S(2)}, u32[]{:S(2)}) %collective-permute-start.18) | collective-permute-done | bytes 262176 | tf_op jit(solution)/shard_map/ppermute | solution.py:183
  151.4 4.0 %collective-permute-done.19 = bf16[2,128,512]{2,1,0:T(8,128)(2,1)S(1)} collective-permute-done((bf16[2,128,512]{2,1,0:T(8,128)(2,1)S(1)}, bf16[2,128,512]{2,1,0:T(8,128)(2,1)S(1)}, u32[]{:S(2)}, u32[]{:S(2)}) %collective-permute-start.19) | collective-permute-done | bytes 262176 | tf_op jit(solution)/shard_map/ppermute | solution.py:184
  162.1 2.1 %fusion.214 = (bf16[2,512,512]{2,1,0:T(8,128)(2,1)S(1)}, f32[2,512,512]{2,1,0:T(8,128)}) fusion(bf16[256,512]{1,0:T(8,128)(2,1)S(1)} %copy-done.17, bf16[256,512]{1,0:T(8,128)(2,1)S(1)} %bitcast.262, bf16[2,256,512]{1,2,0:T(8,128)(2,1)S(1)} %convolution_convert_fusion), kind=kOutput, calls=%fused_computation.322 | convolution fusion | flops 540540928 | bytes 4194304 | tf_op jit(solution)/shard_map/ij,sid->sjd/dot_general | solution.py:165
  165.0 4.2 %collective-permute-start.20 = (bf16[2,128,512]{2,1,0:T(8,128)(2,1)}, bf16[2,128,512]{2,1,0:T(8,128)(2,1)}, u32[]{:S(2)}, u32[]{:S(2)}) collective-permute-start(bf16[2,128,512]{2,1,0:T(8,128)(2,1)} %get-tuple-element.22), channel_id=1, source_target_pairs={{0,12},{4,0},{8,4},{12,8},{16,28},{20,16},{24,20},{28,24}} | collective-permute-start | bytes 786440 | tf_op jit(solution)/shard_map/ppermute | solution.py:191
  169.3 1.9 collective-permute-start.21
  172.2 2.1 %collective-permute-start.22 = (bf16[2,256,512]{2,1,0:T(8,128)(2,1)}, bf16[2,256,512]{2,1,0:T(8,128)(2,1)}, u32[]{:S(2)}, u32[]{:S(2)}) collective-permute-start(bf16[2,256,512]{2,1,0:T(8,128)(2,1)} %select_select_fusion.2), channel_id=1, source_target_pairs={{0,1},{1,2},{2,3},{4,5},{5,6},{6,7},{8,9},{9,10},{10,11},{12,13},{... | collective-permute-start | bytes 1572872 | tf_op jit(solution)/shard_map/ppermute | solution.py:238
  174.3 5.1 %collective-permute-done.23 = bf16[2,400,512]{2,1,0:T(8,128)(2,1)S(1)} collective-permute-done((bf16[2,400,512]{2,1,0:T(8,128)(2,1)S(1)}, bf16[2,400,512]{2,1,0:T(8,128)(2,1)S(1)}, u32[]{:S(2)}, u32[]{:S(2)}) %collective-permute-start.23) | collective-permute-done | bytes 819232 | tf_op jit(solution)/shard_map/ppermute | solution.py:41
  182.5 2.4 %collective-permute-done.20 = bf16[2,128,512]{2,1,0:T(8,128)(2,1)} collective-permute-done((bf16[2,128,512]{2,1,0:T(8,128)(2,1)}, bf16[2,128,512]{2,1,0:T(8,128)(2,1)}, u32[]{:S(2)}, u32[]{:S(2)}) %collective-permute-start.20) | collective-permute-done | bytes 262176 | tf_op jit(solution)/shard_map/ppermute | solution.py:191
  186.1 3.0 %collective-permute-done.21 = bf16[2,128,512]{2,1,0:T(8,128)(2,1)S(1)} collective-permute-done((bf16[2,128,512]{2,1,0:T(8,128)(2,1)}, bf16[2,128,512]{2,1,0:T(8,128)(2,1)S(1)}, u32[]{:S(2)}, u32[]{:S(2)}) %collective-permute-start.21) | collective-permute-done | bytes 262176 | tf_op jit(solution)/shard_map/ppermute | solution.py:192
  190.8 11.3 %collective-permute-done.24 = bf16[1,400,512]{2,1,0:T(8,128)(2,1)} collective-permute-done((bf16[1,400,512]{2,1,0:T(8,128)(2,1)}, bf16[1,400,512]{2,1,0:T(8,128)(2,1)}, u32[]{:S(2)}, u32[]{:S(2)}) %collective-permute-start.24) | collective-permute-done | bytes 409632 | tf_op jit(solution)/shard_map/ppermute | solution.py:41
  (270 shorter events, 96.3 us)
Async XLA Ops:
  5.3 13.1 %collective-permute-start = (bf16[2,128,512]{1,2,0:T(8,128)(2,1)}, bf16[2,128,512]{1,2,0:T(8,128)(2,1)S(1)}, u32[]{:S(2)}, u32[]{:S(2)}) collective-permute-start(bf16[2,128,512]{1,2,0:T(8,128)(2,1)} %bitcast.13), channel_id=1, source_target_pairs={{0,4},{4,8},{8,12},{12,0},{16,20},{20,24},{24,28},{28,16}} | collective-permute-start | bytes 786440 | tf_op jit(solution)/shard_map/ppermute | solution.py:127
  11.1 8.5 %collective-permute-start.1 = (bf16[2,128,512]{1,2,0:T(8,128)(2,1)}, bf16[2,128,512]{1,2,0:T(8,128)(2,1)S(1)}, u32[]{:S(2)}, u32[]{:S(2)}) collective-permute-start(bf16[2,128,512]{1,2,0:T(8,128)(2,1)} %bitcast.14), channel_id=1, source_target_pairs={{0,12},{4,0},{8,4},{12,8},{16,28},{20,16},{24,20},{28,24}} | collective-permute-start | bytes 786440 | tf_op jit(solution)/shard_map/ppermute | solution.py:128
  23.8 16.6 %collective-permute-start.2 = (bf16[2,256,512]{2,1,0:T(8,128)(2,1)}, bf16[2,256,512]{2,1,0:T(8,128)(2,1)}, u32[]{:S(2)}, u32[]{:S(2)}) collective-permute-start(bf16[2,256,512]{2,1,0:T(8,128)(2,1)} %add_convert_fusion.3), channel_id=1, source_target_pairs={{0,1},{4,5},{8,9},{12,13},{16,17},{20,21},{24,25},{28,29}} | collective-permute-start | bytes 1572872 | tf_op jit(solution)/shard_map/ppermute | solution.py:138
  29.5 5.5 %collective-permute-start.3 = (bf16[2,128,512]{1,2,0:T(8,128)(2,1)}, bf16[2,128,512]{1,2,0:T(8,128)(2,1)}, u32[]{:S(2)}, u32[]{:S(2)}) collective-permute-start(bf16[2,128,512]{1,2,0:T(8,128)(2,1)} %bitcast.283), channel_id=1, source_target_pairs={{0,5},{4,9},{8,13},{12,1},{16,21},{20,25},{24,29},{28,17}} | collective-permute-start | bytes 786440 | tf_op jit(solution)/shard_map/ppermute | solution.py:139
  33.3 5.6 %collective-permute-start.4 = (bf16[2,128,512]{1,2,0:T(8,128)(2,1)}, bf16[2,128,512]{1,2,0:T(8,128)(2,1)S(1)}, u32[]{:S(2)}, u32[]{:S(2)}) collective-permute-start(bf16[2,128,512]{1,2,0:T(8,128)(2,1)} %bitcast.285), channel_id=1, source_target_pairs={{0,13},{4,1},{8,5},{12,9},{16,29},{20,17},{24,21},{28,25}} | collective-permute-start | bytes 786440 | tf_op jit(solution)/shard_map/ppermute | solution.py:140
  48.6 10.6 %collective-permute-start.5 = (bf16[2,256,512]{2,1,0:T(8,128)(2,1)}, bf16[2,256,512]{2,1,0:T(8,128)(2,1)}, u32[]{:S(2)}, u32[]{:S(2)}) collective-permute-start(bf16[2,256,512]{2,1,0:T(8,128)(2,1)} %add_convert_fusion.2), channel_id=1, source_target_pairs={{1,2},{5,6},{9,10},{13,14},{17,18},{21,22},{25,26},{29,30}} | collective-permute-start | bytes 1572872 | tf_op jit(solution)/shard_map/ppermute | solution.py:138
  53.8 4.0 %collective-permute-start.6 = (bf16[2,128,512]{1,2,0:T(8,128)(2,1)}, bf16[2,128,512]{1,2,0:T(8,128)(2,1)}, u32[]{:S(2)}, u32[]{:S(2)}) collective-permute-start(bf16[2,128,512]{1,2,0:T(8,128)(2,1)} %bitcast.284), channel_id=1, source_target_pairs={{1,6},{5,10},{9,14},{13,2},{17,22},{21,26},{25,30},{29,18}} | collective-permute-start | bytes 786440 | tf_op jit(solution)/shard_map/ppermute | solution.py:139
  67.7 12.7 %collective-permute-start.8 = (bf16[2,256,512]{2,1,0:T(8,128)(2,1)}, bf16[2,256,512]{2,1,0:T(8,128)(2,1)}, u32[]{:S(2)}, u32[]{:S(2)}) collective-permute-start(bf16[2,256,512]{2,1,0:T(8,128)(2,1)} %add_convert_fusion.1), channel_id=1, source_target_pairs={{2,3},{6,7},{10,11},{14,15},{18,19},{22,23},{26,27},{30,31}} | collective-permute-start | bytes 1572872 | tf_op jit(solution)/shard_map/ppermute | solution.py:138
  72.9 5.8 %collective-permute-start.10 = (bf16[2,128,512]{1,2,0:T(8,128)(2,1)}, bf16[2,128,512]{1,2,0:T(8,128)(2,1)}, u32[]{:S(2)}, u32[]{:S(2)}) collective-permute-start(bf16[2,128,512]{1,2,0:T(8,128)(2,1)} %bitcast.281), channel_id=1, source_target_pairs={{2,15},{6,3},{10,7},{14,11},{18,31},{22,19},{26,23},{30,27}} | collective-permute-start | bytes 786440 | tf_op jit(solution)/shard_map/ppermute | solution.py:140
  76.0 2.7 %collective-permute-start.9 = (bf16[2,128,512]{1,2,0:T(8,128)(2,1)}, bf16[2,128,512]{1,2,0:T(8,128)(2,1)}, u32[]{:S(2)}, u32[]{:S(2)}) collective-permute-start(bf16[2,128,512]{1,2,0:T(8,128)(2,1)} %bitcast.282), channel_id=1, source_target_pairs={{2,7},{6,11},{10,15},{14,3},{18,23},{22,27},{26,31},{30,19}} | collective-permute-start | bytes 786440 | tf_op jit(solution)/shard_map/ppermute | solution.py:139
  91.5 2.5 %collective-permute-start.11 = (bf16[2,256,512]{2,1,0:T(8,128)(2,1)S(1)}, bf16[2,256,512]{2,1,0:T(8,128)(2,1)S(1)}, u32[]{:S(2)}, u32[]{:S(2)}) collective-permute-start(bf16[2,256,512]{2,1,0:T(8,128)(2,1)S(1)} %fusion.20), channel_id=1, source_target_pairs={{3,2},{7,6},{11,10},{15,14},{19,18},{23,22},{27,26},{31,30}} | collective-permute-start | bytes 1572872 | tf_op jit(solution)/shard_map/ppermute | solution.py:182
  92.4 1.5 collective-permute-start.12
  93.1 0.8 collective-permute-start.13
  98.6 7.3 %collective-permute-start.14 = (bf16[2,256,512]{2,1,0:T(8,128)(2,1)}, bf16[2,256,512]{2,1,0:T(8,128)(2,1)}, u32[]{:S(2)}, u32[]{:S(2)}) collective-permute-start(bf16[2,256,512]{2,1,0:T(8,128)(2,1)} %fusion.21), channel_id=1, source_target_pairs={{2,1},{6,5},{10,9},{14,13},{18,17},{22,21},{26,25},{30,29}} | collective-permute-start | bytes 1572872 | tf_op jit(solution)/shard_map/ppermute | solution.py:182
  101.0 2.7 %collective-permute-start.15 = (bf16[2,128,512]{2,1,0:T(8,128)(2,1)}, bf16[2,128,512]{2,1,0:T(8,128)(2,1)}, u32[]{:S(2)}, u32[]{:S(2)}) collective-permute-start(bf16[2,128,512]{2,1,0:T(8,128)(2,1)} %get-tuple-element.26), channel_id=1, source_target_pairs={{2,13},{6,1},{10,5},{14,9},{18,29},{22,17},{26,21},{30,25}} | collective-permute-start | bytes 786440 | tf_op jit(solution)/shard_map/ppermute | solution.py:183
  102.4 2.5 %collective-permute-start.16 = (bf16[2,128,512]{2,1,0:T(8,128)(2,1)}, bf16[2,128,512]{2,1,0:T(8,128)(2,1)}, u32[]{:S(2)}, u32[]{:S(2)}) collective-permute-start(bf16[2,128,512]{2,1,0:T(8,128)(2,1)} %get-tuple-element.27), channel_id=1, source_target_pairs={{2,5},{6,9},{10,13},{14,1},{18,21},{22,25},{26,29},{30,17}} | collective-permute-start | bytes 786440 | tf_op jit(solution)/shard_map/ppermute | solution.py:184
  110.7 44.8 %collective-permute-start.17 = (bf16[2,256,512]{2,1,0:T(8,128)(2,1)S(1)}, bf16[2,256,512]{2,1,0:T(8,128)(2,1)S(1)}, u32[]{:S(2)}, u32[]{:S(2)}) collective-permute-start(bf16[2,256,512]{2,1,0:T(8,128)(2,1)S(1)} %fusion.22), channel_id=1, source_target_pairs={{1,0},{5,4},{9,8},{13,12},{17,16},{21,20},{25,24},{29,28}} | collective-permute-start | bytes 1572872 | tf_op jit(solution)/shard_map/ppermute | solution.py:182
  112.0 39.3 %collective-permute-start.18 = (bf16[2,128,512]{2,1,0:T(8,128)(2,1)S(1)}, bf16[2,128,512]{2,1,0:T(8,128)(2,1)S(1)}, u32[]{:S(2)}, u32[]{:S(2)}) collective-permute-start(bf16[2,128,512]{2,1,0:T(8,128)(2,1)S(1)} %get-tuple-element.24), channel_id=1, source_target_pairs={{1,12},{5,0},{9,4},{13,8},{17,28},{21,16},{25,20},{29,24}} | collective-permute-start | bytes 786440 | tf_op jit(solution)/shard_map/ppermute | solution.py:183
  113.3 42.1 %collective-permute-start.19 = (bf16[2,128,512]{2,1,0:T(8,128)(2,1)S(1)}, bf16[2,128,512]{2,1,0:T(8,128)(2,1)S(1)}, u32[]{:S(2)}, u32[]{:S(2)}) collective-permute-start(bf16[2,128,512]{2,1,0:T(8,128)(2,1)S(1)} %get-tuple-element.25), channel_id=1, source_target_pairs={{1,4},{5,8},{9,12},{13,0},{17,20},{21,24},{25,28},{29,16}} | collective-permute-start | bytes 786440 | tf_op jit(solution)/shard_map/ppermute | solution.py:184
  161.4 18.0 %collective-permute-start.23 = (bf16[2,400,512]{2,1,0:T(8,128)(2,1)S(1)}, bf16[2,400,512]{2,1,0:T(8,128)(2,1)S(1)}, u32[]{:S(2)}, u32[]{:S(2)}) collective-permute-start(bf16[2,400,512]{2,1,0:T(8,128)(2,1)S(1)} %fusion.76), channel_id=1, source_target_pairs={{0,4},{4,0},{8,12},{12,8},{1,5},{5,1},{9,13},{13,9},{2,6},{6,2},{1... | collective-permute-start | bytes 2457608 | tf_op jit(solution)/shard_map/ppermute | solution.py:41
  165.0 19.8 %collective-permute-start.20 = (bf16[2,128,512]{2,1,0:T(8,128)(2,1)}, bf16[2,128,512]{2,1,0:T(8,128)(2,1)}, u32[]{:S(2)}, u32[]{:S(2)}) collective-permute-start(bf16[2,128,512]{2,1,0:T(8,128)(2,1)} %get-tuple-element.22), channel_id=1, source_target_pairs={{0,12},{4,0},{8,4},{12,8},{16,28},{20,16},{24,20},{28,24}} | collective-permute-start | bytes 786440 | tf_op jit(solution)/shard_map/ppermute | solution.py:191
  169.3 19.8 %collective-permute-start.21 = (bf16[2,128,512]{2,1,0:T(8,128)(2,1)}, bf16[2,128,512]{2,1,0:T(8,128)(2,1)S(1)}, u32[]{:S(2)}, u32[]{:S(2)}) collective-permute-start(bf16[2,128,512]{2,1,0:T(8,128)(2,1)} %get-tuple-element.23), channel_id=1, source_target_pairs={{0,4},{4,8},{8,12},{12,0},{16,20},{20,24},{24,28},{28,16}} | collective-permute-start | bytes 786440 | tf_op jit(solution)/shard_map/ppermute | solution.py:192
  172.2 17.1 %collective-permute-start.22 = (bf16[2,256,512]{2,1,0:T(8,128)(2,1)}, bf16[2,256,512]{2,1,0:T(8,128)(2,1)}, u32[]{:S(2)}, u32[]{:S(2)}) collective-permute-start(bf16[2,256,512]{2,1,0:T(8,128)(2,1)} %select_select_fusion.2), channel_id=1, source_target_pairs={{0,1},{1,2},{2,3},{4,5},{5,6},{6,7},{8,9},{9,10},{10,11},{12,13},{... | collective-permute-start | bytes 1572872 | tf_op jit(solution)/shard_map/ppermute | solution.py:238
  180.7 21.3 %collective-permute-start.24 = (bf16[1,400,512]{2,1,0:T(8,128)(2,1)}, bf16[1,400,512]{2,1,0:T(8,128)(2,1)}, u32[]{:S(2)}, u32[]{:S(2)}) collective-permute-start(bf16[1,400,512]{2,1,0:T(8,128)(2,1)} %fusion.157), channel_id=1, source_target_pairs={{0,8},{4,12},{8,0},{12,4},{1,9},{5,13},{9,1},{13,5},{2,10},{6,14},... | collective-permute-start | bytes 1228808 | tf_op jit(solution)/shard_map/ppermute | solution.py:41
  (62 other events, 268.8 us)

commit v14 on v12

--- a/solution.py
+++ b/solution.py
@@ -81,9 +81,7 @@
     pair = (row_oh[:, :, None] * col_oh[:, None, :]).reshape(slot_count, nb * ext)
     adj = jnp.einsum("tp,tij->pij", pair, tile_weights.astype(F32), precision=HIGHEST_PRECISION)
     adj = adj.reshape(nb, ext, blk, blk).transpose(0, 2, 1, 3).reshape(nb * blk, ext * blk)
-    adj_hi = adj.astype(BF16)
-    adj_lo = (adj - adj_hi.astype(F32)).astype(BF16)
-    adj2 = jnp.concatenate([adj_hi, adj_lo], axis=0)
+    adj2 = adj.astype(BF16)
 
     w_a = w_one[0, :width]
     w_b = w_one[0, width:]
@@ -112,7 +110,7 @@
         else:
             h_ext = jnp.concatenate([left, h, right], axis=1)
             agg2 = jnp.einsum("ij,sjd->sid", adj2, h_ext, preferred_element_type=F32)
-        agg = (agg2[:, : nb * blk] + agg2[:, nb * blk :]).astype(BF16)
+        agg = agg2.astype(BF16)
         pre = jnp.einsum("sic,ct->sit", h, w_a, preferred_element_type=F32)
         pre = pre + jnp.einsum("sic,ct->sit", agg, w_b, preferred_element_type=F32)
         act = jax.nn.silu(pre).astype(BF16)
@@ -163,7 +161,7 @@
         gnode = gf + jnp.einsum("sip,vp->siv", dpre, w_a, preferred_element_type=F32)
         dagg = jnp.einsum("sip,vp->siv", dpre, w_b, preferred_element_type=F32).astype(BF16)
         spread = jnp.einsum(
-            "ij,sid->sjd", adj2, jnp.concatenate([dagg, dagg], axis=1), preferred_element_type=F32
+            "ij,sid->sjd", adj2, dagg, preferred_element_type=F32
         )
         left_grad = spread[:, :margin].astype(BF16)
         right_grad = spread[:, margin + nb * blk :].astype(BF16)

time: 182 us -> 209 us (1.15)
  matrix products: 26.6 us -> 42.5 us
  local copies, waits for them, and re-layouts: 13.5 us -> 21 us
    dot_general x8 -> x4, matrix products: 6.3 us -> 13 us  [shards(): spread = jnp.einsum('ij,sid->sjd', adj2, dagg, preferred_element_type=F32)]
    ppermute x1, waiting for transfers between devices: 0.01 us -> 6.21 us  [shards(): lax.ppermute(pick_blocks(in_blocks, send_right, hs), both, route(0, 0, 1))]
    dot_general x4, matrix products: 3.68 us -> 8.6 us  [shards(): jnp.einsum('sip,vp->siv', dpre, w_a, preferred_element_type=F32)]
    unnamed x114, local copies, waits for them, and re-layouts: 6.45 us -> 11 us
    select_n x2 -> x1, other arithmetic: 6.01 us -> 2.73 us  [own_forward(): return lax.select_n(section_index, *[r[i] for r in res_list])]
    ppermute x1, starting transfers between devices: 5.05 us -> 1.91 us  [shards(): lax.ppermute(pick_blocks(in_blocks, send_right, hs), both, route(0, 0, 1))]
    ppermute x1, starting transfers between devices: 3.95 us -> 6.95 us  [shards(): lax.ppermute(pick_blocks(in_blocks, send_left, hs), both, route(0, 0, -1))]
    ppermute x1, waiting for transfers between devices: 5.45 us -> 2.77 us  [shards(): lax.ppermute(right_grad, both, route(active, active, 1))]
  transfers between devices with their start and end apart: 25 -> 25, of which waited for: 9 -> 8; matrix products, arithmetic and copies ran while one was open for 10% -> 11% of each run, Pallas kernels for 0% -> 0%
where the time goes in v14:
time: 209 us; the launch traced here: 207 us
  waiting for transfers between devices  72.8 us (35%)
  matrix products  42.5 us (20%)
  starting transfers between devices  42 us (20%)
  other arithmetic  25.1 us (12%)
  local copies, waits for them, and re-layouts  21 us (10%)
  between operations  3.78 us (2%)
    ppermute x3, waiting for transfers between devices, shards(): lax.ppermute(left_grad, both, route(active, active - 1, -1))  38.4 us
    ppermute x2, waiting for transfers between devices, halving_reduce_scatter(): recv = lax.ppermute(send, axis, pairs)  17.6 us
    dot_general x4, matrix products, shards(): spread = jnp.einsum('ij,sid->sjd', adj2, dagg, preferred_element_type=F32)  13 us
    unnamed x114, local copies, waits for them, and re-layouts  11 us
    dot_general x4, matrix products, shards(): jnp.einsum('sip,vp->siv', dpre, w_a, preferred_element_type=F32)  8.6 us
    ppermute x1, starting transfers between devices, shards(): lax.ppermute(pick_blocks(in_blocks, send_left, hs), both, route(0, 0, -1))  6.95 us
    ppermute x1, waiting for transfers between devices, shards(): lax.ppermute(pick_blocks(in_blocks, send_right, hs), both, route(0, 0, 1))  6.21 us
    dot_general x4, matrix products, shards(): dact = jnp.einsum('sip,vp->siv', dout, w_2, preferred_element_type=F32)  5.03 us
  transfers between devices with their start and end apart: 25, of which 8 were waited for; matrix products, arithmetic and copies ran while one was open for 11% of the time, Pallas kernels for 0%

profile of v14, /device:TPU:0, one launch (start us, length us, event | category | flops | bytes accessed | tf_op | source)
XLA Modules:
  0.0 207.1 jit_solution(7856384511962693431)
XLA Ops:
  4.8 6.9 %collective-permute-start.1 = (bf16[2,128,512]{1,2,0:T(8,128)(2,1)S(1)}, bf16[2,128,512]{1,2,0:T(8,128)(2,1)S(1)}, u32[]{:S(2)}, u32[]{:S(2)}) collective-permute-start(bf16[2,128,512]{1,2,0:T(8,128)(2,1)S(1)} %bitcast.287), channel_id=1, source_target_pairs={{0,12},{4,0},{8,4},{12,8},{16,28},{20,16},{24,20},{28,24}} | collective-permute-start | bytes 786440 | tf_op jit(solution)/shard_map/ppermute | solution.py:126
  16.6 6.2 %collective-permute-done = bf16[2,128,512]{1,2,0:T(8,128)(2,1)S(1)} collective-permute-done((bf16[2,128,512]{1,2,0:T(8,128)(2,1)}, bf16[2,128,512]{1,2,0:T(8,128)(2,1)S(1)}, u32[]{:S(2)}, u32[]{:S(2)}) %collective-permute-start) | collective-permute-done | bytes 262176 | tf_op jit(solution)/shard_map/ppermute | solution.py:125
  26.0 2.1 %collective-permute-start.2 = (bf16[2,256,512]{2,1,0:T(8,128)(2,1)}, bf16[2,256,512]{2,1,0:T(8,128)(2,1)}, u32[]{:S(2)}, u32[]{:S(2)}) collective-permute-start(bf16[2,256,512]{2,1,0:T(8,128)(2,1)} %add_convert_fusion.3), channel_id=1, source_target_pairs={{0,1},{4,5},{8,9},{12,13},{16,17},{20,21},{24,25},{28,29}} | collective-permute-start | bytes 1572872 | tf_op jit(solution)/shard_map/ppermute | solution.py:136
  31.9 2.0 collective-permute-start.4
  35.4 2.8 %collective-permute-done.4 = bf16[2,128,512]{2,1,0:T(8,128)(2,1)} collective-permute-done((bf16[2,128,512]{2,1,0:T(8,128)(2,1)}, bf16[2,128,512]{2,1,0:T(8,128)(2,1)}, u32[]{:S(2)}, u32[]{:S(2)}) %collective-permute-start.4) | collective-permute-done | bytes 262176 | tf_op jit(solution)/shard_map/ppermute | solution.py:138
  57.3 2.8 %select_select_fusion = (bf16[2,256,512]{2,1,0:T(8,128)(2,1)}, bf16[2,256,512]{2,1,0:T(8,128)(2,1)S(1)}) fusion(bf16[2,256,512]{2,1,0:T(8,128)(2,1)} %copy-done.50, bf16[2,256,512]{2,1,0:T(8,128)(2,1)} %copy-done.30, bf16[2,256,512]{2,1,0:T(8,128)(2,1)} %copy-done.49, pred[]{:T(512)S(6)} %select_n.323, pred[]{:T(512)S(6)} %select_n.314, ...), kind=kOutput, calls=%fused_computation.204 | convolution fusion | flops 272629760 | bytes 3932163 | tf_op jit(solution)/shard_map/ij,sjd->sid/dot_general | solution.py:112
  66.7 3.6 %fusion.198 = (bf16[2,512,512]{2,1,0:T(8,128)(2,1)}, f32[2,512,512]{2,1,0:T(8,128)}) fusion(bf16[256,512,1]{1,0,2:T(8,128)(2,1)S(1)} %reshape.379, bf16[2,256,512]{2,1,0:T(8,128)(2,1)} %multiply_convert_fusion.2, bf16[1,1024,512]{2,1,0:T(8,128)(2,1)S(1)} %copy-done.1), kind=kOutput, calls=%fused_computation.294 | convolution fusion | flops 537657344 | bytes 4456448 | tf_op jit(solution)/shard_map/ij,sid->sjd/dot_general | solution.py:163
  70.2 2.1 %fusion.21 = bf16[2,256,512]{2,1,0:T(8,128)(2,1)S(1)} fusion(bf16[2,256,512]{2,1,0:T(8,128)(2,1)} %multiply_convert_fusion.2, bf16[2,256,512]{2,1,0:T(8,128)(2,1)} %param.12, f32[2,512,512]{2,1,0:T(8,128)} %get-tuple-element.49, bf16[1,1024,512]{2,1,0:T(8,128)(2,1)S(1)} %copy-done.1), kind=kOutput, calls=%fused_computation.53 | convolution fusion | flops 269484032 | bytes 3145728 | tf_op jit(solution)/shard_map/sip,vp->siv/dot_general | solution.py:161
  78.9 3.6 %fusion.201 = (bf16[2,512,512]{2,1,0:T(8,128)(2,1)}, f32[2,512,512]{2,1,0:T(8,128)}) fusion(bf16[256,512,1]{1,0,2:T(8,128)(2,1)S(1)} %reshape.379, bf16[2,256,512]{2,1,0:T(8,128)(2,1)} %multiply_convert_fusion.1, bf16[1,1024,512]{2,1,0:T(8,128)(2,1)S(1)} %copy-done.1), kind=kOutput, calls=%fused_computation.295 | convolution fusion | flops 537657344 | bytes 4456448 | tf_op jit(solution)/shard_map/ij,sid->sjd/dot_general | solution.py:163
  82.5 2.9 %fusion.22 = bf16[2,256,512]{2,1,0:T(8,128)(2,1)} fusion(bf16[2,256,512]{2,1,0:T(8,128)(2,1)} %multiply_convert_fusion.1, bf16[2,256,512]{2,1,0:T(8,128)(2,1)} %copy-done.12, f32[2,512,512]{2,1,0:T(8,128)} %get-tuple-element.51, bf16[1,1024,512]{2,1,0:T(8,128)(2,1)S(1)} %copy-done.1), kind=kOutput, calls=%fused_computation.54 | convolution fusion | flops 269484032 | bytes 3145728 | tf_op jit(solution)/shard_map/sip,vp->siv/dot_general | solution.py:161
  97.6 3.6 %fusion.204 = (bf16[2,512,512]{2,1,0:T(8,128)(2,1)}, f32[2,512,512]{2,1,0:T(8,128)}) fusion(bf16[256,512,1]{1,0,2:T(8,128)(2,1)S(1)} %reshape.379, bf16[2,256,512]{2,1,0:T(8,128)(2,1)} %multiply_convert_fusion, bf16[1,1024,512]{2,1,0:T(8,128)(2,1)S(1)} %copy-done.1), kind=kOutput, calls=%fused_computation.296 | convolution fusion | flops 537657344 | bytes 4456448 | tf_op jit(solution)/shard_map/ij,sid->sjd/dot_general | solution.py:163
  101.2 2.2 %fusion.23 = bf16[2,256,512]{2,1,0:T(8,128)(2,1)S(1)} fusion(bf16[2,256,512]{2,1,0:T(8,128)(2,1)} %multiply_convert_fusion, bf16[2,256,512]{2,1,0:T(8,128)(2,1)} %copy-done.14, f32[2,512,512]{2,1,0:T(8,128)} %get-tuple-element.53, bf16[1,1024,512]{2,1,0:T(8,128)(2,1)S(1)} %copy-done.1), kind=kOutput, calls=%fused_computation.55 | convolution fusion | flops 269484032 | bytes 3145728 | tf_op jit(solution)/shard_map/sip,vp->siv/dot_general | solution.py:161
  107.4 2.7 %select_select_fusion.1 = (bf16[2,256,512]{2,1,0:T(8,128)(2,1)S(1)}, bf16[1,2,256,512]{3,2,1,0:T(8,128)(2,1)}) fusion(bf16[2,256,512]{2,1,0:T(8,128)(2,1)S(1)} %copy-done.21, bf16[2,256,512]{2,1,0:T(8,128)(2,1)} %collective-permute-done.8, bf16[2,256,512]{2,1,0:T(8,128)(2,1)S(1)} %copy-done.9, bf16[2,256,512]{2,1,0:T(8,128)(2,1)} %collective-permute-done.2, ...), kind=kLoop, calls=%fused_computation.205 | loop fusion | flops 3145728 | bytes 5773315 | tf_op jit(solution)/shard_map/select_n | solution.py:197
  110.1 38.4 %collective-permute-done.18 = bf16[2,128,512]{2,1,0:T(8,128)(2,1)S(1)} collective-permute-done((bf16[2,128,512]{2,1,0:T(8,128)(2,1)S(1)}, bf16[2,128,512]{2,1,0:T(8,128)(2,1)S(1)}, u32[]{:S(2)}, u32[]{:S(2)}) %collective-permute-start.18) | collective-permute-done | bytes 262176 | tf_op jit(solution)/shard_map/ppermute | solution.py:181
  148.6 4.5 %collective-permute-done.19 = bf16[2,128,512]{2,1,0:T(8,128)(2,1)S(1)} collective-permute-done((bf16[2,128,512]{2,1,0:T(8,128)(2,1)S(1)}, bf16[2,128,512]{2,1,0:T(8,128)(2,1)S(1)}, u32[]{:S(2)}, u32[]{:S(2)}) %collective-permute-start.19) | collective-permute-done | bytes 262176 | tf_op jit(solution)/shard_map/ppermute | solution.py:182
  162.5 2.1 %collective-permute-start.22 = (bf16[2,256,512]{2,1,0:T(8,128)(2,1)}, bf16[2,256,512]{2,1,0:T(8,128)(2,1)}, u32[]{:S(2)}, u32[]{:S(2)}) collective-permute-start(bf16[2,256,512]{2,1,0:T(8,128)(2,1)} %select_select_fusion.2), channel_id=1, source_target_pairs={{0,1},{1,2},{2,3},{4,5},{5,6},{6,7},{8,9},{9,10},{10,11},{12,13},{... | collective-permute-start | bytes 1572872 | tf_op jit(solution)/shard_map/ppermute | solution.py:236
  164.6 2.2 %fusion.207 = (bf16[2,512,512]{2,1,0:T(8,128)(2,1)S(1)}, f32[2,512,512]{2,1,0:T(8,128)}) fusion(bf16[256,512,1]{1,0,2:T(8,128)(2,1)S(1)} %reshape.379, bf16[2,256,512]{2,1,0:T(8,128)(2,1)S(1)} %fusion.24, bf16[1,1024,512]{2,1,0:T(8,128)(2,1)S(1)} %copy-done.1), kind=kOutput, calls=%fused_computation.297 | convolution fusion | flops 537657344 | bytes 4456448 | tf_op jit(solution)/shard_map/ij,sid->sjd/dot_general | solution.py:163
  167.7 3.8 %collective-permute-start.20 = (bf16[2,128,512]{2,1,0:T(8,128)(2,1)}, bf16[2,128,512]{2,1,0:T(8,128)(2,1)S(1)}, u32[]{:S(2)}, u32[]{:S(2)}) collective-permute-start(bf16[2,128,512]{2,1,0:T(8,128)(2,1)} %get-tuple-element.20), channel_id=1, source_target_pairs={{0,12},{4,0},{8,4},{12,8},{16,28},{20,16},{24,20},{28,24}} | collective-permute-start | bytes 786440 | tf_op jit(solution)/shard_map/ppermute | solution.py:189
  171.5 2.1 collective-permute-start.21
  173.5 5.5 %collective-permute-done.23 = bf16[2,400,512]{2,1,0:T(8,128)(2,1)} collective-permute-done((bf16[2,400,512]{2,1,0:T(8,128)(2,1)}, bf16[2,400,512]{2,1,0:T(8,128)(2,1)}, u32[]{:S(2)}, u32[]{:S(2)}) %collective-permute-start.23) | collective-permute-done | bytes 819232 | tf_op jit(solution)/shard_map/ppermute | solution.py:41
  179.0 2.6 %fusion = f32[1,2,400,512]{3,2,1,0:T(8,128)S(1)} fusion(bf16[2,400,512]{2,1,0:T(8,128)(2,1)} %collective-permute-done.23, f32[2,2,400,512]{3,2,0,1:T(8,128)} %copy-done.2, pred[]{:T(512)S(6)} %eq.126), kind=kLoop, calls=%fused_computation.3 | loop fusion | flops 1228800 | bytes 5734401 | tf_op jit(solution)/shard_map/reshape | solution.py:35
  182.4 2.3 %collective-permute-start.24 = (bf16[1,400,512]{2,1,0:T(8,128)(2,1)}, bf16[1,400,512]{2,1,0:T(8,128)(2,1)}, u32[]{:S(2)}, u32[]{:S(2)}) collective-permute-start(bf16[1,400,512]{2,1,0:T(8,128)(2,1)} %fusion.150), channel_id=1, source_target_pairs={{0,8},{4,12},{8,0},{12,4},{1,9},{5,13},{9,1},{13,5},{2,10},{6,14},... | collective-permute-start | bytes 1228808 | tf_op jit(solution)/shard_map/ppermute | solution.py:41
  184.7 2.8 %collective-permute-done.21 = bf16[2,128,512]{2,1,0:T(8,128)(2,1)} collective-permute-done((bf16[2,128,512]{2,1,0:T(8,128)(2,1)}, bf16[2,128,512]{2,1,0:T(8,128)(2,1)}, u32[]{:S(2)}, u32[]{:S(2)}) %collective-permute-start.21) | collective-permute-done | bytes 262176 | tf_op jit(solution)/shard_map/ppermute | solution.py:190
  191.8 12.1 %collective-permute-done.24 = bf16[1,400,512]{2,1,0:T(8,128)(2,1)} collective-permute-done((bf16[1,400,512]{2,1,0:T(8,128)(2,1)}, bf16[1,400,512]{2,1,0:T(8,128)(2,1)}, u32[]{:S(2)}, u32[]{:S(2)}) %collective-permute-start.24) | collective-permute-done | bytes 409632 | tf_op jit(solution)/shard_map/ppermute | solution.py:41
  (243 shorter events, 81.6 us)
Async XLA Ops:
  4.8 11.8 %collective-permute-start.1 = (bf16[2,128,512]{1,2,0:T(8,128)(2,1)S(1)}, bf16[2,128,512]{1,2,0:T(8,128)(2,1)S(1)}, u32[]{:S(2)}, u32[]{:S(2)}) collective-permute-start(bf16[2,128,512]{1,2,0:T(8,128)(2,1)S(1)} %bitcast.287), channel_id=1, source_target_pairs={{0,12},{4,0},{8,4},{12,8},{16,28},{20,16},{24,20},{28,24}} | collective-permute-start | bytes 786440 | tf_op jit(solution)/shard_map/ppermute | solution.py:126
  12.6 10.3 %collective-permute-start = (bf16[2,128,512]{1,2,0:T(8,128)(2,1)}, bf16[2,128,512]{1,2,0:T(8,128)(2,1)S(1)}, u32[]{:S(2)}, u32[]{:S(2)}) collective-permute-start(bf16[2,128,512]{1,2,0:T(8,128)(2,1)} %bitcast.288), channel_id=1, source_target_pairs={{0,4},{4,8},{8,12},{12,0},{16,20},{20,24},{24,28},{28,16}} | collective-permute-start | bytes 786440 | tf_op jit(solution)/shard_map/ppermute | solution.py:125
  26.0 12.3 %collective-permute-start.2 = (bf16[2,256,512]{2,1,0:T(8,128)(2,1)}, bf16[2,256,512]{2,1,0:T(8,128)(2,1)}, u32[]{:S(2)}, u32[]{:S(2)}) collective-permute-start(bf16[2,256,512]{2,1,0:T(8,128)(2,1)} %add_convert_fusion.3), channel_id=1, source_target_pairs={{0,1},{4,5},{8,9},{12,13},{16,17},{20,21},{24,25},{28,29}} | collective-permute-start | bytes 1572872 | tf_op jit(solution)/shard_map/ppermute | solution.py:136
  30.0 5.5 %collective-permute-start.3 = (bf16[2,128,512]{2,1,0:T(8,128)(2,1)}, bf16[2,128,512]{2,1,0:T(8,128)(2,1)}, u32[]{:S(2)}, u32[]{:S(2)}) collective-permute-start(bf16[2,128,512]{2,1,0:T(8,128)(2,1)} %get-tuple-element.34), channel_id=1, source_target_pairs={{0,5},{4,9},{8,13},{12,1},{16,21},{20,25},{24,29},{28,17}} | collective-permute-start | bytes 786440 | tf_op jit(solution)/shard_map/ppermute | solution.py:137
  31.9 6.3 %collective-permute-start.4 = (bf16[2,128,512]{2,1,0:T(8,128)(2,1)}, bf16[2,128,512]{2,1,0:T(8,128)(2,1)}, u32[]{:S(2)}, u32[]{:S(2)}) collective-permute-start(bf16[2,128,512]{2,1,0:T(8,128)(2,1)} %get-tuple-element.35), channel_id=1, source_target_pairs={{0,13},{4,1},{8,5},{12,9},{16,29},{20,17},{24,21},{28,25}} | collective-permute-start | bytes 786440 | tf_op jit(solution)/shard_map/ppermute | solution.py:138
  44.9 2.2 %collective-permute-start.5 = (bf16[2,256,512]{2,1,0:T(8,128)(2,1)S(1)}, bf16[2,256,512]{2,1,0:T(8,128)(2,1)S(1)}, u32[]{:S(2)}, u32[]{:S(2)}) collective-permute-start(bf16[2,256,512]{2,1,0:T(8,128)(2,1)S(1)} %add_convert_fusion.2), channel_id=1, source_target_pairs={{1,2},{5,6},{9,10},{13,14},{17,18},{21,22},{25,26},{29,30}} | collective-permute-start | bytes 1572872 | tf_op jit(solution)/shard_map/ppermute | solution.py:136
  45.6 1.4 collective-permute-start.6
  51.1 6.2 %collective-permute-start.8 = (bf16[2,256,512]{2,1,0:T(8,128)(2,1)}, bf16[2,256,512]{2,1,0:T(8,128)(2,1)}, u32[]{:S(2)}, u32[]{:S(2)}) collective-permute-start(bf16[2,256,512]{2,1,0:T(8,128)(2,1)} %add_convert_fusion.1), channel_id=1, source_target_pairs={{2,3},{6,7},{10,11},{14,15},{18,19},{22,23},{26,27},{30,31}} | collective-permute-start | bytes 1572872 | tf_op jit(solution)/shard_map/ppermute | solution.py:136
  54.5 2.8 %collective-permute-start.9 = (bf16[2,128,512]{2,1,0:T(8,128)(2,1)}, bf16[2,128,512]{2,1,0:T(8,128)(2,1)}, u32[]{:S(2)}, u32[]{:S(2)}) collective-permute-start(bf16[2,128,512]{2,1,0:T(8,128)(2,1)} %get-tuple-element.30), channel_id=1, source_target_pairs={{2,7},{6,11},{10,15},{14,3},{18,23},{22,27},{26,31},{30,19}} | collective-permute-start | bytes 786440 | tf_op jit(solution)/shard_map/ppermute | solution.py:137
  55.8 1.5 collective-permute-start.10
  72.3 2.7 %collective-permute-start.11 = (bf16[2,256,512]{2,1,0:T(8,128)(2,1)S(1)}, bf16[2,256,512]{2,1,0:T(8,128)(2,1)S(1)}, u32[]{:S(2)}, u32[]{:S(2)}) collective-permute-start(bf16[2,256,512]{2,1,0:T(8,128)(2,1)S(1)} %fusion.21), channel_id=1, source_target_pairs={{3,2},{7,6},{11,10},{15,14},{19,18},{23,22},{27,26},{31,30}} | collective-permute-start | bytes 1572872 | tf_op jit(solution)/shard_map/ppermute | solution.py:180
  73.2 1.6 collective-permute-start.12
  74.1 0.8 collective-permute-start.13
  85.4 7.2 %collective-permute-start.14 = (bf16[2,256,512]{2,1,0:T(8,128)(2,1)}, bf16[2,256,512]{2,1,0:T(8,128)(2,1)}, u32[]{:S(2)}, u32[]{:S(2)}) collective-permute-start(bf16[2,256,512]{2,1,0:T(8,128)(2,1)} %fusion.22), channel_id=1, source_target_pairs={{2,1},{6,5},{10,9},{14,13},{18,17},{22,21},{26,25},{30,29}} | collective-permute-start | bytes 1572872 | tf_op jit(solution)/shard_map/ppermute | solution.py:180
  87.7 2.7 %collective-permute-start.15 = (bf16[2,128,512]{2,1,0:T(8,128)(2,1)}, bf16[2,128,512]{2,1,0:T(8,128)(2,1)}, u32[]{:S(2)}, u32[]{:S(2)}) collective-permute-start(bf16[2,128,512]{2,1,0:T(8,128)(2,1)} %get-tuple-element.24), channel_id=1, source_target_pairs={{2,13},{6,1},{10,5},{14,9},{18,29},{22,17},{26,21},{30,25}} | collective-permute-start | bytes 786440 | tf_op jit(solution)/shard_map/ppermute | solution.py:181
  89.0 2.5 %collective-permute-start.16 = (bf16[2,128,512]{2,1,0:T(8,128)(2,1)}, bf16[2,128,512]{2,1,0:T(8,128)(2,1)}, u32[]{:S(2)}, u32[]{:S(2)}) collective-permute-start(bf16[2,128,512]{2,1,0:T(8,128)(2,1)} %get-tuple-element.25), channel_id=1, source_target_pairs={{2,5},{6,9},{10,13},{14,1},{18,21},{22,25},{26,29},{30,17}} | collective-permute-start | bytes 786440 | tf_op jit(solution)/shard_map/ppermute | solution.py:182
  103.4 49.8 %collective-permute-start.17 = (bf16[2,256,512]{2,1,0:T(8,128)(2,1)S(1)}, bf16[2,256,512]{2,1,0:T(8,128)(2,1)S(1)}, u32[]{:S(2)}, u32[]{:S(2)}) collective-permute-start(bf16[2,256,512]{2,1,0:T(8,128)(2,1)S(1)} %fusion.23), channel_id=1, source_target_pairs={{1,0},{5,4},{9,8},{13,12},{17,16},{21,20},{25,24},{29,28}} | collective-permute-start | bytes 1572872 | tf_op jit(solution)/shard_map/ppermute | solution.py:180
  104.7 43.8 %collective-permute-start.18 = (bf16[2,128,512]{2,1,0:T(8,128)(2,1)S(1)}, bf16[2,128,512]{2,1,0:T(8,128)(2,1)S(1)}, u32[]{:S(2)}, u32[]{:S(2)}) collective-permute-start(bf16[2,128,512]{2,1,0:T(8,128)(2,1)S(1)} %get-tuple-element.22), channel_id=1, source_target_pairs={{1,12},{5,0},{9,4},{13,8},{17,28},{21,16},{25,20},{29,24}} | collective-permute-start | bytes 786440 | tf_op jit(solution)/shard_map/ppermute | solution.py:181
  106.0 47.1 %collective-permute-start.19 = (bf16[2,128,512]{2,1,0:T(8,128)(2,1)S(1)}, bf16[2,128,512]{2,1,0:T(8,128)(2,1)S(1)}, u32[]{:S(2)}, u32[]{:S(2)}) collective-permute-start(bf16[2,128,512]{2,1,0:T(8,128)(2,1)S(1)} %get-tuple-element.23), channel_id=1, source_target_pairs={{1,4},{5,8},{9,12},{13,0},{17,20},{21,24},{25,28},{29,16}} | collective-permute-start | bytes 786440 | tf_op jit(solution)/shard_map/ppermute | solution.py:182
  160.7 18.3 %collective-permute-start.23 = (bf16[2,400,512]{2,1,0:T(8,128)(2,1)}, bf16[2,400,512]{2,1,0:T(8,128)(2,1)}, u32[]{:S(2)}, u32[]{:S(2)}) collective-permute-start(bf16[2,400,512]{2,1,0:T(8,128)(2,1)} %fusion.80), channel_id=1, source_target_pairs={{0,4},{4,0},{8,12},{12,8},{1,5},{5,1},{9,13},{13,9},{2,6},{6,2},{1... | collective-permute-start | bytes 2457608 | tf_op jit(solution)/shard_map/ppermute | solution.py:41
  162.5 26.4 %collective-permute-start.22 = (bf16[2,256,512]{2,1,0:T(8,128)(2,1)}, bf16[2,256,512]{2,1,0:T(8,128)(2,1)}, u32[]{:S(2)}, u32[]{:S(2)}) collective-permute-start(bf16[2,256,512]{2,1,0:T(8,128)(2,1)} %select_select_fusion.2), channel_id=1, source_target_pairs={{0,1},{1,2},{2,3},{4,5},{5,6},{6,7},{8,9},{9,10},{10,11},{12,13},{... | collective-permute-start | bytes 1572872 | tf_op jit(solution)/shard_map/ppermute | solution.py:236
  167.7 21.0 %collective-permute-start.20 = (bf16[2,128,512]{2,1,0:T(8,128)(2,1)}, bf16[2,128,512]{2,1,0:T(8,128)(2,1)S(1)}, u32[]{:S(2)}, u32[]{:S(2)}) collective-permute-start(bf16[2,128,512]{2,1,0:T(8,128)(2,1)} %get-tuple-element.20), channel_id=1, source_target_pairs={{0,12},{4,0},{8,4},{12,8},{16,28},{20,16},{24,20},{28,24}} | collective-permute-start | bytes 786440 | tf_op jit(solution)/shard_map/ppermute | solution.py:189
  171.5 16.0 %collective-permute-start.21 = (bf16[2,128,512]{2,1,0:T(8,128)(2,1)}, bf16[2,128,512]{2,1,0:T(8,128)(2,1)}, u32[]{:S(2)}, u32[]{:S(2)}) collective-permute-start(bf16[2,128,512]{2,1,0:T(8,128)(2,1)} %get-tuple-element.21), channel_id=1, source_target_pairs={{0,4},{4,8},{8,12},{12,0},{16,20},{20,24},{24,28},{28,16}} | collective-permute-start | bytes 786440 | tf_op jit(solution)/shard_map/ppermute | solution.py:190
  182.4 21.4 %collective-permute-start.24 = (bf16[1,400,512]{2,1,0:T(8,128)(2,1)}, bf16[1,400,512]{2,1,0:T(8,128)(2,1)}, u32[]{:S(2)}, u32[]{:S(2)}) collective-permute-start(bf16[1,400,512]{2,1,0:T(8,128)(2,1)} %fusion.150), channel_id=1, source_target_pairs={{0,8},{4,12},{8,0},{12,4},{1,9},{5,13},{9,1},{13,5},{2,10},{6,14},... | collective-permute-start | bytes 1228808 | tf_op jit(solution)/shard_map/ppermute | solution.py:41
  (56 other events, 212.1 us)
